TPU v7x, 32 devices: a whole 2x2x4 slice. The times are simulated.
32 devices in a mesh: axial: 8 (over y, x, core), radial: 4 (over z).
Axes of the slice: x: 2, y: 2, z: 4, core: 2. Of those that a mesh axis runs over, the one named last changes fastest.
Arguments:
- composition_deviations: float32 [38, 1024, 512], P(None, 'axial', 'radial'), may hold values from -6 to 6
- flow_speed_vector: float32 [2, 1024, 512], P(None, 'axial', 'radial'), may hold values from -1 to 1
- thermal_field: float32 [1024, 512], P('axial', 'radial'), may hold values from 0.4 to 4
- linearized_kinetics_operator: float32 [38, 38], replicated, may hold values from -0.5 to 0.5
- frozen_jacobian_inverse_addend: float32 [38, 38], replicated, may hold values from -0.25 to 0.25
- rigid_block_indicator: int32 [512, 4], P('axial', 'radial'), may hold values from 0 to 1, as said below
- molar_absorptivity_table: float32 [4, 38], replicated, may hold values from -1 to 1
- spokewise_sightline_length: float32 [512], P('radial'), may hold values from 0.3 to 3
- sightline_lengthwise_index: int32 [4, 32768], replicated, may hold values from 0 to 1023
- observed_absorbance_traces: float32 [4, 32768], P(None, ('axial', 'radial')), may hold values from -6 to 6
Outputs:
- species_out: float32 [38, 1024, 512], P(None, 'axial', 'radial')
- misfit: float32 [4, 32768], P(None, ('axial', 'radial'))
Inputs may be any that keep to these rules, and one draw needn't show every extreme that they name: `rigid_block_indicator`: in each radial column of tiles, the tiles of 2 cyclically consecutive axial devices are all stiff and every other axial device holds exactly 8 stiff tiles, so the column holds 176 stiff tiles.
All inputs are finite; a program needn't handle non-finite values.
Results may differ from a plain program's by a relative error of at most 0.0001.
Values sent between devices are 32-bit elements; how exact they have to be, the bound alone decides.
No kernel may reach another device: no remote copies, remote signals or barrier semaphores. Data moves between devices by JAX's collectives and lax.ppermute only.
A program may use at most 192 MiB of HBM per device.

v0:
```python
import math

import jax
import jax.numpy as jnp
from jax import lax
from jax.sharding import PartitionSpec as P
from jax.experimental import pallas as pl
from jax.experimental.pallas import tpu as pltpu

TILE_ROWS = 2
ITERS = 3


TIME_STEP = 0.4
CHEM_STEP = 0.5
ARRHENIUS_BARRIER = 1.0
WENO_EPS = 1e-06
HIGHEST = lax.Precision.HIGHEST
CHEMISTRY_PRECISION = lax.Precision.HIGH


def edge_layers(shard, axis, dim, width):
    peers, length = (lax.axis_size(axis), shard.shape[dim])
    up = [(i, i + 1) for i in range(peers - 1)]
    down = [(j, i) for i, j in up]
    last = lax.slice_in_dim(shard, length - width, length, axis=dim)
    initial = lax.slice_in_dim(shard, 0, width, axis=dim)
    return lax.ppermute(last, axis, up), lax.ppermute(initial, axis, down)


def weno_side(minus_two, minus_one, centre, plus_one, plus_two):
    curve_zero = minus_two - 2.0 * minus_one + centre
    curve_one = minus_one - 2.0 * centre + plus_one
    curve_two = centre - 2.0 * plus_one + plus_two
    slope_zero = minus_two - 4.0 * minus_one + 3.0 * centre
    slope_one = minus_one - plus_one
    slope_two = 3.0 * centre - 4.0 * plus_one + plus_two
    beta_zero = 13.0 / 12.0 * curve_zero * curve_zero + 0.25 * slope_zero * slope_zero
    beta_one = 13.0 / 12.0 * curve_one * curve_one + 0.25 * slope_one * slope_one
    beta_two = 13.0 / 12.0 * curve_two * curve_two + 0.25 * slope_two * slope_two
    guard_zero = WENO_EPS + beta_zero
    guard_one = WENO_EPS + beta_one
    guard_two = WENO_EPS + beta_two
    guard_zero = guard_zero * guard_zero
    guard_one = guard_one * guard_one
    guard_two = guard_two * guard_two
    cross_zero = guard_one * guard_two
    cross_one = 6.0 * (guard_zero * guard_two)
    cross_two = 3.0 * (guard_zero * guard_one)
    blended = cross_zero * (2.0 * minus_two - 7.0 * minus_one + 11.0 * centre)
    blended = blended + cross_one * (-minus_one + 5.0 * centre + 2.0 * plus_one)
    blended = blended + cross_two * (2.0 * centre + 5.0 * plus_one - plus_two)
    return blended / (6.0 * (cross_zero + cross_one + cross_two))


HALO = 8
CHUNK = 8


def upwind_divergence(ext_ref, vel_ref, flux_ref, rows):
    faces = flux_ref.shape[0]
    for low in range(0, faces, CHUNK):

        def cut(offset):
            return ext_ref[pl.ds(HALO - 3 + offset + low, CHUNK), :]

        face_speed = 0.5 * (
            vel_ref[pl.ds(HALO - 1 + low, CHUNK), :] + vel_ref[pl.ds(HALO + low, CHUNK), :]
        )
        forward = face_speed >= 0.0
        stencil = [
            jnp.where(forward, cut(lower), cut(upper))
            for lower, upper in ((0, 5), (1, 4), (2, 3), (3, 2), (4, 1))
        ]
        flux_ref[pl.ds(low, CHUNK), :] = face_speed * weno_side(*stencil)
    return flux_ref[pl.ds(1, rows), :] - flux_ref[pl.ds(0, rows), :]


def transport_kernel(
    field_ref, speed_ref, top_ref, top_speed_ref, bottom_ref, bottom_speed_ref,
    left_ref, left_speed_ref, right_ref, right_speed_ref, out_ref,
    ext_ref, vel_ref, flux_ref,
):
    rows, cols = field_ref.shape[1], field_ref.shape[2]
    span = ext_ref.shape[0]
    tail = span - HALO - rows
    zeros = jnp.zeros((tail - HALO, cols), jnp.float32)
    field = field_ref[0]

    ext_ref[pl.ds(0, HALO), :] = top_ref[0]
    ext_ref[pl.ds(HALO, rows), :] = field
    ext_ref[pl.ds(HALO + rows, HALO), :] = bottom_ref[0]
    ext_ref[pl.ds(2 * HALO + rows, tail - HALO), :] = zeros
    vel_ref[pl.ds(0, HALO), :] = top_speed_ref[0]
    vel_ref[pl.ds(HALO, rows), :] = speed_ref[0]
    vel_ref[pl.ds(HALO + rows, HALO), :] = bottom_speed_ref[0]
    vel_ref[pl.ds(2 * HALO + rows, tail - HALO), :] = zeros
    along_axial = upwind_divergence(ext_ref, vel_ref, flux_ref, rows)

    ext_ref[pl.ds(0, HALO), :] = left_ref[0]
    ext_ref[pl.ds(HALO, cols), :] = field.T
    ext_ref[pl.ds(HALO + cols, HALO), :] = right_ref[0]
    vel_ref[pl.ds(0, HALO), :] = left_speed_ref[0]
    vel_ref[pl.ds(HALO, cols), :] = speed_ref[1].T
    vel_ref[pl.ds(HALO + cols, HALO), :] = right_speed_ref[0]
    along_radial = upwind_divergence(ext_ref, vel_ref, flux_ref, cols).T

    moved = field - TIME_STEP * (along_axial + along_radial)
    out_ref[:, pl.ds(pl.program_id(0), 1), :] = moved[:, None, :]


def transport(species, speed, width=3):
    species_count, rows, cols = species.shape
    assert rows == cols and rows % CHUNK == 0
    axial_edges = jnp.concatenate([species, speed[0:1]], axis=0)
    top, bottom = edge_layers(axial_edges, "axial", 1, width)
    radial_edges = jnp.swapaxes(jnp.concatenate([species, speed[1:2]], axis=0), 1, 2)
    left, right = edge_layers(radial_edges, "radial", 1, width)
    before = ((0, 0), (HALO - width, 0), (0, 0))
    after = ((0, 0), (0, HALO - width), (0, 0))
    top, left = (jnp.pad(top, before), jnp.pad(left, before))
    bottom, right = (jnp.pad(bottom, after), jnp.pad(right, after))
    faces = rows + CHUNK
    span = HALO + faces + HALO
    plane = pl.BlockSpec((1, rows, cols), lambda s: (s, 0, 0))
    speeds = pl.BlockSpec((2, rows, cols), lambda s: (0, 0, 0))
    edge = pl.BlockSpec((1, HALO, cols), lambda s: (s, 0, 0))
    edge_speed = pl.BlockSpec((1, HALO, cols), lambda s: (species_count, 0, 0))
    moved_rows = pl.pallas_call(
        transport_kernel,
        grid=(species_count,),
        in_specs=[plane, speeds] + [edge, edge_speed] * 4,
        out_specs=pl.BlockSpec((rows, species_count, cols), lambda s: (0, 0, 0)),
        out_shape=jax.ShapeDtypeStruct((rows, species_count, cols), jnp.float32),
        scratch_shapes=[
            pltpu.VMEM((span, cols), jnp.float32),
            pltpu.VMEM((span, cols), jnp.float32),
            pltpu.VMEM((faces, cols), jnp.float32),
        ],
    )(species, speed, top, top, bottom, bottom, left, left, right, right)
    return jnp.transpose(moved_rows, (1, 0, 2))


def kinetics_advance(
    starting_composition_field,
    thermal_field,
    linearized_kinetics_operator,
    frozen_jacobian_inverse_addend,
):
    acceleration_factor = jnp.exp(-ARRHENIUS_BARRIER / thermal_field)
    current = starting_composition_field
    for newton_step in range(ITERS):
        source = jnp.tensordot(
            linearized_kinetics_operator, current, axes=(1, 0), precision=CHEMISTRY_PRECISION
        ) - jnp.tanh(current)
        defect = current - starting_composition_field - CHEM_STEP * acceleration_factor * source
        current = (
            current
            - defect
            - jnp.tensordot(frozen_jacobian_inverse_addend, defect, axes=(1, 0), precision=CHEMISTRY_PRECISION)
        )
    return current


def absorbance_profile(field, molar_absorptivity_table, spokewise_sightline_length):
    mixed = jnp.tensordot(molar_absorptivity_table, field, axes=(1, 0), precision=HIGHEST)
    return jnp.dot(mixed, spokewise_sightline_length, precision=HIGHEST)


def butterfly_sum(part, axis):
    peers, stride = (lax.axis_size(axis), 1)
    if peers & (peers - 1):
        return lax.psum(part, axis)
    while stride < peers:
        pairs = [(j, j ^ stride) for j in range(peers)]
        part = part + lax.ppermute(part, axis, pairs)
        stride *= 2
    return part


def doubling_gather(part, axis):
    peers, stride = (lax.axis_size(axis), 1)
    if peers & (peers - 1):
        return lax.all_gather(part, axis, axis=1, tiled=True)
    position = lax.axis_index(axis)
    blocks = part[None]
    while stride < peers:
        pairs = [(j, j ^ stride) for j in range(peers)]
        other = lax.ppermute(blocks, axis, pairs)
        upper = (position // stride) % 2 == 1
        blocks = jnp.where(
            upper, jnp.concatenate([other, blocks], 0), jnp.concatenate([blocks, other], 0)
        )
        stride *= 2
    return jnp.transpose(blocks, (1, 0, 2)).reshape(part.shape[0], -1)


def gathered_profile(profile):
    return doubling_gather(butterfly_sum(profile, "radial"), "axial")


def local(
    composition_deviations,
    flow_speed_vector,
    thermal_field,
    linearized_kinetics_operator,
    frozen_jacobian_inverse_addend,
    rigid_block_indicator,
    molar_absorptivity_table,
    spokewise_sightline_length,
    sightline_lengthwise_index,
    observed_absorbance_traces,
):
    advected_composition_field = transport(composition_deviations, flow_speed_vector)
    combusted_composition_field = kinetics_advance(
        advected_composition_field,
        thermal_field,
        linearized_kinetics_operator,
        frozen_jacobian_inverse_addend,
    )
    flag_cells = jnp.repeat(
        jnp.repeat(rigid_block_indicator, TILE_ROWS, axis=0),
        advected_composition_field.shape[2],
        axis=1,
    )
    species_out = jnp.where(
        flag_cells[None] > 0, combusted_composition_field, advected_composition_field
    )
    path_scale = 1.0 / math.sqrt(advected_composition_field.shape[2] * lax.axis_size("radial"))
    profile = (
        absorbance_profile(species_out, molar_absorptivity_table, spokewise_sightline_length)
        * path_scale
    )
    whole_profile = gathered_profile(profile)
    device = lax.axis_index(("axial", "radial"))
    sample_count = observed_absorbance_traces.shape[1]
    own_rows = lax.dynamic_slice_in_dim(
        sightline_lengthwise_index, device * sample_count, sample_count, 1
    )
    cells = lax.broadcasted_iota(jnp.int32, (1, whole_profile.shape[1], 1), 1)
    values = jnp.sum(
        jnp.where(own_rows[:, None, :] == cells, whole_profile[:, :, None], 0.0), axis=1
    )
    return (species_out, values - observed_absorbance_traces)


def solution(mesh):
    in_specs = (
        P(None, "axial", "radial"),
        P(None, "axial", "radial"),
        P("axial", "radial"),
        P(),
        P(),
        P("axial", "radial"),
        P(),
        P("radial"),
        P(),
        P(None, ("axial", "radial")),
    )
    out_specs = (P(None, "axial", "radial"), P(None, ("axial", "radial")))
    return jax.shard_map(local, mesh=mesh, in_specs=in_specs, out_specs=out_specs, check_vma=False)
```

profile of v0, /device:TPU:0, one launch (start us, length us, event | category | flops | bytes accessed | tf_op | source)
XLA Modules:
  0.0 88.8 jit_solution(14991809824655142214)
XLA Ops:
  0.6 0.9 %fusion.40 = (f32[1,128,128]{2,1,0:T(8,128)S(1)}, f32[1,128,128]{2,1,0:T(8,128)S(1)}) fusion(f32[2,128,128]{2,1,0:T(8,128)} %speed_ref.1), kind=kLoop, calls=%fused_computation.55 | loop fusion | bytes 262144 | tf_op jit(solution)/shard_map/slice | solution.py:117
  1.7 3.1 %copy.19 = f32[38,128,128]{1,2,0:T(8,128)} copy(f32[38,128,128]{2,1,0:T(8,128)} %field_ref.1) | data formatting | bytes 4980736 | tf_op args[0]
  4.8 2.0 %maximum_bitcast_fusion = f32[39,128,128]{2,1,0:T(8,128)S(1)} fusion(f32[1,128,128]{1,2,0:T(8,128)S(1)} %copy.23, f32[38,128,128]{1,2,0:T(8,128)} %copy.19), kind=kLoop, calls=%fused_computation.24 | loop fusion | flops 638976 | bytes 5111808 | tf_op jit(solution)/shard_map/transpose | solution.py:117
  6.9 4.9 %collective-permute-start.2 = (f32[39,3,128]{2,1,0:T(4,128)S(1)}, f32[39,3,128]{2,1,0:T(4,128)S(1)}, u32[]{:S(2)}, u32[]{:S(2)}) collective-permute-start(f32[39,3,128]{2,1,0:T(4,128)S(1)} %get-tuple-element.9), channel_id=1, source_target_pairs={{0,1},{1,2},{2,3},{4,5},{5,6},{6,7},{8,9},{9,10},{10,11},{12,13},{... | collective-permute-start | bytes 179720 | tf_op jit(solution)/shard_map/ppermute | solution.py:28
  11.9 1.3 %collective-permute-start.3 = (f32[39,3,128]{2,1,0:T(4,128)S(1)}, f32[39,3,128]{2,1,0:T(4,128)S(1)}, u32[]{:S(2)}, u32[]{:S(2)}) collective-permute-start(f32[39,3,128]{2,1,0:T(4,128)S(1)} %get-tuple-element.8), channel_id=1, source_target_pairs={{1,0},{2,1},{3,2},{5,4},{6,5},{7,6},{9,8},{10,9},{11,10},{13,12},{... | collective-permute-start | bytes 179720 | tf_op jit(solution)/shard_map/ppermute | solution.py:28
  13.2 0.7 pad_maximum_fusion
  13.9 1.5 %collective-permute-start = (f32[39,3,128]{2,1,0:T(4,128)}, f32[39,3,128]{2,1,0:T(4,128)S(1)}, u32[]{:S(2)}, u32[]{:S(2)}) collective-permute-start(f32[39,3,128]{2,1,0:T(4,128)} %get-tuple-element.11), channel_id=1, source_target_pairs={{0,4},{4,8},{8,12},{12,16},{16,20},{20,24},{24,28},{1,5},{5,9},{9,... | collective-permute-start | bytes 179720 | tf_op jit(solution)/shard_map/ppermute | solution.py:28
  15.3 1.3 %collective-permute-start.1 = (f32[39,3,128]{2,1,0:T(4,128)}, f32[39,3,128]{2,1,0:T(4,128)S(1)}, u32[]{:S(2)}, u32[]{:S(2)}) collective-permute-start(f32[39,3,128]{2,1,0:T(4,128)} %get-tuple-element.10), channel_id=1, source_target_pairs={{4,0},{8,4},{12,8},{16,12},{20,16},{24,20},{28,24},{5,1},{9,5},{13... | collective-permute-start | bytes 179720 | tf_op jit(solution)/shard_map/ppermute | solution.py:28
  16.9 0.7 pad.16.left_ref.left_speed_ref
  18.2 0.7 pad.17.right_ref.right_speed_ref
  18.9 0.7 pad.14.top_ref.top_speed_ref
  19.5 0.7 collective-permute-done.1
  20.2 0.7 pad.15.bottom_ref.bottom_speed_ref
  20.9 28.3 %shard_map.113 = f32[128,38,128]{2,1,0:T(8,128)} custom-call(f32[38,128,128]{2,1,0:T(8,128)} %field_ref.1, f32[2,128,128]{2,1,0:T(8,128)} %speed_ref.1, f32[39,8,128]{2,1,0:T(8,128)} %pad.14.top_ref.top_speed_ref, f32[39,8,128]{2,1,0:T(8,128)} %pad.14.top_ref.top_speed_ref, f32[39,8,128]{2,1,0:T(8,128)} %pad.15.bottom_ref.bottom_speed_ref, ...), custom_call_target="tpu_custom_call" | custom-call | tf_op jit(solution)/shard_map/pallas_call | solution.py:129
  49.2 3.1 %fusion.13 = f32[128,128,38]{1,2,0:T(8,128)S(1)} fusion(f32[128,38,128]{2,1,0:T(8,128)} %shard_map.113, f32[38,38]{1,0:T(8,128)S(1)} %copy-done.3), kind=kOutput, calls=%fused_computation.22 | convolution fusion | flops 141950976 | bytes 4986512 | tf_op jit(solution)/shard_map/dot_general | solution.py:153
  52.4 2.5 %bitcast_subtract_fusion.4 = f32[38,128,128]{2,0,1:T(8,128)S(1)} fusion(f32[128,128,38]{1,2,0:T(8,128)S(1)} %fusion.13, f32[128,38,128]{2,1,0:T(8,128)S(1)} %copy-done.1, f32[128,128]{1,0:T(8,128)S(1)} %exponential_multiply_fusion, f32[38,38]{1,0:T(8,128)S(1)} %copy-done.4), kind=kOutput, calls=%fused_computation.11 | convolution fusion | flops 148176896 | bytes 7542416 | tf_op jit(solution)/shard_map/dot_general | solution.py:160
  54.9 1.3 %fusion.32 = f32[128,128,38]{1,2,0:T(8,128)S(1)} fusion(f32[38,128,128]{2,0,1:T(8,128)S(1)} %bitcast_subtract_fusion.4, f32[38,38]{1,0:T(8,128)S(1)} %copy-done.3), kind=kOutput, calls=%fused_computation.40 | convolution fusion | flops 141950976 | bytes 4986512 | tf_op jit(solution)/shard_map/dot_general | solution.py:153
  56.2 2.9 %bitcast_subtract_fusion.2 = f32[38,128,128]{2,0,1:T(8,128)S(1)} fusion(f32[38,128,128]{2,0,1:T(8,128)S(1)} %bitcast_subtract_fusion.4, f32[128,128,38]{1,2,0:T(8,128)S(1)} %fusion.32, f32[128,38,128]{2,1,0:T(8,128)S(1)} %copy-done.1, f32[128,128]{1,0:T(8,128)S(1)} %exponential_multiply_fusion, f32[38,38]{1,0:T(8,128)S(1)} %copy-done.4), kind=kOutput, calls=%fused_computation.7 | convolution fusion | flops 148176896 | bytes 10032784 | tf_op jit(solution)/shard_map/dot_general | solution.py:160
  59.1 1.3 %fusion.30 = f32[128,128,38]{1,2,0:T(8,128)S(1)} fusion(f32[38,128,128]{2,0,1:T(8,128)S(1)} %bitcast_subtract_fusion.2, f32[38,38]{1,0:T(8,128)S(1)} %copy-done.3), kind=kOutput, calls=%fused_computation.38 | convolution fusion | flops 141950976 | bytes 4986512 | tf_op jit(solution)/shard_map/dot_general | solution.py:153
  60.4 3.2 %fusion = f32[38,128,128]{2,0,1:T(8,128)S(1)} fusion(f32[128,38,128]{2,1,0:T(8,128)S(1)} %copy-done.1, f32[38,128,128]{2,0,1:T(8,128)S(1)} %bitcast_subtract_fusion.2, f32[128,128,38]{1,2,0:T(8,128)S(1)} %fusion.30, f32[128,128]{1,0:T(8,128)S(1)} %exponential_multiply_fusion, pred[128]{0:T(512)(128)(4,1)S(1)} %gt.22, f32[38,38]{1,0:T(8,128)S(1)} %copy-done.4), kind=kOutput, calls=%fused_computation.3 | convolution fusion | flops 148799488 | bytes 10032912 | tf_op jit(solution)/shard_map/dot_general | solution.py:160
  63.7 1.7 %convolution_bitcast_fusion = f32[4,128,128]{2,0,1:T(4,128)S(1)} fusion(f32[38,128,128]{2,0,1:T(8,128)S(1)} %fusion, f32[4,38]{1,0:T(4,128)S(1)} %copy-done.7), kind=kOutput, calls=%fused_computation.29 | convolution fusion | flops 29884416 | bytes 2753120 | tf_op jit(solution)/shard_map/dot_general | solution.py:166
  65.7 2.7 %collective-permute-start.4 = (f32[4,128]{1,0:T(4,128)S(1)}, f32[4,128]{1,0:T(4,128)S(1)}, u32[]{:S(2)}, u32[]{:S(2)}) collective-permute-start(f32[4,128]{1,0:T(4,128)S(1)} %broadcast_multiply_fusion), channel_id=1, source_target_pairs={{0,1},{1,0},{2,3},{3,2},{4,5},{5,4},{6,7},{7,6},{8,9},{9,8},{10,11... | collective-permute-start | bytes 6152 | tf_op jit(solution)/shard_map/ppermute | solution.py:176
  68.4 1.6 %collective-permute-done.4 = f32[4,128]{1,0:T(4,128)S(1)} collective-permute-done((f32[4,128]{1,0:T(4,128)S(1)}, f32[4,128]{1,0:T(4,128)S(1)}, u32[]{:S(2)}, u32[]{:S(2)}) %collective-permute-start.4) | collective-permute-done | bytes 2080 | tf_op jit(solution)/shard_map/ppermute | solution.py:176
  69.9 3.0 %collective-permute-start.5 = (f32[4,128]{1,0:T(4,128)S(1)}, f32[4,128]{1,0:T(4,128)S(1)}, u32[]{:S(2)}, u32[]{:S(2)}) collective-permute-start(f32[4,128]{1,0:T(4,128)S(1)} %fusion.38), channel_id=1, source_target_pairs={{0,2},{1,3},{2,0},{3,1},{4,6},{5,7},{6,4},{7,5},{8,10},{9,11},{10,... | collective-permute-start | bytes 6152 | tf_op jit(solution)/shard_map/ppermute | solution.py:176
  73.0 1.6 %collective-permute-done.5 = f32[4,128]{1,0:T(4,128)S(1)} collective-permute-done((f32[4,128]{1,0:T(4,128)S(1)}, f32[4,128]{1,0:T(4,128)S(1)}, u32[]{:S(2)}, u32[]{:S(2)}) %collective-permute-start.5) | collective-permute-done | bytes 2080 | tf_op jit(solution)/shard_map/ppermute | solution.py:176
  74.5 1.1 %collective-permute-start.6 = (f32[1,4,128]{2,0,1:T(1,128)S(1)}, f32[1,4,128]{2,0,1:T(1,128)S(1)}, u32[]{:S(2)}, u32[]{:S(2)}) collective-permute-start(f32[1,4,128]{2,0,1:T(1,128)S(1)} %bitcast.109), channel_id=1, source_target_pairs={{0,4},{4,0},{8,12},{12,8},{16,20},{20,16},{24,28},{28,24},{1,5},{5... | collective-permute-start | bytes 6152 | tf_op jit(solution)/shard_map/ppermute | solution.py:189
  75.6 0.8 collective-permute-done.6
  76.4 2.5 %collective-permute-start.7 = (f32[2,4,128]{2,0,1:T(2,128)S(1)}, f32[2,4,128]{2,0,1:T(2,128)S(1)}, u32[]{:S(2)}, u32[]{:S(2)}) collective-permute-start(f32[2,4,128]{2,0,1:T(2,128)S(1)} %maximum_select_fusion.2), channel_id=1, source_target_pairs={{0,8},{4,12},{8,0},{12,4},{16,24},{20,28},{24,16},{28,20},{1,9},{5... | collective-permute-start | bytes 12296 | tf_op jit(solution)/shard_map/ppermute | solution.py:189
  78.9 1.6 %collective-permute-done.7 = f32[2,4,128]{2,0,1:T(2,128)S(1)} collective-permute-done((f32[2,4,128]{2,0,1:T(2,128)S(1)}, f32[2,4,128]{2,0,1:T(2,128)S(1)}, u32[]{:S(2)}, u32[]{:S(2)}) %collective-permute-start.7) | collective-permute-done | bytes 4128 | tf_op jit(solution)/shard_map/ppermute | solution.py:189
  80.5 2.9 %collective-permute-start.8 = (f32[4,4,128]{2,0,1:T(4,128)S(1)}, f32[4,4,128]{2,0,1:T(4,128)S(1)}, u32[]{:S(2)}, u32[]{:S(2)}) collective-permute-start(f32[4,4,128]{2,0,1:T(4,128)S(1)} %maximum_select_fusion.1), channel_id=1, source_target_pairs={{0,16},{4,20},{8,24},{12,28},{16,0},{20,4},{24,8},{28,12},{1,17},{... | collective-permute-start | bytes 24584 | tf_op jit(solution)/shard_map/ppermute | solution.py:189
  83.4 1.9 %copy.20 = f32[38,128,128]{2,1,0:T(8,128)} copy(f32[38,128,128]{2,0,1:T(8,128)S(1)} %fusion) | data formatting | bytes 4980736
  85.4 2.8 %select_reduce_fusion = f32[4,1024]{1,0:T(4,128)S(1)} fusion(f32[4,1024]{1,0:T(4,128)S(1)} %bitcast.106, s32[4,1024]{1,0:T(4,128)S(1)} %constant_dynamic-slice_fusion), kind=kLoop, calls=%fused_computation | loop fusion | flops 12578816 | bytes 49152 | tf_op jit(solution)/shard_map/reduce_sum | solution.py:241
  (40 shorter events, 2.0 us)
Async XLA Ops:
  0.6 82.8 %copy-start = (s32[4,32768]{1,0:T(4,128)S(1)}, s32[4,32768]{1,0:T(4,128)}, u32[]{:S(2)}) copy-start(s32[4,32768]{1,0:T(4,128)} %param.18) | copy-start | bytes 1572868
  4.8 8.3 %copy-start.2 = (f32[38,128,128]{2,1,0:T(8,128)S(1)}, f32[38,128,128]{2,1,0:T(8,128)}, u32[]{:S(2)}) copy-start(f32[38,128,128]{2,1,0:T(8,128)} %field_ref.1) | copy-start | bytes 7471108
  6.9 9.8 %copy-start.5 = (f32[128,128]{1,0:T(8,128)S(1)}, f32[128,128]{1,0:T(8,128)}, u32[]{:S(2)}) copy-start(f32[128,128]{1,0:T(8,128)} %param.12) | copy-start | bytes 196612
  6.9 9.8 %copy-start.9 = (s32[64,1]{0,1:T(1,128)S(1)}, s32[64,1]{0,1:T(1,128)}, u32[]{:S(2)}) copy-start(s32[64,1]{0,1:T(1,128)} %param.15) | copy-start | bytes 772
  6.9 10.0 %collective-permute-start.2 = (f32[39,3,128]{2,1,0:T(4,128)S(1)}, f32[39,3,128]{2,1,0:T(4,128)S(1)}, u32[]{:S(2)}, u32[]{:S(2)}) collective-permute-start(f32[39,3,128]{2,1,0:T(4,128)S(1)} %get-tuple-element.9), channel_id=1, source_target_pairs={{0,1},{1,2},{2,3},{4,5},{5,6},{6,7},{8,9},{9,10},{10,11},{12,13},{... | collective-permute-start | bytes 179720 | tf_op jit(solution)/shard_map/ppermute | solution.py:28
  11.9 6.3 %collective-permute-start.3 = (f32[39,3,128]{2,1,0:T(4,128)S(1)}, f32[39,3,128]{2,1,0:T(4,128)S(1)}, u32[]{:S(2)}, u32[]{:S(2)}) collective-permute-start(f32[39,3,128]{2,1,0:T(4,128)S(1)} %get-tuple-element.8), channel_id=1, source_target_pairs={{1,0},{2,1},{3,2},{5,4},{6,5},{7,6},{9,8},{10,9},{11,10},{13,12},{... | collective-permute-start | bytes 179720 | tf_op jit(solution)/shard_map/ppermute | solution.py:28
  13.9 5.0 %collective-permute-start = (f32[39,3,128]{2,1,0:T(4,128)}, f32[39,3,128]{2,1,0:T(4,128)S(1)}, u32[]{:S(2)}, u32[]{:S(2)}) collective-permute-start(f32[39,3,128]{2,1,0:T(4,128)} %get-tuple-element.11), channel_id=1, source_target_pairs={{0,4},{4,8},{8,12},{12,16},{16,20},{20,24},{24,28},{1,5},{5,9},{9,... | collective-permute-start | bytes 179720 | tf_op jit(solution)/shard_map/ppermute | solution.py:28
  15.3 4.9 %collective-permute-start.1 = (f32[39,3,128]{2,1,0:T(4,128)}, f32[39,3,128]{2,1,0:T(4,128)S(1)}, u32[]{:S(2)}, u32[]{:S(2)}) collective-permute-start(f32[39,3,128]{2,1,0:T(4,128)} %get-tuple-element.10), channel_id=1, source_target_pairs={{4,0},{8,4},{12,8},{16,12},{20,16},{24,20},{28,24},{5,1},{9,5},{13... | collective-permute-start | bytes 179720 | tf_op jit(solution)/shard_map/ppermute | solution.py:28
  20.9 28.3 %copy-start.3 = (f32[38,38]{1,0:T(8,128)S(1)}, f32[38,38]{1,0:T(8,128)}, u32[]{:S(2)}) copy-start(f32[38,38]{1,0:T(8,128)} %param.13) | copy-start | bytes 17332
  49.2 3.1 %copy-start.1 = (f32[128,38,128]{2,1,0:T(8,128)S(1)}, f32[128,38,128]{2,1,0:T(8,128)}, u32[]{:S(2)}) copy-start(f32[128,38,128]{2,1,0:T(8,128)} %shard_map.113) | copy-start | bytes 7471108
  49.2 3.1 %copy-start.4 = (f32[38,38]{1,0:T(8,128)S(1)}, f32[38,38]{1,0:T(8,128)}, u32[]{:S(2)}) copy-start(f32[38,38]{1,0:T(8,128)} %param.14) | copy-start | bytes 17332
  60.4 3.3 %copy-start.7 = (f32[4,38]{1,0:T(4,128)S(1)}, f32[4,38]{1,0:T(4,128)}, u32[]{:S(2)}) copy-start(f32[4,38]{1,0:T(4,128)} %param.16) | copy-start | bytes 1828
  63.7 1.7 %copy-start.8 = (f32[128]{0:T(128)S(1)}, f32[128]{0:T(128)}, u32[]{:S(2)}) copy-start(f32[128]{0:T(128)} %param.17) | copy-start | bytes 1540
  65.7 4.3 %collective-permute-start.4 = (f32[4,128]{1,0:T(4,128)S(1)}, f32[4,128]{1,0:T(4,128)S(1)}, u32[]{:S(2)}, u32[]{:S(2)}) collective-permute-start(f32[4,128]{1,0:T(4,128)S(1)} %broadcast_multiply_fusion), channel_id=1, source_target_pairs={{0,1},{1,0},{2,3},{3,2},{4,5},{5,4},{6,7},{7,6},{8,9},{9,8},{10,11... | collective-permute-start | bytes 6152 | tf_op jit(solution)/shard_map/ppermute | solution.py:176
  69.9 4.6 %collective-permute-start.5 = (f32[4,128]{1,0:T(4,128)S(1)}, f32[4,128]{1,0:T(4,128)S(1)}, u32[]{:S(2)}, u32[]{:S(2)}) collective-permute-start(f32[4,128]{1,0:T(4,128)S(1)} %fusion.38), channel_id=1, source_target_pairs={{0,2},{1,3},{2,0},{3,1},{4,6},{5,7},{6,4},{7,5},{8,10},{9,11},{10,... | collective-permute-start | bytes 6152 | tf_op jit(solution)/shard_map/ppermute | solution.py:176
  74.5 1.9 %collective-permute-start.6 = (f32[1,4,128]{2,0,1:T(1,128)S(1)}, f32[1,4,128]{2,0,1:T(1,128)S(1)}, u32[]{:S(2)}, u32[]{:S(2)}) collective-permute-start(f32[1,4,128]{2,0,1:T(1,128)S(1)} %bitcast.109), channel_id=1, source_target_pairs={{0,4},{4,0},{8,12},{12,8},{16,20},{20,16},{24,28},{28,24},{1,5},{5... | collective-permute-start | bytes 6152 | tf_op jit(solution)/shard_map/ppermute | solution.py:189
  76.4 4.0 %collective-permute-start.7 = (f32[2,4,128]{2,0,1:T(2,128)S(1)}, f32[2,4,128]{2,0,1:T(2,128)S(1)}, u32[]{:S(2)}, u32[]{:S(2)}) collective-permute-start(f32[2,4,128]{2,0,1:T(2,128)S(1)} %maximum_select_fusion.2), channel_id=1, source_target_pairs={{0,8},{4,12},{8,0},{12,4},{16,24},{20,28},{24,16},{28,20},{1,9},{5... | collective-permute-start | bytes 12296 | tf_op jit(solution)/shard_map/ppermute | solution.py:189
  80.5 4.8 %collective-permute-start.8 = (f32[4,4,128]{2,0,1:T(4,128)S(1)}, f32[4,4,128]{2,0,1:T(4,128)S(1)}, u32[]{:S(2)}, u32[]{:S(2)}) collective-permute-start(f32[4,4,128]{2,0,1:T(4,128)S(1)} %maximum_select_fusion.1), channel_id=1, source_target_pairs={{0,16},{4,20},{8,24},{12,28},{16,0},{20,4},{24,8},{28,12},{1,17},{... | collective-permute-start | bytes 24584 | tf_op jit(solution)/shard_map/ppermute | solution.py:189
  83.4 4.8 %copy-start.6 = (f32[4,1024]{1,0:T(4,128)S(1)}, f32[4,1024]{1,0:T(4,128)}, u32[]{:S(2)}) copy-start(f32[4,1024]{1,0:T(4,128)} %param.19) | copy-start | bytes 49156
where the time goes:
time: 90.4 us; the launch traced here: 88.8 us
  Pallas kernels  28.3 us (31%)
  starting transfers between devices  21.1 us (23%)
  matrix products  16.3 us (18%)
  local copies, waits for them, and re-layouts  9.11 us (10%)
  waiting for transfers between devices  6.82 us (8%)
  other arithmetic  6.21 us (7%)
  between operations  0.91 us (1%)
    pallas_call x1, Pallas kernels, transport(): pl.pallas_call(transport_kernel, grid=(species_count,), in_specs=[plane,...  28.3 us
    ppermute x4, starting transfers between devices, edge_layers(): return (lax.ppermute(last, axis, up), lax.ppermute(initial, axis, down))  8.97 us
    dot_general x3, matrix products, kinetics_advance(): jnp.tensordot(frozen_jacobian_inverse_addend, defect, axes=(1, 0), precis...  8.61 us
    ppermute x3, starting transfers between devices, doubling_gather(): other = lax.ppermute(blocks, axis, pairs)  6.44 us
    ppermute x2, starting transfers between devices, butterfly_sum(): part = part + lax.ppermute(part, axis, pairs)  5.74 us
    dot_general x3, matrix products, kinetics_advance(): jnp.tensordot(linearized_kinetics_operator, current, axes=(1, 0), precisi...  5.73 us
    unnamed x24, local copies, waits for them, and re-layouts  5.2 us
    ppermute x2, waiting for transfers between devices, butterfly_sum(): part = part + lax.ppermute(part, axis, pairs)  3.13 us
  transfers between devices with their start and end apart: 9, of which 6 were waited for; matrix products, arithmetic and copies ran while one was open for 6% of the time, Pallas kernels for 0%

commit v1 on v0

--- a/solution.py
+++ b/solution.py
@@ -57,16 +57,14 @@
 CHUNK = 8
 
 
-def upwind_divergence(ext_ref, vel_ref, flux_ref, rows):
+def upwind_divergence(ext_ref, speed_ref, flux_ref, rows):
     faces = flux_ref.shape[0]
     for low in range(0, faces, CHUNK):
 
         def cut(offset):
             return ext_ref[pl.ds(HALO - 3 + offset + low, CHUNK), :]
 
-        face_speed = 0.5 * (
-            vel_ref[pl.ds(HALO - 1 + low, CHUNK), :] + vel_ref[pl.ds(HALO + low, CHUNK), :]
-        )
+        face_speed = speed_ref[pl.ds(low, CHUNK), :]
         forward = face_speed >= 0.0
         stencil = [
             jnp.where(forward, cut(lower), cut(upper))
@@ -77,36 +75,33 @@
 
 
 def transport_kernel(
-    field_ref, speed_ref, top_ref, top_speed_ref, bottom_ref, bottom_speed_ref,
-    left_ref, left_speed_ref, right_ref, right_speed_ref, out_ref,
-    ext_ref, vel_ref, flux_ref,
+    field_ref, axial_speed_ref, radial_speed_ref, top_ref, bottom_ref, left_ref, right_ref,
+    out_ref, ext_ref, flux_ref,
 ):
     rows, cols = field_ref.shape[1], field_ref.shape[2]
     span = ext_ref.shape[0]
     tail = span - HALO - rows
-    zeros = jnp.zeros((tail - HALO, cols), jnp.float32)
     field = field_ref[0]
 
     ext_ref[pl.ds(0, HALO), :] = top_ref[0]
     ext_ref[pl.ds(HALO, rows), :] = field
     ext_ref[pl.ds(HALO + rows, HALO), :] = bottom_ref[0]
-    ext_ref[pl.ds(2 * HALO + rows, tail - HALO), :] = zeros
-    vel_ref[pl.ds(0, HALO), :] = top_speed_ref[0]
-    vel_ref[pl.ds(HALO, rows), :] = speed_ref[0]
-    vel_ref[pl.ds(HALO + rows, HALO), :] = bottom_speed_ref[0]
-    vel_ref[pl.ds(2 * HALO + rows, tail - HALO), :] = zeros
-    along_axial = upwind_divergence(ext_ref, vel_ref, flux_ref, rows)
+    ext_ref[pl.ds(2 * HALO + rows, tail - HALO), :] = jnp.zeros((tail - HALO, cols), jnp.float32)
+    along_axial = upwind_divergence(ext_ref, axial_speed_ref, flux_ref, rows)
 
     ext_ref[pl.ds(0, HALO), :] = left_ref[0]
     ext_ref[pl.ds(HALO, cols), :] = field.T
     ext_ref[pl.ds(HALO + cols, HALO), :] = right_ref[0]
-    vel_ref[pl.ds(0, HALO), :] = left_speed_ref[0]
-    vel_ref[pl.ds(HALO, cols), :] = speed_ref[1].T
-    vel_ref[pl.ds(HALO + cols, HALO), :] = right_speed_ref[0]
-    along_radial = upwind_divergence(ext_ref, vel_ref, flux_ref, cols).T
+    along_radial = upwind_divergence(ext_ref, radial_speed_ref, flux_ref, cols).T
 
     moved = field - TIME_STEP * (along_axial + along_radial)
     out_ref[:, pl.ds(pl.program_id(0), 1), :] = moved[:, None, :]
+
+
+def face_speeds(edges_before, speed, edges_after, faces):
+    extended = jnp.concatenate([edges_before[-1:], speed, edges_after[:1]], axis=0)
+    extended = jnp.pad(extended, ((0, faces + 1 - extended.shape[0]), (0, 0)))
+    return 0.5 * (extended[:-1] + extended[1:])
 
 
 def transport(species, speed, width=3):
@@ -116,28 +111,28 @@
     top, bottom = edge_layers(axial_edges, "axial", 1, width)
     radial_edges = jnp.swapaxes(jnp.concatenate([species, speed[1:2]], axis=0), 1, 2)
     left, right = edge_layers(radial_edges, "radial", 1, width)
+    faces = rows + CHUNK
+    axial_speed = face_speeds(top[species_count], speed[0], bottom[species_count], faces)
+    radial_speed = face_speeds(left[species_count], speed[1].T, right[species_count], faces)
     before = ((0, 0), (HALO - width, 0), (0, 0))
     after = ((0, 0), (0, HALO - width), (0, 0))
-    top, left = (jnp.pad(top, before), jnp.pad(left, before))
-    bottom, right = (jnp.pad(bottom, after), jnp.pad(right, after))
-    faces = rows + CHUNK
+    top, left = (jnp.pad(top[:species_count], before), jnp.pad(left[:species_count], before))
+    bottom, right = (jnp.pad(bottom[:species_count], after), jnp.pad(right[:species_count], after))
     span = HALO + faces + HALO
     plane = pl.BlockSpec((1, rows, cols), lambda s: (s, 0, 0))
-    speeds = pl.BlockSpec((2, rows, cols), lambda s: (0, 0, 0))
+    face_plane = pl.BlockSpec((faces, cols), lambda s: (0, 0))
     edge = pl.BlockSpec((1, HALO, cols), lambda s: (s, 0, 0))
-    edge_speed = pl.BlockSpec((1, HALO, cols), lambda s: (species_count, 0, 0))
     moved_rows = pl.pallas_call(
         transport_kernel,
         grid=(species_count,),
-        in_specs=[plane, speeds] + [edge, edge_speed] * 4,
+        in_specs=[plane, face_plane, face_plane] + [edge] * 4,
         out_specs=pl.BlockSpec((rows, species_count, cols), lambda s: (0, 0, 0)),
         out_shape=jax.ShapeDtypeStruct((rows, species_count, cols), jnp.float32),
         scratch_shapes=[
             pltpu.VMEM((span, cols), jnp.float32),
-            pltpu.VMEM((span, cols), jnp.float32),
             pltpu.VMEM((faces, cols), jnp.float32),
         ],
-    )(species, speed, top, top, bottom, bottom, left, left, right, right)
+    )(species, axial_speed, radial_speed, top, bottom, left, right)
     return jnp.transpose(moved_rows, (1, 0, 2))
 
 

time: 90.4 us -> 95.5 us (1.056)
  local copies, waits for them, and re-layouts: 9.11 us -> 12.3 us
  starting transfers between devices: 21.1 us -> 22.5 us
  other arithmetic: 6.21 us -> 7.49 us
    slice x1 -> x9, local copies, waits for them, and re-layouts: 0.03 us -> 3.21 us  [the longest x1 0.9 us: transport(): left[:species_count]]
    ppermute x4, starting transfers between devices: 8.97 us -> 11.8 us  [edge_layers(): return (lax.ppermute(last, axis, up), lax.ppermute(initial, axis, down))]
    mul x0 -> x2, other arithmetic: none -> 1.28 us  [face_speeds(): return 0.5 * (extended[:-1] + extended[1:])]
    ppermute x4, waiting for transfers between devices: 1.28 us -> 0.01 us  [edge_layers(): return (lax.ppermute(last, axis, up), lax.ppermute(initial, axis, down))]
    ppermute x2, starting transfers between devices: 5.74 us -> 4.5 us  [butterfly_sum(): part = part + lax.ppermute(part, axis, pairs)]
  transfers between devices with their start and end apart: 9 -> 9, of which waited for: 6 -> 4; matrix products, arithmetic and copies ran while one was open for 6% -> 5% of each run, Pallas kernels for 0% -> 0%
where the time goes in v1:
time: 95.5 us; the launch traced here: 93.7 us
  Pallas kernels  27.7 us (29%)
  starting transfers between devices  22.5 us (24%)
  matrix products  16.3 us (17%)
  local copies, waits for them, and re-layouts  12.3 us (13%)
  other arithmetic  7.49 us (8%)
  waiting for transfers between devices  6.49 us (7%)
    pallas_call x1, Pallas kernels, transport(): pl.pallas_call(transport_kernel, grid=(species_count,), in_specs=[plane,...  27.7 us
    ppermute x4, starting transfers between devices, edge_layers(): return (lax.ppermute(last, axis, up), lax.ppermute(initial, axis, down))  11.8 us
    dot_general x3, matrix products, kinetics_advance(): jnp.tensordot(frozen_jacobian_inverse_addend, defect, axes=(1, 0), precis...  8.61 us
    ppermute x3, starting transfers between devices, doubling_gather(): other = lax.ppermute(blocks, axis, pairs)  6.2 us
    dot_general x3, matrix products, kinetics_advance(): jnp.tensordot(linearized_kinetics_operator, current, axes=(1, 0), precisi...  5.72 us
    unnamed x24, local copies, waits for them, and re-layouts  5.2 us
    ppermute x2, starting transfers between devices, butterfly_sum(): part = part + lax.ppermute(part, axis, pairs)  4.5 us
    ppermute x2, waiting for transfers between devices, butterfly_sum(): part = part + lax.ppermute(part, axis, pairs)  3.74 us
  transfers between devices with their start and end apart: 9, of which 4 were waited for; matrix products, arithmetic and copies ran while one was open for 5% of the time, Pallas kernels for 0%

profile of v1, /device:TPU:0, one launch (start us, length us, event | category | flops | bytes accessed | tf_op | source)
XLA Modules:
  0.0 93.7 jit_solution(14393865968371123056)
XLA Ops:
  0.6 0.9 %fusion.42 = (f32[1,128,128]{2,1,0:T(8,128)S(1)}, f32[128,128]{1,0:T(8,128)S(1)}, f32[1,128,128]{2,1,0:T(8,128)S(1)}) fusion(f32[2,128,128]{2,1,0:T(8,128)} %param.11), kind=kLoop, calls=%fused_computation.69 | loop fusion | bytes 327680 | tf_op jit(solution)/shard_map/slice | solution.py:112
  1.7 3.1 %copy.19 = f32[38,128,128]{1,2,0:T(8,128)} copy(f32[38,128,128]{2,1,0:T(8,128)} %field_ref.1) | data formatting | bytes 4980736 | tf_op args[0]
  4.8 2.0 %maximum_bitcast_fusion = f32[39,128,128]{2,1,0:T(8,128)S(1)} fusion(f32[1,128,128]{1,2,0:T(8,128)S(1)} %copy.23, f32[38,128,128]{1,2,0:T(8,128)} %copy.19), kind=kLoop, calls=%fused_computation.24 | loop fusion | flops 638976 | bytes 5111808 | tf_op jit(solution)/shard_map/transpose | solution.py:112
  6.9 1.3 %collective-permute-start.3 = (f32[39,3,128]{2,1,0:T(4,128)S(1)}, f32[39,3,128]{2,1,0:T(4,128)}, u32[]{:S(2)}, u32[]{:S(2)}) collective-permute-start(f32[39,3,128]{2,1,0:T(4,128)S(1)} %get-tuple-element.9), channel_id=1, source_target_pairs={{1,0},{2,1},{3,2},{5,4},{6,5},{7,6},{9,8},{10,9},{11,10},{13,12},{... | collective-permute-start | bytes 179720 | tf_op jit(solution)/shard_map/ppermute | solution.py:28
  8.2 6.2 %collective-permute-start.2 = (f32[39,3,128]{2,1,0:T(4,128)S(1)}, f32[39,3,128]{2,1,0:T(4,128)}, u32[]{:S(2)}, u32[]{:S(2)}) collective-permute-start(f32[39,3,128]{2,1,0:T(4,128)S(1)} %get-tuple-element.8), channel_id=1, source_target_pairs={{0,1},{1,2},{2,3},{4,5},{5,6},{6,7},{8,9},{9,10},{10,11},{12,13},{... | collective-permute-start | bytes 179720 | tf_op jit(solution)/shard_map/ppermute | solution.py:28
  15.1 1.3 %collective-permute-start.1 = (f32[39,3,128]{2,1,0:T(4,128)}, f32[39,3,128]{2,1,0:T(4,128)S(1)}, u32[]{:S(2)}, u32[]{:S(2)}) collective-permute-start(f32[39,3,128]{2,1,0:T(4,128)} %get-tuple-element.11), channel_id=1, source_target_pairs={{4,0},{8,4},{12,8},{16,12},{20,16},{24,20},{28,24},{5,1},{9,5},{13... | collective-permute-start | bytes 179720 | tf_op jit(solution)/shard_map/ppermute | solution.py:28
  16.4 3.0 %collective-permute-start = (f32[39,3,128]{2,1,0:T(4,128)S(1)}, f32[39,3,128]{2,1,0:T(4,128)S(1)}, u32[]{:S(2)}, u32[]{:S(2)}) collective-permute-start(f32[39,3,128]{2,1,0:T(4,128)S(1)} %get-tuple-element.10), channel_id=1, source_target_pairs={{0,4},{4,8},{8,12},{12,16},{16,20},{20,24},{24,28},{1,5},{5,9},{9,... | collective-permute-start | bytes 179720 | tf_op jit(solution)/shard_map/ppermute | solution.py:28
  19.7 0.7 slice_bitcast_fusion
  22.4 0.9 slice.110
  23.3 0.7 pad.25.left_ref
  24.0 0.9 slice.111
  24.9 0.7 pad.26.right_ref
  25.6 0.7 pad.23.top_ref
  26.3 0.7 pad.24.bottom_ref
  27.0 27.7 %shard_map.113 = f32[128,38,128]{2,1,0:T(8,128)} custom-call(f32[38,128,128]{2,1,0:T(8,128)} %field_ref.1, f32[136,128]{1,0:T(8,128)} %fusion.28.axial_speed_ref, f32[136,128]{1,0:T(8,128)} %fusion.27.radial_speed_ref, f32[38,8,128]{2,1,0:T(8,128)} %pad.23.top_ref, f32[38,8,128]{2,1,0:T(8,128)} %pad.24.bottom_ref, f32[38,8,128]{2,1,0:T(8,128)} %pad.25.left_ref, ...), custom_call_target="tpu_custom_call" | custom-call | tf_op jit(solution)/shard_map/pallas_call | solution.py:125
  54.7 3.1 %fusion.13 = f32[128,128,38]{1,2,0:T(8,128)S(1)} fusion(f32[128,38,128]{2,1,0:T(8,128)} %shard_map.113, f32[38,38]{1,0:T(8,128)S(1)} %copy-done.3), kind=kOutput, calls=%fused_computation.22 | convolution fusion | flops 141950976 | bytes 4986512 | tf_op jit(solution)/shard_map/dot_general | solution.py:148
  57.8 2.5 %bitcast_subtract_fusion.4 = f32[38,128,128]{2,0,1:T(8,128)S(1)} fusion(f32[128,128,38]{1,2,0:T(8,128)S(1)} %fusion.13, f32[128,38,128]{2,1,0:T(8,128)S(1)} %copy-done.1, f32[128,128]{1,0:T(8,128)S(1)} %exponential_multiply_fusion, f32[38,38]{1,0:T(8,128)S(1)} %copy-done.4), kind=kOutput, calls=%fused_computation.11 | convolution fusion | flops 148176896 | bytes 7542416 | tf_op jit(solution)/shard_map/dot_general | solution.py:155
  60.3 1.3 %fusion.34 = f32[128,128,38]{1,2,0:T(8,128)S(1)} fusion(f32[38,128,128]{2,0,1:T(8,128)S(1)} %bitcast_subtract_fusion.4, f32[38,38]{1,0:T(8,128)S(1)} %copy-done.3), kind=kOutput, calls=%fused_computation.49 | convolution fusion | flops 141950976 | bytes 4986512 | tf_op jit(solution)/shard_map/dot_general | solution.py:148
  61.6 2.9 %bitcast_subtract_fusion.2 = f32[38,128,128]{2,0,1:T(8,128)S(1)} fusion(f32[38,128,128]{2,0,1:T(8,128)S(1)} %bitcast_subtract_fusion.4, f32[128,128,38]{1,2,0:T(8,128)S(1)} %fusion.34, f32[128,38,128]{2,1,0:T(8,128)S(1)} %copy-done.1, f32[128,128]{1,0:T(8,128)S(1)} %exponential_multiply_fusion, f32[38,38]{1,0:T(8,128)S(1)} %copy-done.4), kind=kOutput, calls=%fused_computation.7 | convolution fusion | flops 148176896 | bytes 10032784 | tf_op jit(solution)/shard_map/dot_general | solution.py:155
  64.5 1.3 %fusion.32 = f32[128,128,38]{1,2,0:T(8,128)S(1)} fusion(f32[38,128,128]{2,0,1:T(8,128)S(1)} %bitcast_subtract_fusion.2, f32[38,38]{1,0:T(8,128)S(1)} %copy-done.3), kind=kOutput, calls=%fused_computation.47 | convolution fusion | flops 141950976 | bytes 4986512 | tf_op jit(solution)/shard_map/dot_general | solution.py:148
  65.9 3.2 %fusion = f32[38,128,128]{2,0,1:T(8,128)S(1)} fusion(f32[128,38,128]{2,1,0:T(8,128)S(1)} %copy-done.1, f32[38,128,128]{2,0,1:T(8,128)S(1)} %bitcast_subtract_fusion.2, f32[128,128,38]{1,2,0:T(8,128)S(1)} %fusion.32, f32[128,128]{1,0:T(8,128)S(1)} %exponential_multiply_fusion, pred[128]{0:T(512)(128)(4,1)S(1)} %gt.22, f32[38,38]{1,0:T(8,128)S(1)} %copy-done.4), kind=kOutput, calls=%fused_computation.3 | convolution fusion | flops 148799488 | bytes 10032912 | tf_op jit(solution)/shard_map/dot_general | solution.py:155
  69.1 1.7 %convolution_bitcast_fusion = f32[4,128,128]{2,0,1:T(4,128)S(1)} fusion(f32[38,128,128]{2,0,1:T(8,128)S(1)} %fusion, f32[4,38]{1,0:T(4,128)S(1)} %copy-done.7), kind=kOutput, calls=%fused_computation.29 | convolution fusion | flops 29884416 | bytes 2753120 | tf_op jit(solution)/shard_map/dot_general | solution.py:161
  71.1 1.5 %collective-permute-start.4 = (f32[4,128]{1,0:T(4,128)S(1)}, f32[4,128]{1,0:T(4,128)S(1)}, u32[]{:S(2)}, u32[]{:S(2)}) collective-permute-start(f32[4,128]{1,0:T(4,128)S(1)} %broadcast_multiply_fusion), channel_id=1, source_target_pairs={{0,1},{1,0},{2,3},{3,2},{4,5},{5,4},{6,7},{7,6},{8,9},{9,8},{10,11... | collective-permute-start | bytes 6152 | tf_op jit(solution)/shard_map/ppermute | solution.py:171
  72.6 2.2 %collective-permute-done.4 = f32[4,128]{1,0:T(4,128)S(1)} collective-permute-done((f32[4,128]{1,0:T(4,128)S(1)}, f32[4,128]{1,0:T(4,128)S(1)}, u32[]{:S(2)}, u32[]{:S(2)}) %collective-permute-start.4) | collective-permute-done | bytes 2080 | tf_op jit(solution)/shard_map/ppermute | solution.py:171
  74.8 3.0 %collective-permute-start.5 = (f32[4,128]{1,0:T(4,128)S(1)}, f32[4,128]{1,0:T(4,128)S(1)}, u32[]{:S(2)}, u32[]{:S(2)}) collective-permute-start(f32[4,128]{1,0:T(4,128)S(1)} %fusion.40), channel_id=1, source_target_pairs={{0,2},{1,3},{2,0},{3,1},{4,6},{5,7},{6,4},{7,5},{8,10},{9,11},{10,... | collective-permute-start | bytes 6152 | tf_op jit(solution)/shard_map/ppermute | solution.py:171
  77.8 1.6 %collective-permute-done.5 = f32[4,128]{1,0:T(4,128)S(1)} collective-permute-done((f32[4,128]{1,0:T(4,128)S(1)}, f32[4,128]{1,0:T(4,128)S(1)}, u32[]{:S(2)}, u32[]{:S(2)}) %collective-permute-start.5) | collective-permute-done | bytes 2080 | tf_op jit(solution)/shard_map/ppermute | solution.py:171
  79.4 1.2 %collective-permute-done.6 = f32[1,4,128]{2,0,1:T(1,128)S(1)} collective-permute-done((f32[1,4,128]{2,0,1:T(1,128)S(1)}, f32[1,4,128]{2,0,1:T(1,128)S(1)}, u32[]{:S(2)}, u32[]{:S(2)}) %collective-permute-start.6) | collective-permute-done | bytes 2080 | tf_op jit(solution)/shard_map/ppermute | solution.py:184
  80.5 2.9 %collective-permute-start.7 = (f32[2,4,128]{2,0,1:T(2,128)S(1)}, f32[2,4,128]{2,0,1:T(2,128)S(1)}, u32[]{:S(2)}, u32[]{:S(2)}) collective-permute-start(f32[2,4,128]{2,0,1:T(2,128)S(1)} %maximum_select_fusion.2), channel_id=1, source_target_pairs={{0,8},{4,12},{8,0},{12,4},{16,24},{20,28},{24,16},{28,20},{1,9},{5... | collective-permute-start | bytes 12296 | tf_op jit(solution)/shard_map/ppermute | solution.py:184
  83.4 1.6 %collective-permute-done.7 = f32[2,4,128]{2,0,1:T(2,128)S(1)} collective-permute-done((f32[2,4,128]{2,0,1:T(2,128)S(1)}, f32[2,4,128]{2,0,1:T(2,128)S(1)}, u32[]{:S(2)}, u32[]{:S(2)}) %collective-permute-start.7) | collective-permute-done | bytes 4128 | tf_op jit(solution)/shard_map/ppermute | solution.py:184
  85.0 3.3 %collective-permute-start.8 = (f32[4,4,128]{2,0,1:T(4,128)S(1)}, f32[4,4,128]{2,0,1:T(4,128)S(1)}, u32[]{:S(2)}, u32[]{:S(2)}) collective-permute-start(f32[4,4,128]{2,0,1:T(4,128)S(1)} %maximum_select_fusion.1), channel_id=1, source_target_pairs={{0,16},{4,20},{8,24},{12,28},{16,0},{20,4},{24,8},{28,12},{1,17},{... | collective-permute-start | bytes 24584 | tf_op jit(solution)/shard_map/ppermute | solution.py:184
  88.4 1.9 %copy.20 = f32[38,128,128]{2,1,0:T(8,128)} copy(f32[38,128,128]{2,0,1:T(8,128)S(1)} %fusion) | data formatting | bytes 4980736
  90.3 2.8 %select_reduce_fusion = f32[4,1024]{1,0:T(4,128)S(1)} fusion(f32[4,1024]{1,0:T(4,128)S(1)} %bitcast.120, s32[4,1024]{1,0:T(4,128)S(1)} %constant_dynamic-slice_fusion), kind=kLoop, calls=%fused_computation | loop fusion | flops 12578816 | bytes 49152 | tf_op jit(solution)/shard_map/reduce_sum | solution.py:236
  (52 shorter events, 4.1 us)
Async XLA Ops:
  0.6 87.7 %copy-start = (s32[4,32768]{1,0:T(4,128)S(1)}, s32[4,32768]{1,0:T(4,128)}, u32[]{:S(2)}) copy-start(s32[4,32768]{1,0:T(4,128)} %param.18) | copy-start | bytes 1572868
  4.8 9.6 %copy-start.2 = (f32[38,128,128]{2,1,0:T(8,128)S(1)}, f32[38,128,128]{2,1,0:T(8,128)}, u32[]{:S(2)}) copy-start(f32[38,128,128]{2,1,0:T(8,128)} %field_ref.1) | copy-start | bytes 7471108
  6.9 12.5 %copy-start.5 = (f32[128,128]{1,0:T(8,128)S(1)}, f32[128,128]{1,0:T(8,128)}, u32[]{:S(2)}) copy-start(f32[128,128]{1,0:T(8,128)} %param.12) | copy-start | bytes 196612
  6.9 12.6 %copy-start.9 = (s32[64,1]{0,1:T(1,128)S(1)}, s32[64,1]{0,1:T(1,128)}, u32[]{:S(2)}) copy-start(s32[64,1]{0,1:T(1,128)} %param.15) | copy-start | bytes 772
  6.9 12.8 %collective-permute-start.3 = (f32[39,3,128]{2,1,0:T(4,128)S(1)}, f32[39,3,128]{2,1,0:T(4,128)}, u32[]{:S(2)}, u32[]{:S(2)}) collective-permute-start(f32[39,3,128]{2,1,0:T(4,128)S(1)} %get-tuple-element.9), channel_id=1, source_target_pairs={{1,0},{2,1},{3,2},{5,4},{6,5},{7,6},{9,8},{10,9},{11,10},{13,12},{... | collective-permute-start | bytes 179720 | tf_op jit(solution)/shard_map/ppermute | solution.py:28
  8.2 12.2 %collective-permute-start.2 = (f32[39,3,128]{2,1,0:T(4,128)S(1)}, f32[39,3,128]{2,1,0:T(4,128)}, u32[]{:S(2)}, u32[]{:S(2)}) collective-permute-start(f32[39,3,128]{2,1,0:T(4,128)S(1)} %get-tuple-element.8), channel_id=1, source_target_pairs={{0,1},{1,2},{2,3},{4,5},{5,6},{6,7},{8,9},{9,10},{10,11},{12,13},{... | collective-permute-start | bytes 179720 | tf_op jit(solution)/shard_map/ppermute | solution.py:28
  15.1 6.6 %collective-permute-start.1 = (f32[39,3,128]{2,1,0:T(4,128)}, f32[39,3,128]{2,1,0:T(4,128)S(1)}, u32[]{:S(2)}, u32[]{:S(2)}) collective-permute-start(f32[39,3,128]{2,1,0:T(4,128)} %get-tuple-element.11), channel_id=1, source_target_pairs={{4,0},{8,4},{12,8},{16,12},{20,16},{24,20},{28,24},{5,1},{9,5},{13... | collective-permute-start | bytes 179720 | tf_op jit(solution)/shard_map/ppermute | solution.py:28
  16.4 5.4 %collective-permute-start = (f32[39,3,128]{2,1,0:T(4,128)S(1)}, f32[39,3,128]{2,1,0:T(4,128)S(1)}, u32[]{:S(2)}, u32[]{:S(2)}) collective-permute-start(f32[39,3,128]{2,1,0:T(4,128)S(1)} %get-tuple-element.10), channel_id=1, source_target_pairs={{0,4},{4,8},{8,12},{12,16},{16,20},{20,24},{24,28},{1,5},{5,9},{9,... | collective-permute-start | bytes 179720 | tf_op jit(solution)/shard_map/ppermute | solution.py:28
  27.0 27.7 %copy-start.3 = (f32[38,38]{1,0:T(8,128)S(1)}, f32[38,38]{1,0:T(8,128)}, u32[]{:S(2)}) copy-start(f32[38,38]{1,0:T(8,128)} %param.13) | copy-start | bytes 17332
  54.7 3.1 %copy-start.1 = (f32[128,38,128]{2,1,0:T(8,128)S(1)}, f32[128,38,128]{2,1,0:T(8,128)}, u32[]{:S(2)}) copy-start(f32[128,38,128]{2,1,0:T(8,128)} %shard_map.113) | copy-start | bytes 7471108
  54.7 3.1 %copy-start.4 = (f32[38,38]{1,0:T(8,128)S(1)}, f32[38,38]{1,0:T(8,128)}, u32[]{:S(2)}) copy-start(f32[38,38]{1,0:T(8,128)} %param.14) | copy-start | bytes 17332
  65.9 3.3 %copy-start.7 = (f32[4,38]{1,0:T(4,128)S(1)}, f32[4,38]{1,0:T(4,128)}, u32[]{:S(2)}) copy-start(f32[4,38]{1,0:T(4,128)} %param.16) | copy-start | bytes 1828
  69.1 1.7 %copy-start.8 = (f32[128]{0:T(128)S(1)}, f32[128]{0:T(128)}, u32[]{:S(2)}) copy-start(f32[128]{0:T(128)} %param.17) | copy-start | bytes 1540
  71.1 3.6 %collective-permute-start.4 = (f32[4,128]{1,0:T(4,128)S(1)}, f32[4,128]{1,0:T(4,128)S(1)}, u32[]{:S(2)}, u32[]{:S(2)}) collective-permute-start(f32[4,128]{1,0:T(4,128)S(1)} %broadcast_multiply_fusion), channel_id=1, source_target_pairs={{0,1},{1,0},{2,3},{3,2},{4,5},{5,4},{6,7},{7,6},{8,9},{9,8},{10,11... | collective-permute-start | bytes 6152 | tf_op jit(solution)/shard_map/ppermute | solution.py:171
  74.8 4.6 %collective-permute-start.5 = (f32[4,128]{1,0:T(4,128)S(1)}, f32[4,128]{1,0:T(4,128)S(1)}, u32[]{:S(2)}, u32[]{:S(2)}) collective-permute-start(f32[4,128]{1,0:T(4,128)S(1)} %fusion.40), channel_id=1, source_target_pairs={{0,2},{1,3},{2,0},{3,1},{4,6},{5,7},{6,4},{7,5},{8,10},{9,11},{10,... | collective-permute-start | bytes 6152 | tf_op jit(solution)/shard_map/ppermute | solution.py:171
  79.4 1.2 %collective-permute-start.6 = (f32[1,4,128]{2,0,1:T(1,128)S(1)}, f32[1,4,128]{2,0,1:T(1,128)S(1)}, u32[]{:S(2)}, u32[]{:S(2)}) collective-permute-start(f32[1,4,128]{2,0,1:T(1,128)S(1)} %bitcast.123), channel_id=1, source_target_pairs={{0,4},{4,0},{8,12},{12,8},{16,20},{20,16},{24,28},{28,24},{1,5},{5... | collective-permute-start | bytes 6152 | tf_op jit(solution)/shard_map/ppermute | solution.py:184
  80.5 4.5 %collective-permute-start.7 = (f32[2,4,128]{2,0,1:T(2,128)S(1)}, f32[2,4,128]{2,0,1:T(2,128)S(1)}, u32[]{:S(2)}, u32[]{:S(2)}) collective-permute-start(f32[2,4,128]{2,0,1:T(2,128)S(1)} %maximum_select_fusion.2), channel_id=1, source_target_pairs={{0,8},{4,12},{8,0},{12,4},{16,24},{20,28},{24,16},{28,20},{1,9},{5... | collective-permute-start | bytes 12296 | tf_op jit(solution)/shard_map/ppermute | solution.py:184
  85.0 5.2 %collective-permute-start.8 = (f32[4,4,128]{2,0,1:T(4,128)S(1)}, f32[4,4,128]{2,0,1:T(4,128)S(1)}, u32[]{:S(2)}, u32[]{:S(2)}) collective-permute-start(f32[4,4,128]{2,0,1:T(4,128)S(1)} %maximum_select_fusion.1), channel_id=1, source_target_pairs={{0,16},{4,20},{8,24},{12,28},{16,0},{20,4},{24,8},{28,12},{1,17},{... | collective-permute-start | bytes 24584 | tf_op jit(solution)/shard_map/ppermute | solution.py:184
  88.4 4.8 %copy-start.6 = (f32[4,1024]{1,0:T(4,128)S(1)}, f32[4,1024]{1,0:T(4,128)}, u32[]{:S(2)}) copy-start(f32[4,1024]{1,0:T(4,128)} %param.19) | copy-start | bytes 49156

commit v2 on v0

--- a/solution.py
+++ b/solution.py
@@ -19,12 +19,12 @@
 CHEMISTRY_PRECISION = lax.Precision.HIGH
 
 
-def edge_layers(shard, axis, dim, width):
+def edge_layers(shard, axis, dim, width, arrange=lambda layers: layers):
     peers, length = (lax.axis_size(axis), shard.shape[dim])
     up = [(i, i + 1) for i in range(peers - 1)]
     down = [(j, i) for i, j in up]
-    last = lax.slice_in_dim(shard, length - width, length, axis=dim)
-    initial = lax.slice_in_dim(shard, 0, width, axis=dim)
+    last = arrange(lax.slice_in_dim(shard, length - width, length, axis=dim))
+    initial = arrange(lax.slice_in_dim(shard, 0, width, axis=dim))
     return lax.ppermute(last, axis, up), lax.ppermute(initial, axis, down)
 
 
@@ -114,8 +114,14 @@
     assert rows == cols and rows % CHUNK == 0
     axial_edges = jnp.concatenate([species, speed[0:1]], axis=0)
     top, bottom = edge_layers(axial_edges, "axial", 1, width)
-    radial_edges = jnp.swapaxes(jnp.concatenate([species, speed[1:2]], axis=0), 1, 2)
-    left, right = edge_layers(radial_edges, "radial", 1, width)
+    radial_edges = jnp.concatenate([species, speed[1:2]], axis=0)
+    left, right = edge_layers(
+        radial_edges, "radial", 2, width, lambda layers: layers.reshape(layers.shape[0], -1)
+    )
+    left, right = (
+        jnp.swapaxes(layers.reshape(species_count + 1, rows, width), 1, 2)
+        for layers in (left, right)
+    )
     before = ((0, 0), (HALO - width, 0), (0, 0))
     after = ((0, 0), (0, HALO - width), (0, 0))
     top, left = (jnp.pad(top, before), jnp.pad(left, before))

time: 90.4 us -> 99.8 us (1.10)
  local copies, waits for them, and re-layouts: 9.11 us -> 14.5 us
  other arithmetic: 6.21 us -> 9.68 us
  waiting for transfers between devices: 6.82 us -> 9.81 us
  starting transfers between devices: 21.1 us -> 18.5 us
    reshape x0 -> x8, local copies, waits for them, and re-layouts: none -> 8.67 us  [the longest x4 7.32 us: transport(): layers.reshape(layers.shape[0], -1)]
    concatenate x0 -> x1, other arithmetic: none -> 5.51 us  [transport(): radial_edges = jnp.concatenate([species, speed[1:2]], axis=0)]
    unnamed x24 -> x22, local copies, waits for them, and re-layouts: 5.2 us -> 1.96 us
    transpose x1 -> x0, other arithmetic: 2.02 us -> none  [transport(): jnp.swapaxes(jnp.concatenate([species, speed[1:2]], axis=0), 1, 2)]
    ppermute x4, waiting for transfers between devices: 1.28 us -> 3.15 us  [edge_layers(): return (lax.ppermute(last, axis, up), lax.ppermute(initial, axis, down))]
    ppermute x2, starting transfers between devices: 5.74 us -> 4.21 us  [butterfly_sum(): part = part + lax.ppermute(part, axis, pairs)]
    ppermute x3, starting transfers between devices: 6.44 us -> 5.2 us  [doubling_gather(): other = lax.ppermute(blocks, axis, pairs)]
  transfers between devices with their start and end apart: 9 -> 9, of which waited for: 6 -> 5; matrix products, arithmetic and copies ran while one was open for 6% -> 10% of each run, Pallas kernels for 0% -> 0%
where the time goes in v2:
time: 99.8 us; the launch traced here: 98.1 us
  Pallas kernels  28.3 us (28%)
  starting transfers between devices  18.5 us (19%)
  matrix products  16.3 us (16%)
  local copies, waits for them, and re-layouts  14.5 us (15%)
  waiting for transfers between devices  9.81 us (10%)
  other arithmetic  9.68 us (10%)
    pallas_call x1, Pallas kernels, transport(): pl.pallas_call(transport_kernel, grid=(species_count,), in_specs=[plane,...  28.3 us
    ppermute x4, starting transfers between devices, edge_layers(): return (lax.ppermute(last, axis, up), lax.ppermute(initial, axis, down))  9.13 us
    dot_general x3, matrix products, kinetics_advance(): jnp.tensordot(frozen_jacobian_inverse_addend, defect, axes=(1, 0), precis...  8.65 us
    reshape x4, local copies, waits for them, and re-layouts, transport(): layers.reshape(layers.shape[0], -1)  7.32 us
    dot_general x3, matrix products, kinetics_advance(): jnp.tensordot(linearized_kinetics_operator, current, axes=(1, 0), precisi...  5.72 us
    concatenate x1, other arithmetic, transport(): radial_edges = jnp.concatenate([species, speed[1:2]], axis=0)  5.51 us
    ppermute x3, starting transfers between devices, doubling_gather(): other = lax.ppermute(blocks, axis, pairs)  5.2 us
    ppermute x2, starting transfers between devices, butterfly_sum(): part = part + lax.ppermute(part, axis, pairs)  4.21 us
  transfers between devices with their start and end apart: 9, of which 5 were waited for; matrix products, arithmetic and copies ran while one was open for 10% of the time, Pallas kernels for 0%

profile of v2, /device:TPU:0, one launch (start us, length us, event | category | flops | bytes accessed | tf_op | source)
XLA Modules:
  0.0 98.1 jit_solution(13538449032058679810)
XLA Ops:
  0.6 0.9 fusion.40
  1.6 5.5 %pad_maximum_fusion = (f32[39,128,3]{2,1,0:T(8,128)}, f32[39,128,3]{2,1,0:T(8,128)}) fusion(f32[1,128,128]{2,1,0:T(8,128)S(1)} %get-tuple-element.12, f32[38,128,128]{2,1,0:T(8,128)} %field_ref.1), kind=kLoop, calls=%fused_computation.24 | loop fusion | flops 29952 | bytes 2675712 | tf_op jit(solution)/shard_map/concatenate | solution.py:117
  7.1 2.9 %reshape.50 = f32[39,384]{1,0:T(8,128)S(1)} reshape(f32[39,128,3]{2,1,0:T(8,128)} %get-tuple-element.9) | data formatting | bytes 119808 | tf_op jit(solution)/shard_map/reshape | solution.py:119
  10.0 0.8 copy.25
  10.8 4.9 %collective-permute-start.2 = (f32[39,384]{0,1:T(8,128)}, f32[39,384]{0,1:T(8,128)S(1)}, u32[]{:S(2)}, u32[]{:S(2)}) collective-permute-start(f32[39,384]{0,1:T(8,128)} %copy.25), channel_id=1, source_target_pairs={{0,1},{1,2},{2,3},{4,5},{5,6},{6,7},{8,9},{9,10},{10,11},{12,13},{... | collective-permute-start | bytes 179720 | tf_op jit(solution)/shard_map/ppermute | solution.py:28
  15.8 2.8 %reshape.51 = f32[39,384]{1,0:T(8,128)S(1)} reshape(f32[39,128,3]{2,1,0:T(8,128)} %get-tuple-element.8) | data formatting | bytes 119808 | tf_op jit(solution)/shard_map/reshape | solution.py:119
  18.6 0.8 copy.26
  19.4 1.3 %collective-permute-start.3 = (f32[39,384]{0,1:T(8,128)}, f32[39,384]{0,1:T(8,128)}, u32[]{:S(2)}, u32[]{:S(2)}) collective-permute-start(f32[39,384]{0,1:T(8,128)} %copy.26), channel_id=1, source_target_pairs={{1,0},{2,1},{3,2},{5,4},{6,5},{7,6},{9,8},{10,9},{11,10},{13,12},{... | collective-permute-start | bytes 179720 | tf_op jit(solution)/shard_map/ppermute | solution.py:28
  21.3 1.5 %collective-permute-start = (f32[39,3,128]{2,1,0:T(4,128)}, f32[39,3,128]{2,1,0:T(4,128)S(1)}, u32[]{:S(2)}, u32[]{:S(2)}) collective-permute-start(f32[39,3,128]{2,1,0:T(4,128)} %get-tuple-element.11), channel_id=1, source_target_pairs={{0,4},{4,8},{8,12},{12,16},{16,20},{20,24},{24,28},{1,5},{5,9},{9,... | collective-permute-start | bytes 179720 | tf_op jit(solution)/shard_map/ppermute | solution.py:28
  22.8 1.5 %collective-permute-start.1 = (f32[39,3,128]{2,1,0:T(4,128)S(1)}, f32[39,3,128]{2,1,0:T(4,128)S(1)}, u32[]{:S(2)}, u32[]{:S(2)}) collective-permute-start(f32[39,3,128]{2,1,0:T(4,128)S(1)} %get-tuple-element.10), channel_id=1, source_target_pairs={{4,0},{8,4},{12,8},{16,12},{20,16},{24,20},{28,24},{5,1},{9,5},{13... | collective-permute-start | bytes 179720 | tf_op jit(solution)/shard_map/ppermute | solution.py:28
  24.8 3.1 %collective-permute-done.3 = f32[39,384]{0,1:T(8,128)} collective-permute-done((f32[39,384]{0,1:T(8,128)}, f32[39,384]{0,1:T(8,128)}, u32[]{:S(2)}, u32[]{:S(2)}) %collective-permute-start.3) | collective-permute-done | bytes 59936 | tf_op jit(solution)/shard_map/ppermute | solution.py:28
  28.0 1.0 %reshape.44 = f32[39,128,3]{0,2,1:T(4,128)S(1)} reshape(f32[39,384]{0,1:T(8,128)} %collective-permute-done.3) | data formatting | bytes 119808 | tf_op jit(solution)/shard_map/reshape | solution.py:122
  29.1 0.7 pad.16.left_ref.left_speed_ref
  30.5 0.7 pad.14.top_ref.top_speed_ref
  31.8 28.3 %shard_map.113 = f32[128,38,128]{2,1,0:T(8,128)} custom-call(f32[38,128,128]{2,1,0:T(8,128)} %field_ref.1, f32[2,128,128]{2,1,0:T(8,128)} %speed_ref.1, f32[39,8,128]{2,1,0:T(8,128)} %pad.14.top_ref.top_speed_ref, f32[39,8,128]{2,1,0:T(8,128)} %pad.14.top_ref.top_speed_ref, f32[39,8,128]{2,1,0:T(8,128)} %pad.15.bottom_ref.bottom_speed_ref, ...), custom_call_target="tpu_custom_call" | custom-call | tf_op jit(solution)/shard_map/pallas_call | solution.py:135
  60.1 3.1 %fusion.13 = f32[128,128,38]{1,2,0:T(8,128)S(1)} fusion(f32[128,38,128]{2,1,0:T(8,128)} %shard_map.113, f32[38,38]{1,0:T(8,128)S(1)} %copy-done.3), kind=kOutput, calls=%fused_computation.22 | convolution fusion | flops 141950976 | bytes 4986512 | tf_op jit(solution)/shard_map/dot_general | solution.py:159
  63.3 2.5 %bitcast_subtract_fusion.4 = f32[38,128,128]{2,0,1:T(8,128)S(1)} fusion(f32[128,128,38]{1,2,0:T(8,128)S(1)} %fusion.13, f32[128,38,128]{2,1,0:T(8,128)S(1)} %copy-done.1, f32[128,128]{1,0:T(8,128)S(1)} %exponential_multiply_fusion, f32[38,38]{1,0:T(8,128)S(1)} %copy-done.4), kind=kOutput, calls=%fused_computation.11 | convolution fusion | flops 148176896 | bytes 7542416 | tf_op jit(solution)/shard_map/dot_general | solution.py:166
  65.8 1.3 %fusion.33 = f32[128,128,38]{1,2,0:T(8,128)S(1)} fusion(f32[38,128,128]{2,0,1:T(8,128)S(1)} %bitcast_subtract_fusion.4, f32[38,38]{1,0:T(8,128)S(1)} %copy-done.3), kind=kOutput, calls=%fused_computation.43 | convolution fusion | flops 141950976 | bytes 4986512 | tf_op jit(solution)/shard_map/dot_general | solution.py:159
  67.1 2.9 %bitcast_subtract_fusion.2 = f32[38,128,128]{2,0,1:T(8,128)S(1)} fusion(f32[38,128,128]{2,0,1:T(8,128)S(1)} %bitcast_subtract_fusion.4, f32[128,128,38]{1,2,0:T(8,128)S(1)} %fusion.33, f32[128,38,128]{2,1,0:T(8,128)S(1)} %copy-done.1, f32[128,128]{1,0:T(8,128)S(1)} %exponential_multiply_fusion, f32[38,38]{1,0:T(8,128)S(1)} %copy-done.4), kind=kOutput, calls=%fused_computation.7 | convolution fusion | flops 148176896 | bytes 10032784 | tf_op jit(solution)/shard_map/dot_general | solution.py:166
  70.0 1.3 %fusion.31 = f32[128,128,38]{1,2,0:T(8,128)S(1)} fusion(f32[38,128,128]{2,0,1:T(8,128)S(1)} %bitcast_subtract_fusion.2, f32[38,38]{1,0:T(8,128)S(1)} %copy-done.3), kind=kOutput, calls=%fused_computation.41 | convolution fusion | flops 141950976 | bytes 4986512 | tf_op jit(solution)/shard_map/dot_general | solution.py:159
  71.3 3.3 %fusion = f32[38,128,128]{2,0,1:T(8,128)S(1)} fusion(f32[128,38,128]{2,1,0:T(8,128)S(1)} %copy-done.1, f32[38,128,128]{2,0,1:T(8,128)S(1)} %bitcast_subtract_fusion.2, f32[128,128,38]{1,2,0:T(8,128)S(1)} %fusion.31, f32[128,128]{1,0:T(8,128)S(1)} %exponential_multiply_fusion, pred[128]{0:T(512)(128)(4,1)S(1)} %gt.22, f32[38,38]{1,0:T(8,128)S(1)} %copy-done.4), kind=kOutput, calls=%fused_computation.3 | convolution fusion | flops 148799488 | bytes 10032912 | tf_op jit(solution)/shard_map/dot_general | solution.py:166
  74.6 1.7 %convolution_bitcast_fusion = f32[4,128,128]{2,0,1:T(4,128)S(1)} fusion(f32[38,128,128]{2,0,1:T(8,128)S(1)} %fusion, f32[4,38]{1,0:T(4,128)S(1)} %copy-done.7), kind=kOutput, calls=%fused_computation.32 | convolution fusion | flops 29884416 | bytes 2753120 | tf_op jit(solution)/shard_map/dot_general | solution.py:172
  76.6 1.6 %collective-permute-start.4 = (f32[4,128]{1,0:T(4,128)S(1)}, f32[4,128]{1,0:T(4,128)S(1)}, u32[]{:S(2)}, u32[]{:S(2)}) collective-permute-start(f32[4,128]{1,0:T(4,128)S(1)} %broadcast_multiply_fusion), channel_id=1, source_target_pairs={{0,1},{1,0},{2,3},{3,2},{4,5},{5,4},{6,7},{7,6},{8,9},{9,8},{10,11... | collective-permute-start | bytes 6152 | tf_op jit(solution)/shard_map/ppermute | solution.py:182
  78.2 2.0 %collective-permute-done.4 = f32[4,128]{1,0:T(4,128)S(1)} collective-permute-done((f32[4,128]{1,0:T(4,128)S(1)}, f32[4,128]{1,0:T(4,128)S(1)}, u32[]{:S(2)}, u32[]{:S(2)}) %collective-permute-start.4) | collective-permute-done | bytes 2080 | tf_op jit(solution)/shard_map/ppermute | solution.py:182
  80.3 2.6 %collective-permute-start.5 = (f32[4,128]{1,0:T(4,128)S(1)}, f32[4,128]{1,0:T(4,128)S(1)}, u32[]{:S(2)}, u32[]{:S(2)}) collective-permute-start(f32[4,128]{1,0:T(4,128)S(1)} %fusion.39), channel_id=1, source_target_pairs={{0,2},{1,3},{2,0},{3,1},{4,6},{5,7},{6,4},{7,5},{8,10},{9,11},{10,... | collective-permute-start | bytes 6152 | tf_op jit(solution)/shard_map/ppermute | solution.py:182
  82.9 1.9 %collective-permute-done.5 = f32[4,128]{1,0:T(4,128)S(1)} collective-permute-done((f32[4,128]{1,0:T(4,128)S(1)}, f32[4,128]{1,0:T(4,128)S(1)}, u32[]{:S(2)}, u32[]{:S(2)}) %collective-permute-start.5) | collective-permute-done | bytes 2080 | tf_op jit(solution)/shard_map/ppermute | solution.py:182
  84.8 1.2 %collective-permute-done.6 = f32[1,4,128]{2,0,1:T(1,128)S(1)} collective-permute-done((f32[1,4,128]{2,0,1:T(1,128)S(1)}, f32[1,4,128]{2,0,1:T(1,128)S(1)}, u32[]{:S(2)}, u32[]{:S(2)}) %collective-permute-start.6) | collective-permute-done | bytes 2080 | tf_op jit(solution)/shard_map/ppermute | solution.py:195
  85.9 2.2 %collective-permute-start.7 = (f32[2,4,128]{2,0,1:T(2,128)S(1)}, f32[2,4,128]{2,0,1:T(2,128)S(1)}, u32[]{:S(2)}, u32[]{:S(2)}) collective-permute-start(f32[2,4,128]{2,0,1:T(2,128)S(1)} %maximum_select_fusion.2), channel_id=1, source_target_pairs={{0,8},{4,12},{8,0},{12,4},{16,24},{20,28},{24,16},{28,20},{1,9},{5... | collective-permute-start | bytes 12296 | tf_op jit(solution)/shard_map/ppermute | solution.py:195
  88.1 1.6 %collective-permute-done.7 = f32[2,4,128]{2,0,1:T(2,128)S(1)} collective-permute-done((f32[2,4,128]{2,0,1:T(2,128)S(1)}, f32[2,4,128]{2,0,1:T(2,128)S(1)}, u32[]{:S(2)}, u32[]{:S(2)}) %collective-permute-start.7) | collective-permute-done | bytes 4128 | tf_op jit(solution)/shard_map/ppermute | solution.py:195
  89.7 3.0 %collective-permute-start.8 = (f32[4,4,128]{2,0,1:T(4,128)S(1)}, f32[4,4,128]{2,0,1:T(4,128)S(1)}, u32[]{:S(2)}, u32[]{:S(2)}) collective-permute-start(f32[4,4,128]{2,0,1:T(4,128)S(1)} %maximum_select_fusion.1), channel_id=1, source_target_pairs={{0,16},{4,20},{8,24},{12,28},{16,0},{20,4},{24,8},{28,12},{1,17},{... | collective-permute-start | bytes 24584 | tf_op jit(solution)/shard_map/ppermute | solution.py:195
  92.7 1.9 %copy.22 = f32[38,128,128]{2,1,0:T(8,128)} copy(f32[38,128,128]{2,0,1:T(8,128)S(1)} %fusion) | data formatting | bytes 4980736
  94.7 2.8 %select_reduce_fusion = f32[4,1024]{1,0:T(4,128)S(1)} fusion(f32[4,1024]{1,0:T(4,128)S(1)} %bitcast.112, s32[4,1024]{1,0:T(4,128)S(1)} %constant_dynamic-slice_fusion), kind=kLoop, calls=%fused_computation | loop fusion | flops 12578816 | bytes 49152 | tf_op jit(solution)/shard_map/reduce_sum | solution.py:247
  (45 shorter events, 3.7 us)
Async XLA Ops:
  0.6 92.1 %copy-start = (s32[4,32768]{1,0:T(4,128)S(1)}, s32[4,32768]{1,0:T(4,128)}, u32[]{:S(2)}) copy-start(s32[4,32768]{1,0:T(4,128)} %param.18) | copy-start | bytes 1572868
  7.1 13.6 %copy-start.2 = (f32[38,128,128]{2,1,0:T(8,128)S(1)}, f32[38,128,128]{2,1,0:T(8,128)}, u32[]{:S(2)}) copy-start(f32[38,128,128]{2,1,0:T(8,128)} %field_ref.1) | copy-start | bytes 7471108
  10.8 13.8 %collective-permute-start.2 = (f32[39,384]{0,1:T(8,128)}, f32[39,384]{0,1:T(8,128)S(1)}, u32[]{:S(2)}, u32[]{:S(2)}) collective-permute-start(f32[39,384]{0,1:T(8,128)} %copy.25), channel_id=1, source_target_pairs={{0,1},{1,2},{2,3},{4,5},{5,6},{6,7},{8,9},{9,10},{10,11},{12,13},{... | collective-permute-start | bytes 179720 | tf_op jit(solution)/shard_map/ppermute | solution.py:28
  15.8 8.5 %copy-start.5 = (f32[128,128]{1,0:T(8,128)S(1)}, f32[128,128]{1,0:T(8,128)}, u32[]{:S(2)}) copy-start(f32[128,128]{1,0:T(8,128)} %param.12) | copy-start | bytes 196612
  15.8 8.6 %copy-start.9 = (s32[64,1]{0,1:T(1,128)S(1)}, s32[64,1]{0,1:T(1,128)}, u32[]{:S(2)}) copy-start(s32[64,1]{0,1:T(1,128)} %param.15) | copy-start | bytes 772
  19.4 8.6 %collective-permute-start.3 = (f32[39,384]{0,1:T(8,128)}, f32[39,384]{0,1:T(8,128)}, u32[]{:S(2)}, u32[]{:S(2)}) collective-permute-start(f32[39,384]{0,1:T(8,128)} %copy.26), channel_id=1, source_target_pairs={{1,0},{2,1},{3,2},{5,4},{6,5},{7,6},{9,8},{10,9},{11,10},{13,12},{... | collective-permute-start | bytes 179720 | tf_op jit(solution)/shard_map/ppermute | solution.py:28
  21.3 9.1 %collective-permute-start = (f32[39,3,128]{2,1,0:T(4,128)}, f32[39,3,128]{2,1,0:T(4,128)S(1)}, u32[]{:S(2)}, u32[]{:S(2)}) collective-permute-start(f32[39,3,128]{2,1,0:T(4,128)} %get-tuple-element.11), channel_id=1, source_target_pairs={{0,4},{4,8},{8,12},{12,16},{16,20},{20,24},{24,28},{1,5},{5,9},{9,... | collective-permute-start | bytes 179720 | tf_op jit(solution)/shard_map/ppermute | solution.py:28
  22.8 8.4 %collective-permute-start.1 = (f32[39,3,128]{2,1,0:T(4,128)S(1)}, f32[39,3,128]{2,1,0:T(4,128)S(1)}, u32[]{:S(2)}, u32[]{:S(2)}) collective-permute-start(f32[39,3,128]{2,1,0:T(4,128)S(1)} %get-tuple-element.10), channel_id=1, source_target_pairs={{4,0},{8,4},{12,8},{16,12},{20,16},{24,20},{28,24},{5,1},{9,5},{13... | collective-permute-start | bytes 179720 | tf_op jit(solution)/shard_map/ppermute | solution.py:28
  31.8 28.3 %copy-start.3 = (f32[38,38]{1,0:T(8,128)S(1)}, f32[38,38]{1,0:T(8,128)}, u32[]{:S(2)}) copy-start(f32[38,38]{1,0:T(8,128)} %param.13) | copy-start | bytes 17332
  60.1 3.1 %copy-start.1 = (f32[128,38,128]{2,1,0:T(8,128)S(1)}, f32[128,38,128]{2,1,0:T(8,128)}, u32[]{:S(2)}) copy-start(f32[128,38,128]{2,1,0:T(8,128)} %shard_map.113) | copy-start | bytes 7471108
  60.1 3.1 %copy-start.4 = (f32[38,38]{1,0:T(8,128)S(1)}, f32[38,38]{1,0:T(8,128)}, u32[]{:S(2)}) copy-start(f32[38,38]{1,0:T(8,128)} %param.14) | copy-start | bytes 17332
  71.3 3.3 %copy-start.7 = (f32[4,38]{1,0:T(4,128)S(1)}, f32[4,38]{1,0:T(4,128)}, u32[]{:S(2)}) copy-start(f32[4,38]{1,0:T(4,128)} %param.16) | copy-start | bytes 1828
  74.6 1.7 %copy-start.8 = (f32[128]{0:T(128)S(1)}, f32[128]{0:T(128)}, u32[]{:S(2)}) copy-start(f32[128]{0:T(128)} %param.17) | copy-start | bytes 1540
  76.6 3.6 %collective-permute-start.4 = (f32[4,128]{1,0:T(4,128)S(1)}, f32[4,128]{1,0:T(4,128)S(1)}, u32[]{:S(2)}, u32[]{:S(2)}) collective-permute-start(f32[4,128]{1,0:T(4,128)S(1)} %broadcast_multiply_fusion), channel_id=1, source_target_pairs={{0,1},{1,0},{2,3},{3,2},{4,5},{5,4},{6,7},{7,6},{8,9},{9,8},{10,11... | collective-permute-start | bytes 6152 | tf_op jit(solution)/shard_map/ppermute | solution.py:182
  80.3 4.5 %collective-permute-start.5 = (f32[4,128]{1,0:T(4,128)S(1)}, f32[4,128]{1,0:T(4,128)S(1)}, u32[]{:S(2)}, u32[]{:S(2)}) collective-permute-start(f32[4,128]{1,0:T(4,128)S(1)} %fusion.39), channel_id=1, source_target_pairs={{0,2},{1,3},{2,0},{3,1},{4,6},{5,7},{6,4},{7,5},{8,10},{9,11},{10,... | collective-permute-start | bytes 6152 | tf_op jit(solution)/shard_map/ppermute | solution.py:182
  84.8 1.2 %collective-permute-start.6 = (f32[1,4,128]{2,0,1:T(1,128)S(1)}, f32[1,4,128]{2,0,1:T(1,128)S(1)}, u32[]{:S(2)}, u32[]{:S(2)}) collective-permute-start(f32[1,4,128]{2,0,1:T(1,128)S(1)} %bitcast.115), channel_id=1, source_target_pairs={{0,4},{4,0},{8,12},{12,8},{16,20},{20,16},{24,28},{28,24},{1,5},{5... | collective-permute-start | bytes 6152 | tf_op jit(solution)/shard_map/ppermute | solution.py:195
  85.9 3.8 %collective-permute-start.7 = (f32[2,4,128]{2,0,1:T(2,128)S(1)}, f32[2,4,128]{2,0,1:T(2,128)S(1)}, u32[]{:S(2)}, u32[]{:S(2)}) collective-permute-start(f32[2,4,128]{2,0,1:T(2,128)S(1)} %maximum_select_fusion.2), channel_id=1, source_target_pairs={{0,8},{4,12},{8,0},{12,4},{16,24},{20,28},{24,16},{28,20},{1,9},{5... | collective-permute-start | bytes 12296 | tf_op jit(solution)/shard_map/ppermute | solution.py:195
  89.7 4.9 %collective-permute-start.8 = (f32[4,4,128]{2,0,1:T(4,128)S(1)}, f32[4,4,128]{2,0,1:T(4,128)S(1)}, u32[]{:S(2)}, u32[]{:S(2)}) collective-permute-start(f32[4,4,128]{2,0,1:T(4,128)S(1)} %maximum_select_fusion.1), channel_id=1, source_target_pairs={{0,16},{4,20},{8,24},{12,28},{16,0},{20,4},{24,8},{28,12},{1,17},{... | collective-permute-start | bytes 24584 | tf_op jit(solution)/shard_map/ppermute | solution.py:195
  92.7 4.8 %copy-start.6 = (f32[4,1024]{1,0:T(4,128)S(1)}, f32[4,1024]{1,0:T(4,128)}, u32[]{:S(2)}) copy-start(f32[4,1024]{1,0:T(4,128)} %param.19) | copy-start | bytes 49156

commit v3 on v0

--- a/solution.py
+++ b/solution.py
@@ -28,29 +28,30 @@
     return lax.ppermute(last, axis, up), lax.ppermute(initial, axis, down)
 
 
+SCALED_EPS = WENO_EPS * 12.0 / 13.0
+SLOPE_WEIGHT = 3.0 / 13.0
+
+
 def weno_side(minus_two, minus_one, centre, plus_one, plus_two):
-    curve_zero = minus_two - 2.0 * minus_one + centre
-    curve_one = minus_one - 2.0 * centre + plus_one
-    curve_two = centre - 2.0 * plus_one + plus_two
-    slope_zero = minus_two - 4.0 * minus_one + 3.0 * centre
+    curve_zero = (minus_two + centre) - (minus_one + minus_one)
+    curve_one = (minus_one + plus_one) - (centre + centre)
+    curve_two = (centre + plus_two) - (plus_one + plus_one)
+    slope_zero = curve_zero + 2.0 * (centre - minus_one)
     slope_one = minus_one - plus_one
-    slope_two = 3.0 * centre - 4.0 * plus_one + plus_two
-    beta_zero = 13.0 / 12.0 * curve_zero * curve_zero + 0.25 * slope_zero * slope_zero
-    beta_one = 13.0 / 12.0 * curve_one * curve_one + 0.25 * slope_one * slope_one
-    beta_two = 13.0 / 12.0 * curve_two * curve_two + 0.25 * slope_two * slope_two
-    guard_zero = WENO_EPS + beta_zero
-    guard_one = WENO_EPS + beta_one
-    guard_two = WENO_EPS + beta_two
+    slope_two = curve_two + 2.0 * (centre - plus_one)
+    guard_zero = (SCALED_EPS + curve_zero * curve_zero) + SLOPE_WEIGHT * (slope_zero * slope_zero)
+    guard_one = (SCALED_EPS + curve_one * curve_one) + SLOPE_WEIGHT * (slope_one * slope_one)
+    guard_two = (SCALED_EPS + curve_two * curve_two) + SLOPE_WEIGHT * (slope_two * slope_two)
     guard_zero = guard_zero * guard_zero
     guard_one = guard_one * guard_one
     guard_two = guard_two * guard_two
     cross_zero = guard_one * guard_two
     cross_one = 6.0 * (guard_zero * guard_two)
     cross_two = 3.0 * (guard_zero * guard_one)
-    blended = cross_zero * (2.0 * minus_two - 7.0 * minus_one + 11.0 * centre)
-    blended = blended + cross_one * (-minus_one + 5.0 * centre + 2.0 * plus_one)
-    blended = blended + cross_two * (2.0 * centre + 5.0 * plus_one - plus_two)
-    return blended / (6.0 * (cross_zero + cross_one + cross_two))
+    blended = cross_zero * (curve_zero + 3.0 * slope_zero)
+    blended = blended + cross_one * (curve_one - 3.0 * slope_one)
+    blended = blended + cross_two * (curve_two - 3.0 * slope_two)
+    return centre + blended / (12.0 * (cross_zero + cross_one + cross_two))
 
 
 HALO = 8

time: 90.4 us -> 89.6 us (level)
  no operation moved by 1% of the time
where the time goes in v3:
time: 89.6 us; the launch traced here: 88 us
  Pallas kernels  27.5 us (31%)
  starting transfers between devices  21.1 us (24%)
  matrix products  16.3 us (18%)
  local copies, waits for them, and re-layouts  9.11 us (10%)
  waiting for transfers between devices  6.82 us (8%)
  other arithmetic  6.21 us (7%)
  between operations  0.91 us (1%)
    pallas_call x1, Pallas kernels, transport(): pl.pallas_call(transport_kernel, grid=(species_count,), in_specs=[plane,...  27.5 us
    ppermute x4, starting transfers between devices, edge_layers(): return (lax.ppermute(last, axis, up), lax.ppermute(initial, axis, down))  8.97 us
    dot_general x3, matrix products, kinetics_advance(): jnp.tensordot(frozen_jacobian_inverse_addend, defect, axes=(1, 0), precis...  8.61 us
    ppermute x3, starting transfers between devices, doubling_gather(): other = lax.ppermute(blocks, axis, pairs)  6.45 us
    ppermute x2, starting transfers between devices, butterfly_sum(): part = part + lax.ppermute(part, axis, pairs)  5.74 us
    dot_general x3, matrix products, kinetics_advance(): jnp.tensordot(linearized_kinetics_operator, current, axes=(1, 0), precisi...  5.73 us
    unnamed x24, local copies, waits for them, and re-layouts  5.2 us
    ppermute x2, waiting for transfers between devices, butterfly_sum(): part = part + lax.ppermute(part, axis, pairs)  3.13 us
  transfers between devices with their start and end apart: 9, of which 6 were waited for; matrix products, arithmetic and copies ran while one was open for 6% of the time, Pallas kernels for 0%

profile of v3, /device:TPU:0, one launch (start us, length us, event | category | flops | bytes accessed | tf_op | source)
XLA Modules:
  0.0 88.0 jit_solution(12659619529188567416)
XLA Ops:
  0.6 0.9 %fusion.40 = (f32[1,128,128]{2,1,0:T(8,128)S(1)}, f32[1,128,128]{2,1,0:T(8,128)S(1)}) fusion(f32[2,128,128]{2,1,0:T(8,128)} %speed_ref.1), kind=kLoop, calls=%fused_computation.55 | loop fusion | bytes 262144 | tf_op jit(solution)/shard_map/slice | solution.py:118
  1.7 3.1 %copy.19 = f32[38,128,128]{1,2,0:T(8,128)} copy(f32[38,128,128]{2,1,0:T(8,128)} %field_ref.1) | data formatting | bytes 4980736 | tf_op args[0]
  4.8 2.0 %maximum_bitcast_fusion = f32[39,128,128]{2,1,0:T(8,128)S(1)} fusion(f32[1,128,128]{1,2,0:T(8,128)S(1)} %copy.23, f32[38,128,128]{1,2,0:T(8,128)} %copy.19), kind=kLoop, calls=%fused_computation.24 | loop fusion | flops 638976 | bytes 5111808 | tf_op jit(solution)/shard_map/transpose | solution.py:118
  6.9 4.9 %collective-permute-start.2 = (f32[39,3,128]{2,1,0:T(4,128)S(1)}, f32[39,3,128]{2,1,0:T(4,128)S(1)}, u32[]{:S(2)}, u32[]{:S(2)}) collective-permute-start(f32[39,3,128]{2,1,0:T(4,128)S(1)} %get-tuple-element.9), channel_id=1, source_target_pairs={{0,1},{1,2},{2,3},{4,5},{5,6},{6,7},{8,9},{9,10},{10,11},{12,13},{... | collective-permute-start | bytes 179720 | tf_op jit(solution)/shard_map/ppermute | solution.py:28
  11.9 1.3 %collective-permute-start.3 = (f32[39,3,128]{2,1,0:T(4,128)S(1)}, f32[39,3,128]{2,1,0:T(4,128)S(1)}, u32[]{:S(2)}, u32[]{:S(2)}) collective-permute-start(f32[39,3,128]{2,1,0:T(4,128)S(1)} %get-tuple-element.8), channel_id=1, source_target_pairs={{1,0},{2,1},{3,2},{5,4},{6,5},{7,6},{9,8},{10,9},{11,10},{13,12},{... | collective-permute-start | bytes 179720 | tf_op jit(solution)/shard_map/ppermute | solution.py:28
  13.2 0.7 pad_maximum_fusion
  13.9 1.5 %collective-permute-start = (f32[39,3,128]{2,1,0:T(4,128)}, f32[39,3,128]{2,1,0:T(4,128)S(1)}, u32[]{:S(2)}, u32[]{:S(2)}) collective-permute-start(f32[39,3,128]{2,1,0:T(4,128)} %get-tuple-element.11), channel_id=1, source_target_pairs={{0,4},{4,8},{8,12},{12,16},{16,20},{20,24},{24,28},{1,5},{5,9},{9,... | collective-permute-start | bytes 179720 | tf_op jit(solution)/shard_map/ppermute | solution.py:28
  15.3 1.3 %collective-permute-start.1 = (f32[39,3,128]{2,1,0:T(4,128)}, f32[39,3,128]{2,1,0:T(4,128)S(1)}, u32[]{:S(2)}, u32[]{:S(2)}) collective-permute-start(f32[39,3,128]{2,1,0:T(4,128)} %get-tuple-element.10), channel_id=1, source_target_pairs={{4,0},{8,4},{12,8},{16,12},{20,16},{24,20},{28,24},{5,1},{9,5},{13... | collective-permute-start | bytes 179720 | tf_op jit(solution)/shard_map/ppermute | solution.py:28
  16.9 0.7 pad.16.left_ref.left_speed_ref
  18.2 0.7 pad.17.right_ref.right_speed_ref
  18.9 0.7 pad.14.top_ref.top_speed_ref
  19.5 0.7 collective-permute-done.1
  20.2 0.7 pad.15.bottom_ref.bottom_speed_ref
  20.9 27.5 %shard_map.113 = f32[128,38,128]{2,1,0:T(8,128)} custom-call(f32[38,128,128]{2,1,0:T(8,128)} %field_ref.1, f32[2,128,128]{2,1,0:T(8,128)} %speed_ref.1, f32[39,8,128]{2,1,0:T(8,128)} %pad.14.top_ref.top_speed_ref, f32[39,8,128]{2,1,0:T(8,128)} %pad.14.top_ref.top_speed_ref, f32[39,8,128]{2,1,0:T(8,128)} %pad.15.bottom_ref.bottom_speed_ref, ...), custom_call_target="tpu_custom_call" | custom-call | tf_op jit(solution)/shard_map/pallas_call | solution.py:130
  48.4 3.1 %fusion.13 = f32[128,128,38]{1,2,0:T(8,128)S(1)} fusion(f32[128,38,128]{2,1,0:T(8,128)} %shard_map.113, f32[38,38]{1,0:T(8,128)S(1)} %copy-done.3), kind=kOutput, calls=%fused_computation.22 | convolution fusion | flops 141950976 | bytes 4986512 | tf_op jit(solution)/shard_map/dot_general | solution.py:154
  51.6 2.5 %bitcast_subtract_fusion.4 = f32[38,128,128]{2,0,1:T(8,128)S(1)} fusion(f32[128,128,38]{1,2,0:T(8,128)S(1)} %fusion.13, f32[128,38,128]{2,1,0:T(8,128)S(1)} %copy-done.1, f32[128,128]{1,0:T(8,128)S(1)} %exponential_multiply_fusion, f32[38,38]{1,0:T(8,128)S(1)} %copy-done.4), kind=kOutput, calls=%fused_computation.11 | convolution fusion | flops 148176896 | bytes 7542416 | tf_op jit(solution)/shard_map/dot_general | solution.py:161
  54.1 1.3 %fusion.32 = f32[128,128,38]{1,2,0:T(8,128)S(1)} fusion(f32[38,128,128]{2,0,1:T(8,128)S(1)} %bitcast_subtract_fusion.4, f32[38,38]{1,0:T(8,128)S(1)} %copy-done.3), kind=kOutput, calls=%fused_computation.40 | convolution fusion | flops 141950976 | bytes 4986512 | tf_op jit(solution)/shard_map/dot_general | solution.py:154
  55.4 2.9 %bitcast_subtract_fusion.2 = f32[38,128,128]{2,0,1:T(8,128)S(1)} fusion(f32[38,128,128]{2,0,1:T(8,128)S(1)} %bitcast_subtract_fusion.4, f32[128,128,38]{1,2,0:T(8,128)S(1)} %fusion.32, f32[128,38,128]{2,1,0:T(8,128)S(1)} %copy-done.1, f32[128,128]{1,0:T(8,128)S(1)} %exponential_multiply_fusion, f32[38,38]{1,0:T(8,128)S(1)} %copy-done.4), kind=kOutput, calls=%fused_computation.7 | convolution fusion | flops 148176896 | bytes 10032784 | tf_op jit(solution)/shard_map/dot_general | solution.py:161
  58.3 1.3 %fusion.30 = f32[128,128,38]{1,2,0:T(8,128)S(1)} fusion(f32[38,128,128]{2,0,1:T(8,128)S(1)} %bitcast_subtract_fusion.2, f32[38,38]{1,0:T(8,128)S(1)} %copy-done.3), kind=kOutput, calls=%fused_computation.38 | convolution fusion | flops 141950976 | bytes 4986512 | tf_op jit(solution)/shard_map/dot_general | solution.py:154
  59.6 3.2 %fusion = f32[38,128,128]{2,0,1:T(8,128)S(1)} fusion(f32[128,38,128]{2,1,0:T(8,128)S(1)} %copy-done.1, f32[38,128,128]{2,0,1:T(8,128)S(1)} %bitcast_subtract_fusion.2, f32[128,128,38]{1,2,0:T(8,128)S(1)} %fusion.30, f32[128,128]{1,0:T(8,128)S(1)} %exponential_multiply_fusion, pred[128]{0:T(512)(128)(4,1)S(1)} %gt.22, f32[38,38]{1,0:T(8,128)S(1)} %copy-done.4), kind=kOutput, calls=%fused_computation.3 | convolution fusion | flops 148799488 | bytes 10032912 | tf_op jit(solution)/shard_map/dot_general | solution.py:161
  62.9 1.7 %convolution_bitcast_fusion = f32[4,128,128]{2,0,1:T(4,128)S(1)} fusion(f32[38,128,128]{2,0,1:T(8,128)S(1)} %fusion, f32[4,38]{1,0:T(4,128)S(1)} %copy-done.7), kind=kOutput, calls=%fused_computation.29 | convolution fusion | flops 29884416 | bytes 2753120 | tf_op jit(solution)/shard_map/dot_general | solution.py:167
  64.9 2.7 %collective-permute-start.4 = (f32[4,128]{1,0:T(4,128)S(1)}, f32[4,128]{1,0:T(4,128)S(1)}, u32[]{:S(2)}, u32[]{:S(2)}) collective-permute-start(f32[4,128]{1,0:T(4,128)S(1)} %broadcast_multiply_fusion), channel_id=1, source_target_pairs={{0,1},{1,0},{2,3},{3,2},{4,5},{5,4},{6,7},{7,6},{8,9},{9,8},{10,11... | collective-permute-start | bytes 6152 | tf_op jit(solution)/shard_map/ppermute | solution.py:177
  67.6 1.6 %collective-permute-done.4 = f32[4,128]{1,0:T(4,128)S(1)} collective-permute-done((f32[4,128]{1,0:T(4,128)S(1)}, f32[4,128]{1,0:T(4,128)S(1)}, u32[]{:S(2)}, u32[]{:S(2)}) %collective-permute-start.4) | collective-permute-done | bytes 2080 | tf_op jit(solution)/shard_map/ppermute | solution.py:177
  69.2 3.0 %collective-permute-start.5 = (f32[4,128]{1,0:T(4,128)S(1)}, f32[4,128]{1,0:T(4,128)S(1)}, u32[]{:S(2)}, u32[]{:S(2)}) collective-permute-start(f32[4,128]{1,0:T(4,128)S(1)} %fusion.38), channel_id=1, source_target_pairs={{0,2},{1,3},{2,0},{3,1},{4,6},{5,7},{6,4},{7,5},{8,10},{9,11},{10,... | collective-permute-start | bytes 6152 | tf_op jit(solution)/shard_map/ppermute | solution.py:177
  72.2 1.6 %collective-permute-done.5 = f32[4,128]{1,0:T(4,128)S(1)} collective-permute-done((f32[4,128]{1,0:T(4,128)S(1)}, f32[4,128]{1,0:T(4,128)S(1)}, u32[]{:S(2)}, u32[]{:S(2)}) %collective-permute-start.5) | collective-permute-done | bytes 2080 | tf_op jit(solution)/shard_map/ppermute | solution.py:177
  73.8 1.1 %collective-permute-start.6 = (f32[1,4,128]{2,0,1:T(1,128)S(1)}, f32[1,4,128]{2,0,1:T(1,128)S(1)}, u32[]{:S(2)}, u32[]{:S(2)}) collective-permute-start(f32[1,4,128]{2,0,1:T(1,128)S(1)} %bitcast.109), channel_id=1, source_target_pairs={{0,4},{4,0},{8,12},{12,8},{16,20},{20,16},{24,28},{28,24},{1,5},{5... | collective-permute-start | bytes 6152 | tf_op jit(solution)/shard_map/ppermute | solution.py:190
  74.8 0.8 collective-permute-done.6
  75.6 2.5 %collective-permute-start.7 = (f32[2,4,128]{2,0,1:T(2,128)S(1)}, f32[2,4,128]{2,0,1:T(2,128)S(1)}, u32[]{:S(2)}, u32[]{:S(2)}) collective-permute-start(f32[2,4,128]{2,0,1:T(2,128)S(1)} %maximum_select_fusion.2), channel_id=1, source_target_pairs={{0,8},{4,12},{8,0},{12,4},{16,24},{20,28},{24,16},{28,20},{1,9},{5... | collective-permute-start | bytes 12296 | tf_op jit(solution)/shard_map/ppermute | solution.py:190
  78.1 1.6 %collective-permute-done.7 = f32[2,4,128]{2,0,1:T(2,128)S(1)} collective-permute-done((f32[2,4,128]{2,0,1:T(2,128)S(1)}, f32[2,4,128]{2,0,1:T(2,128)S(1)}, u32[]{:S(2)}, u32[]{:S(2)}) %collective-permute-start.7) | collective-permute-done | bytes 4128 | tf_op jit(solution)/shard_map/ppermute | solution.py:190
  79.7 2.9 %collective-permute-start.8 = (f32[4,4,128]{2,0,1:T(4,128)S(1)}, f32[4,4,128]{2,0,1:T(4,128)S(1)}, u32[]{:S(2)}, u32[]{:S(2)}) collective-permute-start(f32[4,4,128]{2,0,1:T(4,128)S(1)} %maximum_select_fusion.1), channel_id=1, source_target_pairs={{0,16},{4,20},{8,24},{12,28},{16,0},{20,4},{24,8},{28,12},{1,17},{... | collective-permute-start | bytes 24584 | tf_op jit(solution)/shard_map/ppermute | solution.py:190
  82.6 1.9 %copy.20 = f32[38,128,128]{2,1,0:T(8,128)} copy(f32[38,128,128]{2,0,1:T(8,128)S(1)} %fusion) | data formatting | bytes 4980736
  84.6 2.8 %select_reduce_fusion = f32[4,1024]{1,0:T(4,128)S(1)} fusion(f32[4,1024]{1,0:T(4,128)S(1)} %bitcast.106, s32[4,1024]{1,0:T(4,128)S(1)} %constant_dynamic-slice_fusion), kind=kLoop, calls=%fused_computation | loop fusion | flops 12578816 | bytes 49152 | tf_op jit(solution)/shard_map/reduce_sum | solution.py:242
  (40 shorter events, 2.0 us)
Async XLA Ops:
  0.6 82.0 %copy-start = (s32[4,32768]{1,0:T(4,128)S(1)}, s32[4,32768]{1,0:T(4,128)}, u32[]{:S(2)}) copy-start(s32[4,32768]{1,0:T(4,128)} %param.18) | copy-start | bytes 1572868
  4.8 8.3 %copy-start.2 = (f32[38,128,128]{2,1,0:T(8,128)S(1)}, f32[38,128,128]{2,1,0:T(8,128)}, u32[]{:S(2)}) copy-start(f32[38,128,128]{2,1,0:T(8,128)} %field_ref.1) | copy-start | bytes 7471108
  6.9 9.8 %copy-start.5 = (f32[128,128]{1,0:T(8,128)S(1)}, f32[128,128]{1,0:T(8,128)}, u32[]{:S(2)}) copy-start(f32[128,128]{1,0:T(8,128)} %param.12) | copy-start | bytes 196612
  6.9 9.8 %copy-start.9 = (s32[64,1]{0,1:T(1,128)S(1)}, s32[64,1]{0,1:T(1,128)}, u32[]{:S(2)}) copy-start(s32[64,1]{0,1:T(1,128)} %param.15) | copy-start | bytes 772
  6.9 10.0 %collective-permute-start.2 = (f32[39,3,128]{2,1,0:T(4,128)S(1)}, f32[39,3,128]{2,1,0:T(4,128)S(1)}, u32[]{:S(2)}, u32[]{:S(2)}) collective-permute-start(f32[39,3,128]{2,1,0:T(4,128)S(1)} %get-tuple-element.9), channel_id=1, source_target_pairs={{0,1},{1,2},{2,3},{4,5},{5,6},{6,7},{8,9},{9,10},{10,11},{12,13},{... | collective-permute-start | bytes 179720 | tf_op jit(solution)/shard_map/ppermute | solution.py:28
  11.9 6.3 %collective-permute-start.3 = (f32[39,3,128]{2,1,0:T(4,128)S(1)}, f32[39,3,128]{2,1,0:T(4,128)S(1)}, u32[]{:S(2)}, u32[]{:S(2)}) collective-permute-start(f32[39,3,128]{2,1,0:T(4,128)S(1)} %get-tuple-element.8), channel_id=1, source_target_pairs={{1,0},{2,1},{3,2},{5,4},{6,5},{7,6},{9,8},{10,9},{11,10},{13,12},{... | collective-permute-start | bytes 179720 | tf_op jit(solution)/shard_map/ppermute | solution.py:28
  13.9 5.0 %collective-permute-start = (f32[39,3,128]{2,1,0:T(4,128)}, f32[39,3,128]{2,1,0:T(4,128)S(1)}, u32[]{:S(2)}, u32[]{:S(2)}) collective-permute-start(f32[39,3,128]{2,1,0:T(4,128)} %get-tuple-element.11), channel_id=1, source_target_pairs={{0,4},{4,8},{8,12},{12,16},{16,20},{20,24},{24,28},{1,5},{5,9},{9,... | collective-permute-start | bytes 179720 | tf_op jit(solution)/shard_map/ppermute | solution.py:28
  15.3 4.9 %collective-permute-start.1 = (f32[39,3,128]{2,1,0:T(4,128)}, f32[39,3,128]{2,1,0:T(4,128)S(1)}, u32[]{:S(2)}, u32[]{:S(2)}) collective-permute-start(f32[39,3,128]{2,1,0:T(4,128)} %get-tuple-element.10), channel_id=1, source_target_pairs={{4,0},{8,4},{12,8},{16,12},{20,16},{24,20},{28,24},{5,1},{9,5},{13... | collective-permute-start | bytes 179720 | tf_op jit(solution)/shard_map/ppermute | solution.py:28
  20.9 27.5 %copy-start.3 = (f32[38,38]{1,0:T(8,128)S(1)}, f32[38,38]{1,0:T(8,128)}, u32[]{:S(2)}) copy-start(f32[38,38]{1,0:T(8,128)} %param.13) | copy-start | bytes 17332
  48.4 3.1 %copy-start.1 = (f32[128,38,128]{2,1,0:T(8,128)S(1)}, f32[128,38,128]{2,1,0:T(8,128)}, u32[]{:S(2)}) copy-start(f32[128,38,128]{2,1,0:T(8,128)} %shard_map.113) | copy-start | bytes 7471108
  48.4 3.1 %copy-start.4 = (f32[38,38]{1,0:T(8,128)S(1)}, f32[38,38]{1,0:T(8,128)}, u32[]{:S(2)}) copy-start(f32[38,38]{1,0:T(8,128)} %param.14) | copy-start | bytes 17332
  59.6 3.3 %copy-start.7 = (f32[4,38]{1,0:T(4,128)S(1)}, f32[4,38]{1,0:T(4,128)}, u32[]{:S(2)}) copy-start(f32[4,38]{1,0:T(4,128)} %param.16) | copy-start | bytes 1828
  62.9 1.7 %copy-start.8 = (f32[128]{0:T(128)S(1)}, f32[128]{0:T(128)}, u32[]{:S(2)}) copy-start(f32[128]{0:T(128)} %param.17) | copy-start | bytes 1540
  64.9 4.3 %collective-permute-start.4 = (f32[4,128]{1,0:T(4,128)S(1)}, f32[4,128]{1,0:T(4,128)S(1)}, u32[]{:S(2)}, u32[]{:S(2)}) collective-permute-start(f32[4,128]{1,0:T(4,128)S(1)} %broadcast_multiply_fusion), channel_id=1, source_target_pairs={{0,1},{1,0},{2,3},{3,2},{4,5},{5,4},{6,7},{7,6},{8,9},{9,8},{10,11... | collective-permute-start | bytes 6152 | tf_op jit(solution)/shard_map/ppermute | solution.py:177
  69.2 4.6 %collective-permute-start.5 = (f32[4,128]{1,0:T(4,128)S(1)}, f32[4,128]{1,0:T(4,128)S(1)}, u32[]{:S(2)}, u32[]{:S(2)}) collective-permute-start(f32[4,128]{1,0:T(4,128)S(1)} %fusion.38), channel_id=1, source_target_pairs={{0,2},{1,3},{2,0},{3,1},{4,6},{5,7},{6,4},{7,5},{8,10},{9,11},{10,... | collective-permute-start | bytes 6152 | tf_op jit(solution)/shard_map/ppermute | solution.py:177
  73.8 1.9 %collective-permute-start.6 = (f32[1,4,128]{2,0,1:T(1,128)S(1)}, f32[1,4,128]{2,0,1:T(1,128)S(1)}, u32[]{:S(2)}, u32[]{:S(2)}) collective-permute-start(f32[1,4,128]{2,0,1:T(1,128)S(1)} %bitcast.109), channel_id=1, source_target_pairs={{0,4},{4,0},{8,12},{12,8},{16,20},{20,16},{24,28},{28,24},{1,5},{5... | collective-permute-start | bytes 6152 | tf_op jit(solution)/shard_map/ppermute | solution.py:190
  75.6 4.0 %collective-permute-start.7 = (f32[2,4,128]{2,0,1:T(2,128)S(1)}, f32[2,4,128]{2,0,1:T(2,128)S(1)}, u32[]{:S(2)}, u32[]{:S(2)}) collective-permute-start(f32[2,4,128]{2,0,1:T(2,128)S(1)} %maximum_select_fusion.2), channel_id=1, source_target_pairs={{0,8},{4,12},{8,0},{12,4},{16,24},{20,28},{24,16},{28,20},{1,9},{5... | collective-permute-start | bytes 12296 | tf_op jit(solution)/shard_map/ppermute | solution.py:190
  79.7 4.8 %collective-permute-start.8 = (f32[4,4,128]{2,0,1:T(4,128)S(1)}, f32[4,4,128]{2,0,1:T(4,128)S(1)}, u32[]{:S(2)}, u32[]{:S(2)}) collective-permute-start(f32[4,4,128]{2,0,1:T(4,128)S(1)} %maximum_select_fusion.1), channel_id=1, source_target_pairs={{0,16},{4,20},{8,24},{12,28},{16,0},{20,4},{24,8},{28,12},{1,17},{... | collective-permute-start | bytes 24584 | tf_op jit(solution)/shard_map/ppermute | solution.py:190
  82.6 4.8 %copy-start.6 = (f32[4,1024]{1,0:T(4,128)S(1)}, f32[4,1024]{1,0:T(4,128)}, u32[]{:S(2)}) copy-start(f32[4,1024]{1,0:T(4,128)} %param.19) | copy-start | bytes 49156

commit v4 on v3

--- a/solution.py
+++ b/solution.py
@@ -110,13 +110,25 @@
     out_ref[:, pl.ds(pl.program_id(0), 1), :] = moved[:, None, :]
 
 
+def edge_columns(field, start, width):
+    cols = field.shape[2]
+    pick = lax.broadcasted_iota(jnp.int32, (width, cols), 1) == (
+        lax.broadcasted_iota(jnp.int32, (width, cols), 0) + start
+    )
+    return jnp.einsum("kr,sar->ska", pick.astype(field.dtype), field, precision=HIGHEST)
+
+
 def transport(species, speed, width=3):
     species_count, rows, cols = species.shape
     assert rows == cols and rows % CHUNK == 0
     axial_edges = jnp.concatenate([species, speed[0:1]], axis=0)
     top, bottom = edge_layers(axial_edges, "axial", 1, width)
-    radial_edges = jnp.swapaxes(jnp.concatenate([species, speed[1:2]], axis=0), 1, 2)
-    left, right = edge_layers(radial_edges, "radial", 1, width)
+    radial_edges = jnp.concatenate([species, speed[1:2]], axis=0)
+    peers = lax.axis_size("radial")
+    up = [(i, i + 1) for i in range(peers - 1)]
+    down = [(j, i) for i, j in up]
+    left = lax.ppermute(edge_columns(radial_edges, cols - width, width), "radial", up)
+    right = lax.ppermute(edge_columns(radial_edges, 0, width), "radial", down)
     before = ((0, 0), (HALO - width, 0), (0, 0))
     after = ((0, 0), (0, HALO - width), (0, 0))
     top, left = (jnp.pad(top, before), jnp.pad(left, before))

time: 89.6 us -> 90.7 us (1.012)
  matrix products: 16.3 us -> 19.6 us
  local copies, waits for them, and re-layouts: 9.11 us -> 5.97 us
  waiting for transfers between devices: 6.82 us -> 9.48 us
  other arithmetic: 6.21 us -> 5.17 us
    ppermute x0 -> x2, starting transfers between devices: none -> 5.6 us  [the longest x1 4.32 us: transport(): lax.ppermute(edge_columns(radial_edges, cols - width, width), 'radial', up)]
    ppermute x4 -> x2, starting transfers between devices: 8.97 us -> 3.64 us  [edge_layers(): return (lax.ppermute(last, axis, up), lax.ppermute(initial, axis, down))]
    unnamed x24 -> x22, local copies, waits for them, and re-layouts: 5.2 us -> 1.96 us
    dot_general x0 -> x2, matrix products: none -> 3.2 us  [edge_columns(): jnp.einsum('kr,sar->ska', pick.astype(field.dtype), field, precision=HIGH...]
    ppermute x0 -> x2, waiting for transfers between devices: none -> 2.84 us  [the longest x1 2.84 us: transport(): right = lax.ppermute(edge_columns(radial_edges, 0, width), 'radial', down)]
    transpose x1 -> x0, other arithmetic: 2.02 us -> none  [transport(): jnp.swapaxes(jnp.concatenate([species, speed[1:2]], axis=0), 1, 2)]
    ppermute x2, starting transfers between devices: 5.74 us -> 4.24 us  [butterfly_sum(): part = part + lax.ppermute(part, axis, pairs)]
    ppermute x4 -> x2, waiting for transfers between devices: 1.28 us -> 0.01 us  [edge_layers(): return (lax.ppermute(last, axis, up), lax.ppermute(initial, axis, down))]
  transfers between devices with their start and end apart: 9 -> 9, of which waited for: 6 -> 5; matrix products, arithmetic and copies ran while one was open for 6% -> 8% of each run, Pallas kernels for 0% -> 0%
where the time goes in v4:
time: 90.7 us; the launch traced here: 89.2 us
  Pallas kernels  27.5 us (30%)
  starting transfers between devices  20.6 us (23%)
  matrix products  19.6 us (22%)
  waiting for transfers between devices  9.48 us (10%)
  local copies, waits for them, and re-layouts  5.97 us (7%)
  other arithmetic  5.17 us (6%)
  between operations  0.91 us (1%)
    pallas_call x1, Pallas kernels, transport(): pl.pallas_call(transport_kernel, grid=(species_count,), in_specs=[plane,...  27.5 us
    dot_general x3, matrix products, kinetics_advance(): jnp.tensordot(frozen_jacobian_inverse_addend, defect, axes=(1, 0), precis...  8.57 us
    ppermute x3, starting transfers between devices, doubling_gather(): other = lax.ppermute(blocks, axis, pairs)  7.09 us
    dot_general x3, matrix products, kinetics_advance(): jnp.tensordot(linearized_kinetics_operator, current, axes=(1, 0), precisi...  5.81 us
    ppermute x1, starting transfers between devices, transport(): lax.ppermute(edge_columns(radial_edges, cols - width, width), 'radial', up)  4.32 us
    ppermute x2, starting transfers between devices, butterfly_sum(): part = part + lax.ppermute(part, axis, pairs)  4.24 us
    ppermute x2, waiting for transfers between devices, butterfly_sum(): part = part + lax.ppermute(part, axis, pairs)  3.9 us
    ppermute x2, starting transfers between devices, edge_layers(): return (lax.ppermute(last, axis, up), lax.ppermute(initial, axis, down))  3.64 us
  transfers between devices with their start and end apart: 9, of which 5 were waited for; matrix products, arithmetic and copies ran while one was open for 8% of the time, Pallas kernels for 0%

profile of v4, /device:TPU:0, one launch (start us, length us, event | category | flops | bytes accessed | tf_op | source)
XLA Modules:
  0.0 89.2 jit_solution(9889623396678694684)
XLA Ops:
  0.7 1.0 %fusion.51 = (f32[1,128,128]{2,1,0:T(8,128)S(1)}, f32[1,128,128]{2,1,0:T(8,128)S(1)}) fusion(f32[2,128,128]{2,1,0:T(8,128)} %speed_ref.1), kind=kLoop, calls=%fused_computation.68 | loop fusion | bytes 262144 | tf_op jit(solution)/shard_map/slice | solution.py:126
  1.7 1.7 %pad_maximum_fusion.7 = (f32[39,3,128]{2,1,0:T(4,128)S(1)}, f32[39,3,128]{2,1,0:T(4,128)}) fusion(f32[1,128,128]{2,1,0:T(8,128)S(1)} %get-tuple-element.11, f32[38,128,128]{2,1,0:T(8,128)} %field_ref.1), kind=kLoop, calls=%fused_computation.39 | loop fusion | flops 29952 | bytes 2675712 | tf_op jit(solution)/shard_map/concatenate | solution.py:124
  3.4 2.3 %collective-permute-start = (f32[39,3,128]{2,1,0:T(4,128)}, f32[39,3,128]{2,1,0:T(4,128)S(1)}, u32[]{:S(2)}, u32[]{:S(2)}) collective-permute-start(f32[39,3,128]{2,1,0:T(4,128)} %get-tuple-element.9), channel_id=1, source_target_pairs={{0,4},{4,8},{8,12},{12,16},{16,20},{20,24},{24,28},{1,5},{5,9},{9,... | collective-permute-start | bytes 179720 | tf_op jit(solution)/shard_map/ppermute | solution.py:28
  5.7 1.3 %collective-permute-start.1 = (f32[39,3,128]{2,1,0:T(4,128)S(1)}, f32[39,3,128]{2,1,0:T(4,128)S(1)}, u32[]{:S(2)}, u32[]{:S(2)}) collective-permute-start(f32[39,3,128]{2,1,0:T(4,128)S(1)} %get-tuple-element.8), channel_id=1, source_target_pairs={{4,0},{8,4},{12,8},{16,12},{20,16},{24,20},{28,24},{5,1},{9,5},{13... | collective-permute-start | bytes 179720 | tf_op jit(solution)/shard_map/ppermute | solution.py:28
  7.1 1.3 %fusion.27 = f32[39,3,128]{2,1,0:T(4,128)S(1)} fusion(f32[1,128,128]{2,1,0:T(8,128)S(1)} %get-tuple-element.10, f32[38,128,128]{2,1,0:T(8,128)S(1)} %copy-done.2, s32[3]{0:T(128)S(1)} %iota_add_fusion), kind=kOutput, calls=%fused_computation.34 | convolution fusion | flops 23642496 | bytes 2615820 | tf_op jit(solution)/shard_map/kr,sar->ska/dot_general | solution.py:118
  8.3 4.3 %collective-permute-start.2 = (f32[39,3,128]{2,1,0:T(4,128)S(1)}, f32[39,3,128]{2,1,0:T(4,128)S(1)}, u32[]{:S(2)}, u32[]{:S(2)}) collective-permute-start(f32[39,3,128]{2,1,0:T(4,128)S(1)} %fusion.27), channel_id=1, source_target_pairs={{0,1},{1,2},{2,3},{4,5},{5,6},{6,7},{8,9},{9,10},{10,11},{12,13},{... | collective-permute-start | bytes 179720 | tf_op jit(solution)/shard_map/ppermute | solution.py:130
  12.6 1.9 %fusion.28 = f32[39,3,128]{2,1,0:T(4,128)} fusion(f32[1,128,128]{2,1,0:T(8,128)S(1)} %get-tuple-element.10, f32[38,128,128]{2,1,0:T(8,128)S(1)} %copy-done.2), kind=kOutput, calls=%fused_computation.35 | convolution fusion | flops 23642496 | bytes 2615808 | tf_op jit(solution)/shard_map/kr,sar->ska/dot_general | solution.py:118
  14.6 1.3 %collective-permute-start.3 = (f32[39,3,128]{2,1,0:T(4,128)}, f32[39,3,128]{2,1,0:T(4,128)S(1)}, u32[]{:S(2)}, u32[]{:S(2)}) collective-permute-start(f32[39,3,128]{2,1,0:T(4,128)} %fusion.28), channel_id=1, source_target_pairs={{1,0},{2,1},{3,2},{5,4},{6,5},{7,6},{9,8},{10,9},{11,10},{13,12},{... | collective-permute-start | bytes 179720 | tf_op jit(solution)/shard_map/ppermute | solution.py:131
  16.2 0.7 pad.14.top_ref.top_speed_ref
  16.9 0.7 pad.15.bottom_ref.bottom_speed_ref
  17.5 0.7 pad.16.left_ref.left_speed_ref
  18.2 2.8 %collective-permute-done.3 = f32[39,3,128]{2,1,0:T(4,128)S(1)} collective-permute-done((f32[39,3,128]{2,1,0:T(4,128)}, f32[39,3,128]{2,1,0:T(4,128)S(1)}, u32[]{:S(2)}, u32[]{:S(2)}) %collective-permute-start.3) | collective-permute-done | bytes 59936 | tf_op jit(solution)/shard_map/ppermute | solution.py:131
  21.1 0.7 pad.17.right_ref.right_speed_ref
  21.8 27.5 %shard_map.113 = f32[128,38,128]{2,1,0:T(8,128)} custom-call(f32[38,128,128]{2,1,0:T(8,128)} %field_ref.1, f32[2,128,128]{2,1,0:T(8,128)} %speed_ref.1, f32[39,8,128]{2,1,0:T(8,128)} %pad.14.top_ref.top_speed_ref, f32[39,8,128]{2,1,0:T(8,128)} %pad.14.top_ref.top_speed_ref, f32[39,8,128]{2,1,0:T(8,128)} %pad.15.bottom_ref.bottom_speed_ref, ...), custom_call_target="tpu_custom_call" | custom-call | tf_op jit(solution)/shard_map/pallas_call | solution.py:142
  49.3 3.2 %fusion.13 = f32[128,128,38]{1,2,0:T(8,128)S(1)} fusion(f32[128,38,128]{2,1,0:T(8,128)} %shard_map.113, f32[38,38]{1,0:T(8,128)S(1)} %copy-done.3), kind=kOutput, calls=%fused_computation.22 | convolution fusion | flops 141950976 | bytes 4986512 | tf_op jit(solution)/shard_map/dot_general | solution.py:166
  52.5 2.5 %bitcast_subtract_fusion.4 = f32[38,128,128]{2,0,1:T(8,128)S(1)} fusion(f32[128,128,38]{1,2,0:T(8,128)S(1)} %fusion.13, f32[128,38,128]{2,1,0:T(8,128)S(1)} %copy-done.1, f32[128,128]{1,0:T(8,128)S(1)} %exponential_multiply_fusion, f32[38,38]{1,0:T(8,128)S(1)} %copy-done.4), kind=kOutput, calls=%fused_computation.11 | convolution fusion | flops 148176896 | bytes 7542416 | tf_op jit(solution)/shard_map/dot_general | solution.py:173
  55.0 1.3 %fusion.37 = f32[128,128,38]{1,2,0:T(8,128)S(1)} fusion(f32[38,128,128]{2,0,1:T(8,128)S(1)} %bitcast_subtract_fusion.4, f32[38,38]{1,0:T(8,128)S(1)} %copy-done.3), kind=kOutput, calls=%fused_computation.46 | convolution fusion | flops 141950976 | bytes 4986512 | tf_op jit(solution)/shard_map/dot_general | solution.py:166
  56.4 2.8 %bitcast_subtract_fusion.2 = f32[38,128,128]{2,0,1:T(8,128)S(1)} fusion(f32[38,128,128]{2,0,1:T(8,128)S(1)} %bitcast_subtract_fusion.4, f32[128,128,38]{1,2,0:T(8,128)S(1)} %fusion.37, f32[128,38,128]{2,1,0:T(8,128)S(1)} %copy-done.1, f32[128,128]{1,0:T(8,128)S(1)} %exponential_multiply_fusion, f32[38,38]{1,0:T(8,128)S(1)} %copy-done.4), kind=kOutput, calls=%fused_computation.7 | convolution fusion | flops 148176896 | bytes 10032784 | tf_op jit(solution)/shard_map/dot_general | solution.py:173
  59.2 1.3 %fusion.35 = f32[128,128,38]{1,2,0:T(8,128)S(1)} fusion(f32[38,128,128]{2,0,1:T(8,128)S(1)} %bitcast_subtract_fusion.2, f32[38,38]{1,0:T(8,128)S(1)} %copy-done.3), kind=kOutput, calls=%fused_computation.44 | convolution fusion | flops 141950976 | bytes 4986512 | tf_op jit(solution)/shard_map/dot_general | solution.py:166
  60.5 3.2 %fusion = f32[38,128,128]{2,0,1:T(8,128)S(1)} fusion(f32[128,38,128]{2,1,0:T(8,128)S(1)} %copy-done.1, f32[38,128,128]{2,0,1:T(8,128)S(1)} %bitcast_subtract_fusion.2, f32[128,128,38]{1,2,0:T(8,128)S(1)} %fusion.35, f32[128,128]{1,0:T(8,128)S(1)} %exponential_multiply_fusion, pred[128]{0:T(512)(128)(4,1)S(1)} %gt.22, f32[38,38]{1,0:T(8,128)S(1)} %copy-done.4), kind=kOutput, calls=%fused_computation.3 | convolution fusion | flops 148799488 | bytes 10032912 | tf_op jit(solution)/shard_map/dot_general | solution.py:173
  63.8 1.7 %convolution_bitcast_fusion = f32[4,128,128]{2,0,1:T(4,128)S(1)} fusion(f32[38,128,128]{2,0,1:T(8,128)S(1)} %fusion, f32[4,38]{1,0:T(4,128)S(1)} %copy-done.7), kind=kOutput, calls=%fused_computation.33 | convolution fusion | flops 29884416 | bytes 2753120 | tf_op jit(solution)/shard_map/dot_general | solution.py:179
  65.8 1.6 %collective-permute-start.4 = (f32[4,128]{1,0:T(4,128)S(1)}, f32[4,128]{1,0:T(4,128)S(1)}, u32[]{:S(2)}, u32[]{:S(2)}) collective-permute-start(f32[4,128]{1,0:T(4,128)S(1)} %broadcast_multiply_fusion), channel_id=1, source_target_pairs={{0,1},{1,0},{2,3},{3,2},{4,5},{5,4},{6,7},{7,6},{8,9},{9,8},{10,11... | collective-permute-start | bytes 6152 | tf_op jit(solution)/shard_map/ppermute | solution.py:189
  67.4 2.0 %collective-permute-done.4 = f32[4,128]{1,0:T(4,128)S(1)} collective-permute-done((f32[4,128]{1,0:T(4,128)S(1)}, f32[4,128]{1,0:T(4,128)S(1)}, u32[]{:S(2)}, u32[]{:S(2)}) %collective-permute-start.4) | collective-permute-done | bytes 2080 | tf_op jit(solution)/shard_map/ppermute | solution.py:189
  69.4 2.6 %collective-permute-start.5 = (f32[4,128]{1,0:T(4,128)S(1)}, f32[4,128]{1,0:T(4,128)S(1)}, u32[]{:S(2)}, u32[]{:S(2)}) collective-permute-start(f32[4,128]{1,0:T(4,128)S(1)} %fusion.50), channel_id=1, source_target_pairs={{0,2},{1,3},{2,0},{3,1},{4,6},{5,7},{6,4},{7,5},{8,10},{9,11},{10,... | collective-permute-start | bytes 6152 | tf_op jit(solution)/shard_map/ppermute | solution.py:189
  72.0 1.9 %collective-permute-done.5 = f32[4,128]{1,0:T(4,128)S(1)} collective-permute-done((f32[4,128]{1,0:T(4,128)S(1)}, f32[4,128]{1,0:T(4,128)S(1)}, u32[]{:S(2)}, u32[]{:S(2)}) %collective-permute-start.5) | collective-permute-done | bytes 2080 | tf_op jit(solution)/shard_map/ppermute | solution.py:189
  73.9 1.2 %collective-permute-done.6 = f32[1,4,128]{2,0,1:T(1,128)S(1)} collective-permute-done((f32[1,4,128]{2,0,1:T(1,128)S(1)}, f32[1,4,128]{2,0,1:T(1,128)S(1)}, u32[]{:S(2)}, u32[]{:S(2)}) %collective-permute-start.6) | collective-permute-done | bytes 2080 | tf_op jit(solution)/shard_map/ppermute | solution.py:202
  75.1 4.1 %collective-permute-start.7 = (f32[2,4,128]{2,0,1:T(2,128)S(1)}, f32[2,4,128]{2,0,1:T(2,128)S(1)}, u32[]{:S(2)}, u32[]{:S(2)}) collective-permute-start(f32[2,4,128]{2,0,1:T(2,128)S(1)} %maximum_select_fusion.2), channel_id=1, source_target_pairs={{0,8},{4,12},{8,0},{12,4},{16,24},{20,28},{24,16},{28,20},{1,9},{5... | collective-permute-start | bytes 12296 | tf_op jit(solution)/shard_map/ppermute | solution.py:202
  79.2 1.6 %collective-permute-done.7 = f32[2,4,128]{2,0,1:T(2,128)S(1)} collective-permute-done((f32[2,4,128]{2,0,1:T(2,128)S(1)}, f32[2,4,128]{2,0,1:T(2,128)S(1)}, u32[]{:S(2)}, u32[]{:S(2)}) %collective-permute-start.7) | collective-permute-done | bytes 4128 | tf_op jit(solution)/shard_map/ppermute | solution.py:202
  80.8 3.0 %collective-permute-start.8 = (f32[4,4,128]{2,0,1:T(4,128)S(1)}, f32[4,4,128]{2,0,1:T(4,128)S(1)}, u32[]{:S(2)}, u32[]{:S(2)}) collective-permute-start(f32[4,4,128]{2,0,1:T(4,128)S(1)} %maximum_select_fusion.1), channel_id=1, source_target_pairs={{0,16},{4,20},{8,24},{12,28},{16,0},{20,4},{24,8},{28,12},{1,17},{... | collective-permute-start | bytes 24584 | tf_op jit(solution)/shard_map/ppermute | solution.py:202
  83.8 1.9 %copy.14 = f32[38,128,128]{2,1,0:T(8,128)} copy(f32[38,128,128]{2,0,1:T(8,128)S(1)} %fusion) | data formatting | bytes 4980736
  85.7 2.8 %select_reduce_fusion = f32[4,1024]{1,0:T(4,128)S(1)} fusion(f32[4,1024]{1,0:T(4,128)S(1)} %bitcast.114, s32[4,1024]{1,0:T(4,128)S(1)} %constant_dynamic-slice_fusion), kind=kLoop, calls=%fused_computation | loop fusion | flops 12578816 | bytes 49152 | tf_op jit(solution)/shard_map/reduce_sum | solution.py:254
  88.6 0.6 sub.73
  (39 shorter events, 0.7 us)
Async XLA Ops:
  0.6 83.2 %copy-start = (s32[4,32768]{1,0:T(4,128)S(1)}, s32[4,32768]{1,0:T(4,128)}, u32[]{:S(2)}) copy-start(s32[4,32768]{1,0:T(4,128)} %param.18) | copy-start | bytes 1572868
  0.6 6.4 %copy-start.2 = (f32[38,128,128]{2,1,0:T(8,128)S(1)}, f32[38,128,128]{2,1,0:T(8,128)}, u32[]{:S(2)}) copy-start(f32[38,128,128]{2,1,0:T(8,128)} %field_ref.1) | copy-start | bytes 7471108
  3.4 12.8 %collective-permute-start = (f32[39,3,128]{2,1,0:T(4,128)}, f32[39,3,128]{2,1,0:T(4,128)S(1)}, u32[]{:S(2)}, u32[]{:S(2)}) collective-permute-start(f32[39,3,128]{2,1,0:T(4,128)} %get-tuple-element.9), channel_id=1, source_target_pairs={{0,4},{4,8},{8,12},{12,16},{16,20},{20,24},{24,28},{1,5},{5,9},{9,... | collective-permute-start | bytes 179720 | tf_op jit(solution)/shard_map/ppermute | solution.py:28
  5.7 11.2 %collective-permute-start.1 = (f32[39,3,128]{2,1,0:T(4,128)S(1)}, f32[39,3,128]{2,1,0:T(4,128)S(1)}, u32[]{:S(2)}, u32[]{:S(2)}) collective-permute-start(f32[39,3,128]{2,1,0:T(4,128)S(1)} %get-tuple-element.8), channel_id=1, source_target_pairs={{4,0},{8,4},{12,8},{16,12},{20,16},{24,20},{28,24},{5,1},{9,5},{13... | collective-permute-start | bytes 179720 | tf_op jit(solution)/shard_map/ppermute | solution.py:28
  7.0 8.8 %copy-start.5 = (f32[128,128]{1,0:T(8,128)S(1)}, f32[128,128]{1,0:T(8,128)}, u32[]{:S(2)}) copy-start(f32[128,128]{1,0:T(8,128)} %param.12) | copy-start | bytes 196612
  7.0 8.9 %copy-start.9 = (s32[64,1]{0,1:T(1,128)S(1)}, s32[64,1]{0,1:T(1,128)}, u32[]{:S(2)}) copy-start(s32[64,1]{0,1:T(1,128)} %param.15) | copy-start | bytes 772
  8.3 9.2 %collective-permute-start.2 = (f32[39,3,128]{2,1,0:T(4,128)S(1)}, f32[39,3,128]{2,1,0:T(4,128)S(1)}, u32[]{:S(2)}, u32[]{:S(2)}) collective-permute-start(f32[39,3,128]{2,1,0:T(4,128)S(1)} %fusion.27), channel_id=1, source_target_pairs={{0,1},{1,2},{2,3},{4,5},{5,6},{6,7},{8,9},{9,10},{10,11},{12,13},{... | collective-permute-start | bytes 179720 | tf_op jit(solution)/shard_map/ppermute | solution.py:130
  14.6 6.5 %collective-permute-start.3 = (f32[39,3,128]{2,1,0:T(4,128)}, f32[39,3,128]{2,1,0:T(4,128)S(1)}, u32[]{:S(2)}, u32[]{:S(2)}) collective-permute-start(f32[39,3,128]{2,1,0:T(4,128)} %fusion.28), channel_id=1, source_target_pairs={{1,0},{2,1},{3,2},{5,4},{6,5},{7,6},{9,8},{10,9},{11,10},{13,12},{... | collective-permute-start | bytes 179720 | tf_op jit(solution)/shard_map/ppermute | solution.py:131
  21.8 27.5 %copy-start.3 = (f32[38,38]{1,0:T(8,128)S(1)}, f32[38,38]{1,0:T(8,128)}, u32[]{:S(2)}) copy-start(f32[38,38]{1,0:T(8,128)} %param.13) | copy-start | bytes 17332
  49.3 3.2 %copy-start.1 = (f32[128,38,128]{2,1,0:T(8,128)S(1)}, f32[128,38,128]{2,1,0:T(8,128)}, u32[]{:S(2)}) copy-start(f32[128,38,128]{2,1,0:T(8,128)} %shard_map.113) | copy-start | bytes 7471108
  49.3 3.2 %copy-start.4 = (f32[38,38]{1,0:T(8,128)S(1)}, f32[38,38]{1,0:T(8,128)}, u32[]{:S(2)}) copy-start(f32[38,38]{1,0:T(8,128)} %param.14) | copy-start | bytes 17332
  60.5 3.3 %copy-start.7 = (f32[4,38]{1,0:T(4,128)S(1)}, f32[4,38]{1,0:T(4,128)}, u32[]{:S(2)}) copy-start(f32[4,38]{1,0:T(4,128)} %param.16) | copy-start | bytes 1828
  63.8 1.7 %copy-start.8 = (f32[128]{0:T(128)S(1)}, f32[128]{0:T(128)}, u32[]{:S(2)}) copy-start(f32[128]{0:T(128)} %param.17) | copy-start | bytes 1540
  65.8 3.7 %collective-permute-start.4 = (f32[4,128]{1,0:T(4,128)S(1)}, f32[4,128]{1,0:T(4,128)S(1)}, u32[]{:S(2)}, u32[]{:S(2)}) collective-permute-start(f32[4,128]{1,0:T(4,128)S(1)} %broadcast_multiply_fusion), channel_id=1, source_target_pairs={{0,1},{1,0},{2,3},{3,2},{4,5},{5,4},{6,7},{7,6},{8,9},{9,8},{10,11... | collective-permute-start | bytes 6152 | tf_op jit(solution)/shard_map/ppermute | solution.py:189
  69.4 4.5 %collective-permute-start.5 = (f32[4,128]{1,0:T(4,128)S(1)}, f32[4,128]{1,0:T(4,128)S(1)}, u32[]{:S(2)}, u32[]{:S(2)}) collective-permute-start(f32[4,128]{1,0:T(4,128)S(1)} %fusion.50), channel_id=1, source_target_pairs={{0,2},{1,3},{2,0},{3,1},{4,6},{5,7},{6,4},{7,5},{8,10},{9,11},{10,... | collective-permute-start | bytes 6152 | tf_op jit(solution)/shard_map/ppermute | solution.py:189
  73.9 1.2 %collective-permute-start.6 = (f32[1,4,128]{2,0,1:T(1,128)S(1)}, f32[1,4,128]{2,0,1:T(1,128)S(1)}, u32[]{:S(2)}, u32[]{:S(2)}) collective-permute-start(f32[1,4,128]{2,0,1:T(1,128)S(1)} %bitcast.117), channel_id=1, source_target_pairs={{0,4},{4,0},{8,12},{12,8},{16,20},{20,16},{24,28},{28,24},{1,5},{5... | collective-permute-start | bytes 6152 | tf_op jit(solution)/shard_map/ppermute | solution.py:202
  75.1 5.7 %collective-permute-start.7 = (f32[2,4,128]{2,0,1:T(2,128)S(1)}, f32[2,4,128]{2,0,1:T(2,128)S(1)}, u32[]{:S(2)}, u32[]{:S(2)}) collective-permute-start(f32[2,4,128]{2,0,1:T(2,128)S(1)} %maximum_select_fusion.2), channel_id=1, source_target_pairs={{0,8},{4,12},{8,0},{12,4},{16,24},{20,28},{24,16},{28,20},{1,9},{5... | collective-permute-start | bytes 12296 | tf_op jit(solution)/shard_map/ppermute | solution.py:202
  80.8 4.9 %collective-permute-start.8 = (f32[4,4,128]{2,0,1:T(4,128)S(1)}, f32[4,4,128]{2,0,1:T(4,128)S(1)}, u32[]{:S(2)}, u32[]{:S(2)}) collective-permute-start(f32[4,4,128]{2,0,1:T(4,128)S(1)} %maximum_select_fusion.1), channel_id=1, source_target_pairs={{0,16},{4,20},{8,24},{12,28},{16,0},{20,4},{24,8},{28,12},{1,17},{... | collective-permute-start | bytes 24584 | tf_op jit(solution)/shard_map/ppermute | solution.py:202
  83.8 4.8 %copy-start.6 = (f32[4,1024]{1,0:T(4,128)S(1)}, f32[4,1024]{1,0:T(4,128)}, u32[]{:S(2)}) copy-start(f32[4,1024]{1,0:T(4,128)} %param.19) | copy-start | bytes 49156

commit v5 on v4

--- a/solution.py
+++ b/solution.py
@@ -83,27 +83,29 @@
     ext_ref, vel_ref, flux_ref,
 ):
     rows, cols = field_ref.shape[1], field_ref.shape[2]
+    width = top_ref.shape[1]
     span = ext_ref.shape[0]
-    tail = span - HALO - rows
-    zeros = jnp.zeros((tail - HALO, cols), jnp.float32)
     field = field_ref[0]
 
-    ext_ref[pl.ds(0, HALO), :] = top_ref[0]
+    for scratch in (ext_ref, vel_ref):
+        scratch[pl.ds(0, HALO), :] = jnp.zeros((HALO, cols), jnp.float32)
+        scratch[pl.ds(HALO + rows, span - HALO - rows), :] = jnp.zeros(
+            (span - HALO - rows, cols), jnp.float32
+        )
+    ext_ref[pl.ds(HALO - width, width), :] = top_ref[0]
     ext_ref[pl.ds(HALO, rows), :] = field
-    ext_ref[pl.ds(HALO + rows, HALO), :] = bottom_ref[0]
-    ext_ref[pl.ds(2 * HALO + rows, tail - HALO), :] = zeros
-    vel_ref[pl.ds(0, HALO), :] = top_speed_ref[0]
+    ext_ref[pl.ds(HALO + rows, width), :] = bottom_ref[0]
+    vel_ref[pl.ds(HALO - width, width), :] = top_speed_ref[0]
     vel_ref[pl.ds(HALO, rows), :] = speed_ref[0]
-    vel_ref[pl.ds(HALO + rows, HALO), :] = bottom_speed_ref[0]
-    vel_ref[pl.ds(2 * HALO + rows, tail - HALO), :] = zeros
+    vel_ref[pl.ds(HALO + rows, width), :] = bottom_speed_ref[0]
     along_axial = upwind_divergence(ext_ref, vel_ref, flux_ref, rows)
 
-    ext_ref[pl.ds(0, HALO), :] = left_ref[0]
+    ext_ref[pl.ds(HALO - width, width), :] = left_ref[0]
     ext_ref[pl.ds(HALO, cols), :] = field.T
-    ext_ref[pl.ds(HALO + cols, HALO), :] = right_ref[0]
-    vel_ref[pl.ds(0, HALO), :] = left_speed_ref[0]
+    ext_ref[pl.ds(HALO + cols, width), :] = right_ref[0]
+    vel_ref[pl.ds(HALO - width, width), :] = left_speed_ref[0]
     vel_ref[pl.ds(HALO, cols), :] = speed_ref[1].T
-    vel_ref[pl.ds(HALO + cols, HALO), :] = right_speed_ref[0]
+    vel_ref[pl.ds(HALO + cols, width), :] = right_speed_ref[0]
     along_radial = upwind_divergence(ext_ref, vel_ref, flux_ref, cols).T
 
     moved = field - TIME_STEP * (along_axial + along_radial)
@@ -129,16 +131,12 @@
     down = [(j, i) for i, j in up]
     left = lax.ppermute(edge_columns(radial_edges, cols - width, width), "radial", up)
     right = lax.ppermute(edge_columns(radial_edges, 0, width), "radial", down)
-    before = ((0, 0), (HALO - width, 0), (0, 0))
-    after = ((0, 0), (0, HALO - width), (0, 0))
-    top, left = (jnp.pad(top, before), jnp.pad(left, before))
-    bottom, right = (jnp.pad(bottom, after), jnp.pad(right, after))
     faces = rows + CHUNK
     span = HALO + faces + HALO
     plane = pl.BlockSpec((1, rows, cols), lambda s: (s, 0, 0))
     speeds = pl.BlockSpec((2, rows, cols), lambda s: (0, 0, 0))
-    edge = pl.BlockSpec((1, HALO, cols), lambda s: (s, 0, 0))
-    edge_speed = pl.BlockSpec((1, HALO, cols), lambda s: (species_count, 0, 0))
+    edge = pl.BlockSpec((1, width, cols), lambda s: (s, 0, 0))
+    edge_speed = pl.BlockSpec((1, width, cols), lambda s: (species_count, 0, 0))
     moved_rows = pl.pallas_call(
         transport_kernel,
         grid=(species_count,),

time: 90.7 us -> 90.6 us (level)
  local copies, waits for them, and re-layouts: 5.97 us -> 3.86 us
  waiting for transfers between devices: 9.48 us -> 11.5 us
    pad x4 -> x0, local copies, waits for them, and re-layouts: 2.75 us -> none  [the longest x2 1.39 us: transport(): top, left = (jnp.pad(top, before), jnp.pad(left, before))]
    ppermute x1, waiting for transfers between devices: 2.84 us -> 4.85 us  [transport(): right = lax.ppermute(edge_columns(radial_edges, 0, width), 'radial', down)]
    unnamed x22 -> x30, local copies, waits for them, and re-layouts: 1.96 us -> 2.6 us
  transfers between devices with their start and end apart: 9 -> 9, of which waited for: 5 -> 5; matrix products, arithmetic and copies ran while one was open for 8% -> 6% of each run, Pallas kernels for 0% -> 0%
where the time goes in v5:
time: 90.6 us; the launch traced here: 89.1 us
  Pallas kernels  27.5 us (30%)
  starting transfers between devices  20.6 us (23%)
  matrix products  19.5 us (22%)
  waiting for transfers between devices  11.5 us (13%)
  other arithmetic  5.17 us (6%)
  local copies, waits for them, and re-layouts  3.86 us (4%)
  between operations  0.96 us (1%)
    pallas_call x1, Pallas kernels, transport(): pl.pallas_call(transport_kernel, grid=(species_count,), in_specs=[plane,...  27.5 us
    dot_general x3, matrix products, kinetics_advance(): jnp.tensordot(frozen_jacobian_inverse_addend, defect, axes=(1, 0), precis...  8.58 us
    ppermute x3, starting transfers between devices, doubling_gather(): other = lax.ppermute(blocks, axis, pairs)  7.09 us
    dot_general x3, matrix products, kinetics_advance(): jnp.tensordot(linearized_kinetics_operator, current, axes=(1, 0), precisi...  5.82 us
    ppermute x1, waiting for transfers between devices, transport(): right = lax.ppermute(edge_columns(radial_edges, 0, width), 'radial', down)  4.85 us
    ppermute x1, starting transfers between devices, transport(): lax.ppermute(edge_columns(radial_edges, cols - width, width), 'radial', up)  4.32 us
    ppermute x2, starting transfers between devices, butterfly_sum(): part = part + lax.ppermute(part, axis, pairs)  4.22 us
    ppermute x2, waiting for transfers between devices, butterfly_sum(): part = part + lax.ppermute(part, axis, pairs)  3.92 us
  transfers between devices with their start and end apart: 9, of which 5 were waited for; matrix products, arithmetic and copies ran while one was open for 6% of the time, Pallas kernels for 0%

profile of v5, /device:TPU:0, one launch (start us, length us, event | category | flops | bytes accessed | tf_op | source)
XLA Modules:
  0.0 89.1 jit_solution(4438554911365093036)
XLA Ops:
  0.7 1.0 %fusion.51 = (f32[1,128,128]{2,1,0:T(8,128)S(1)}, f32[1,128,128]{2,1,0:T(8,128)S(1)}) fusion(f32[2,128,128]{2,1,0:T(8,128)} %speed_ref.1), kind=kLoop, calls=%fused_computation.68 | loop fusion | bytes 262144 | tf_op jit(solution)/shard_map/slice | solution.py:128
  1.7 1.7 %pad_maximum_fusion.7 = (f32[39,3,128]{2,1,0:T(4,128)S(1)}, f32[39,3,128]{2,1,0:T(4,128)}) fusion(f32[1,128,128]{2,1,0:T(8,128)S(1)} %get-tuple-element.11, f32[38,128,128]{2,1,0:T(8,128)} %field_ref.1), kind=kLoop, calls=%fused_computation.39 | loop fusion | flops 29952 | bytes 2675712 | tf_op jit(solution)/shard_map/concatenate | solution.py:126
  3.4 2.3 %collective-permute-start = (f32[39,3,128]{2,1,0:T(4,128)}, f32[39,3,128]{2,1,0:T(4,128)S(1)}, u32[]{:S(2)}, u32[]{:S(2)}) collective-permute-start(f32[39,3,128]{2,1,0:T(4,128)} %get-tuple-element.9), channel_id=1, source_target_pairs={{0,4},{4,8},{8,12},{12,16},{16,20},{20,24},{24,28},{1,5},{5,9},{9,... | collective-permute-start | bytes 179720 | tf_op jit(solution)/shard_map/ppermute | solution.py:28
  5.7 1.3 %collective-permute-start.1 = (f32[39,3,128]{2,1,0:T(4,128)S(1)}, f32[39,3,128]{2,1,0:T(4,128)S(1)}, u32[]{:S(2)}, u32[]{:S(2)}) collective-permute-start(f32[39,3,128]{2,1,0:T(4,128)S(1)} %get-tuple-element.8), channel_id=1, source_target_pairs={{4,0},{8,4},{12,8},{16,12},{20,16},{24,20},{28,24},{5,1},{9,5},{13... | collective-permute-start | bytes 179720 | tf_op jit(solution)/shard_map/ppermute | solution.py:28
  7.1 1.3 %fusion.27 = f32[39,3,128]{2,1,0:T(4,128)S(1)} fusion(f32[1,128,128]{2,1,0:T(8,128)S(1)} %get-tuple-element.10, f32[38,128,128]{2,1,0:T(8,128)S(1)} %copy-done.2, s32[3]{0:T(128)S(1)} %iota_add_fusion), kind=kOutput, calls=%fused_computation.34 | convolution fusion | flops 23642496 | bytes 2615820 | tf_op jit(solution)/shard_map/kr,sar->ska/dot_general | solution.py:120
  8.3 4.3 %collective-permute-start.2 = (f32[39,3,128]{2,1,0:T(4,128)S(1)}, f32[39,3,128]{2,1,0:T(4,128)S(1)}, u32[]{:S(2)}, u32[]{:S(2)}) collective-permute-start(f32[39,3,128]{2,1,0:T(4,128)S(1)} %fusion.27), channel_id=1, source_target_pairs={{0,1},{1,2},{2,3},{4,5},{5,6},{6,7},{8,9},{9,10},{10,11},{12,13},{... | collective-permute-start | bytes 179720 | tf_op jit(solution)/shard_map/ppermute | solution.py:132
  12.6 1.9 %fusion.28 = f32[39,3,128]{2,1,0:T(4,128)} fusion(f32[1,128,128]{2,1,0:T(8,128)S(1)} %get-tuple-element.10, f32[38,128,128]{2,1,0:T(8,128)S(1)} %copy-done.2), kind=kOutput, calls=%fused_computation.35 | convolution fusion | flops 23642496 | bytes 2615808 | tf_op jit(solution)/shard_map/kr,sar->ska/dot_general | solution.py:120
  14.6 1.3 %collective-permute-start.3 = (f32[39,3,128]{2,1,0:T(4,128)}, f32[39,3,128]{2,1,0:T(4,128)S(1)}, u32[]{:S(2)}, u32[]{:S(2)}) collective-permute-start(f32[39,3,128]{2,1,0:T(4,128)} %fusion.28), channel_id=1, source_target_pairs={{1,0},{2,1},{3,2},{5,4},{6,5},{7,6},{9,8},{10,9},{11,10},{13,12},{... | collective-permute-start | bytes 179720 | tf_op jit(solution)/shard_map/ppermute | solution.py:133
  15.9 0.1 broadcast_in_dim.33
  16.0 0.2 gt.22
  16.2 4.9 %collective-permute-done.3.right_ref.right_speed_ref = f32[39,3,128]{2,1,0:T(4,128)S(1)} collective-permute-done((f32[39,3,128]{2,1,0:T(4,128)}, f32[39,3,128]{2,1,0:T(4,128)S(1)}, u32[]{:S(2)}, u32[]{:S(2)}) %collective-permute-start.3) | collective-permute-done | bytes 59936 | tf_op jit(solution)/shard_map/ppermute | solution.py:133
  21.1 0.6 copy-done.6
  21.7 27.5 %shard_map.113 = f32[128,38,128]{2,1,0:T(8,128)} custom-call(f32[38,128,128]{2,1,0:T(8,128)} %field_ref.1, f32[2,128,128]{2,1,0:T(8,128)} %speed_ref.1, f32[39,3,128]{2,1,0:T(4,128)} %copy-done.3, f32[39,3,128]{2,1,0:T(4,128)} %copy-done.3, f32[39,3,128]{2,1,0:T(4,128)} %copy-done.4, f32[39,3,128]{2,1,0:T(4,128)} %copy-done.4, f32[39,3,128]{2,1,0:T(4,128)} %copy-done.5, ...), custom_call_target="tpu_custom_call" | custom-call | tf_op jit(solution)/shard_map/pallas_call | solution.py:140
  49.2 3.2 %fusion.13 = f32[128,128,38]{1,2,0:T(8,128)S(1)} fusion(f32[128,38,128]{2,1,0:T(8,128)} %shard_map.113, f32[38,38]{1,0:T(8,128)S(1)} %copy-done.7), kind=kOutput, calls=%fused_computation.22 | convolution fusion | flops 141950976 | bytes 4986512 | tf_op jit(solution)/shard_map/dot_general | solution.py:164
  52.4 2.6 %bitcast_subtract_fusion.4 = f32[38,128,128]{2,0,1:T(8,128)S(1)} fusion(f32[128,128,38]{1,2,0:T(8,128)S(1)} %fusion.13, f32[128,38,128]{2,1,0:T(8,128)S(1)} %copy-done.1, f32[128,128]{1,0:T(8,128)S(1)} %exponential_multiply_fusion, f32[38,38]{1,0:T(8,128)S(1)} %copy-done.8), kind=kOutput, calls=%fused_computation.11 | convolution fusion | flops 148176896 | bytes 7542416 | tf_op jit(solution)/shard_map/dot_general | solution.py:171
  54.9 1.3 %fusion.37 = f32[128,128,38]{1,2,0:T(8,128)S(1)} fusion(f32[38,128,128]{2,0,1:T(8,128)S(1)} %bitcast_subtract_fusion.4, f32[38,38]{1,0:T(8,128)S(1)} %copy-done.7), kind=kOutput, calls=%fused_computation.46 | convolution fusion | flops 141950976 | bytes 4986512 | tf_op jit(solution)/shard_map/dot_general | solution.py:164
  56.3 2.8 %bitcast_subtract_fusion.2 = f32[38,128,128]{2,0,1:T(8,128)S(1)} fusion(f32[38,128,128]{2,0,1:T(8,128)S(1)} %bitcast_subtract_fusion.4, f32[128,128,38]{1,2,0:T(8,128)S(1)} %fusion.37, f32[128,38,128]{2,1,0:T(8,128)S(1)} %copy-done.1, f32[128,128]{1,0:T(8,128)S(1)} %exponential_multiply_fusion, f32[38,38]{1,0:T(8,128)S(1)} %copy-done.8), kind=kOutput, calls=%fused_computation.7 | convolution fusion | flops 148176896 | bytes 10032784 | tf_op jit(solution)/shard_map/dot_general | solution.py:171
  59.1 1.3 %fusion.35 = f32[128,128,38]{1,2,0:T(8,128)S(1)} fusion(f32[38,128,128]{2,0,1:T(8,128)S(1)} %bitcast_subtract_fusion.2, f32[38,38]{1,0:T(8,128)S(1)} %copy-done.7), kind=kOutput, calls=%fused_computation.44 | convolution fusion | flops 141950976 | bytes 4986512 | tf_op jit(solution)/shard_map/dot_general | solution.py:164
  60.4 3.2 %fusion = f32[38,128,128]{2,0,1:T(8,128)S(1)} fusion(f32[128,38,128]{2,1,0:T(8,128)S(1)} %copy-done.1, f32[38,128,128]{2,0,1:T(8,128)S(1)} %bitcast_subtract_fusion.2, f32[128,128,38]{1,2,0:T(8,128)S(1)} %fusion.35, f32[128,128]{1,0:T(8,128)S(1)} %exponential_multiply_fusion, pred[128]{0:T(512)(128)(4,1)S(1)} %gt.22, f32[38,38]{1,0:T(8,128)S(1)} %copy-done.8), kind=kOutput, calls=%fused_computation.3 | convolution fusion | flops 148799488 | bytes 10032912 | tf_op jit(solution)/shard_map/dot_general | solution.py:171
  63.7 1.7 %convolution_bitcast_fusion = f32[4,128,128]{2,0,1:T(4,128)S(1)} fusion(f32[38,128,128]{2,0,1:T(8,128)S(1)} %fusion, f32[4,38]{1,0:T(4,128)S(1)} %copy-done.11), kind=kOutput, calls=%fused_computation.33 | convolution fusion | flops 29884416 | bytes 2753120 | tf_op jit(solution)/shard_map/dot_general | solution.py:177
  65.3 0.3 fusion.29
  65.7 1.6 %collective-permute-start.4 = (f32[4,128]{1,0:T(4,128)S(1)}, f32[4,128]{1,0:T(4,128)S(1)}, u32[]{:S(2)}, u32[]{:S(2)}) collective-permute-start(f32[4,128]{1,0:T(4,128)S(1)} %broadcast_multiply_fusion), channel_id=1, source_target_pairs={{0,1},{1,0},{2,3},{3,2},{4,5},{5,4},{6,7},{7,6},{8,9},{9,8},{10,11... | collective-permute-start | bytes 6152 | tf_op jit(solution)/shard_map/ppermute | solution.py:187
  67.3 2.0 %collective-permute-done.4 = f32[4,128]{1,0:T(4,128)S(1)} collective-permute-done((f32[4,128]{1,0:T(4,128)S(1)}, f32[4,128]{1,0:T(4,128)S(1)}, u32[]{:S(2)}, u32[]{:S(2)}) %collective-permute-start.4) | collective-permute-done | bytes 2080 | tf_op jit(solution)/shard_map/ppermute | solution.py:187
  69.3 2.6 %collective-permute-start.5 = (f32[4,128]{1,0:T(4,128)S(1)}, f32[4,128]{1,0:T(4,128)S(1)}, u32[]{:S(2)}, u32[]{:S(2)}) collective-permute-start(f32[4,128]{1,0:T(4,128)S(1)} %fusion.50), channel_id=1, source_target_pairs={{0,2},{1,3},{2,0},{3,1},{4,6},{5,7},{6,4},{7,5},{8,10},{9,11},{10,... | collective-permute-start | bytes 6152 | tf_op jit(solution)/shard_map/ppermute | solution.py:187
  71.9 1.9 %collective-permute-done.5 = f32[4,128]{1,0:T(4,128)S(1)} collective-permute-done((f32[4,128]{1,0:T(4,128)S(1)}, f32[4,128]{1,0:T(4,128)S(1)}, u32[]{:S(2)}, u32[]{:S(2)}) %collective-permute-start.5) | collective-permute-done | bytes 2080 | tf_op jit(solution)/shard_map/ppermute | solution.py:187
  73.8 1.2 %collective-permute-done.6 = f32[1,4,128]{2,0,1:T(1,128)S(1)} collective-permute-done((f32[1,4,128]{2,0,1:T(1,128)S(1)}, f32[1,4,128]{2,0,1:T(1,128)S(1)}, u32[]{:S(2)}, u32[]{:S(2)}) %collective-permute-start.6) | collective-permute-done | bytes 2080 | tf_op jit(solution)/shard_map/ppermute | solution.py:200
  75.0 4.1 %collective-permute-start.7 = (f32[2,4,128]{2,0,1:T(2,128)S(1)}, f32[2,4,128]{2,0,1:T(2,128)S(1)}, u32[]{:S(2)}, u32[]{:S(2)}) collective-permute-start(f32[2,4,128]{2,0,1:T(2,128)S(1)} %maximum_select_fusion.2), channel_id=1, source_target_pairs={{0,8},{4,12},{8,0},{12,4},{16,24},{20,28},{24,16},{28,20},{1,9},{5... | collective-permute-start | bytes 12296 | tf_op jit(solution)/shard_map/ppermute | solution.py:200
  79.1 1.6 %collective-permute-done.7 = f32[2,4,128]{2,0,1:T(2,128)S(1)} collective-permute-done((f32[2,4,128]{2,0,1:T(2,128)S(1)}, f32[2,4,128]{2,0,1:T(2,128)S(1)}, u32[]{:S(2)}, u32[]{:S(2)}) %collective-permute-start.7) | collective-permute-done | bytes 4128 | tf_op jit(solution)/shard_map/ppermute | solution.py:200
  80.7 3.0 %collective-permute-start.8 = (f32[4,4,128]{2,0,1:T(4,128)S(1)}, f32[4,4,128]{2,0,1:T(4,128)S(1)}, u32[]{:S(2)}, u32[]{:S(2)}) collective-permute-start(f32[4,4,128]{2,0,1:T(4,128)S(1)} %maximum_select_fusion.1), channel_id=1, source_target_pairs={{0,16},{4,20},{8,24},{12,28},{16,0},{20,4},{24,8},{28,12},{1,17},{... | collective-permute-start | bytes 24584 | tf_op jit(solution)/shard_map/ppermute | solution.py:200
  83.7 1.9 %copy.14 = f32[38,128,128]{2,1,0:T(8,128)} copy(f32[38,128,128]{2,0,1:T(8,128)S(1)} %fusion) | data formatting | bytes 4980736
  85.6 2.8 %select_reduce_fusion = f32[4,1024]{1,0:T(4,128)S(1)} fusion(f32[4,1024]{1,0:T(4,128)S(1)} %bitcast.114, s32[4,1024]{1,0:T(4,128)S(1)} %constant_dynamic-slice_fusion), kind=kLoop, calls=%fused_computation | loop fusion | flops 12578816 | bytes 49152 | tf_op jit(solution)/shard_map/reduce_sum | solution.py:252
  88.5 0.6 sub.73
  (43 shorter events, 0.2 us)
Async XLA Ops:
  0.6 83.1 %copy-start = (s32[4,32768]{1,0:T(4,128)S(1)}, s32[4,32768]{1,0:T(4,128)}, u32[]{:S(2)}) copy-start(s32[4,32768]{1,0:T(4,128)} %param.18) | copy-start | bytes 1572868
  0.6 6.4 %copy-start.2 = (f32[38,128,128]{2,1,0:T(8,128)S(1)}, f32[38,128,128]{2,1,0:T(8,128)}, u32[]{:S(2)}) copy-start(f32[38,128,128]{2,1,0:T(8,128)} %field_ref.1) | copy-start | bytes 7471108
  3.4 12.8 %collective-permute-start = (f32[39,3,128]{2,1,0:T(4,128)}, f32[39,3,128]{2,1,0:T(4,128)S(1)}, u32[]{:S(2)}, u32[]{:S(2)}) collective-permute-start(f32[39,3,128]{2,1,0:T(4,128)} %get-tuple-element.9), channel_id=1, source_target_pairs={{0,4},{4,8},{8,12},{12,16},{16,20},{20,24},{24,28},{1,5},{5,9},{9,... | collective-permute-start | bytes 179720 | tf_op jit(solution)/shard_map/ppermute | solution.py:28
  5.7 10.5 %collective-permute-start.1 = (f32[39,3,128]{2,1,0:T(4,128)S(1)}, f32[39,3,128]{2,1,0:T(4,128)S(1)}, u32[]{:S(2)}, u32[]{:S(2)}) collective-permute-start(f32[39,3,128]{2,1,0:T(4,128)S(1)} %get-tuple-element.8), channel_id=1, source_target_pairs={{4,0},{8,4},{12,8},{16,12},{20,16},{24,20},{28,24},{5,1},{9,5},{13... | collective-permute-start | bytes 179720 | tf_op jit(solution)/shard_map/ppermute | solution.py:28
  7.0 8.8 %copy-start.9 = (f32[128,128]{1,0:T(8,128)S(1)}, f32[128,128]{1,0:T(8,128)}, u32[]{:S(2)}) copy-start(f32[128,128]{1,0:T(8,128)} %param.12) | copy-start | bytes 196612
  7.0 8.8 %copy-start.13 = (s32[64,1]{0,1:T(1,128)S(1)}, s32[64,1]{0,1:T(1,128)}, u32[]{:S(2)}) copy-start(s32[64,1]{0,1:T(1,128)} %param.15) | copy-start | bytes 772
  8.3 7.9 %collective-permute-start.2 = (f32[39,3,128]{2,1,0:T(4,128)S(1)}, f32[39,3,128]{2,1,0:T(4,128)S(1)}, u32[]{:S(2)}, u32[]{:S(2)}) collective-permute-start(f32[39,3,128]{2,1,0:T(4,128)S(1)} %fusion.27), channel_id=1, source_target_pairs={{0,1},{1,2},{2,3},{4,5},{5,6},{6,7},{8,9},{9,10},{10,11},{12,13},{... | collective-permute-start | bytes 179720 | tf_op jit(solution)/shard_map/ppermute | solution.py:132
  14.6 6.5 %collective-permute-start.3 = (f32[39,3,128]{2,1,0:T(4,128)}, f32[39,3,128]{2,1,0:T(4,128)S(1)}, u32[]{:S(2)}, u32[]{:S(2)}) collective-permute-start(f32[39,3,128]{2,1,0:T(4,128)} %fusion.28), channel_id=1, source_target_pairs={{1,0},{2,1},{3,2},{5,4},{6,5},{7,6},{9,8},{10,9},{11,10},{13,12},{... | collective-permute-start | bytes 179720 | tf_op jit(solution)/shard_map/ppermute | solution.py:133
  16.1 33.0 %copy-start.7 = (f32[38,38]{1,0:T(8,128)S(1)}, f32[38,38]{1,0:T(8,128)}, u32[]{:S(2)}) copy-start(f32[38,38]{1,0:T(8,128)} %param.13) | copy-start | bytes 17332
  16.2 4.9 %copy-start.3 = (f32[39,3,128]{2,1,0:T(4,128)}, f32[39,3,128]{2,1,0:T(4,128)S(1)}, u32[]{:S(2)}) copy-start(f32[39,3,128]{2,1,0:T(4,128)S(1)} %collective-permute-done.top_ref.top_speed_ref) | copy-start | bytes 179716
  16.2 4.9 %copy-start.4 = (f32[39,3,128]{2,1,0:T(4,128)}, f32[39,3,128]{2,1,0:T(4,128)S(1)}, u32[]{:S(2)}) copy-start(f32[39,3,128]{2,1,0:T(4,128)S(1)} %collective-permute-done.1.bottom_ref.bottom_speed_ref) | copy-start | bytes 179716
  16.2 4.9 %copy-start.5 = (f32[39,3,128]{2,1,0:T(4,128)}, f32[39,3,128]{2,1,0:T(4,128)S(1)}, u32[]{:S(2)}) copy-start(f32[39,3,128]{2,1,0:T(4,128)S(1)} %collective-permute-done.2.left_ref.left_speed_ref) | copy-start | bytes 179716
  21.1 0.6 copy-start.6
  49.2 3.2 %copy-start.1 = (f32[128,38,128]{2,1,0:T(8,128)S(1)}, f32[128,38,128]{2,1,0:T(8,128)}, u32[]{:S(2)}) copy-start(f32[128,38,128]{2,1,0:T(8,128)} %shard_map.113) | copy-start | bytes 7471108
  49.2 3.2 %copy-start.8 = (f32[38,38]{1,0:T(8,128)S(1)}, f32[38,38]{1,0:T(8,128)}, u32[]{:S(2)}) copy-start(f32[38,38]{1,0:T(8,128)} %param.14) | copy-start | bytes 17332
  60.4 3.3 %copy-start.11 = (f32[4,38]{1,0:T(4,128)S(1)}, f32[4,38]{1,0:T(4,128)}, u32[]{:S(2)}) copy-start(f32[4,38]{1,0:T(4,128)} %param.16) | copy-start | bytes 1828
  63.7 1.7 %copy-start.12 = (f32[128]{0:T(128)S(1)}, f32[128]{0:T(128)}, u32[]{:S(2)}) copy-start(f32[128]{0:T(128)} %param.17) | copy-start | bytes 1540
  65.7 3.7 %collective-permute-start.4 = (f32[4,128]{1,0:T(4,128)S(1)}, f32[4,128]{1,0:T(4,128)S(1)}, u32[]{:S(2)}, u32[]{:S(2)}) collective-permute-start(f32[4,128]{1,0:T(4,128)S(1)} %broadcast_multiply_fusion), channel_id=1, source_target_pairs={{0,1},{1,0},{2,3},{3,2},{4,5},{5,4},{6,7},{7,6},{8,9},{9,8},{10,11... | collective-permute-start | bytes 6152 | tf_op jit(solution)/shard_map/ppermute | solution.py:187
  69.3 4.5 %collective-permute-start.5 = (f32[4,128]{1,0:T(4,128)S(1)}, f32[4,128]{1,0:T(4,128)S(1)}, u32[]{:S(2)}, u32[]{:S(2)}) collective-permute-start(f32[4,128]{1,0:T(4,128)S(1)} %fusion.50), channel_id=1, source_target_pairs={{0,2},{1,3},{2,0},{3,1},{4,6},{5,7},{6,4},{7,5},{8,10},{9,11},{10,... | collective-permute-start | bytes 6152 | tf_op jit(solution)/shard_map/ppermute | solution.py:187
  73.8 1.2 %collective-permute-start.6 = (f32[1,4,128]{2,0,1:T(1,128)S(1)}, f32[1,4,128]{2,0,1:T(1,128)S(1)}, u32[]{:S(2)}, u32[]{:S(2)}) collective-permute-start(f32[1,4,128]{2,0,1:T(1,128)S(1)} %bitcast.117), channel_id=1, source_target_pairs={{0,4},{4,0},{8,12},{12,8},{16,20},{20,16},{24,28},{28,24},{1,5},{5... | collective-permute-start | bytes 6152 | tf_op jit(solution)/shard_map/ppermute | solution.py:200
  75.0 5.7 %collective-permute-start.7 = (f32[2,4,128]{2,0,1:T(2,128)S(1)}, f32[2,4,128]{2,0,1:T(2,128)S(1)}, u32[]{:S(2)}, u32[]{:S(2)}) collective-permute-start(f32[2,4,128]{2,0,1:T(2,128)S(1)} %maximum_select_fusion.2), channel_id=1, source_target_pairs={{0,8},{4,12},{8,0},{12,4},{16,24},{20,28},{24,16},{28,20},{1,9},{5... | collective-permute-start | bytes 12296 | tf_op jit(solution)/shard_map/ppermute | solution.py:200
  80.7 4.9 %collective-permute-start.8 = (f32[4,4,128]{2,0,1:T(4,128)S(1)}, f32[4,4,128]{2,0,1:T(4,128)S(1)}, u32[]{:S(2)}, u32[]{:S(2)}) collective-permute-start(f32[4,4,128]{2,0,1:T(4,128)S(1)} %maximum_select_fusion.1), channel_id=1, source_target_pairs={{0,16},{4,20},{8,24},{12,28},{16,0},{20,4},{24,8},{28,12},{1,17},{... | collective-permute-start | bytes 24584 | tf_op jit(solution)/shard_map/ppermute | solution.py:200
  83.7 4.8 %copy-start.10 = (f32[4,1024]{1,0:T(4,128)S(1)}, f32[4,1024]{1,0:T(4,128)}, u32[]{:S(2)}) copy-start(f32[4,1024]{1,0:T(4,128)} %param.19) | copy-start | bytes 49156

commit v6 on v5

--- a/solution.py
+++ b/solution.py
@@ -55,6 +55,7 @@
 
 
 HALO = 8
+SPECIES_GROUP = 19
 CHUNK = 8
 
 
@@ -83,33 +84,33 @@
     ext_ref, vel_ref, flux_ref,
 ):
     rows, cols = field_ref.shape[1], field_ref.shape[2]
-    width = top_ref.shape[1]
-    span = ext_ref.shape[0]
-    field = field_ref[0]
-
-    for scratch in (ext_ref, vel_ref):
-        scratch[pl.ds(0, HALO), :] = jnp.zeros((HALO, cols), jnp.float32)
-        scratch[pl.ds(HALO + rows, span - HALO - rows), :] = jnp.zeros(
-            (span - HALO - rows, cols), jnp.float32
-        )
-    ext_ref[pl.ds(HALO - width, width), :] = top_ref[0]
-    ext_ref[pl.ds(HALO, rows), :] = field
-    ext_ref[pl.ds(HALO + rows, width), :] = bottom_ref[0]
-    vel_ref[pl.ds(HALO - width, width), :] = top_speed_ref[0]
-    vel_ref[pl.ds(HALO, rows), :] = speed_ref[0]
-    vel_ref[pl.ds(HALO + rows, width), :] = bottom_speed_ref[0]
-    along_axial = upwind_divergence(ext_ref, vel_ref, flux_ref, rows)
-
-    ext_ref[pl.ds(HALO - width, width), :] = left_ref[0]
-    ext_ref[pl.ds(HALO, cols), :] = field.T
-    ext_ref[pl.ds(HALO + cols, width), :] = right_ref[0]
-    vel_ref[pl.ds(HALO - width, width), :] = left_speed_ref[0]
-    vel_ref[pl.ds(HALO, cols), :] = speed_ref[1].T
-    vel_ref[pl.ds(HALO + cols, width), :] = right_speed_ref[0]
-    along_radial = upwind_divergence(ext_ref, vel_ref, flux_ref, cols).T
-
-    moved = field - TIME_STEP * (along_axial + along_radial)
-    out_ref[:, pl.ds(pl.program_id(0), 1), :] = moved[:, None, :]
+    group = field_ref.shape[0]
+
+    def one_species(member, carry):
+        field = field_ref[member]
+        fill_scratch(ext_ref, top_ref[member], field, bottom_ref[member])
+        fill_scratch(vel_ref, top_speed_ref[0], speed_ref[0], bottom_speed_ref[0])
+        along_axial = upwind_divergence(ext_ref, vel_ref, flux_ref, rows)
+        fill_scratch(ext_ref, left_ref[member], field.T, right_ref[member])
+        fill_scratch(vel_ref, left_speed_ref[0], speed_ref[1].T, right_speed_ref[0])
+        along_radial = upwind_divergence(ext_ref, vel_ref, flux_ref, cols).T
+        moved = field - TIME_STEP * (along_axial + along_radial)
+        out_ref[:, pl.ds(pl.program_id(0) * group + member, 1), :] = moved[:, None, :]
+        return carry
+
+    lax.fori_loop(0, group, one_species, 0)
+
+
+def fill_scratch(scratch, before, body, after):
+    span, cols = scratch.shape
+    width, rows = (before.shape[0], body.shape[0])
+    scratch[pl.ds(0, HALO), :] = jnp.zeros((HALO, cols), jnp.float32)
+    scratch[pl.ds(HALO + rows, span - HALO - rows), :] = jnp.zeros(
+        (span - HALO - rows, cols), jnp.float32
+    )
+    scratch[pl.ds(HALO - width, width), :] = before
+    scratch[pl.ds(HALO, rows), :] = body
+    scratch[pl.ds(HALO + rows, width), :] = after
 
 
 def edge_columns(field, start, width):
@@ -133,13 +134,14 @@
     right = lax.ppermute(edge_columns(radial_edges, 0, width), "radial", down)
     faces = rows + CHUNK
     span = HALO + faces + HALO
-    plane = pl.BlockSpec((1, rows, cols), lambda s: (s, 0, 0))
+    group = max(g for g in range(1, SPECIES_GROUP + 1) if species_count % g == 0)
+    plane = pl.BlockSpec((group, rows, cols), lambda s: (s, 0, 0))
     speeds = pl.BlockSpec((2, rows, cols), lambda s: (0, 0, 0))
-    edge = pl.BlockSpec((1, width, cols), lambda s: (s, 0, 0))
+    edge = pl.BlockSpec((group, width, cols), lambda s: (s, 0, 0))
     edge_speed = pl.BlockSpec((1, width, cols), lambda s: (species_count, 0, 0))
     moved_rows = pl.pallas_call(
         transport_kernel,
-        grid=(species_count,),
+        grid=(species_count // group,),
         in_specs=[plane, speeds] + [edge, edge_speed] * 4,
         out_specs=pl.BlockSpec((rows, species_count, cols), lambda s: (0, 0, 0)),
         out_shape=jax.ShapeDtypeStruct((rows, species_count, cols), jnp.float32),

time: 90.6 us -> 81.6 us (0.901); the launches traced: 89.1 us -> 81.4 us
  Pallas kernels: 27.5 us -> 19.8 us
    pallas_call x1, Pallas kernels: 27.5 us -> 19.8 us  [transport(): pl.pallas_call(transport_kernel, grid=(species_count // group,), in_specs...]
  transfers between devices with their start and end apart: 9 -> 9, of which waited for: 5 -> 5; matrix products, arithmetic and copies ran while one was open for 6% -> 7% of each run, Pallas kernels for 0% -> 0%
where the time goes in v6:
time: 81.6 us; the launch traced here: 81.4 us
  starting transfers between devices  20.5 us (25%)
  Pallas kernels  19.8 us (24%)
  matrix products  19.5 us (24%)
  waiting for transfers between devices  11.5 us (14%)
  other arithmetic  5.17 us (6%)
  local copies, waits for them, and re-layouts  3.86 us (5%)
  between operations  0.96 us (1%)
    pallas_call x1, Pallas kernels, transport(): pl.pallas_call(transport_kernel, grid=(species_count // group,), in_specs...  19.8 us
    dot_general x3, matrix products, kinetics_advance(): jnp.tensordot(frozen_jacobian_inverse_addend, defect, axes=(1, 0), precis...  8.58 us
    ppermute x3, starting transfers between devices, doubling_gather(): other = lax.ppermute(blocks, axis, pairs)  7.08 us
    dot_general x3, matrix products, kinetics_advance(): jnp.tensordot(linearized_kinetics_operator, current, axes=(1, 0), precisi...  5.82 us
    ppermute x1, waiting for transfers between devices, transport(): right = lax.ppermute(edge_columns(radial_edges, 0, width), 'radial', down)  4.85 us
    ppermute x1, starting transfers between devices, transport(): lax.ppermute(edge_columns(radial_edges, cols - width, width), 'radial', up)  4.32 us
    ppermute x2, starting transfers between devices, butterfly_sum(): part = part + lax.ppermute(part, axis, pairs)  4.22 us
    ppermute x2, waiting for transfers between devices, butterfly_sum(): part = part + lax.ppermute(part, axis, pairs)  3.93 us
  transfers between devices with their start and end apart: 9, of which 5 were waited for; matrix products, arithmetic and copies ran while one was open for 7% of the time, Pallas kernels for 0%

profile of v6, /device:TPU:0, one launch (start us, length us, event | category | flops | bytes accessed | tf_op | source)
XLA Modules:
  0.0 81.4 jit_solution(7353362443100944585)
XLA Ops:
  0.7 1.0 %fusion.51 = (f32[1,128,128]{2,1,0:T(8,128)S(1)}, f32[1,128,128]{2,1,0:T(8,128)S(1)}) fusion(f32[2,128,128]{2,1,0:T(8,128)} %speed_ref.1), kind=kLoop, calls=%fused_computation.68 | loop fusion | bytes 262144 | tf_op jit(solution)/shard_map/slice | solution.py:129
  1.7 1.7 %pad_maximum_fusion.7 = (f32[39,3,128]{2,1,0:T(4,128)S(1)}, f32[39,3,128]{2,1,0:T(4,128)}) fusion(f32[1,128,128]{2,1,0:T(8,128)S(1)} %get-tuple-element.11, f32[38,128,128]{2,1,0:T(8,128)} %field_ref.1), kind=kLoop, calls=%fused_computation.39 | loop fusion | flops 29952 | bytes 2675712 | tf_op jit(solution)/shard_map/concatenate | solution.py:127
  3.4 2.3 %collective-permute-start = (f32[39,3,128]{2,1,0:T(4,128)}, f32[39,3,128]{2,1,0:T(4,128)S(1)}, u32[]{:S(2)}, u32[]{:S(2)}) collective-permute-start(f32[39,3,128]{2,1,0:T(4,128)} %get-tuple-element.9), channel_id=1, source_target_pairs={{0,4},{4,8},{8,12},{12,16},{16,20},{20,24},{24,28},{1,5},{5,9},{9,... | collective-permute-start | bytes 179720 | tf_op jit(solution)/shard_map/ppermute | solution.py:28
  5.7 1.3 %collective-permute-start.1 = (f32[39,3,128]{2,1,0:T(4,128)S(1)}, f32[39,3,128]{2,1,0:T(4,128)S(1)}, u32[]{:S(2)}, u32[]{:S(2)}) collective-permute-start(f32[39,3,128]{2,1,0:T(4,128)S(1)} %get-tuple-element.8), channel_id=1, source_target_pairs={{4,0},{8,4},{12,8},{16,12},{20,16},{24,20},{28,24},{5,1},{9,5},{13... | collective-permute-start | bytes 179720 | tf_op jit(solution)/shard_map/ppermute | solution.py:28
  7.1 1.3 %fusion.27 = f32[39,3,128]{2,1,0:T(4,128)S(1)} fusion(f32[1,128,128]{2,1,0:T(8,128)S(1)} %get-tuple-element.10, f32[38,128,128]{2,1,0:T(8,128)S(1)} %copy-done.2, s32[3]{0:T(128)S(1)} %iota_add_fusion), kind=kOutput, calls=%fused_computation.34 | convolution fusion | flops 23642496 | bytes 2615820 | tf_op jit(solution)/shard_map/kr,sar->ska/dot_general | solution.py:121
  8.3 4.3 %collective-permute-start.2 = (f32[39,3,128]{2,1,0:T(4,128)S(1)}, f32[39,3,128]{2,1,0:T(4,128)S(1)}, u32[]{:S(2)}, u32[]{:S(2)}) collective-permute-start(f32[39,3,128]{2,1,0:T(4,128)S(1)} %fusion.27), channel_id=1, source_target_pairs={{0,1},{1,2},{2,3},{4,5},{5,6},{6,7},{8,9},{9,10},{10,11},{12,13},{... | collective-permute-start | bytes 179720 | tf_op jit(solution)/shard_map/ppermute | solution.py:133
  12.6 1.9 %fusion.28 = f32[39,3,128]{2,1,0:T(4,128)} fusion(f32[1,128,128]{2,1,0:T(8,128)S(1)} %get-tuple-element.10, f32[38,128,128]{2,1,0:T(8,128)S(1)} %copy-done.2), kind=kOutput, calls=%fused_computation.35 | convolution fusion | flops 23642496 | bytes 2615808 | tf_op jit(solution)/shard_map/kr,sar->ska/dot_general | solution.py:121
  14.6 1.3 %collective-permute-start.3 = (f32[39,3,128]{2,1,0:T(4,128)}, f32[39,3,128]{2,1,0:T(4,128)S(1)}, u32[]{:S(2)}, u32[]{:S(2)}) collective-permute-start(f32[39,3,128]{2,1,0:T(4,128)} %fusion.28), channel_id=1, source_target_pairs={{1,0},{2,1},{3,2},{5,4},{6,5},{7,6},{9,8},{10,9},{11,10},{13,12},{... | collective-permute-start | bytes 179720 | tf_op jit(solution)/shard_map/ppermute | solution.py:134
  15.9 0.1 broadcast_in_dim.33
  16.0 0.2 gt.22
  16.2 4.9 %collective-permute-done.3.right_ref.right_speed_ref = f32[39,3,128]{2,1,0:T(4,128)S(1)} collective-permute-done((f32[39,3,128]{2,1,0:T(4,128)}, f32[39,3,128]{2,1,0:T(4,128)S(1)}, u32[]{:S(2)}, u32[]{:S(2)}) %collective-permute-start.3) | collective-permute-done | bytes 59936 | tf_op jit(solution)/shard_map/ppermute | solution.py:134
  21.1 0.6 copy-done.6
  21.7 19.8 %shard_map.113 = f32[128,38,128]{2,1,0:T(8,128)} custom-call(f32[38,128,128]{2,1,0:T(8,128)} %field_ref.1, f32[2,128,128]{2,1,0:T(8,128)} %speed_ref.1, f32[39,3,128]{2,1,0:T(4,128)} %copy-done.3, f32[39,3,128]{2,1,0:T(4,128)} %copy-done.3, f32[39,3,128]{2,1,0:T(4,128)} %copy-done.4, f32[39,3,128]{2,1,0:T(4,128)} %copy-done.4, f32[39,3,128]{2,1,0:T(4,128)} %copy-done.5, ...), custom_call_target="tpu_custom_call" | custom-call | tf_op jit(solution)/shard_map/pallas_call | solution.py:142
  41.5 3.2 %fusion.13 = f32[128,128,38]{1,2,0:T(8,128)S(1)} fusion(f32[128,38,128]{2,1,0:T(8,128)} %shard_map.113, f32[38,38]{1,0:T(8,128)S(1)} %copy-done.7), kind=kOutput, calls=%fused_computation.22 | convolution fusion | flops 141950976 | bytes 4986512 | tf_op jit(solution)/shard_map/dot_general | solution.py:166
  44.7 2.6 %bitcast_subtract_fusion.4 = f32[38,128,128]{2,0,1:T(8,128)S(1)} fusion(f32[128,128,38]{1,2,0:T(8,128)S(1)} %fusion.13, f32[128,38,128]{2,1,0:T(8,128)S(1)} %copy-done.1, f32[128,128]{1,0:T(8,128)S(1)} %exponential_multiply_fusion, f32[38,38]{1,0:T(8,128)S(1)} %copy-done.8), kind=kOutput, calls=%fused_computation.11 | convolution fusion | flops 148176896 | bytes 7542416 | tf_op jit(solution)/shard_map/dot_general | solution.py:173
  47.2 1.3 %fusion.37 = f32[128,128,38]{1,2,0:T(8,128)S(1)} fusion(f32[38,128,128]{2,0,1:T(8,128)S(1)} %bitcast_subtract_fusion.4, f32[38,38]{1,0:T(8,128)S(1)} %copy-done.7), kind=kOutput, calls=%fused_computation.46 | convolution fusion | flops 141950976 | bytes 4986512 | tf_op jit(solution)/shard_map/dot_general | solution.py:166
  48.6 2.8 %bitcast_subtract_fusion.2 = f32[38,128,128]{2,0,1:T(8,128)S(1)} fusion(f32[38,128,128]{2,0,1:T(8,128)S(1)} %bitcast_subtract_fusion.4, f32[128,128,38]{1,2,0:T(8,128)S(1)} %fusion.37, f32[128,38,128]{2,1,0:T(8,128)S(1)} %copy-done.1, f32[128,128]{1,0:T(8,128)S(1)} %exponential_multiply_fusion, f32[38,38]{1,0:T(8,128)S(1)} %copy-done.8), kind=kOutput, calls=%fused_computation.7 | convolution fusion | flops 148176896 | bytes 10032784 | tf_op jit(solution)/shard_map/dot_general | solution.py:173
  51.4 1.3 %fusion.35 = f32[128,128,38]{1,2,0:T(8,128)S(1)} fusion(f32[38,128,128]{2,0,1:T(8,128)S(1)} %bitcast_subtract_fusion.2, f32[38,38]{1,0:T(8,128)S(1)} %copy-done.7), kind=kOutput, calls=%fused_computation.44 | convolution fusion | flops 141950976 | bytes 4986512 | tf_op jit(solution)/shard_map/dot_general | solution.py:166
  52.7 3.2 %fusion = f32[38,128,128]{2,0,1:T(8,128)S(1)} fusion(f32[128,38,128]{2,1,0:T(8,128)S(1)} %copy-done.1, f32[38,128,128]{2,0,1:T(8,128)S(1)} %bitcast_subtract_fusion.2, f32[128,128,38]{1,2,0:T(8,128)S(1)} %fusion.35, f32[128,128]{1,0:T(8,128)S(1)} %exponential_multiply_fusion, pred[128]{0:T(512)(128)(4,1)S(1)} %gt.22, f32[38,38]{1,0:T(8,128)S(1)} %copy-done.8), kind=kOutput, calls=%fused_computation.3 | convolution fusion | flops 148799488 | bytes 10032912 | tf_op jit(solution)/shard_map/dot_general | solution.py:173
  56.0 1.7 %convolution_bitcast_fusion = f32[4,128,128]{2,0,1:T(4,128)S(1)} fusion(f32[38,128,128]{2,0,1:T(8,128)S(1)} %fusion, f32[4,38]{1,0:T(4,128)S(1)} %copy-done.11), kind=kOutput, calls=%fused_computation.33 | convolution fusion | flops 29884416 | bytes 2753120 | tf_op jit(solution)/shard_map/dot_general | solution.py:179
  57.7 0.3 fusion.29
  58.0 1.6 %collective-permute-start.4 = (f32[4,128]{1,0:T(4,128)S(1)}, f32[4,128]{1,0:T(4,128)S(1)}, u32[]{:S(2)}, u32[]{:S(2)}) collective-permute-start(f32[4,128]{1,0:T(4,128)S(1)} %broadcast_multiply_fusion), channel_id=1, source_target_pairs={{0,1},{1,0},{2,3},{3,2},{4,5},{5,4},{6,7},{7,6},{8,9},{9,8},{10,11... | collective-permute-start | bytes 6152 | tf_op jit(solution)/shard_map/ppermute | solution.py:189
  59.6 2.0 %collective-permute-done.4 = f32[4,128]{1,0:T(4,128)S(1)} collective-permute-done((f32[4,128]{1,0:T(4,128)S(1)}, f32[4,128]{1,0:T(4,128)S(1)}, u32[]{:S(2)}, u32[]{:S(2)}) %collective-permute-start.4) | collective-permute-done | bytes 2080 | tf_op jit(solution)/shard_map/ppermute | solution.py:189
  61.7 2.6 %collective-permute-start.5 = (f32[4,128]{1,0:T(4,128)S(1)}, f32[4,128]{1,0:T(4,128)S(1)}, u32[]{:S(2)}, u32[]{:S(2)}) collective-permute-start(f32[4,128]{1,0:T(4,128)S(1)} %fusion.50), channel_id=1, source_target_pairs={{0,2},{1,3},{2,0},{3,1},{4,6},{5,7},{6,4},{7,5},{8,10},{9,11},{10,... | collective-permute-start | bytes 6152 | tf_op jit(solution)/shard_map/ppermute | solution.py:189
  64.2 1.9 %collective-permute-done.5 = f32[4,128]{1,0:T(4,128)S(1)} collective-permute-done((f32[4,128]{1,0:T(4,128)S(1)}, f32[4,128]{1,0:T(4,128)S(1)}, u32[]{:S(2)}, u32[]{:S(2)}) %collective-permute-start.5) | collective-permute-done | bytes 2080 | tf_op jit(solution)/shard_map/ppermute | solution.py:189
  66.1 1.2 %collective-permute-done.6 = f32[1,4,128]{2,0,1:T(1,128)S(1)} collective-permute-done((f32[1,4,128]{2,0,1:T(1,128)S(1)}, f32[1,4,128]{2,0,1:T(1,128)S(1)}, u32[]{:S(2)}, u32[]{:S(2)}) %collective-permute-start.6) | collective-permute-done | bytes 2080 | tf_op jit(solution)/shard_map/ppermute | solution.py:202
  67.3 4.1 %collective-permute-start.7 = (f32[2,4,128]{2,0,1:T(2,128)S(1)}, f32[2,4,128]{2,0,1:T(2,128)S(1)}, u32[]{:S(2)}, u32[]{:S(2)}) collective-permute-start(f32[2,4,128]{2,0,1:T(2,128)S(1)} %maximum_select_fusion.2), channel_id=1, source_target_pairs={{0,8},{4,12},{8,0},{12,4},{16,24},{20,28},{24,16},{28,20},{1,9},{5... | collective-permute-start | bytes 12296 | tf_op jit(solution)/shard_map/ppermute | solution.py:202
  71.4 1.6 %collective-permute-done.7 = f32[2,4,128]{2,0,1:T(2,128)S(1)} collective-permute-done((f32[2,4,128]{2,0,1:T(2,128)S(1)}, f32[2,4,128]{2,0,1:T(2,128)S(1)}, u32[]{:S(2)}, u32[]{:S(2)}) %collective-permute-start.7) | collective-permute-done | bytes 4128 | tf_op jit(solution)/shard_map/ppermute | solution.py:202
  73.0 3.0 %collective-permute-start.8 = (f32[4,4,128]{2,0,1:T(4,128)S(1)}, f32[4,4,128]{2,0,1:T(4,128)S(1)}, u32[]{:S(2)}, u32[]{:S(2)}) collective-permute-start(f32[4,4,128]{2,0,1:T(4,128)S(1)} %maximum_select_fusion.1), channel_id=1, source_target_pairs={{0,16},{4,20},{8,24},{12,28},{16,0},{20,4},{24,8},{28,12},{1,17},{... | collective-permute-start | bytes 24584 | tf_op jit(solution)/shard_map/ppermute | solution.py:202
  76.0 1.9 %copy.14 = f32[38,128,128]{2,1,0:T(8,128)} copy(f32[38,128,128]{2,0,1:T(8,128)S(1)} %fusion) | data formatting | bytes 4980736
  77.9 2.8 %select_reduce_fusion = f32[4,1024]{1,0:T(4,128)S(1)} fusion(f32[4,1024]{1,0:T(4,128)S(1)} %bitcast.114, s32[4,1024]{1,0:T(4,128)S(1)} %constant_dynamic-slice_fusion), kind=kLoop, calls=%fused_computation | loop fusion | flops 12578816 | bytes 49152 | tf_op jit(solution)/shard_map/reduce_sum | solution.py:254
  80.8 0.6 sub.73
  (43 shorter events, 0.2 us)
Async XLA Ops:
  0.6 75.4 %copy-start = (s32[4,32768]{1,0:T(4,128)S(1)}, s32[4,32768]{1,0:T(4,128)}, u32[]{:S(2)}) copy-start(s32[4,32768]{1,0:T(4,128)} %param.18) | copy-start | bytes 1572868
  0.6 6.4 %copy-start.2 = (f32[38,128,128]{2,1,0:T(8,128)S(1)}, f32[38,128,128]{2,1,0:T(8,128)}, u32[]{:S(2)}) copy-start(f32[38,128,128]{2,1,0:T(8,128)} %field_ref.1) | copy-start | bytes 7471108
  3.4 12.8 %collective-permute-start = (f32[39,3,128]{2,1,0:T(4,128)}, f32[39,3,128]{2,1,0:T(4,128)S(1)}, u32[]{:S(2)}, u32[]{:S(2)}) collective-permute-start(f32[39,3,128]{2,1,0:T(4,128)} %get-tuple-element.9), channel_id=1, source_target_pairs={{0,4},{4,8},{8,12},{12,16},{16,20},{20,24},{24,28},{1,5},{5,9},{9,... | collective-permute-start | bytes 179720 | tf_op jit(solution)/shard_map/ppermute | solution.py:28
  5.7 10.5 %collective-permute-start.1 = (f32[39,3,128]{2,1,0:T(4,128)S(1)}, f32[39,3,128]{2,1,0:T(4,128)S(1)}, u32[]{:S(2)}, u32[]{:S(2)}) collective-permute-start(f32[39,3,128]{2,1,0:T(4,128)S(1)} %get-tuple-element.8), channel_id=1, source_target_pairs={{4,0},{8,4},{12,8},{16,12},{20,16},{24,20},{28,24},{5,1},{9,5},{13... | collective-permute-start | bytes 179720 | tf_op jit(solution)/shard_map/ppermute | solution.py:28
  7.0 8.8 %copy-start.9 = (f32[128,128]{1,0:T(8,128)S(1)}, f32[128,128]{1,0:T(8,128)}, u32[]{:S(2)}) copy-start(f32[128,128]{1,0:T(8,128)} %param.12) | copy-start | bytes 196612
  7.0 8.8 %copy-start.13 = (s32[64,1]{0,1:T(1,128)S(1)}, s32[64,1]{0,1:T(1,128)}, u32[]{:S(2)}) copy-start(s32[64,1]{0,1:T(1,128)} %param.15) | copy-start | bytes 772
  8.3 7.9 %collective-permute-start.2 = (f32[39,3,128]{2,1,0:T(4,128)S(1)}, f32[39,3,128]{2,1,0:T(4,128)S(1)}, u32[]{:S(2)}, u32[]{:S(2)}) collective-permute-start(f32[39,3,128]{2,1,0:T(4,128)S(1)} %fusion.27), channel_id=1, source_target_pairs={{0,1},{1,2},{2,3},{4,5},{5,6},{6,7},{8,9},{9,10},{10,11},{12,13},{... | collective-permute-start | bytes 179720 | tf_op jit(solution)/shard_map/ppermute | solution.py:133
  14.6 6.5 %collective-permute-start.3 = (f32[39,3,128]{2,1,0:T(4,128)}, f32[39,3,128]{2,1,0:T(4,128)S(1)}, u32[]{:S(2)}, u32[]{:S(2)}) collective-permute-start(f32[39,3,128]{2,1,0:T(4,128)} %fusion.28), channel_id=1, source_target_pairs={{1,0},{2,1},{3,2},{5,4},{6,5},{7,6},{9,8},{10,9},{11,10},{13,12},{... | collective-permute-start | bytes 179720 | tf_op jit(solution)/shard_map/ppermute | solution.py:134
  16.1 25.3 %copy-start.7 = (f32[38,38]{1,0:T(8,128)S(1)}, f32[38,38]{1,0:T(8,128)}, u32[]{:S(2)}) copy-start(f32[38,38]{1,0:T(8,128)} %param.13) | copy-start | bytes 17332
  16.2 4.9 %copy-start.3 = (f32[39,3,128]{2,1,0:T(4,128)}, f32[39,3,128]{2,1,0:T(4,128)S(1)}, u32[]{:S(2)}) copy-start(f32[39,3,128]{2,1,0:T(4,128)S(1)} %collective-permute-done.top_ref.top_speed_ref) | copy-start | bytes 179716
  16.2 4.9 %copy-start.4 = (f32[39,3,128]{2,1,0:T(4,128)}, f32[39,3,128]{2,1,0:T(4,128)S(1)}, u32[]{:S(2)}) copy-start(f32[39,3,128]{2,1,0:T(4,128)S(1)} %collective-permute-done.1.bottom_ref.bottom_speed_ref) | copy-start | bytes 179716
  16.2 4.9 %copy-start.5 = (f32[39,3,128]{2,1,0:T(4,128)}, f32[39,3,128]{2,1,0:T(4,128)S(1)}, u32[]{:S(2)}) copy-start(f32[39,3,128]{2,1,0:T(4,128)S(1)} %collective-permute-done.2.left_ref.left_speed_ref) | copy-start | bytes 179716
  21.1 0.6 copy-start.6
  41.5 3.2 %copy-start.1 = (f32[128,38,128]{2,1,0:T(8,128)S(1)}, f32[128,38,128]{2,1,0:T(8,128)}, u32[]{:S(2)}) copy-start(f32[128,38,128]{2,1,0:T(8,128)} %shard_map.113) | copy-start | bytes 7471108
  41.5 3.2 %copy-start.8 = (f32[38,38]{1,0:T(8,128)S(1)}, f32[38,38]{1,0:T(8,128)}, u32[]{:S(2)}) copy-start(f32[38,38]{1,0:T(8,128)} %param.14) | copy-start | bytes 17332
  52.7 3.3 %copy-start.11 = (f32[4,38]{1,0:T(4,128)S(1)}, f32[4,38]{1,0:T(4,128)}, u32[]{:S(2)}) copy-start(f32[4,38]{1,0:T(4,128)} %param.16) | copy-start | bytes 1828
  56.0 1.7 %copy-start.12 = (f32[128]{0:T(128)S(1)}, f32[128]{0:T(128)}, u32[]{:S(2)}) copy-start(f32[128]{0:T(128)} %param.17) | copy-start | bytes 1540
  58.0 3.7 %collective-permute-start.4 = (f32[4,128]{1,0:T(4,128)S(1)}, f32[4,128]{1,0:T(4,128)S(1)}, u32[]{:S(2)}, u32[]{:S(2)}) collective-permute-start(f32[4,128]{1,0:T(4,128)S(1)} %broadcast_multiply_fusion), channel_id=1, source_target_pairs={{0,1},{1,0},{2,3},{3,2},{4,5},{5,4},{6,7},{7,6},{8,9},{9,8},{10,11... | collective-permute-start | bytes 6152 | tf_op jit(solution)/shard_map/ppermute | solution.py:189
  61.7 4.5 %collective-permute-start.5 = (f32[4,128]{1,0:T(4,128)S(1)}, f32[4,128]{1,0:T(4,128)S(1)}, u32[]{:S(2)}, u32[]{:S(2)}) collective-permute-start(f32[4,128]{1,0:T(4,128)S(1)} %fusion.50), channel_id=1, source_target_pairs={{0,2},{1,3},{2,0},{3,1},{4,6},{5,7},{6,4},{7,5},{8,10},{9,11},{10,... | collective-permute-start | bytes 6152 | tf_op jit(solution)/shard_map/ppermute | solution.py:189
  66.1 1.2 %collective-permute-start.6 = (f32[1,4,128]{2,0,1:T(1,128)S(1)}, f32[1,4,128]{2,0,1:T(1,128)S(1)}, u32[]{:S(2)}, u32[]{:S(2)}) collective-permute-start(f32[1,4,128]{2,0,1:T(1,128)S(1)} %bitcast.117), channel_id=1, source_target_pairs={{0,4},{4,0},{8,12},{12,8},{16,20},{20,16},{24,28},{28,24},{1,5},{5... | collective-permute-start | bytes 6152 | tf_op jit(solution)/shard_map/ppermute | solution.py:202
  67.3 5.6 %collective-permute-start.7 = (f32[2,4,128]{2,0,1:T(2,128)S(1)}, f32[2,4,128]{2,0,1:T(2,128)S(1)}, u32[]{:S(2)}, u32[]{:S(2)}) collective-permute-start(f32[2,4,128]{2,0,1:T(2,128)S(1)} %maximum_select_fusion.2), channel_id=1, source_target_pairs={{0,8},{4,12},{8,0},{12,4},{16,24},{20,28},{24,16},{28,20},{1,9},{5... | collective-permute-start | bytes 12296 | tf_op jit(solution)/shard_map/ppermute | solution.py:202
  73.0 4.9 %collective-permute-start.8 = (f32[4,4,128]{2,0,1:T(4,128)S(1)}, f32[4,4,128]{2,0,1:T(4,128)S(1)}, u32[]{:S(2)}, u32[]{:S(2)}) collective-permute-start(f32[4,4,128]{2,0,1:T(4,128)S(1)} %maximum_select_fusion.1), channel_id=1, source_target_pairs={{0,16},{4,20},{8,24},{12,28},{16,0},{20,4},{24,8},{28,12},{1,17},{... | collective-permute-start | bytes 24584 | tf_op jit(solution)/shard_map/ppermute | solution.py:202
  76.0 4.8 %copy-start.10 = (f32[4,1024]{1,0:T(4,128)S(1)}, f32[4,1024]{1,0:T(4,128)}, u32[]{:S(2)}) copy-start(f32[4,1024]{1,0:T(4,128)} %param.19) | copy-start | bytes 49156

commit v7 on v6

--- a/solution.py
+++ b/solution.py
@@ -113,12 +113,13 @@
     scratch[pl.ds(HALO + rows, width), :] = after
 
 
-def edge_columns(field, start, width):
+def edge_columns(field, width):
     cols = field.shape[2]
-    pick = lax.broadcasted_iota(jnp.int32, (width, cols), 1) == (
-        lax.broadcasted_iota(jnp.int32, (width, cols), 0) + start
-    )
-    return jnp.einsum("kr,sar->ska", pick.astype(field.dtype), field, precision=HIGHEST)
+    row = lax.broadcasted_iota(jnp.int32, (2 * width, cols), 0)
+    column = lax.broadcasted_iota(jnp.int32, (2 * width, cols), 1)
+    pick = column == jnp.where(row < width, row + cols - width, row - width)
+    picked = jnp.einsum("kr,sar->ska", pick.astype(field.dtype), field, precision=HIGHEST)
+    return picked[:, :width], picked[:, width:]
 
 
 def transport(species, speed, width=3):
@@ -130,8 +131,9 @@
     peers = lax.axis_size("radial")
     up = [(i, i + 1) for i in range(peers - 1)]
     down = [(j, i) for i, j in up]
-    left = lax.ppermute(edge_columns(radial_edges, cols - width, width), "radial", up)
-    right = lax.ppermute(edge_columns(radial_edges, 0, width), "radial", down)
+    high_columns, low_columns = edge_columns(radial_edges, width)
+    left = lax.ppermute(high_columns, "radial", up)
+    right = lax.ppermute(low_columns, "radial", down)
     faces = rows + CHUNK
     span = HALO + faces + HALO
     group = max(g for g in range(1, SPECIES_GROUP + 1) if species_count % g == 0)

time: 81.6 us -> 78 us (0.956)
  waiting for transfers between devices: 11.5 us -> 8.63 us
  other arithmetic: 5.17 us -> 4.18 us
    ppermute x2, waiting for transfers between devices: 4.85 us -> 1.25 us  [the longest x1 1.25 us: transport(): right = lax.ppermute(low_columns, 'radial', down)]
    ppermute x2, waiting for transfers between devices: 0.01 us -> 1.84 us  [edge_layers(): return (lax.ppermute(last, axis, up), lax.ppermute(initial, axis, down))]
    ppermute x2, starting transfers between devices: 4.22 us -> 5.74 us  [butterfly_sum(): part = part + lax.ppermute(part, axis, pairs)]
    concatenate x1, other arithmetic: 1.66 us -> 0.66 us  [transport(): axial_edges = jnp.concatenate([species, speed[0:1]], axis=0)]
    ppermute x2, starting transfers between devices: 3.64 us -> 2.74 us  [edge_layers(): return (lax.ppermute(last, axis, up), lax.ppermute(initial, axis, down))]
    dot_general x2 -> x1, matrix products: 3.17 us -> 2.98 us  [edge_columns(): jnp.einsum('kr,sar->ska', pick.astype(field.dtype), field, precision=HIGH...]
  transfers between devices with their start and end apart: 9 -> 9, of which waited for: 5 -> 6; matrix products, arithmetic and copies ran while one was open for 7% -> 4% of each run, Pallas kernels for 0% -> 0%
where the time goes in v7:
time: 78 us; the launch traced here: 77.8 us
  starting transfers between devices  21 us (27%)
  Pallas kernels  19.8 us (25%)
  matrix products  19.3 us (25%)
  waiting for transfers between devices  8.63 us (11%)
  other arithmetic  4.18 us (5%)
  local copies, waits for them, and re-layouts  3.91 us (5%)
  between operations  0.95 us (1%)
    pallas_call x1, Pallas kernels, transport(): pl.pallas_call(transport_kernel, grid=(species_count // group,), in_specs...  19.8 us
    dot_general x3, matrix products, kinetics_advance(): jnp.tensordot(frozen_jacobian_inverse_addend, defect, axes=(1, 0), precis...  8.57 us
    ppermute x3, starting transfers between devices, doubling_gather(): other = lax.ppermute(blocks, axis, pairs)  6.31 us
    dot_general x3, matrix products, kinetics_advance(): jnp.tensordot(linearized_kinetics_operator, current, axes=(1, 0), precisi...  5.81 us
    ppermute x2, starting transfers between devices, butterfly_sum(): part = part + lax.ppermute(part, axis, pairs)  5.74 us
    ppermute x1, starting transfers between devices, transport(): left = lax.ppermute(high_columns, 'radial', up)  4.93 us
    ppermute x2, waiting for transfers between devices, butterfly_sum(): part = part + lax.ppermute(part, axis, pairs)  3.13 us
    dot_general x1, matrix products, edge_columns(): jnp.einsum('kr,sar->ska', pick.astype(field.dtype), field, precision=HIGH...  2.98 us
  transfers between devices with their start and end apart: 9, of which 6 were waited for; matrix products, arithmetic and copies ran while one was open for 4% of the time, Pallas kernels for 0%

profile of v7, /device:TPU:0, one launch (start us, length us, event | category | flops | bytes accessed | tf_op | source)
XLA Modules:
  0.0 77.8 jit_solution(10960601055077758993)
XLA Ops:
  0.7 1.0 %fusion.54 = (f32[1,128,128]{2,1,0:T(8,128)S(1)}, f32[1,128,128]{2,1,0:T(8,128)S(1)}) fusion(f32[2,128,128]{2,1,0:T(8,128)} %speed_ref.1), kind=kLoop, calls=%fused_computation.70 | loop fusion | bytes 262144 | tf_op jit(solution)/shard_map/slice | solution.py:130
  1.7 3.0 %fusion.29 = f32[39,6,128]{2,1,0:T(8,128)S(1)} fusion(f32[1,128,128]{2,1,0:T(8,128)S(1)} %get-tuple-element.12, f32[38,128,128]{2,1,0:T(8,128)} %field_ref.1, s32[6]{0:T(128)S(1)} %get-tuple-element.14, s32[6]{0:T(128)S(1)} %get-tuple-element.15, pred[6]{0:T(512)(128)(4,1)S(1)} %iota_compare_fusion.1), kind=kOutput, calls=%fused_computation.35 | convolution fusion | flops 46646784 | bytes 2675766 | tf_op jit(solution)/shard_map/kr,sar->ska/dot_general | solution.py:121
  4.8 4.9 %collective-permute-start.2 = (f32[39,3,128]{2,1,0:T(4,128)S(1)}, f32[39,3,128]{2,1,0:T(4,128)S(1)}, u32[]{:S(2)}, u32[]{:S(2)}) collective-permute-start(f32[39,3,128]{2,1,0:T(4,128)S(1)} %get-tuple-element.11), channel_id=1, source_target_pairs={{0,1},{1,2},{2,3},{4,5},{5,6},{6,7},{8,9},{9,10},{10,11},{12,13},{... | collective-permute-start | bytes 179720 | tf_op jit(solution)/shard_map/ppermute | solution.py:135
  9.7 1.3 %collective-permute-start.3 = (f32[39,3,128]{2,1,0:T(4,128)S(1)}, f32[39,3,128]{2,1,0:T(4,128)S(1)}, u32[]{:S(2)}, u32[]{:S(2)}) collective-permute-start(f32[39,3,128]{2,1,0:T(4,128)S(1)} %get-tuple-element.10), channel_id=1, source_target_pairs={{1,0},{2,1},{3,2},{5,4},{6,5},{7,6},{9,8},{10,9},{11,10},{13,12},{... | collective-permute-start | bytes 179720 | tf_op jit(solution)/shard_map/ppermute | solution.py:136
  11.0 0.7 pad_maximum_fusion
  11.7 1.5 %collective-permute-start = (f32[39,3,128]{2,1,0:T(4,128)}, f32[39,3,128]{2,1,0:T(4,128)S(1)}, u32[]{:S(2)}, u32[]{:S(2)}) collective-permute-start(f32[39,3,128]{2,1,0:T(4,128)} %get-tuple-element.9), channel_id=1, source_target_pairs={{0,4},{4,8},{8,12},{12,16},{16,20},{20,24},{24,28},{1,5},{5,9},{9,... | collective-permute-start | bytes 179720 | tf_op jit(solution)/shard_map/ppermute | solution.py:28
  13.1 1.3 %collective-permute-start.1 = (f32[39,3,128]{2,1,0:T(4,128)S(1)}, f32[39,3,128]{2,1,0:T(4,128)S(1)}, u32[]{:S(2)}, u32[]{:S(2)}) collective-permute-start(f32[39,3,128]{2,1,0:T(4,128)S(1)} %get-tuple-element.8), channel_id=1, source_target_pairs={{4,0},{8,4},{12,8},{16,12},{20,16},{24,20},{28,24},{5,1},{9,5},{13... | collective-permute-start | bytes 179720 | tf_op jit(solution)/shard_map/ppermute | solution.py:28
  14.6 0.2 gt.22
  14.8 1.3 %collective-permute-done.3.right_ref.right_speed_ref = f32[39,3,128]{2,1,0:T(4,128)S(1)} collective-permute-done((f32[39,3,128]{2,1,0:T(4,128)S(1)}, f32[39,3,128]{2,1,0:T(4,128)S(1)}, u32[]{:S(2)}, u32[]{:S(2)}) %collective-permute-start.3) | collective-permute-done | bytes 59936 | tf_op jit(solution)/shard_map/ppermute | solution.py:136
  16.0 1.8 %collective-permute-done.1.bottom_ref.bottom_speed_ref = f32[39,3,128]{2,1,0:T(4,128)S(1)} collective-permute-done((f32[39,3,128]{2,1,0:T(4,128)S(1)}, f32[39,3,128]{2,1,0:T(4,128)S(1)}, u32[]{:S(2)}, u32[]{:S(2)}) %collective-permute-start.1) | collective-permute-done | bytes 59936 | tf_op jit(solution)/shard_map/ppermute | solution.py:28
  17.9 0.6 copy-done.6
  18.5 19.8 %shard_map.113 = f32[128,38,128]{2,1,0:T(8,128)} custom-call(f32[38,128,128]{2,1,0:T(8,128)} %field_ref.1, f32[2,128,128]{2,1,0:T(8,128)} %speed_ref.1, f32[39,3,128]{2,1,0:T(4,128)} %copy-done.5, f32[39,3,128]{2,1,0:T(4,128)} %copy-done.5, f32[39,3,128]{2,1,0:T(4,128)} %copy-done.6, f32[39,3,128]{2,1,0:T(4,128)} %copy-done.6, f32[39,3,128]{2,1,0:T(4,128)} %copy-done.3, ...), custom_call_target="tpu_custom_call" | custom-call | tf_op jit(solution)/shard_map/pallas_call | solution.py:144
  38.3 3.2 %fusion.13 = f32[128,128,38]{1,2,0:T(8,128)S(1)} fusion(f32[128,38,128]{2,1,0:T(8,128)} %shard_map.113, f32[38,38]{1,0:T(8,128)S(1)} %copy-done.7), kind=kOutput, calls=%fused_computation.22 | convolution fusion | flops 141950976 | bytes 4986512 | tf_op jit(solution)/shard_map/dot_general | solution.py:168
  41.5 2.5 %bitcast_subtract_fusion.4 = f32[38,128,128]{2,0,1:T(8,128)S(1)} fusion(f32[128,128,38]{1,2,0:T(8,128)S(1)} %fusion.13, f32[128,38,128]{2,1,0:T(8,128)S(1)} %copy-done.1, f32[128,128]{1,0:T(8,128)S(1)} %exponential_multiply_fusion, f32[38,38]{1,0:T(8,128)S(1)} %copy-done.8), kind=kOutput, calls=%fused_computation.11 | convolution fusion | flops 148176896 | bytes 7542416 | tf_op jit(solution)/shard_map/dot_general | solution.py:175
  44.1 1.3 %fusion.40 = f32[128,128,38]{1,2,0:T(8,128)S(1)} fusion(f32[38,128,128]{2,0,1:T(8,128)S(1)} %bitcast_subtract_fusion.4, f32[38,38]{1,0:T(8,128)S(1)} %copy-done.7), kind=kOutput, calls=%fused_computation.46 | convolution fusion | flops 141950976 | bytes 4986512 | tf_op jit(solution)/shard_map/dot_general | solution.py:168
  45.4 2.8 %bitcast_subtract_fusion.2 = f32[38,128,128]{2,0,1:T(8,128)S(1)} fusion(f32[38,128,128]{2,0,1:T(8,128)S(1)} %bitcast_subtract_fusion.4, f32[128,128,38]{1,2,0:T(8,128)S(1)} %fusion.40, f32[128,38,128]{2,1,0:T(8,128)S(1)} %copy-done.1, f32[128,128]{1,0:T(8,128)S(1)} %exponential_multiply_fusion, f32[38,38]{1,0:T(8,128)S(1)} %copy-done.8), kind=kOutput, calls=%fused_computation.7 | convolution fusion | flops 148176896 | bytes 10032784 | tf_op jit(solution)/shard_map/dot_general | solution.py:175
  48.2 1.3 %fusion.38 = f32[128,128,38]{1,2,0:T(8,128)S(1)} fusion(f32[38,128,128]{2,0,1:T(8,128)S(1)} %bitcast_subtract_fusion.2, f32[38,38]{1,0:T(8,128)S(1)} %copy-done.7), kind=kOutput, calls=%fused_computation.44 | convolution fusion | flops 141950976 | bytes 4986512 | tf_op jit(solution)/shard_map/dot_general | solution.py:168
  49.5 3.2 %fusion = f32[38,128,128]{2,0,1:T(8,128)S(1)} fusion(f32[128,38,128]{2,1,0:T(8,128)S(1)} %copy-done.1, f32[38,128,128]{2,0,1:T(8,128)S(1)} %bitcast_subtract_fusion.2, f32[128,128,38]{1,2,0:T(8,128)S(1)} %fusion.38, f32[128,128]{1,0:T(8,128)S(1)} %exponential_multiply_fusion, pred[128]{0:T(512)(128)(4,1)S(1)} %gt.22, f32[38,38]{1,0:T(8,128)S(1)} %copy-done.8), kind=kOutput, calls=%fused_computation.3 | convolution fusion | flops 148799488 | bytes 10032912 | tf_op jit(solution)/shard_map/dot_general | solution.py:175
  52.8 1.7 %convolution_bitcast_fusion = f32[4,128,128]{2,0,1:T(4,128)S(1)} fusion(f32[38,128,128]{2,0,1:T(8,128)S(1)} %fusion, f32[4,38]{1,0:T(4,128)S(1)} %copy-done.11), kind=kOutput, calls=%fused_computation.34 | convolution fusion | flops 29884416 | bytes 2753120 | tf_op jit(solution)/shard_map/dot_general | solution.py:181
  54.5 0.3 fusion.32
  54.8 2.7 %collective-permute-start.4 = (f32[4,128]{1,0:T(4,128)S(1)}, f32[4,128]{1,0:T(4,128)S(1)}, u32[]{:S(2)}, u32[]{:S(2)}) collective-permute-start(f32[4,128]{1,0:T(4,128)S(1)} %broadcast_multiply_fusion), channel_id=1, source_target_pairs={{0,1},{1,0},{2,3},{3,2},{4,5},{5,4},{6,7},{7,6},{8,9},{9,8},{10,11... | collective-permute-start | bytes 6152 | tf_op jit(solution)/shard_map/ppermute | solution.py:191
  57.5 1.6 %collective-permute-done.4 = f32[4,128]{1,0:T(4,128)S(1)} collective-permute-done((f32[4,128]{1,0:T(4,128)S(1)}, f32[4,128]{1,0:T(4,128)S(1)}, u32[]{:S(2)}, u32[]{:S(2)}) %collective-permute-start.4) | collective-permute-done | bytes 2080 | tf_op jit(solution)/shard_map/ppermute | solution.py:191
  59.1 3.0 %collective-permute-start.5 = (f32[4,128]{1,0:T(4,128)S(1)}, f32[4,128]{1,0:T(4,128)S(1)}, u32[]{:S(2)}, u32[]{:S(2)}) collective-permute-start(f32[4,128]{1,0:T(4,128)S(1)} %fusion.52), channel_id=1, source_target_pairs={{0,2},{1,3},{2,0},{3,1},{4,6},{5,7},{6,4},{7,5},{8,10},{9,11},{10,... | collective-permute-start | bytes 6152 | tf_op jit(solution)/shard_map/ppermute | solution.py:191
  62.1 1.6 %collective-permute-done.5 = f32[4,128]{1,0:T(4,128)S(1)} collective-permute-done((f32[4,128]{1,0:T(4,128)S(1)}, f32[4,128]{1,0:T(4,128)S(1)}, u32[]{:S(2)}, u32[]{:S(2)}) %collective-permute-start.5) | collective-permute-done | bytes 2080 | tf_op jit(solution)/shard_map/ppermute | solution.py:191
  63.7 1.0 %collective-permute-start.6 = (f32[1,4,128]{2,0,1:T(1,128)S(1)}, f32[1,4,128]{2,0,1:T(1,128)S(1)}, u32[]{:S(2)}, u32[]{:S(2)}) collective-permute-start(f32[1,4,128]{2,0,1:T(1,128)S(1)} %bitcast.112), channel_id=1, source_target_pairs={{0,4},{4,0},{8,12},{12,8},{16,20},{20,16},{24,28},{28,24},{1,5},{5... | collective-permute-start | bytes 6152 | tf_op jit(solution)/shard_map/ppermute | solution.py:204
  64.7 0.8 %collective-permute-done.6 = f32[1,4,128]{2,0,1:T(1,128)S(1)} collective-permute-done((f32[1,4,128]{2,0,1:T(1,128)S(1)}, f32[1,4,128]{2,0,1:T(1,128)S(1)}, u32[]{:S(2)}, u32[]{:S(2)}) %collective-permute-start.6) | collective-permute-done | bytes 2080 | tf_op jit(solution)/shard_map/ppermute | solution.py:204
  65.6 2.5 %collective-permute-start.7 = (f32[2,4,128]{2,0,1:T(2,128)S(1)}, f32[2,4,128]{2,0,1:T(2,128)S(1)}, u32[]{:S(2)}, u32[]{:S(2)}) collective-permute-start(f32[2,4,128]{2,0,1:T(2,128)S(1)} %maximum_select_fusion.2), channel_id=1, source_target_pairs={{0,8},{4,12},{8,0},{12,4},{16,24},{20,28},{24,16},{28,20},{1,9},{5... | collective-permute-start | bytes 12296 | tf_op jit(solution)/shard_map/ppermute | solution.py:204
  68.0 1.6 %collective-permute-done.7 = f32[2,4,128]{2,0,1:T(2,128)S(1)} collective-permute-done((f32[2,4,128]{2,0,1:T(2,128)S(1)}, f32[2,4,128]{2,0,1:T(2,128)S(1)}, u32[]{:S(2)}, u32[]{:S(2)}) %collective-permute-start.7) | collective-permute-done | bytes 4128 | tf_op jit(solution)/shard_map/ppermute | solution.py:204
  69.6 2.8 %collective-permute-start.8 = (f32[4,4,128]{2,0,1:T(4,128)S(1)}, f32[4,4,128]{2,0,1:T(4,128)S(1)}, u32[]{:S(2)}, u32[]{:S(2)}) collective-permute-start(f32[4,4,128]{2,0,1:T(4,128)S(1)} %maximum_select_fusion.1), channel_id=1, source_target_pairs={{0,16},{4,20},{8,24},{12,28},{16,0},{20,4},{24,8},{28,12},{1,17},{... | collective-permute-start | bytes 24584 | tf_op jit(solution)/shard_map/ppermute | solution.py:204
  72.4 1.9 %copy.14 = f32[38,128,128]{2,1,0:T(8,128)} copy(f32[38,128,128]{2,0,1:T(8,128)S(1)} %fusion) | data formatting | bytes 4980736
  74.4 2.8 %select_reduce_fusion = f32[4,1024]{1,0:T(4,128)S(1)} fusion(f32[4,1024]{1,0:T(4,128)S(1)} %bitcast.109, s32[4,1024]{1,0:T(4,128)S(1)} %constant_dynamic-slice_fusion), kind=kLoop, calls=%fused_computation | loop fusion | flops 12578816 | bytes 49152 | tf_op jit(solution)/shard_map/reduce_sum | solution.py:256
  77.2 0.6 sub.86
  (44 shorter events, 0.3 us)
Async XLA Ops:
  0.6 71.8 %copy-start = (s32[4,32768]{1,0:T(4,128)S(1)}, s32[4,32768]{1,0:T(4,128)}, u32[]{:S(2)}) copy-start(s32[4,32768]{1,0:T(4,128)} %param.18) | copy-start | bytes 1572868
  0.6 10.4 %copy-start.2 = (f32[38,128,128]{2,1,0:T(8,128)S(1)}, f32[38,128,128]{2,1,0:T(8,128)}, u32[]{:S(2)}) copy-start(f32[38,128,128]{2,1,0:T(8,128)} %field_ref.1) | copy-start | bytes 7471108
  1.7 12.7 %copy-start.9 = (f32[128,128]{1,0:T(8,128)S(1)}, f32[128,128]{1,0:T(8,128)}, u32[]{:S(2)}) copy-start(f32[128,128]{1,0:T(8,128)} %param.12) | copy-start | bytes 196612
  1.7 12.8 %copy-start.13 = (s32[64,1]{0,1:T(1,128)S(1)}, s32[64,1]{0,1:T(1,128)}, u32[]{:S(2)}) copy-start(s32[64,1]{0,1:T(1,128)} %param.15) | copy-start | bytes 772
  4.8 10.0 %collective-permute-start.2 = (f32[39,3,128]{2,1,0:T(4,128)S(1)}, f32[39,3,128]{2,1,0:T(4,128)S(1)}, u32[]{:S(2)}, u32[]{:S(2)}) collective-permute-start(f32[39,3,128]{2,1,0:T(4,128)S(1)} %get-tuple-element.11), channel_id=1, source_target_pairs={{0,1},{1,2},{2,3},{4,5},{5,6},{6,7},{8,9},{9,10},{10,11},{12,13},{... | collective-permute-start | bytes 179720 | tf_op jit(solution)/shard_map/ppermute | solution.py:135
  9.7 6.3 %collective-permute-start.3 = (f32[39,3,128]{2,1,0:T(4,128)S(1)}, f32[39,3,128]{2,1,0:T(4,128)S(1)}, u32[]{:S(2)}, u32[]{:S(2)}) collective-permute-start(f32[39,3,128]{2,1,0:T(4,128)S(1)} %get-tuple-element.10), channel_id=1, source_target_pairs={{1,0},{2,1},{3,2},{5,4},{6,5},{7,6},{9,8},{10,9},{11,10},{13,12},{... | collective-permute-start | bytes 179720 | tf_op jit(solution)/shard_map/ppermute | solution.py:136
  11.7 4.3 %collective-permute-start = (f32[39,3,128]{2,1,0:T(4,128)}, f32[39,3,128]{2,1,0:T(4,128)S(1)}, u32[]{:S(2)}, u32[]{:S(2)}) collective-permute-start(f32[39,3,128]{2,1,0:T(4,128)} %get-tuple-element.9), channel_id=1, source_target_pairs={{0,4},{4,8},{8,12},{12,16},{16,20},{20,24},{24,28},{1,5},{5,9},{9,... | collective-permute-start | bytes 179720 | tf_op jit(solution)/shard_map/ppermute | solution.py:28
  13.1 4.7 %collective-permute-start.1 = (f32[39,3,128]{2,1,0:T(4,128)S(1)}, f32[39,3,128]{2,1,0:T(4,128)S(1)}, u32[]{:S(2)}, u32[]{:S(2)}) collective-permute-start(f32[39,3,128]{2,1,0:T(4,128)S(1)} %get-tuple-element.8), channel_id=1, source_target_pairs={{4,0},{8,4},{12,8},{16,12},{20,16},{24,20},{28,24},{5,1},{9,5},{13... | collective-permute-start | bytes 179720 | tf_op jit(solution)/shard_map/ppermute | solution.py:28
  14.7 23.6 %copy-start.7 = (f32[38,38]{1,0:T(8,128)S(1)}, f32[38,38]{1,0:T(8,128)}, u32[]{:S(2)}) copy-start(f32[38,38]{1,0:T(8,128)} %param.13) | copy-start | bytes 17332
  14.8 3.1 %copy-start.3 = (f32[39,3,128]{2,1,0:T(4,128)}, f32[39,3,128]{2,1,0:T(4,128)S(1)}, u32[]{:S(2)}) copy-start(f32[39,3,128]{2,1,0:T(4,128)S(1)} %collective-permute-done.2.left_ref.left_speed_ref) | copy-start | bytes 179716
  16.0 1.8 %copy-start.4 = (f32[39,3,128]{2,1,0:T(4,128)}, f32[39,3,128]{2,1,0:T(4,128)S(1)}, u32[]{:S(2)}) copy-start(f32[39,3,128]{2,1,0:T(4,128)S(1)} %collective-permute-done.3.right_ref.right_speed_ref) | copy-start | bytes 179716
  16.0 1.8 %copy-start.5 = (f32[39,3,128]{2,1,0:T(4,128)}, f32[39,3,128]{2,1,0:T(4,128)S(1)}, u32[]{:S(2)}) copy-start(f32[39,3,128]{2,1,0:T(4,128)S(1)} %collective-permute-done.top_ref.top_speed_ref) | copy-start | bytes 179716
  17.9 0.6 copy-start.6
  38.3 3.2 %copy-start.1 = (f32[128,38,128]{2,1,0:T(8,128)S(1)}, f32[128,38,128]{2,1,0:T(8,128)}, u32[]{:S(2)}) copy-start(f32[128,38,128]{2,1,0:T(8,128)} %shard_map.113) | copy-start | bytes 7471108
  38.3 3.2 %copy-start.8 = (f32[38,38]{1,0:T(8,128)S(1)}, f32[38,38]{1,0:T(8,128)}, u32[]{:S(2)}) copy-start(f32[38,38]{1,0:T(8,128)} %param.14) | copy-start | bytes 17332
  49.5 3.3 %copy-start.11 = (f32[4,38]{1,0:T(4,128)S(1)}, f32[4,38]{1,0:T(4,128)}, u32[]{:S(2)}) copy-start(f32[4,38]{1,0:T(4,128)} %param.16) | copy-start | bytes 1828
  52.8 1.7 %copy-start.12 = (f32[128]{0:T(128)S(1)}, f32[128]{0:T(128)}, u32[]{:S(2)}) copy-start(f32[128]{0:T(128)} %param.17) | copy-start | bytes 1540
  54.8 4.3 %collective-permute-start.4 = (f32[4,128]{1,0:T(4,128)S(1)}, f32[4,128]{1,0:T(4,128)S(1)}, u32[]{:S(2)}, u32[]{:S(2)}) collective-permute-start(f32[4,128]{1,0:T(4,128)S(1)} %broadcast_multiply_fusion), channel_id=1, source_target_pairs={{0,1},{1,0},{2,3},{3,2},{4,5},{5,4},{6,7},{7,6},{8,9},{9,8},{10,11... | collective-permute-start | bytes 6152 | tf_op jit(solution)/shard_map/ppermute | solution.py:191
  59.1 4.6 %collective-permute-start.5 = (f32[4,128]{1,0:T(4,128)S(1)}, f32[4,128]{1,0:T(4,128)S(1)}, u32[]{:S(2)}, u32[]{:S(2)}) collective-permute-start(f32[4,128]{1,0:T(4,128)S(1)} %fusion.52), channel_id=1, source_target_pairs={{0,2},{1,3},{2,0},{3,1},{4,6},{5,7},{6,4},{7,5},{8,10},{9,11},{10,... | collective-permute-start | bytes 6152 | tf_op jit(solution)/shard_map/ppermute | solution.py:191
  63.7 1.9 %collective-permute-start.6 = (f32[1,4,128]{2,0,1:T(1,128)S(1)}, f32[1,4,128]{2,0,1:T(1,128)S(1)}, u32[]{:S(2)}, u32[]{:S(2)}) collective-permute-start(f32[1,4,128]{2,0,1:T(1,128)S(1)} %bitcast.112), channel_id=1, source_target_pairs={{0,4},{4,0},{8,12},{12,8},{16,20},{20,16},{24,28},{28,24},{1,5},{5... | collective-permute-start | bytes 6152 | tf_op jit(solution)/shard_map/ppermute | solution.py:204
  65.6 4.0 %collective-permute-start.7 = (f32[2,4,128]{2,0,1:T(2,128)S(1)}, f32[2,4,128]{2,0,1:T(2,128)S(1)}, u32[]{:S(2)}, u32[]{:S(2)}) collective-permute-start(f32[2,4,128]{2,0,1:T(2,128)S(1)} %maximum_select_fusion.2), channel_id=1, source_target_pairs={{0,8},{4,12},{8,0},{12,4},{16,24},{20,28},{24,16},{28,20},{1,9},{5... | collective-permute-start | bytes 12296 | tf_op jit(solution)/shard_map/ppermute | solution.py:204
  69.6 4.7 %collective-permute-start.8 = (f32[4,4,128]{2,0,1:T(4,128)S(1)}, f32[4,4,128]{2,0,1:T(4,128)S(1)}, u32[]{:S(2)}, u32[]{:S(2)}) collective-permute-start(f32[4,4,128]{2,0,1:T(4,128)S(1)} %maximum_select_fusion.1), channel_id=1, source_target_pairs={{0,16},{4,20},{8,24},{12,28},{16,0},{20,4},{24,8},{28,12},{1,17},{... | collective-permute-start | bytes 24584 | tf_op jit(solution)/shard_map/ppermute | solution.py:204
  72.4 4.8 %copy-start.10 = (f32[4,1024]{1,0:T(4,128)S(1)}, f32[4,1024]{1,0:T(4,128)}, u32[]{:S(2)}) copy-start(f32[4,1024]{1,0:T(4,128)} %param.19) | copy-start | bytes 49156

commit v8 on v7

--- a/solution.py
+++ b/solution.py
@@ -193,25 +193,33 @@
     return part
 
 
-def doubling_gather(part, axis):
+def pick_samples(blocks, first, rows):
+    count, lasers, block = blocks.shape
+    flat = jnp.transpose(blocks, (1, 0, 2)).reshape(lasers, count * block)
+    local = rows - first * block
+    cells = lax.broadcasted_iota(jnp.int32, (1, count * block, 1), 1)
+    return jnp.sum(jnp.where(local[:, None, :] == cells, flat[:, :, None], 0.0), axis=1)
+
+
+def sampled_profile(part, rows, axis="axial"):
+    column = butterfly_sum(part, "radial")
     peers, stride = (lax.axis_size(axis), 1)
     if peers & (peers - 1):
-        return lax.all_gather(part, axis, axis=1, tiled=True)
+        return pick_samples(lax.all_gather(column, axis), 0, rows)
     position = lax.axis_index(axis)
-    blocks = part[None]
+    blocks = column[None]
+    values = pick_samples(blocks, position, rows)
     while stride < peers:
         pairs = [(j, j ^ stride) for j in range(peers)]
         other = lax.ppermute(blocks, axis, pairs)
+        values = values + pick_samples(other, (position // stride) * stride ^ stride, rows)
         upper = (position // stride) % 2 == 1
-        blocks = jnp.where(
-            upper, jnp.concatenate([other, blocks], 0), jnp.concatenate([blocks, other], 0)
-        )
+        if 2 * stride < peers:
+            blocks = jnp.where(
+                upper, jnp.concatenate([other, blocks], 0), jnp.concatenate([blocks, other], 0)
+            )
         stride *= 2
-    return jnp.transpose(blocks, (1, 0, 2)).reshape(part.shape[0], -1)
-
-
-def gathered_profile(profile):
-    return doubling_gather(butterfly_sum(profile, "radial"), "axial")
+    return values
 
 
 def local(
@@ -246,16 +254,12 @@
         absorbance_profile(species_out, molar_absorptivity_table, spokewise_sightline_length)
         * path_scale
     )
-    whole_profile = gathered_profile(profile)
     device = lax.axis_index(("axial", "radial"))
     sample_count = observed_absorbance_traces.shape[1]
     own_rows = lax.dynamic_slice_in_dim(
         sightline_lengthwise_index, device * sample_count, sample_count, 1
     )
-    cells = lax.broadcasted_iota(jnp.int32, (1, whole_profile.shape[1], 1), 1)
-    values = jnp.sum(
-        jnp.where(own_rows[:, None, :] == cells, whole_profile[:, :, None], 0.0), axis=1
-    )
+    values = sampled_profile(profile, own_rows)
     return (species_out, values - observed_absorbance_traces)
 
 

time: 78 us -> 76.9 us (0.986)
  waiting for transfers between devices: 8.63 us -> 7.05 us
    ppermute x2, waiting for transfers between devices: 3.13 us -> 1.57 us  [butterfly_sum(): part = part + lax.ppermute(part, axis, pairs)]
    reduce_sum x1 -> x4, other arithmetic: 2.82 us -> 3.1 us  [pick_samples(): jnp.sum(jnp.where(local[:, None, :] == cells, flat[:, :, None], 0.0), axi...]
    unnamed x30 -> x27, local copies, waits for them, and re-layouts: 2.6 us -> 2.58 us
  transfers between devices with their start and end apart: 9 -> 9, of which waited for: 6 -> 6; matrix products, arithmetic and copies ran while one was open for 4% -> 6% of each run, Pallas kernels for 0% -> 0%
where the time goes in v8:
time: 76.9 us; the launch traced here: 76.6 us
  starting transfers between devices  20.9 us (27%)
  Pallas kernels  19.8 us (26%)
  matrix products  19.5 us (25%)
  waiting for transfers between devices  7.05 us (9%)
  other arithmetic  4.54 us (6%)
  local copies, waits for them, and re-layouts  3.88 us (5%)
  between operations  0.99 us (1%)
    pallas_call x1, Pallas kernels, transport(): pl.pallas_call(transport_kernel, grid=(species_count // group,), in_specs...  19.8 us
    dot_general x3, matrix products, kinetics_advance(): jnp.tensordot(frozen_jacobian_inverse_addend, defect, axes=(1, 0), precis...  8.66 us
    ppermute x3, starting transfers between devices, sampled_profile(): other = lax.ppermute(blocks, axis, pairs)  6.18 us
    dot_general x3, matrix products, kinetics_advance(): jnp.tensordot(linearized_kinetics_operator, current, axes=(1, 0), precisi...  5.81 us
    ppermute x2, starting transfers between devices, butterfly_sum(): part = part + lax.ppermute(part, axis, pairs)  5.74 us
    ppermute x1, starting transfers between devices, transport(): left = lax.ppermute(high_columns, 'radial', up)  4.93 us
    reduce_sum x4, other arithmetic, pick_samples(): jnp.sum(jnp.where(local[:, None, :] == cells, flat[:, :, None], 0.0), axi...  3.1 us
    dot_general x1, matrix products, edge_columns(): jnp.einsum('kr,sar->ska', pick.astype(field.dtype), field, precision=HIGH...  2.98 us
  transfers between devices with their start and end apart: 9, of which 6 were waited for; matrix products, arithmetic and copies ran while one was open for 6% of the time, Pallas kernels for 0%

profile of v8, /device:TPU:0, one launch (start us, length us, event | category | flops | bytes accessed | tf_op | source)
XLA Modules:
  0.0 76.6 jit_solution(7182220514199636494)
XLA Ops:
  0.7 1.0 %fusion.53 = (f32[1,128,128]{2,1,0:T(8,128)S(1)}, f32[1,128,128]{2,1,0:T(8,128)S(1)}) fusion(f32[2,128,128]{2,1,0:T(8,128)} %speed_ref.1), kind=kLoop, calls=%fused_computation.77 | loop fusion | bytes 262144 | tf_op jit(solution)/shard_map/slice | solution.py:130
  1.7 3.0 %fusion.29 = f32[39,6,128]{2,1,0:T(8,128)S(1)} fusion(f32[1,128,128]{2,1,0:T(8,128)S(1)} %get-tuple-element.16, f32[38,128,128]{2,1,0:T(8,128)} %field_ref.1, s32[6]{0:T(128)S(1)} %get-tuple-element.18, s32[6]{0:T(128)S(1)} %get-tuple-element.19, pred[6]{0:T(512)(128)(4,1)S(1)} %iota_compare_fusion.4), kind=kOutput, calls=%fused_computation.41 | convolution fusion | flops 46646784 | bytes 2675766 | tf_op jit(solution)/shard_map/kr,sar->ska/dot_general | solution.py:121
  4.8 4.9 %collective-permute-start.2 = (f32[39,3,128]{2,1,0:T(4,128)S(1)}, f32[39,3,128]{2,1,0:T(4,128)S(1)}, u32[]{:S(2)}, u32[]{:S(2)}) collective-permute-start(f32[39,3,128]{2,1,0:T(4,128)S(1)} %get-tuple-element.15), channel_id=1, source_target_pairs={{0,1},{1,2},{2,3},{4,5},{5,6},{6,7},{8,9},{9,10},{10,11},{12,13},{... | collective-permute-start | bytes 179720 | tf_op jit(solution)/shard_map/ppermute | solution.py:135
  9.7 1.3 %collective-permute-start.3 = (f32[39,3,128]{2,1,0:T(4,128)S(1)}, f32[39,3,128]{2,1,0:T(4,128)S(1)}, u32[]{:S(2)}, u32[]{:S(2)}) collective-permute-start(f32[39,3,128]{2,1,0:T(4,128)S(1)} %get-tuple-element.14), channel_id=1, source_target_pairs={{1,0},{2,1},{3,2},{5,4},{6,5},{7,6},{9,8},{10,9},{11,10},{13,12},{... | collective-permute-start | bytes 179720 | tf_op jit(solution)/shard_map/ppermute | solution.py:136
  11.1 1.5 %collective-permute-start = (f32[39,3,128]{2,1,0:T(4,128)S(1)}, f32[39,3,128]{2,1,0:T(4,128)S(1)}, u32[]{:S(2)}, u32[]{:S(2)}) collective-permute-start(f32[39,3,128]{2,1,0:T(4,128)S(1)} %get-tuple-element.9), channel_id=1, source_target_pairs={{0,4},{4,8},{8,12},{12,16},{16,20},{20,24},{24,28},{1,5},{5,9},{9,... | collective-permute-start | bytes 179720 | tf_op jit(solution)/shard_map/ppermute | solution.py:28
  12.5 1.3 %collective-permute-start.1 = (f32[39,3,128]{2,1,0:T(4,128)S(1)}, f32[39,3,128]{2,1,0:T(4,128)S(1)}, u32[]{:S(2)}, u32[]{:S(2)}) collective-permute-start(f32[39,3,128]{2,1,0:T(4,128)S(1)} %get-tuple-element.8), channel_id=1, source_target_pairs={{4,0},{8,4},{12,8},{16,12},{20,16},{24,20},{28,24},{5,1},{9,5},{13... | collective-permute-start | bytes 179720 | tf_op jit(solution)/shard_map/ppermute | solution.py:28
  14.2 1.9 %collective-permute-done.3.right_ref.right_speed_ref = f32[39,3,128]{2,1,0:T(4,128)S(1)} collective-permute-done((f32[39,3,128]{2,1,0:T(4,128)S(1)}, f32[39,3,128]{2,1,0:T(4,128)S(1)}, u32[]{:S(2)}, u32[]{:S(2)}) %collective-permute-start.3) | collective-permute-done | bytes 59936 | tf_op jit(solution)/shard_map/ppermute | solution.py:136
  16.0 1.2 %collective-permute-done.1.bottom_ref.bottom_speed_ref = f32[39,3,128]{2,1,0:T(4,128)S(1)} collective-permute-done((f32[39,3,128]{2,1,0:T(4,128)S(1)}, f32[39,3,128]{2,1,0:T(4,128)S(1)}, u32[]{:S(2)}, u32[]{:S(2)}) %collective-permute-start.1) | collective-permute-done | bytes 59936 | tf_op jit(solution)/shard_map/ppermute | solution.py:28
  17.3 0.6 copy-done.6
  17.9 19.8 %shard_map.113 = f32[128,38,128]{2,1,0:T(8,128)} custom-call(f32[38,128,128]{2,1,0:T(8,128)} %field_ref.1, f32[2,128,128]{2,1,0:T(8,128)} %speed_ref.1, f32[39,3,128]{2,1,0:T(4,128)} %copy-done.5, f32[39,3,128]{2,1,0:T(4,128)} %copy-done.5, f32[39,3,128]{2,1,0:T(4,128)} %copy-done.6, f32[39,3,128]{2,1,0:T(4,128)} %copy-done.6, f32[39,3,128]{2,1,0:T(4,128)} %copy-done.3, ...), custom_call_target="tpu_custom_call" | custom-call | tf_op jit(solution)/shard_map/pallas_call | solution.py:144
  37.7 3.2 %fusion.13 = f32[128,128,38]{1,2,0:T(8,128)S(1)} fusion(f32[128,38,128]{2,1,0:T(8,128)} %shard_map.113, f32[38,38]{1,0:T(8,128)S(1)} %copy-done), kind=kOutput, calls=%fused_computation.24 | convolution fusion | flops 141950976 | bytes 4986512 | tf_op jit(solution)/shard_map/dot_general | solution.py:168
  40.9 2.6 %bitcast_subtract_fusion.4 = f32[38,128,128]{2,0,1:T(8,128)S(1)} fusion(f32[128,128,38]{1,2,0:T(8,128)S(1)} %fusion.13, f32[128,38,128]{2,1,0:T(8,128)S(1)} %copy-done.1, f32[128,128]{1,0:T(8,128)S(1)} %exponential_multiply_fusion, f32[38,38]{1,0:T(8,128)S(1)} %copy-done.7), kind=kOutput, calls=%fused_computation.13 | convolution fusion | flops 148176896 | bytes 7542416 | tf_op jit(solution)/shard_map/dot_general | solution.py:175
  43.4 1.3 %fusion.40 = f32[128,128,38]{1,2,0:T(8,128)S(1)} fusion(f32[38,128,128]{2,0,1:T(8,128)S(1)} %bitcast_subtract_fusion.4, f32[38,38]{1,0:T(8,128)S(1)} %copy-done), kind=kOutput, calls=%fused_computation.52 | convolution fusion | flops 141950976 | bytes 4986512 | tf_op jit(solution)/shard_map/dot_general | solution.py:168
  44.8 2.8 %bitcast_subtract_fusion.2 = f32[38,128,128]{2,0,1:T(8,128)S(1)} fusion(f32[38,128,128]{2,0,1:T(8,128)S(1)} %bitcast_subtract_fusion.4, f32[128,128,38]{1,2,0:T(8,128)S(1)} %fusion.40, f32[128,38,128]{2,1,0:T(8,128)S(1)} %copy-done.1, f32[128,128]{1,0:T(8,128)S(1)} %exponential_multiply_fusion, f32[38,38]{1,0:T(8,128)S(1)} %copy-done.7), kind=kOutput, calls=%fused_computation.9 | convolution fusion | flops 148176896 | bytes 10032784 | tf_op jit(solution)/shard_map/dot_general | solution.py:175
  47.6 1.3 %fusion.38 = f32[128,128,38]{1,2,0:T(8,128)S(1)} fusion(f32[38,128,128]{2,0,1:T(8,128)S(1)} %bitcast_subtract_fusion.2, f32[38,38]{1,0:T(8,128)S(1)} %copy-done), kind=kOutput, calls=%fused_computation.50 | convolution fusion | flops 141950976 | bytes 4986512 | tf_op jit(solution)/shard_map/dot_general | solution.py:168
  49.0 3.3 %fusion = f32[38,128,128]{2,0,1:T(8,128)S(1)} fusion(f32[128,38,128]{2,1,0:T(8,128)S(1)} %copy-done.1, f32[38,128,128]{2,0,1:T(8,128)S(1)} %bitcast_subtract_fusion.2, f32[128,128,38]{1,2,0:T(8,128)S(1)} %fusion.38, f32[128,128]{1,0:T(8,128)S(1)} %exponential_multiply_fusion, pred[128]{0:T(512)(128)(4,1)S(1)} %gt.22, f32[38,38]{1,0:T(8,128)S(1)} %copy-done.7), kind=kOutput, calls=%fused_computation.5 | convolution fusion | flops 148799488 | bytes 10032912 | tf_op jit(solution)/shard_map/dot_general | solution.py:175
  52.2 1.7 %convolution_bitcast_fusion = f32[4,128,128]{2,0,1:T(4,128)S(1)} fusion(f32[38,128,128]{2,0,1:T(8,128)S(1)} %fusion, f32[4,38]{1,0:T(4,128)S(1)} %copy-done.10), kind=kOutput, calls=%fused_computation.40 | convolution fusion | flops 29884416 | bytes 2753120 | tf_op jit(solution)/shard_map/dot_general | solution.py:181
  54.3 2.7 %collective-permute-start.4 = (f32[4,128]{1,0:T(4,128)S(1)}, f32[4,128]{1,0:T(4,128)S(1)}, u32[]{:S(2)}, u32[]{:S(2)}) collective-permute-start(f32[4,128]{1,0:T(4,128)S(1)} %broadcast_multiply_fusion), channel_id=1, source_target_pairs={{0,1},{1,0},{2,3},{3,2},{4,5},{5,4},{6,7},{7,6},{8,9},{9,8},{10,11... | collective-permute-start | bytes 6152 | tf_op jit(solution)/shard_map/ppermute | solution.py:191
  57.0 1.6 %collective-permute-done.4 = f32[4,128]{1,0:T(4,128)S(1)} collective-permute-done((f32[4,128]{1,0:T(4,128)S(1)}, f32[4,128]{1,0:T(4,128)S(1)}, u32[]{:S(2)}, u32[]{:S(2)}) %collective-permute-start.4) | collective-permute-done | bytes 2080 | tf_op jit(solution)/shard_map/ppermute | solution.py:191
  58.6 3.0 %collective-permute-start.5 = (f32[4,128]{1,0:T(4,128)S(1)}, f32[4,128]{1,0:T(4,128)S(1)}, u32[]{:S(2)}, u32[]{:S(2)}) collective-permute-start(f32[4,128]{1,0:T(4,128)S(1)} %fusion.51), channel_id=1, source_target_pairs={{0,2},{1,3},{2,0},{3,1},{4,6},{5,7},{6,4},{7,5},{8,10},{9,11},{10,... | collective-permute-start | bytes 6152 | tf_op jit(solution)/shard_map/ppermute | solution.py:191
  61.6 0.7 dynamic-slice_subtract_fusion.2
  62.4 1.9 %copy.14 = f32[38,128,128]{2,1,0:T(8,128)} copy(f32[38,128,128]{2,0,1:T(8,128)S(1)} %fusion) | data formatting | bytes 4980736
  64.3 1.6 %collective-permute-start.6 = (f32[1,4,128]{2,1,0:T(4,128)S(1)}, f32[1,4,128]{2,1,0:T(4,128)S(1)}, u32[]{:S(2)}, u32[]{:S(2)}) collective-permute-start(f32[1,4,128]{2,1,0:T(4,128)S(1)} %bitcast.112), channel_id=1, source_target_pairs={{0,4},{4,0},{8,12},{12,8},{16,20},{20,16},{24,28},{28,24},{1,5},{5... | collective-permute-start | bytes 6152 | tf_op jit(solution)/shard_map/ppermute | solution.py:214
  65.9 0.4 select_reduce_fusion.3
  66.7 2.4 %collective-permute-start.7 = (f32[2,4,128]{2,1,0:T(4,128)S(1)}, f32[2,4,128]{2,1,0:T(4,128)S(1)}, u32[]{:S(2)}, u32[]{:S(2)}) collective-permute-start(f32[2,4,128]{2,1,0:T(4,128)S(1)} %maximum_select_fusion.1), channel_id=1, source_target_pairs={{0,8},{4,12},{8,0},{12,4},{16,24},{20,28},{24,16},{28,20},{1,9},{5... | collective-permute-start | bytes 12296 | tf_op jit(solution)/shard_map/ppermute | solution.py:214
  69.1 0.4 select_reduce_fusion.2
  69.6 1.1 %collective-permute-done.7 = f32[2,4,128]{2,1,0:T(4,128)S(1)} collective-permute-done((f32[2,4,128]{2,1,0:T(4,128)S(1)}, f32[2,4,128]{2,1,0:T(4,128)S(1)}, u32[]{:S(2)}, u32[]{:S(2)}) %collective-permute-start.7) | collective-permute-done | bytes 4128 | tf_op jit(solution)/shard_map/ppermute | solution.py:214
  70.7 2.2 %collective-permute-start.8 = (f32[4,4,128]{2,1,0:T(4,128)S(1)}, f32[4,4,128]{2,1,0:T(4,128)S(1)}, u32[]{:S(2)}, u32[]{:S(2)}) collective-permute-start(f32[4,4,128]{2,1,0:T(4,128)S(1)} %maximum_select_fusion), channel_id=1, source_target_pairs={{0,16},{4,20},{8,24},{12,28},{16,0},{20,4},{24,8},{28,12},{1,17},{... | collective-permute-start | bytes 24584 | tf_op jit(solution)/shard_map/ppermute | solution.py:214
  72.9 0.8 select_reduce_fusion.1
  73.6 0.9 %collective-permute-done.8 = f32[4,4,128]{2,1,0:T(4,128)S(1)} collective-permute-done((f32[4,4,128]{2,1,0:T(4,128)S(1)}, f32[4,4,128]{2,1,0:T(4,128)S(1)}, u32[]{:S(2)}, u32[]{:S(2)}) %collective-permute-start.8) | collective-permute-done | bytes 8224 | tf_op jit(solution)/shard_map/ppermute | solution.py:214
  74.5 1.5 %select_reduce_fusion = f32[4,1024]{1,0:T(4,128)S(1)} fusion(f32[4,512]{1,0:T(4,128)S(1)} %bitcast.115, s32[4,1024]{1,0:T(4,128)S(1)} %get-tuple-element.12), kind=kLoop, calls=%fused_computation | loop fusion | flops 6287360 | bytes 40960 | tf_op jit(solution)/shard_map/reduce_sum | solution.py:201
  76.0 0.6 add_subtract_fusion
  (43 shorter events, 1.1 us)
Async XLA Ops:
  0.6 37.0 %copy-start = (f32[38,38]{1,0:T(8,128)S(1)}, f32[38,38]{1,0:T(8,128)}, u32[]{:S(2)}) copy-start(f32[38,38]{1,0:T(8,128)} %param.13) | copy-start | bytes 17332
  0.6 10.4 %copy-start.2 = (f32[38,128,128]{2,1,0:T(8,128)S(1)}, f32[38,128,128]{2,1,0:T(8,128)}, u32[]{:S(2)}) copy-start(f32[38,128,128]{2,1,0:T(8,128)} %field_ref.1) | copy-start | bytes 7471108
  1.7 12.1 %copy-start.8 = (f32[128,128]{1,0:T(8,128)S(1)}, f32[128,128]{1,0:T(8,128)}, u32[]{:S(2)}) copy-start(f32[128,128]{1,0:T(8,128)} %param.12) | copy-start | bytes 196612
  1.7 12.1 %copy-start.12 = (s32[64,1]{0,1:T(1,128)S(1)}, s32[64,1]{0,1:T(1,128)}, u32[]{:S(2)}) copy-start(s32[64,1]{0,1:T(1,128)} %param.15) | copy-start | bytes 772
  4.8 9.4 %collective-permute-start.2 = (f32[39,3,128]{2,1,0:T(4,128)S(1)}, f32[39,3,128]{2,1,0:T(4,128)S(1)}, u32[]{:S(2)}, u32[]{:S(2)}) collective-permute-start(f32[39,3,128]{2,1,0:T(4,128)S(1)} %get-tuple-element.15), channel_id=1, source_target_pairs={{0,1},{1,2},{2,3},{4,5},{5,6},{6,7},{8,9},{9,10},{10,11},{12,13},{... | collective-permute-start | bytes 179720 | tf_op jit(solution)/shard_map/ppermute | solution.py:135
  9.7 6.3 %collective-permute-start.3 = (f32[39,3,128]{2,1,0:T(4,128)S(1)}, f32[39,3,128]{2,1,0:T(4,128)S(1)}, u32[]{:S(2)}, u32[]{:S(2)}) collective-permute-start(f32[39,3,128]{2,1,0:T(4,128)S(1)} %get-tuple-element.14), channel_id=1, source_target_pairs={{1,0},{2,1},{3,2},{5,4},{6,5},{7,6},{9,8},{10,9},{11,10},{13,12},{... | collective-permute-start | bytes 179720 | tf_op jit(solution)/shard_map/ppermute | solution.py:136
  11.1 5.0 %collective-permute-start = (f32[39,3,128]{2,1,0:T(4,128)S(1)}, f32[39,3,128]{2,1,0:T(4,128)S(1)}, u32[]{:S(2)}, u32[]{:S(2)}) collective-permute-start(f32[39,3,128]{2,1,0:T(4,128)S(1)} %get-tuple-element.9), channel_id=1, source_target_pairs={{0,4},{4,8},{8,12},{12,16},{16,20},{20,24},{24,28},{1,5},{5,9},{9,... | collective-permute-start | bytes 179720 | tf_op jit(solution)/shard_map/ppermute | solution.py:28
  12.5 4.7 %collective-permute-start.1 = (f32[39,3,128]{2,1,0:T(4,128)S(1)}, f32[39,3,128]{2,1,0:T(4,128)S(1)}, u32[]{:S(2)}, u32[]{:S(2)}) collective-permute-start(f32[39,3,128]{2,1,0:T(4,128)S(1)} %get-tuple-element.8), channel_id=1, source_target_pairs={{4,0},{8,4},{12,8},{16,12},{20,16},{24,20},{28,24},{5,1},{9,5},{13... | collective-permute-start | bytes 179720 | tf_op jit(solution)/shard_map/ppermute | solution.py:28
  14.1 3.1 %copy-start.3 = (f32[39,3,128]{2,1,0:T(4,128)}, f32[39,3,128]{2,1,0:T(4,128)S(1)}, u32[]{:S(2)}) copy-start(f32[39,3,128]{2,1,0:T(4,128)S(1)} %collective-permute-done.2.left_ref.left_speed_ref) | copy-start | bytes 179716
  16.0 1.2 %copy-start.4 = (f32[39,3,128]{2,1,0:T(4,128)}, f32[39,3,128]{2,1,0:T(4,128)S(1)}, u32[]{:S(2)}) copy-start(f32[39,3,128]{2,1,0:T(4,128)S(1)} %collective-permute-done.3.right_ref.right_speed_ref) | copy-start | bytes 179716
  16.0 1.2 %copy-start.5 = (f32[39,3,128]{2,1,0:T(4,128)}, f32[39,3,128]{2,1,0:T(4,128)S(1)}, u32[]{:S(2)}) copy-start(f32[39,3,128]{2,1,0:T(4,128)S(1)} %collective-permute-done.top_ref.top_speed_ref) | copy-start | bytes 179716
  17.3 0.6 copy-start.6
  37.7 3.2 %copy-start.1 = (f32[128,38,128]{2,1,0:T(8,128)S(1)}, f32[128,38,128]{2,1,0:T(8,128)}, u32[]{:S(2)}) copy-start(f32[128,38,128]{2,1,0:T(8,128)} %shard_map.113) | copy-start | bytes 7471108
  37.7 3.2 %copy-start.7 = (f32[38,38]{1,0:T(8,128)S(1)}, f32[38,38]{1,0:T(8,128)}, u32[]{:S(2)}) copy-start(f32[38,38]{1,0:T(8,128)} %param.14) | copy-start | bytes 17332
  48.9 3.3 %copy-start.10 = (f32[4,38]{1,0:T(4,128)S(1)}, f32[4,38]{1,0:T(4,128)}, u32[]{:S(2)}) copy-start(f32[4,38]{1,0:T(4,128)} %param.16) | copy-start | bytes 1828
  52.2 1.7 %copy-start.11 = (f32[128]{0:T(128)S(1)}, f32[128]{0:T(128)}, u32[]{:S(2)}) copy-start(f32[128]{0:T(128)} %param.17) | copy-start | bytes 1540
  54.3 4.3 %collective-permute-start.4 = (f32[4,128]{1,0:T(4,128)S(1)}, f32[4,128]{1,0:T(4,128)S(1)}, u32[]{:S(2)}, u32[]{:S(2)}) collective-permute-start(f32[4,128]{1,0:T(4,128)S(1)} %broadcast_multiply_fusion), channel_id=1, source_target_pairs={{0,1},{1,0},{2,3},{3,2},{4,5},{5,4},{6,7},{7,6},{8,9},{9,8},{10,11... | collective-permute-start | bytes 6152 | tf_op jit(solution)/shard_map/ppermute | solution.py:191
  58.6 5.7 %collective-permute-start.5 = (f32[4,128]{1,0:T(4,128)S(1)}, f32[4,128]{1,0:T(4,128)S(1)}, u32[]{:S(2)}, u32[]{:S(2)}) collective-permute-start(f32[4,128]{1,0:T(4,128)S(1)} %fusion.51), channel_id=1, source_target_pairs={{0,2},{1,3},{2,0},{3,1},{4,6},{5,7},{6,4},{7,5},{8,10},{9,11},{10,... | collective-permute-start | bytes 6152 | tf_op jit(solution)/shard_map/ppermute | solution.py:191
  62.4 13.6 %copy-start.9 = (f32[4,1024]{1,0:T(4,128)S(1)}, f32[4,1024]{1,0:T(4,128)}, u32[]{:S(2)}) copy-start(f32[4,1024]{1,0:T(4,128)} %param.19) | copy-start | bytes 49156
  64.3 2.5 %collective-permute-start.6 = (f32[1,4,128]{2,1,0:T(4,128)S(1)}, f32[1,4,128]{2,1,0:T(4,128)S(1)}, u32[]{:S(2)}, u32[]{:S(2)}) collective-permute-start(f32[1,4,128]{2,1,0:T(4,128)S(1)} %bitcast.112), channel_id=1, source_target_pairs={{0,4},{4,0},{8,12},{12,8},{16,20},{20,16},{24,28},{28,24},{1,5},{5... | collective-permute-start | bytes 6152 | tf_op jit(solution)/shard_map/ppermute | solution.py:214
  66.7 4.0 %collective-permute-start.7 = (f32[2,4,128]{2,1,0:T(4,128)S(1)}, f32[2,4,128]{2,1,0:T(4,128)S(1)}, u32[]{:S(2)}, u32[]{:S(2)}) collective-permute-start(f32[2,4,128]{2,1,0:T(4,128)S(1)} %maximum_select_fusion.1), channel_id=1, source_target_pairs={{0,8},{4,12},{8,0},{12,4},{16,24},{20,28},{24,16},{28,20},{1,9},{5... | collective-permute-start | bytes 12296 | tf_op jit(solution)/shard_map/ppermute | solution.py:214
  70.7 3.8 %collective-permute-start.8 = (f32[4,4,128]{2,1,0:T(4,128)S(1)}, f32[4,4,128]{2,1,0:T(4,128)S(1)}, u32[]{:S(2)}, u32[]{:S(2)}) collective-permute-start(f32[4,4,128]{2,1,0:T(4,128)S(1)} %maximum_select_fusion), channel_id=1, source_target_pairs={{0,16},{4,20},{8,24},{12,28},{16,0},{20,4},{24,8},{28,12},{1,17},{... | collective-permute-start | bytes 24584 | tf_op jit(solution)/shard_map/ppermute | solution.py:214

commit v9 on v8

--- a/solution.py
+++ b/solution.py
@@ -81,19 +81,19 @@
 def transport_kernel(
     field_ref, speed_ref, top_ref, top_speed_ref, bottom_ref, bottom_speed_ref,
     left_ref, left_speed_ref, right_ref, right_speed_ref, out_ref,
-    ext_ref, vel_ref, flux_ref,
+    ext_ref, axial_speed_ref, radial_speed_ref, flux_ref,
 ):
     rows, cols = field_ref.shape[1], field_ref.shape[2]
     group = field_ref.shape[0]
+    fill_scratch(axial_speed_ref, top_speed_ref[0], speed_ref[0], bottom_speed_ref[0])
+    fill_scratch(radial_speed_ref, left_speed_ref[0], speed_ref[1].T, right_speed_ref[0])
 
     def one_species(member, carry):
         field = field_ref[member]
         fill_scratch(ext_ref, top_ref[member], field, bottom_ref[member])
-        fill_scratch(vel_ref, top_speed_ref[0], speed_ref[0], bottom_speed_ref[0])
-        along_axial = upwind_divergence(ext_ref, vel_ref, flux_ref, rows)
+        along_axial = upwind_divergence(ext_ref, axial_speed_ref, flux_ref, rows)
         fill_scratch(ext_ref, left_ref[member], field.T, right_ref[member])
-        fill_scratch(vel_ref, left_speed_ref[0], speed_ref[1].T, right_speed_ref[0])
-        along_radial = upwind_divergence(ext_ref, vel_ref, flux_ref, cols).T
+        along_radial = upwind_divergence(ext_ref, radial_speed_ref, flux_ref, cols).T
         moved = field - TIME_STEP * (along_axial + along_radial)
         out_ref[:, pl.ds(pl.program_id(0) * group + member, 1), :] = moved[:, None, :]
         return carry
@@ -150,6 +150,7 @@
         scratch_shapes=[
             pltpu.VMEM((span, cols), jnp.float32),
             pltpu.VMEM((span, cols), jnp.float32),
+            pltpu.VMEM((span, cols), jnp.float32),
             pltpu.VMEM((faces, cols), jnp.float32),
         ],
     )(species, speed, top, top, bottom, bottom, left, left, right, right)

time: 76.9 us -> 76.6 us (level)
  no operation moved by 1% of the time
where the time goes in v9:
time: 76.6 us; the launch traced here: 76.3 us
  starting transfers between devices  20.9 us (27%)
  matrix products  19.5 us (25%)
  Pallas kernels  19.5 us (25%)
  waiting for transfers between devices  7.05 us (9%)
  other arithmetic  4.54 us (6%)
  local copies, waits for them, and re-layouts  3.88 us (5%)
  between operations  0.99 us (1%)
    pallas_call x1, Pallas kernels, transport(): pl.pallas_call(transport_kernel, grid=(species_count // group,), in_specs...  19.5 us
    dot_general x3, matrix products, kinetics_advance(): jnp.tensordot(frozen_jacobian_inverse_addend, defect, axes=(1, 0), precis...  8.66 us
    ppermute x3, starting transfers between devices, sampled_profile(): other = lax.ppermute(blocks, axis, pairs)  6.17 us
    dot_general x3, matrix products, kinetics_advance(): jnp.tensordot(linearized_kinetics_operator, current, axes=(1, 0), precisi...  5.81 us
    ppermute x2, starting transfers between devices, butterfly_sum(): part = part + lax.ppermute(part, axis, pairs)  5.74 us
    ppermute x1, starting transfers between devices, transport(): left = lax.ppermute(high_columns, 'radial', up)  4.93 us
    reduce_sum x4, other arithmetic, pick_samples(): jnp.sum(jnp.where(local[:, None, :] == cells, flat[:, :, None], 0.0), axi...  3.1 us
    dot_general x1, matrix products, edge_columns(): jnp.einsum('kr,sar->ska', pick.astype(field.dtype), field, precision=HIGH...  2.98 us
  transfers between devices with their start and end apart: 9, of which 6 were waited for; matrix products, arithmetic and copies ran while one was open for 6% of the time, Pallas kernels for 0%

profile of v9, /device:TPU:0, one launch (start us, length us, event | category | flops | bytes accessed | tf_op | source)
XLA Modules:
  0.0 76.3 jit_solution(15298895413553965645)
XLA Ops:
  0.7 1.0 %fusion.53 = (f32[1,128,128]{2,1,0:T(8,128)S(1)}, f32[1,128,128]{2,1,0:T(8,128)S(1)}) fusion(f32[2,128,128]{2,1,0:T(8,128)} %speed_ref.1), kind=kLoop, calls=%fused_computation.77 | loop fusion | bytes 262144 | tf_op jit(solution)/shard_map/slice | solution.py:130
  1.7 3.0 %fusion.29 = f32[39,6,128]{2,1,0:T(8,128)S(1)} fusion(f32[1,128,128]{2,1,0:T(8,128)S(1)} %get-tuple-element.16, f32[38,128,128]{2,1,0:T(8,128)} %field_ref.1, s32[6]{0:T(128)S(1)} %get-tuple-element.18, s32[6]{0:T(128)S(1)} %get-tuple-element.19, pred[6]{0:T(512)(128)(4,1)S(1)} %iota_compare_fusion.4), kind=kOutput, calls=%fused_computation.41 | convolution fusion | flops 46646784 | bytes 2675766 | tf_op jit(solution)/shard_map/kr,sar->ska/dot_general | solution.py:121
  4.8 4.9 %collective-permute-start.2 = (f32[39,3,128]{2,1,0:T(4,128)S(1)}, f32[39,3,128]{2,1,0:T(4,128)S(1)}, u32[]{:S(2)}, u32[]{:S(2)}) collective-permute-start(f32[39,3,128]{2,1,0:T(4,128)S(1)} %get-tuple-element.15), channel_id=1, source_target_pairs={{0,1},{1,2},{2,3},{4,5},{5,6},{6,7},{8,9},{9,10},{10,11},{12,13},{... | collective-permute-start | bytes 179720 | tf_op jit(solution)/shard_map/ppermute | solution.py:135
  9.7 1.3 %collective-permute-start.3 = (f32[39,3,128]{2,1,0:T(4,128)S(1)}, f32[39,3,128]{2,1,0:T(4,128)S(1)}, u32[]{:S(2)}, u32[]{:S(2)}) collective-permute-start(f32[39,3,128]{2,1,0:T(4,128)S(1)} %get-tuple-element.14), channel_id=1, source_target_pairs={{1,0},{2,1},{3,2},{5,4},{6,5},{7,6},{9,8},{10,9},{11,10},{13,12},{... | collective-permute-start | bytes 179720 | tf_op jit(solution)/shard_map/ppermute | solution.py:136
  11.1 1.5 %collective-permute-start = (f32[39,3,128]{2,1,0:T(4,128)S(1)}, f32[39,3,128]{2,1,0:T(4,128)S(1)}, u32[]{:S(2)}, u32[]{:S(2)}) collective-permute-start(f32[39,3,128]{2,1,0:T(4,128)S(1)} %get-tuple-element.9), channel_id=1, source_target_pairs={{0,4},{4,8},{8,12},{12,16},{16,20},{20,24},{24,28},{1,5},{5,9},{9,... | collective-permute-start | bytes 179720 | tf_op jit(solution)/shard_map/ppermute | solution.py:28
  12.5 1.3 %collective-permute-start.1 = (f32[39,3,128]{2,1,0:T(4,128)S(1)}, f32[39,3,128]{2,1,0:T(4,128)S(1)}, u32[]{:S(2)}, u32[]{:S(2)}) collective-permute-start(f32[39,3,128]{2,1,0:T(4,128)S(1)} %get-tuple-element.8), channel_id=1, source_target_pairs={{4,0},{8,4},{12,8},{16,12},{20,16},{24,20},{28,24},{5,1},{9,5},{13... | collective-permute-start | bytes 179720 | tf_op jit(solution)/shard_map/ppermute | solution.py:28
  14.2 1.9 %collective-permute-done.3.right_ref.right_speed_ref = f32[39,3,128]{2,1,0:T(4,128)S(1)} collective-permute-done((f32[39,3,128]{2,1,0:T(4,128)S(1)}, f32[39,3,128]{2,1,0:T(4,128)S(1)}, u32[]{:S(2)}, u32[]{:S(2)}) %collective-permute-start.3) | collective-permute-done | bytes 59936 | tf_op jit(solution)/shard_map/ppermute | solution.py:136
  16.0 1.2 %collective-permute-done.1.bottom_ref.bottom_speed_ref = f32[39,3,128]{2,1,0:T(4,128)S(1)} collective-permute-done((f32[39,3,128]{2,1,0:T(4,128)S(1)}, f32[39,3,128]{2,1,0:T(4,128)S(1)}, u32[]{:S(2)}, u32[]{:S(2)}) %collective-permute-start.1) | collective-permute-done | bytes 59936 | tf_op jit(solution)/shard_map/ppermute | solution.py:28
  17.3 0.6 copy-done.6
  17.9 19.5 %shard_map.113 = f32[128,38,128]{2,1,0:T(8,128)} custom-call(f32[38,128,128]{2,1,0:T(8,128)} %field_ref.1, f32[2,128,128]{2,1,0:T(8,128)} %speed_ref.1, f32[39,3,128]{2,1,0:T(4,128)} %copy-done.5, f32[39,3,128]{2,1,0:T(4,128)} %copy-done.5, f32[39,3,128]{2,1,0:T(4,128)} %copy-done.6, f32[39,3,128]{2,1,0:T(4,128)} %copy-done.6, f32[39,3,128]{2,1,0:T(4,128)} %copy-done.3, ...), custom_call_target="tpu_custom_call" | custom-call | tf_op jit(solution)/shard_map/pallas_call | solution.py:144
  37.4 3.2 %fusion.13 = f32[128,128,38]{1,2,0:T(8,128)S(1)} fusion(f32[128,38,128]{2,1,0:T(8,128)} %shard_map.113, f32[38,38]{1,0:T(8,128)S(1)} %copy-done), kind=kOutput, calls=%fused_computation.24 | convolution fusion | flops 141950976 | bytes 4986512 | tf_op jit(solution)/shard_map/dot_general | solution.py:169
  40.6 2.5 %bitcast_subtract_fusion.4 = f32[38,128,128]{2,0,1:T(8,128)S(1)} fusion(f32[128,128,38]{1,2,0:T(8,128)S(1)} %fusion.13, f32[128,38,128]{2,1,0:T(8,128)S(1)} %copy-done.1, f32[128,128]{1,0:T(8,128)S(1)} %exponential_multiply_fusion, f32[38,38]{1,0:T(8,128)S(1)} %copy-done.7), kind=kOutput, calls=%fused_computation.13 | convolution fusion | flops 148176896 | bytes 7542416 | tf_op jit(solution)/shard_map/dot_general | solution.py:176
  43.2 1.3 %fusion.40 = f32[128,128,38]{1,2,0:T(8,128)S(1)} fusion(f32[38,128,128]{2,0,1:T(8,128)S(1)} %bitcast_subtract_fusion.4, f32[38,38]{1,0:T(8,128)S(1)} %copy-done), kind=kOutput, calls=%fused_computation.52 | convolution fusion | flops 141950976 | bytes 4986512 | tf_op jit(solution)/shard_map/dot_general | solution.py:169
  44.5 2.9 %bitcast_subtract_fusion.2 = f32[38,128,128]{2,0,1:T(8,128)S(1)} fusion(f32[38,128,128]{2,0,1:T(8,128)S(1)} %bitcast_subtract_fusion.4, f32[128,128,38]{1,2,0:T(8,128)S(1)} %fusion.40, f32[128,38,128]{2,1,0:T(8,128)S(1)} %copy-done.1, f32[128,128]{1,0:T(8,128)S(1)} %exponential_multiply_fusion, f32[38,38]{1,0:T(8,128)S(1)} %copy-done.7), kind=kOutput, calls=%fused_computation.9 | convolution fusion | flops 148176896 | bytes 10032784 | tf_op jit(solution)/shard_map/dot_general | solution.py:176
  47.4 1.3 %fusion.38 = f32[128,128,38]{1,2,0:T(8,128)S(1)} fusion(f32[38,128,128]{2,0,1:T(8,128)S(1)} %bitcast_subtract_fusion.2, f32[38,38]{1,0:T(8,128)S(1)} %copy-done), kind=kOutput, calls=%fused_computation.50 | convolution fusion | flops 141950976 | bytes 4986512 | tf_op jit(solution)/shard_map/dot_general | solution.py:169
  48.7 3.3 %fusion = f32[38,128,128]{2,0,1:T(8,128)S(1)} fusion(f32[128,38,128]{2,1,0:T(8,128)S(1)} %copy-done.1, f32[38,128,128]{2,0,1:T(8,128)S(1)} %bitcast_subtract_fusion.2, f32[128,128,38]{1,2,0:T(8,128)S(1)} %fusion.38, f32[128,128]{1,0:T(8,128)S(1)} %exponential_multiply_fusion, pred[128]{0:T(512)(128)(4,1)S(1)} %gt.22, f32[38,38]{1,0:T(8,128)S(1)} %copy-done.7), kind=kOutput, calls=%fused_computation.5 | convolution fusion | flops 148799488 | bytes 10032912 | tf_op jit(solution)/shard_map/dot_general | solution.py:176
  52.0 1.7 %convolution_bitcast_fusion = f32[4,128,128]{2,0,1:T(4,128)S(1)} fusion(f32[38,128,128]{2,0,1:T(8,128)S(1)} %fusion, f32[4,38]{1,0:T(4,128)S(1)} %copy-done.10), kind=kOutput, calls=%fused_computation.40 | convolution fusion | flops 29884416 | bytes 2753120 | tf_op jit(solution)/shard_map/dot_general | solution.py:182
  54.0 2.7 %collective-permute-start.4 = (f32[4,128]{1,0:T(4,128)S(1)}, f32[4,128]{1,0:T(4,128)S(1)}, u32[]{:S(2)}, u32[]{:S(2)}) collective-permute-start(f32[4,128]{1,0:T(4,128)S(1)} %broadcast_multiply_fusion), channel_id=1, source_target_pairs={{0,1},{1,0},{2,3},{3,2},{4,5},{5,4},{6,7},{7,6},{8,9},{9,8},{10,11... | collective-permute-start | bytes 6152 | tf_op jit(solution)/shard_map/ppermute | solution.py:192
  56.7 1.6 %collective-permute-done.4 = f32[4,128]{1,0:T(4,128)S(1)} collective-permute-done((f32[4,128]{1,0:T(4,128)S(1)}, f32[4,128]{1,0:T(4,128)S(1)}, u32[]{:S(2)}, u32[]{:S(2)}) %collective-permute-start.4) | collective-permute-done | bytes 2080 | tf_op jit(solution)/shard_map/ppermute | solution.py:192
  58.3 3.0 %collective-permute-start.5 = (f32[4,128]{1,0:T(4,128)S(1)}, f32[4,128]{1,0:T(4,128)S(1)}, u32[]{:S(2)}, u32[]{:S(2)}) collective-permute-start(f32[4,128]{1,0:T(4,128)S(1)} %fusion.51), channel_id=1, source_target_pairs={{0,2},{1,3},{2,0},{3,1},{4,6},{5,7},{6,4},{7,5},{8,10},{9,11},{10,... | collective-permute-start | bytes 6152 | tf_op jit(solution)/shard_map/ppermute | solution.py:192
  61.3 0.7 dynamic-slice_subtract_fusion.2
  62.1 1.9 %copy.14 = f32[38,128,128]{2,1,0:T(8,128)} copy(f32[38,128,128]{2,0,1:T(8,128)S(1)} %fusion) | data formatting | bytes 4980736
  64.0 1.6 %collective-permute-start.6 = (f32[1,4,128]{2,1,0:T(4,128)S(1)}, f32[1,4,128]{2,1,0:T(4,128)S(1)}, u32[]{:S(2)}, u32[]{:S(2)}) collective-permute-start(f32[1,4,128]{2,1,0:T(4,128)S(1)} %bitcast.112), channel_id=1, source_target_pairs={{0,4},{4,0},{8,12},{12,8},{16,20},{20,16},{24,28},{28,24},{1,5},{5... | collective-permute-start | bytes 6152 | tf_op jit(solution)/shard_map/ppermute | solution.py:215
  65.7 0.4 select_reduce_fusion.3
  66.5 2.4 %collective-permute-start.7 = (f32[2,4,128]{2,1,0:T(4,128)S(1)}, f32[2,4,128]{2,1,0:T(4,128)S(1)}, u32[]{:S(2)}, u32[]{:S(2)}) collective-permute-start(f32[2,4,128]{2,1,0:T(4,128)S(1)} %maximum_select_fusion.1), channel_id=1, source_target_pairs={{0,8},{4,12},{8,0},{12,4},{16,24},{20,28},{24,16},{28,20},{1,9},{5... | collective-permute-start | bytes 12296 | tf_op jit(solution)/shard_map/ppermute | solution.py:215
  68.9 0.4 select_reduce_fusion.2
  69.3 1.1 %collective-permute-done.7 = f32[2,4,128]{2,1,0:T(4,128)S(1)} collective-permute-done((f32[2,4,128]{2,1,0:T(4,128)S(1)}, f32[2,4,128]{2,1,0:T(4,128)S(1)}, u32[]{:S(2)}, u32[]{:S(2)}) %collective-permute-start.7) | collective-permute-done | bytes 4128 | tf_op jit(solution)/shard_map/ppermute | solution.py:215
  70.5 2.1 %collective-permute-start.8 = (f32[4,4,128]{2,1,0:T(4,128)S(1)}, f32[4,4,128]{2,1,0:T(4,128)S(1)}, u32[]{:S(2)}, u32[]{:S(2)}) collective-permute-start(f32[4,4,128]{2,1,0:T(4,128)S(1)} %maximum_select_fusion), channel_id=1, source_target_pairs={{0,16},{4,20},{8,24},{12,28},{16,0},{20,4},{24,8},{28,12},{1,17},{... | collective-permute-start | bytes 24584 | tf_op jit(solution)/shard_map/ppermute | solution.py:215
  72.6 0.8 select_reduce_fusion.1
  73.4 0.9 %collective-permute-done.8 = f32[4,4,128]{2,1,0:T(4,128)S(1)} collective-permute-done((f32[4,4,128]{2,1,0:T(4,128)S(1)}, f32[4,4,128]{2,1,0:T(4,128)S(1)}, u32[]{:S(2)}, u32[]{:S(2)}) %collective-permute-start.8) | collective-permute-done | bytes 8224 | tf_op jit(solution)/shard_map/ppermute | solution.py:215
  74.2 1.5 %select_reduce_fusion = f32[4,1024]{1,0:T(4,128)S(1)} fusion(f32[4,512]{1,0:T(4,128)S(1)} %bitcast.115, s32[4,1024]{1,0:T(4,128)S(1)} %get-tuple-element.12), kind=kLoop, calls=%fused_computation | loop fusion | flops 6287360 | bytes 40960 | tf_op jit(solution)/shard_map/reduce_sum | solution.py:202
  75.7 0.6 add_subtract_fusion
  (43 shorter events, 1.1 us)
Async XLA Ops:
  0.6 36.8 %copy-start = (f32[38,38]{1,0:T(8,128)S(1)}, f32[38,38]{1,0:T(8,128)}, u32[]{:S(2)}) copy-start(f32[38,38]{1,0:T(8,128)} %param.13) | copy-start | bytes 17332
  0.6 10.4 %copy-start.2 = (f32[38,128,128]{2,1,0:T(8,128)S(1)}, f32[38,128,128]{2,1,0:T(8,128)}, u32[]{:S(2)}) copy-start(f32[38,128,128]{2,1,0:T(8,128)} %field_ref.1) | copy-start | bytes 7471108
  1.7 12.1 %copy-start.8 = (f32[128,128]{1,0:T(8,128)S(1)}, f32[128,128]{1,0:T(8,128)}, u32[]{:S(2)}) copy-start(f32[128,128]{1,0:T(8,128)} %param.12) | copy-start | bytes 196612
  1.7 12.1 %copy-start.12 = (s32[64,1]{0,1:T(1,128)S(1)}, s32[64,1]{0,1:T(1,128)}, u32[]{:S(2)}) copy-start(s32[64,1]{0,1:T(1,128)} %param.15) | copy-start | bytes 772
  4.8 9.4 %collective-permute-start.2 = (f32[39,3,128]{2,1,0:T(4,128)S(1)}, f32[39,3,128]{2,1,0:T(4,128)S(1)}, u32[]{:S(2)}, u32[]{:S(2)}) collective-permute-start(f32[39,3,128]{2,1,0:T(4,128)S(1)} %get-tuple-element.15), channel_id=1, source_target_pairs={{0,1},{1,2},{2,3},{4,5},{5,6},{6,7},{8,9},{9,10},{10,11},{12,13},{... | collective-permute-start | bytes 179720 | tf_op jit(solution)/shard_map/ppermute | solution.py:135
  9.7 6.3 %collective-permute-start.3 = (f32[39,3,128]{2,1,0:T(4,128)S(1)}, f32[39,3,128]{2,1,0:T(4,128)S(1)}, u32[]{:S(2)}, u32[]{:S(2)}) collective-permute-start(f32[39,3,128]{2,1,0:T(4,128)S(1)} %get-tuple-element.14), channel_id=1, source_target_pairs={{1,0},{2,1},{3,2},{5,4},{6,5},{7,6},{9,8},{10,9},{11,10},{13,12},{... | collective-permute-start | bytes 179720 | tf_op jit(solution)/shard_map/ppermute | solution.py:136
  11.1 5.0 %collective-permute-start = (f32[39,3,128]{2,1,0:T(4,128)S(1)}, f32[39,3,128]{2,1,0:T(4,128)S(1)}, u32[]{:S(2)}, u32[]{:S(2)}) collective-permute-start(f32[39,3,128]{2,1,0:T(4,128)S(1)} %get-tuple-element.9), channel_id=1, source_target_pairs={{0,4},{4,8},{8,12},{12,16},{16,20},{20,24},{24,28},{1,5},{5,9},{9,... | collective-permute-start | bytes 179720 | tf_op jit(solution)/shard_map/ppermute | solution.py:28
  12.5 4.7 %collective-permute-start.1 = (f32[39,3,128]{2,1,0:T(4,128)S(1)}, f32[39,3,128]{2,1,0:T(4,128)S(1)}, u32[]{:S(2)}, u32[]{:S(2)}) collective-permute-start(f32[39,3,128]{2,1,0:T(4,128)S(1)} %get-tuple-element.8), channel_id=1, source_target_pairs={{4,0},{8,4},{12,8},{16,12},{20,16},{24,20},{28,24},{5,1},{9,5},{13... | collective-permute-start | bytes 179720 | tf_op jit(solution)/shard_map/ppermute | solution.py:28
  14.1 3.1 %copy-start.3 = (f32[39,3,128]{2,1,0:T(4,128)}, f32[39,3,128]{2,1,0:T(4,128)S(1)}, u32[]{:S(2)}) copy-start(f32[39,3,128]{2,1,0:T(4,128)S(1)} %collective-permute-done.2.left_ref.left_speed_ref) | copy-start | bytes 179716
  16.0 1.2 %copy-start.4 = (f32[39,3,128]{2,1,0:T(4,128)}, f32[39,3,128]{2,1,0:T(4,128)S(1)}, u32[]{:S(2)}) copy-start(f32[39,3,128]{2,1,0:T(4,128)S(1)} %collective-permute-done.3.right_ref.right_speed_ref) | copy-start | bytes 179716
  16.0 1.2 %copy-start.5 = (f32[39,3,128]{2,1,0:T(4,128)}, f32[39,3,128]{2,1,0:T(4,128)S(1)}, u32[]{:S(2)}) copy-start(f32[39,3,128]{2,1,0:T(4,128)S(1)} %collective-permute-done.top_ref.top_speed_ref) | copy-start | bytes 179716
  17.3 0.6 copy-start.6
  37.4 3.2 %copy-start.1 = (f32[128,38,128]{2,1,0:T(8,128)S(1)}, f32[128,38,128]{2,1,0:T(8,128)}, u32[]{:S(2)}) copy-start(f32[128,38,128]{2,1,0:T(8,128)} %shard_map.113) | copy-start | bytes 7471108
  37.4 3.2 %copy-start.7 = (f32[38,38]{1,0:T(8,128)S(1)}, f32[38,38]{1,0:T(8,128)}, u32[]{:S(2)}) copy-start(f32[38,38]{1,0:T(8,128)} %param.14) | copy-start | bytes 17332
  48.7 3.3 %copy-start.10 = (f32[4,38]{1,0:T(4,128)S(1)}, f32[4,38]{1,0:T(4,128)}, u32[]{:S(2)}) copy-start(f32[4,38]{1,0:T(4,128)} %param.16) | copy-start | bytes 1828
  52.0 1.7 %copy-start.11 = (f32[128]{0:T(128)S(1)}, f32[128]{0:T(128)}, u32[]{:S(2)}) copy-start(f32[128]{0:T(128)} %param.17) | copy-start | bytes 1540
  54.0 4.3 %collective-permute-start.4 = (f32[4,128]{1,0:T(4,128)S(1)}, f32[4,128]{1,0:T(4,128)S(1)}, u32[]{:S(2)}, u32[]{:S(2)}) collective-permute-start(f32[4,128]{1,0:T(4,128)S(1)} %broadcast_multiply_fusion), channel_id=1, source_target_pairs={{0,1},{1,0},{2,3},{3,2},{4,5},{5,4},{6,7},{7,6},{8,9},{9,8},{10,11... | collective-permute-start | bytes 6152 | tf_op jit(solution)/shard_map/ppermute | solution.py:192
  58.3 5.7 %collective-permute-start.5 = (f32[4,128]{1,0:T(4,128)S(1)}, f32[4,128]{1,0:T(4,128)S(1)}, u32[]{:S(2)}, u32[]{:S(2)}) collective-permute-start(f32[4,128]{1,0:T(4,128)S(1)} %fusion.51), channel_id=1, source_target_pairs={{0,2},{1,3},{2,0},{3,1},{4,6},{5,7},{6,4},{7,5},{8,10},{9,11},{10,... | collective-permute-start | bytes 6152 | tf_op jit(solution)/shard_map/ppermute | solution.py:192
  62.1 13.6 %copy-start.9 = (f32[4,1024]{1,0:T(4,128)S(1)}, f32[4,1024]{1,0:T(4,128)}, u32[]{:S(2)}) copy-start(f32[4,1024]{1,0:T(4,128)} %param.19) | copy-start | bytes 49156
  64.0 2.5 %collective-permute-start.6 = (f32[1,4,128]{2,1,0:T(4,128)S(1)}, f32[1,4,128]{2,1,0:T(4,128)S(1)}, u32[]{:S(2)}, u32[]{:S(2)}) collective-permute-start(f32[1,4,128]{2,1,0:T(4,128)S(1)} %bitcast.112), channel_id=1, source_target_pairs={{0,4},{4,0},{8,12},{12,8},{16,20},{20,16},{24,28},{28,24},{1,5},{5... | collective-permute-start | bytes 6152 | tf_op jit(solution)/shard_map/ppermute | solution.py:215
  66.5 4.0 %collective-permute-start.7 = (f32[2,4,128]{2,1,0:T(4,128)S(1)}, f32[2,4,128]{2,1,0:T(4,128)S(1)}, u32[]{:S(2)}, u32[]{:S(2)}) collective-permute-start(f32[2,4,128]{2,1,0:T(4,128)S(1)} %maximum_select_fusion.1), channel_id=1, source_target_pairs={{0,8},{4,12},{8,0},{12,4},{16,24},{20,28},{24,16},{28,20},{1,9},{5... | collective-permute-start | bytes 12296 | tf_op jit(solution)/shard_map/ppermute | solution.py:215
  70.5 3.8 %collective-permute-start.8 = (f32[4,4,128]{2,1,0:T(4,128)S(1)}, f32[4,4,128]{2,1,0:T(4,128)S(1)}, u32[]{:S(2)}, u32[]{:S(2)}) collective-permute-start(f32[4,4,128]{2,1,0:T(4,128)S(1)} %maximum_select_fusion), channel_id=1, source_target_pairs={{0,16},{4,20},{8,24},{12,28},{16,0},{20,4},{24,8},{28,12},{1,17},{... | collective-permute-start | bytes 24584 | tf_op jit(solution)/shard_map/ppermute | solution.py:215

commit v10 on v9

--- a/solution.py
+++ b/solution.py
@@ -55,7 +55,7 @@
 
 
 HALO = 8
-SPECIES_GROUP = 19
+SPECIES_GROUP = 38
 CHUNK = 8
 
 

time: 76.6 us -> 77 us (level)
  no operation moved by 1% of the time
where the time goes in v10:
time: 77 us; the launch traced here: 76.7 us
  starting transfers between devices  20.9 us (27%)
  Pallas kernels  19.9 us (26%)
  matrix products  19.5 us (25%)
  waiting for transfers between devices  7.05 us (9%)
  other arithmetic  4.54 us (6%)
  local copies, waits for them, and re-layouts  3.88 us (5%)
  between operations  0.99 us (1%)
    pallas_call x1, Pallas kernels, transport(): pl.pallas_call(transport_kernel, grid=(species_count // group,), in_specs...  19.9 us
    dot_general x3, matrix products, kinetics_advance(): jnp.tensordot(frozen_jacobian_inverse_addend, defect, axes=(1, 0), precis...  8.66 us
    ppermute x3, starting transfers between devices, sampled_profile(): other = lax.ppermute(blocks, axis, pairs)  6.18 us
    dot_general x3, matrix products, kinetics_advance(): jnp.tensordot(linearized_kinetics_operator, current, axes=(1, 0), precisi...  5.81 us
    ppermute x2, starting transfers between devices, butterfly_sum(): part = part + lax.ppermute(part, axis, pairs)  5.74 us
    ppermute x1, starting transfers between devices, transport(): left = lax.ppermute(high_columns, 'radial', up)  4.93 us
    reduce_sum x4, other arithmetic, pick_samples(): jnp.sum(jnp.where(local[:, None, :] == cells, flat[:, :, None], 0.0), axi...  3.1 us
    dot_general x1, matrix products, edge_columns(): jnp.einsum('kr,sar->ska', pick.astype(field.dtype), field, precision=HIGH...  2.98 us
  transfers between devices with their start and end apart: 9, of which 6 were waited for; matrix products, arithmetic and copies ran while one was open for 6% of the time, Pallas kernels for 0%

profile of v10, /device:TPU:0, one launch (start us, length us, event | category | flops | bytes accessed | tf_op | source)
XLA Modules:
  0.0 76.7 jit_solution(1980963532185594863)
XLA Ops:
  0.7 1.0 %fusion.53 = (f32[1,128,128]{2,1,0:T(8,128)S(1)}, f32[1,128,128]{2,1,0:T(8,128)S(1)}) fusion(f32[2,128,128]{2,1,0:T(8,128)} %speed_ref.1), kind=kLoop, calls=%fused_computation.77 | loop fusion | bytes 262144 | tf_op jit(solution)/shard_map/slice | solution.py:130
  1.7 3.0 %fusion.29 = f32[39,6,128]{2,1,0:T(8,128)S(1)} fusion(f32[1,128,128]{2,1,0:T(8,128)S(1)} %get-tuple-element.16, f32[38,128,128]{2,1,0:T(8,128)} %field_ref.1, s32[6]{0:T(128)S(1)} %get-tuple-element.18, s32[6]{0:T(128)S(1)} %get-tuple-element.19, pred[6]{0:T(512)(128)(4,1)S(1)} %iota_compare_fusion.4), kind=kOutput, calls=%fused_computation.41 | convolution fusion | flops 46646784 | bytes 2675766 | tf_op jit(solution)/shard_map/kr,sar->ska/dot_general | solution.py:121
  4.8 4.9 %collective-permute-start.2 = (f32[39,3,128]{2,1,0:T(4,128)S(1)}, f32[39,3,128]{2,1,0:T(4,128)S(1)}, u32[]{:S(2)}, u32[]{:S(2)}) collective-permute-start(f32[39,3,128]{2,1,0:T(4,128)S(1)} %get-tuple-element.15), channel_id=1, source_target_pairs={{0,1},{1,2},{2,3},{4,5},{5,6},{6,7},{8,9},{9,10},{10,11},{12,13},{... | collective-permute-start | bytes 179720 | tf_op jit(solution)/shard_map/ppermute | solution.py:135
  9.7 1.3 %collective-permute-start.3 = (f32[39,3,128]{2,1,0:T(4,128)S(1)}, f32[39,3,128]{2,1,0:T(4,128)S(1)}, u32[]{:S(2)}, u32[]{:S(2)}) collective-permute-start(f32[39,3,128]{2,1,0:T(4,128)S(1)} %get-tuple-element.14), channel_id=1, source_target_pairs={{1,0},{2,1},{3,2},{5,4},{6,5},{7,6},{9,8},{10,9},{11,10},{13,12},{... | collective-permute-start | bytes 179720 | tf_op jit(solution)/shard_map/ppermute | solution.py:136
  11.1 1.5 %collective-permute-start = (f32[39,3,128]{2,1,0:T(4,128)S(1)}, f32[39,3,128]{2,1,0:T(4,128)S(1)}, u32[]{:S(2)}, u32[]{:S(2)}) collective-permute-start(f32[39,3,128]{2,1,0:T(4,128)S(1)} %get-tuple-element.9), channel_id=1, source_target_pairs={{0,4},{4,8},{8,12},{12,16},{16,20},{20,24},{24,28},{1,5},{5,9},{9,... | collective-permute-start | bytes 179720 | tf_op jit(solution)/shard_map/ppermute | solution.py:28
  12.5 1.3 %collective-permute-start.1 = (f32[39,3,128]{2,1,0:T(4,128)S(1)}, f32[39,3,128]{2,1,0:T(4,128)S(1)}, u32[]{:S(2)}, u32[]{:S(2)}) collective-permute-start(f32[39,3,128]{2,1,0:T(4,128)S(1)} %get-tuple-element.8), channel_id=1, source_target_pairs={{4,0},{8,4},{12,8},{16,12},{20,16},{24,20},{28,24},{5,1},{9,5},{13... | collective-permute-start | bytes 179720 | tf_op jit(solution)/shard_map/ppermute | solution.py:28
  14.2 1.9 %collective-permute-done.3.right_ref.right_speed_ref = f32[39,3,128]{2,1,0:T(4,128)S(1)} collective-permute-done((f32[39,3,128]{2,1,0:T(4,128)S(1)}, f32[39,3,128]{2,1,0:T(4,128)S(1)}, u32[]{:S(2)}, u32[]{:S(2)}) %collective-permute-start.3) | collective-permute-done | bytes 59936 | tf_op jit(solution)/shard_map/ppermute | solution.py:136
  16.0 1.2 %collective-permute-done.1.bottom_ref.bottom_speed_ref = f32[39,3,128]{2,1,0:T(4,128)S(1)} collective-permute-done((f32[39,3,128]{2,1,0:T(4,128)S(1)}, f32[39,3,128]{2,1,0:T(4,128)S(1)}, u32[]{:S(2)}, u32[]{:S(2)}) %collective-permute-start.1) | collective-permute-done | bytes 59936 | tf_op jit(solution)/shard_map/ppermute | solution.py:28
  17.3 0.6 copy-done.6
  17.9 19.9 %shard_map.113 = f32[128,38,128]{2,1,0:T(8,128)} custom-call(f32[38,128,128]{2,1,0:T(8,128)} %field_ref.1, f32[2,128,128]{2,1,0:T(8,128)} %speed_ref.1, f32[39,3,128]{2,1,0:T(4,128)} %copy-done.5, f32[39,3,128]{2,1,0:T(4,128)} %copy-done.5, f32[39,3,128]{2,1,0:T(4,128)} %copy-done.6, f32[39,3,128]{2,1,0:T(4,128)} %copy-done.6, f32[39,3,128]{2,1,0:T(4,128)} %copy-done.3, ...), custom_call_target="tpu_custom_call" | custom-call | tf_op jit(solution)/shard_map/pallas_call | solution.py:144
  37.8 3.2 %fusion.13 = f32[128,128,38]{1,2,0:T(8,128)S(1)} fusion(f32[128,38,128]{2,1,0:T(8,128)} %shard_map.113, f32[38,38]{1,0:T(8,128)S(1)} %copy-done), kind=kOutput, calls=%fused_computation.24 | convolution fusion | flops 141950976 | bytes 4986512 | tf_op jit(solution)/shard_map/dot_general | solution.py:169
  41.0 2.6 %bitcast_subtract_fusion.4 = f32[38,128,128]{2,0,1:T(8,128)S(1)} fusion(f32[128,128,38]{1,2,0:T(8,128)S(1)} %fusion.13, f32[128,38,128]{2,1,0:T(8,128)S(1)} %copy-done.1, f32[128,128]{1,0:T(8,128)S(1)} %exponential_multiply_fusion, f32[38,38]{1,0:T(8,128)S(1)} %copy-done.7), kind=kOutput, calls=%fused_computation.13 | convolution fusion | flops 148176896 | bytes 7542416 | tf_op jit(solution)/shard_map/dot_general | solution.py:176
  43.5 1.3 %fusion.40 = f32[128,128,38]{1,2,0:T(8,128)S(1)} fusion(f32[38,128,128]{2,0,1:T(8,128)S(1)} %bitcast_subtract_fusion.4, f32[38,38]{1,0:T(8,128)S(1)} %copy-done), kind=kOutput, calls=%fused_computation.52 | convolution fusion | flops 141950976 | bytes 4986512 | tf_op jit(solution)/shard_map/dot_general | solution.py:169
  44.9 2.8 %bitcast_subtract_fusion.2 = f32[38,128,128]{2,0,1:T(8,128)S(1)} fusion(f32[38,128,128]{2,0,1:T(8,128)S(1)} %bitcast_subtract_fusion.4, f32[128,128,38]{1,2,0:T(8,128)S(1)} %fusion.40, f32[128,38,128]{2,1,0:T(8,128)S(1)} %copy-done.1, f32[128,128]{1,0:T(8,128)S(1)} %exponential_multiply_fusion, f32[38,38]{1,0:T(8,128)S(1)} %copy-done.7), kind=kOutput, calls=%fused_computation.9 | convolution fusion | flops 148176896 | bytes 10032784 | tf_op jit(solution)/shard_map/dot_general | solution.py:176
  47.7 1.3 %fusion.38 = f32[128,128,38]{1,2,0:T(8,128)S(1)} fusion(f32[38,128,128]{2,0,1:T(8,128)S(1)} %bitcast_subtract_fusion.2, f32[38,38]{1,0:T(8,128)S(1)} %copy-done), kind=kOutput, calls=%fused_computation.50 | convolution fusion | flops 141950976 | bytes 4986512 | tf_op jit(solution)/shard_map/dot_general | solution.py:169
  49.0 3.3 %fusion = f32[38,128,128]{2,0,1:T(8,128)S(1)} fusion(f32[128,38,128]{2,1,0:T(8,128)S(1)} %copy-done.1, f32[38,128,128]{2,0,1:T(8,128)S(1)} %bitcast_subtract_fusion.2, f32[128,128,38]{1,2,0:T(8,128)S(1)} %fusion.38, f32[128,128]{1,0:T(8,128)S(1)} %exponential_multiply_fusion, pred[128]{0:T(512)(128)(4,1)S(1)} %gt.22, f32[38,38]{1,0:T(8,128)S(1)} %copy-done.7), kind=kOutput, calls=%fused_computation.5 | convolution fusion | flops 148799488 | bytes 10032912 | tf_op jit(solution)/shard_map/dot_general | solution.py:176
  52.3 1.7 %convolution_bitcast_fusion = f32[4,128,128]{2,0,1:T(4,128)S(1)} fusion(f32[38,128,128]{2,0,1:T(8,128)S(1)} %fusion, f32[4,38]{1,0:T(4,128)S(1)} %copy-done.10), kind=kOutput, calls=%fused_computation.40 | convolution fusion | flops 29884416 | bytes 2753120 | tf_op jit(solution)/shard_map/dot_general | solution.py:182
  54.4 2.7 %collective-permute-start.4 = (f32[4,128]{1,0:T(4,128)S(1)}, f32[4,128]{1,0:T(4,128)S(1)}, u32[]{:S(2)}, u32[]{:S(2)}) collective-permute-start(f32[4,128]{1,0:T(4,128)S(1)} %broadcast_multiply_fusion), channel_id=1, source_target_pairs={{0,1},{1,0},{2,3},{3,2},{4,5},{5,4},{6,7},{7,6},{8,9},{9,8},{10,11... | collective-permute-start | bytes 6152 | tf_op jit(solution)/shard_map/ppermute | solution.py:192
  57.1 1.6 %collective-permute-done.4 = f32[4,128]{1,0:T(4,128)S(1)} collective-permute-done((f32[4,128]{1,0:T(4,128)S(1)}, f32[4,128]{1,0:T(4,128)S(1)}, u32[]{:S(2)}, u32[]{:S(2)}) %collective-permute-start.4) | collective-permute-done | bytes 2080 | tf_op jit(solution)/shard_map/ppermute | solution.py:192
  58.7 3.0 %collective-permute-start.5 = (f32[4,128]{1,0:T(4,128)S(1)}, f32[4,128]{1,0:T(4,128)S(1)}, u32[]{:S(2)}, u32[]{:S(2)}) collective-permute-start(f32[4,128]{1,0:T(4,128)S(1)} %fusion.51), channel_id=1, source_target_pairs={{0,2},{1,3},{2,0},{3,1},{4,6},{5,7},{6,4},{7,5},{8,10},{9,11},{10,... | collective-permute-start | bytes 6152 | tf_op jit(solution)/shard_map/ppermute | solution.py:192
  61.7 0.7 dynamic-slice_subtract_fusion.2
  62.5 1.9 %copy.14 = f32[38,128,128]{2,1,0:T(8,128)} copy(f32[38,128,128]{2,0,1:T(8,128)S(1)} %fusion) | data formatting | bytes 4980736
  64.4 1.6 %collective-permute-start.6 = (f32[1,4,128]{2,1,0:T(4,128)S(1)}, f32[1,4,128]{2,1,0:T(4,128)S(1)}, u32[]{:S(2)}, u32[]{:S(2)}) collective-permute-start(f32[1,4,128]{2,1,0:T(4,128)S(1)} %bitcast.112), channel_id=1, source_target_pairs={{0,4},{4,0},{8,12},{12,8},{16,20},{20,16},{24,28},{28,24},{1,5},{5... | collective-permute-start | bytes 6152 | tf_op jit(solution)/shard_map/ppermute | solution.py:215
  66.0 0.4 select_reduce_fusion.3
  66.8 2.4 %collective-permute-start.7 = (f32[2,4,128]{2,1,0:T(4,128)S(1)}, f32[2,4,128]{2,1,0:T(4,128)S(1)}, u32[]{:S(2)}, u32[]{:S(2)}) collective-permute-start(f32[2,4,128]{2,1,0:T(4,128)S(1)} %maximum_select_fusion.1), channel_id=1, source_target_pairs={{0,8},{4,12},{8,0},{12,4},{16,24},{20,28},{24,16},{28,20},{1,9},{5... | collective-permute-start | bytes 12296 | tf_op jit(solution)/shard_map/ppermute | solution.py:215
  69.2 0.4 select_reduce_fusion.2
  69.7 1.1 %collective-permute-done.7 = f32[2,4,128]{2,1,0:T(4,128)S(1)} collective-permute-done((f32[2,4,128]{2,1,0:T(4,128)S(1)}, f32[2,4,128]{2,1,0:T(4,128)S(1)}, u32[]{:S(2)}, u32[]{:S(2)}) %collective-permute-start.7) | collective-permute-done | bytes 4128 | tf_op jit(solution)/shard_map/ppermute | solution.py:215
  70.8 2.2 %collective-permute-start.8 = (f32[4,4,128]{2,1,0:T(4,128)S(1)}, f32[4,4,128]{2,1,0:T(4,128)S(1)}, u32[]{:S(2)}, u32[]{:S(2)}) collective-permute-start(f32[4,4,128]{2,1,0:T(4,128)S(1)} %maximum_select_fusion), channel_id=1, source_target_pairs={{0,16},{4,20},{8,24},{12,28},{16,0},{20,4},{24,8},{28,12},{1,17},{... | collective-permute-start | bytes 24584 | tf_op jit(solution)/shard_map/ppermute | solution.py:215
  73.0 0.8 select_reduce_fusion.1
  73.7 0.9 %collective-permute-done.8 = f32[4,4,128]{2,1,0:T(4,128)S(1)} collective-permute-done((f32[4,4,128]{2,1,0:T(4,128)S(1)}, f32[4,4,128]{2,1,0:T(4,128)S(1)}, u32[]{:S(2)}, u32[]{:S(2)}) %collective-permute-start.8) | collective-permute-done | bytes 8224 | tf_op jit(solution)/shard_map/ppermute | solution.py:215
  74.6 1.5 %select_reduce_fusion = f32[4,1024]{1,0:T(4,128)S(1)} fusion(f32[4,512]{1,0:T(4,128)S(1)} %bitcast.115, s32[4,1024]{1,0:T(4,128)S(1)} %get-tuple-element.12), kind=kLoop, calls=%fused_computation | loop fusion | flops 6287360 | bytes 40960 | tf_op jit(solution)/shard_map/reduce_sum | solution.py:202
  76.1 0.6 add_subtract_fusion
  (43 shorter events, 1.1 us)
Async XLA Ops:
  0.6 37.1 %copy-start = (f32[38,38]{1,0:T(8,128)S(1)}, f32[38,38]{1,0:T(8,128)}, u32[]{:S(2)}) copy-start(f32[38,38]{1,0:T(8,128)} %param.13) | copy-start | bytes 17332
  0.6 10.4 %copy-start.2 = (f32[38,128,128]{2,1,0:T(8,128)S(1)}, f32[38,128,128]{2,1,0:T(8,128)}, u32[]{:S(2)}) copy-start(f32[38,128,128]{2,1,0:T(8,128)} %field_ref.1) | copy-start | bytes 7471108
  1.7 12.1 %copy-start.8 = (f32[128,128]{1,0:T(8,128)S(1)}, f32[128,128]{1,0:T(8,128)}, u32[]{:S(2)}) copy-start(f32[128,128]{1,0:T(8,128)} %param.12) | copy-start | bytes 196612
  1.7 12.1 %copy-start.12 = (s32[64,1]{0,1:T(1,128)S(1)}, s32[64,1]{0,1:T(1,128)}, u32[]{:S(2)}) copy-start(s32[64,1]{0,1:T(1,128)} %param.15) | copy-start | bytes 772
  4.8 9.4 %collective-permute-start.2 = (f32[39,3,128]{2,1,0:T(4,128)S(1)}, f32[39,3,128]{2,1,0:T(4,128)S(1)}, u32[]{:S(2)}, u32[]{:S(2)}) collective-permute-start(f32[39,3,128]{2,1,0:T(4,128)S(1)} %get-tuple-element.15), channel_id=1, source_target_pairs={{0,1},{1,2},{2,3},{4,5},{5,6},{6,7},{8,9},{9,10},{10,11},{12,13},{... | collective-permute-start | bytes 179720 | tf_op jit(solution)/shard_map/ppermute | solution.py:135
  9.7 6.3 %collective-permute-start.3 = (f32[39,3,128]{2,1,0:T(4,128)S(1)}, f32[39,3,128]{2,1,0:T(4,128)S(1)}, u32[]{:S(2)}, u32[]{:S(2)}) collective-permute-start(f32[39,3,128]{2,1,0:T(4,128)S(1)} %get-tuple-element.14), channel_id=1, source_target_pairs={{1,0},{2,1},{3,2},{5,4},{6,5},{7,6},{9,8},{10,9},{11,10},{13,12},{... | collective-permute-start | bytes 179720 | tf_op jit(solution)/shard_map/ppermute | solution.py:136
  11.1 5.0 %collective-permute-start = (f32[39,3,128]{2,1,0:T(4,128)S(1)}, f32[39,3,128]{2,1,0:T(4,128)S(1)}, u32[]{:S(2)}, u32[]{:S(2)}) collective-permute-start(f32[39,3,128]{2,1,0:T(4,128)S(1)} %get-tuple-element.9), channel_id=1, source_target_pairs={{0,4},{4,8},{8,12},{12,16},{16,20},{20,24},{24,28},{1,5},{5,9},{9,... | collective-permute-start | bytes 179720 | tf_op jit(solution)/shard_map/ppermute | solution.py:28
  12.5 4.7 %collective-permute-start.1 = (f32[39,3,128]{2,1,0:T(4,128)S(1)}, f32[39,3,128]{2,1,0:T(4,128)S(1)}, u32[]{:S(2)}, u32[]{:S(2)}) collective-permute-start(f32[39,3,128]{2,1,0:T(4,128)S(1)} %get-tuple-element.8), channel_id=1, source_target_pairs={{4,0},{8,4},{12,8},{16,12},{20,16},{24,20},{28,24},{5,1},{9,5},{13... | collective-permute-start | bytes 179720 | tf_op jit(solution)/shard_map/ppermute | solution.py:28
  14.1 3.1 %copy-start.3 = (f32[39,3,128]{2,1,0:T(4,128)}, f32[39,3,128]{2,1,0:T(4,128)S(1)}, u32[]{:S(2)}) copy-start(f32[39,3,128]{2,1,0:T(4,128)S(1)} %collective-permute-done.2.left_ref.left_speed_ref) | copy-start | bytes 179716
  16.0 1.2 %copy-start.4 = (f32[39,3,128]{2,1,0:T(4,128)}, f32[39,3,128]{2,1,0:T(4,128)S(1)}, u32[]{:S(2)}) copy-start(f32[39,3,128]{2,1,0:T(4,128)S(1)} %collective-permute-done.3.right_ref.right_speed_ref) | copy-start | bytes 179716
  16.0 1.2 %copy-start.5 = (f32[39,3,128]{2,1,0:T(4,128)}, f32[39,3,128]{2,1,0:T(4,128)S(1)}, u32[]{:S(2)}) copy-start(f32[39,3,128]{2,1,0:T(4,128)S(1)} %collective-permute-done.top_ref.top_speed_ref) | copy-start | bytes 179716
  17.3 0.6 copy-start.6
  37.8 3.2 %copy-start.1 = (f32[128,38,128]{2,1,0:T(8,128)S(1)}, f32[128,38,128]{2,1,0:T(8,128)}, u32[]{:S(2)}) copy-start(f32[128,38,128]{2,1,0:T(8,128)} %shard_map.113) | copy-start | bytes 7471108
  37.8 3.2 %copy-start.7 = (f32[38,38]{1,0:T(8,128)S(1)}, f32[38,38]{1,0:T(8,128)}, u32[]{:S(2)}) copy-start(f32[38,38]{1,0:T(8,128)} %param.14) | copy-start | bytes 17332
  49.0 3.3 %copy-start.10 = (f32[4,38]{1,0:T(4,128)S(1)}, f32[4,38]{1,0:T(4,128)}, u32[]{:S(2)}) copy-start(f32[4,38]{1,0:T(4,128)} %param.16) | copy-start | bytes 1828
  52.3 1.7 %copy-start.11 = (f32[128]{0:T(128)S(1)}, f32[128]{0:T(128)}, u32[]{:S(2)}) copy-start(f32[128]{0:T(128)} %param.17) | copy-start | bytes 1540
  54.4 4.3 %collective-permute-start.4 = (f32[4,128]{1,0:T(4,128)S(1)}, f32[4,128]{1,0:T(4,128)S(1)}, u32[]{:S(2)}, u32[]{:S(2)}) collective-permute-start(f32[4,128]{1,0:T(4,128)S(1)} %broadcast_multiply_fusion), channel_id=1, source_target_pairs={{0,1},{1,0},{2,3},{3,2},{4,5},{5,4},{6,7},{7,6},{8,9},{9,8},{10,11... | collective-permute-start | bytes 6152 | tf_op jit(solution)/shard_map/ppermute | solution.py:192
  58.7 5.7 %collective-permute-start.5 = (f32[4,128]{1,0:T(4,128)S(1)}, f32[4,128]{1,0:T(4,128)S(1)}, u32[]{:S(2)}, u32[]{:S(2)}) collective-permute-start(f32[4,128]{1,0:T(4,128)S(1)} %fusion.51), channel_id=1, source_target_pairs={{0,2},{1,3},{2,0},{3,1},{4,6},{5,7},{6,4},{7,5},{8,10},{9,11},{10,... | collective-permute-start | bytes 6152 | tf_op jit(solution)/shard_map/ppermute | solution.py:192
  62.5 13.6 %copy-start.9 = (f32[4,1024]{1,0:T(4,128)S(1)}, f32[4,1024]{1,0:T(4,128)}, u32[]{:S(2)}) copy-start(f32[4,1024]{1,0:T(4,128)} %param.19) | copy-start | bytes 49156
  64.4 2.5 %collective-permute-start.6 = (f32[1,4,128]{2,1,0:T(4,128)S(1)}, f32[1,4,128]{2,1,0:T(4,128)S(1)}, u32[]{:S(2)}, u32[]{:S(2)}) collective-permute-start(f32[1,4,128]{2,1,0:T(4,128)S(1)} %bitcast.112), channel_id=1, source_target_pairs={{0,4},{4,0},{8,12},{12,8},{16,20},{20,16},{24,28},{28,24},{1,5},{5... | collective-permute-start | bytes 6152 | tf_op jit(solution)/shard_map/ppermute | solution.py:215
  66.8 4.0 %collective-permute-start.7 = (f32[2,4,128]{2,1,0:T(4,128)S(1)}, f32[2,4,128]{2,1,0:T(4,128)S(1)}, u32[]{:S(2)}, u32[]{:S(2)}) collective-permute-start(f32[2,4,128]{2,1,0:T(4,128)S(1)} %maximum_select_fusion.1), channel_id=1, source_target_pairs={{0,8},{4,12},{8,0},{12,4},{16,24},{20,28},{24,16},{28,20},{1,9},{5... | collective-permute-start | bytes 12296 | tf_op jit(solution)/shard_map/ppermute | solution.py:215
  70.8 3.8 %collective-permute-start.8 = (f32[4,4,128]{2,1,0:T(4,128)S(1)}, f32[4,4,128]{2,1,0:T(4,128)S(1)}, u32[]{:S(2)}, u32[]{:S(2)}) collective-permute-start(f32[4,4,128]{2,1,0:T(4,128)S(1)} %maximum_select_fusion), channel_id=1, source_target_pairs={{0,16},{4,20},{8,24},{12,28},{16,0},{20,4},{24,8},{28,12},{1,17},{... | collective-permute-start | bytes 24584 | tf_op jit(solution)/shard_map/ppermute | solution.py:215

commit v11 on v9

--- a/solution.py
+++ b/solution.py
@@ -169,7 +169,8 @@
         source = jnp.tensordot(
             linearized_kinetics_operator, current, axes=(1, 0), precision=CHEMISTRY_PRECISION
         ) - jnp.tanh(current)
-        defect = current - starting_composition_field - CHEM_STEP * acceleration_factor * source
+        step = CHEM_STEP * acceleration_factor * source
+        defect = -step if newton_step == 0 else current - starting_composition_field - step
         current = (
             current
             - defect

time: 76.6 us -> 76.5 us (level)
  no operation moved by 1% of the time
where the time goes in v11:
time: 76.5 us; the launch traced here: 76.2 us
  starting transfers between devices  20.9 us (27%)
  Pallas kernels  19.5 us (25%)
  matrix products  19.3 us (25%)
  waiting for transfers between devices  7.05 us (9%)
  other arithmetic  4.54 us (6%)
  local copies, waits for them, and re-layouts  3.88 us (5%)
  between operations  0.99 us (1%)
    pallas_call x1, Pallas kernels, transport(): pl.pallas_call(transport_kernel, grid=(species_count // group,), in_specs...  19.5 us
    dot_general x3, matrix products, kinetics_advance(): jnp.tensordot(frozen_jacobian_inverse_addend, defect, axes=(1, 0), precis...  8.52 us
    ppermute x3, starting transfers between devices, sampled_profile(): other = lax.ppermute(blocks, axis, pairs)  6.18 us
    dot_general x3, matrix products, kinetics_advance(): jnp.tensordot(linearized_kinetics_operator, current, axes=(1, 0), precisi...  5.81 us
    ppermute x2, starting transfers between devices, butterfly_sum(): part = part + lax.ppermute(part, axis, pairs)  5.74 us
    ppermute x1, starting transfers between devices, transport(): left = lax.ppermute(high_columns, 'radial', up)  4.93 us
    reduce_sum x4, other arithmetic, pick_samples(): jnp.sum(jnp.where(local[:, None, :] == cells, flat[:, :, None], 0.0), axi...  3.1 us
    dot_general x1, matrix products, edge_columns(): jnp.einsum('kr,sar->ska', pick.astype(field.dtype), field, precision=HIGH...  2.98 us
  transfers between devices with their start and end apart: 9, of which 6 were waited for; matrix products, arithmetic and copies ran while one was open for 6% of the time, Pallas kernels for 0%

profile of v11, /device:TPU:0, one launch (start us, length us, event | category | flops | bytes accessed | tf_op | source)
XLA Modules:
  0.0 76.2 jit_solution(8448124393163191917)
XLA Ops:
  0.7 1.0 %fusion.49 = (f32[1,128,128]{2,1,0:T(8,128)S(1)}, f32[1,128,128]{2,1,0:T(8,128)S(1)}) fusion(f32[2,128,128]{2,1,0:T(8,128)} %speed_ref.1), kind=kLoop, calls=%fused_computation.75 | loop fusion | bytes 262144 | tf_op jit(solution)/shard_map/slice | solution.py:130
  1.7 3.0 %fusion.25 = f32[39,6,128]{2,1,0:T(8,128)S(1)} fusion(f32[1,128,128]{2,1,0:T(8,128)S(1)} %get-tuple-element.16, f32[38,128,128]{2,1,0:T(8,128)} %field_ref.1, s32[6]{0:T(128)S(1)} %get-tuple-element.18, s32[6]{0:T(128)S(1)} %get-tuple-element.19, pred[6]{0:T(512)(128)(4,1)S(1)} %iota_compare_fusion.4), kind=kOutput, calls=%fused_computation.39 | convolution fusion | flops 46646784 | bytes 2675766 | tf_op jit(solution)/shard_map/kr,sar->ska/dot_general | solution.py:121
  4.8 4.9 %collective-permute-start.2 = (f32[39,3,128]{2,1,0:T(4,128)S(1)}, f32[39,3,128]{2,1,0:T(4,128)S(1)}, u32[]{:S(2)}, u32[]{:S(2)}) collective-permute-start(f32[39,3,128]{2,1,0:T(4,128)S(1)} %get-tuple-element.15), channel_id=1, source_target_pairs={{0,1},{1,2},{2,3},{4,5},{5,6},{6,7},{8,9},{9,10},{10,11},{12,13},{... | collective-permute-start | bytes 179720 | tf_op jit(solution)/shard_map/ppermute | solution.py:135
  9.7 1.3 %collective-permute-start.3 = (f32[39,3,128]{2,1,0:T(4,128)S(1)}, f32[39,3,128]{2,1,0:T(4,128)S(1)}, u32[]{:S(2)}, u32[]{:S(2)}) collective-permute-start(f32[39,3,128]{2,1,0:T(4,128)S(1)} %get-tuple-element.14), channel_id=1, source_target_pairs={{1,0},{2,1},{3,2},{5,4},{6,5},{7,6},{9,8},{10,9},{11,10},{13,12},{... | collective-permute-start | bytes 179720 | tf_op jit(solution)/shard_map/ppermute | solution.py:136
  11.1 1.5 %collective-permute-start = (f32[39,3,128]{2,1,0:T(4,128)S(1)}, f32[39,3,128]{2,1,0:T(4,128)S(1)}, u32[]{:S(2)}, u32[]{:S(2)}) collective-permute-start(f32[39,3,128]{2,1,0:T(4,128)S(1)} %get-tuple-element.9), channel_id=1, source_target_pairs={{0,4},{4,8},{8,12},{12,16},{16,20},{20,24},{24,28},{1,5},{5,9},{9,... | collective-permute-start | bytes 179720 | tf_op jit(solution)/shard_map/ppermute | solution.py:28
  12.5 1.3 %collective-permute-start.1 = (f32[39,3,128]{2,1,0:T(4,128)S(1)}, f32[39,3,128]{2,1,0:T(4,128)S(1)}, u32[]{:S(2)}, u32[]{:S(2)}) collective-permute-start(f32[39,3,128]{2,1,0:T(4,128)S(1)} %get-tuple-element.8), channel_id=1, source_target_pairs={{4,0},{8,4},{12,8},{16,12},{20,16},{24,20},{28,24},{5,1},{9,5},{13... | collective-permute-start | bytes 179720 | tf_op jit(solution)/shard_map/ppermute | solution.py:28
  14.2 1.9 %collective-permute-done.3.right_ref.right_speed_ref = f32[39,3,128]{2,1,0:T(4,128)S(1)} collective-permute-done((f32[39,3,128]{2,1,0:T(4,128)S(1)}, f32[39,3,128]{2,1,0:T(4,128)S(1)}, u32[]{:S(2)}, u32[]{:S(2)}) %collective-permute-start.3) | collective-permute-done | bytes 59936 | tf_op jit(solution)/shard_map/ppermute | solution.py:136
  16.0 1.2 %collective-permute-done.1.bottom_ref.bottom_speed_ref = f32[39,3,128]{2,1,0:T(4,128)S(1)} collective-permute-done((f32[39,3,128]{2,1,0:T(4,128)S(1)}, f32[39,3,128]{2,1,0:T(4,128)S(1)}, u32[]{:S(2)}, u32[]{:S(2)}) %collective-permute-start.1) | collective-permute-done | bytes 59936 | tf_op jit(solution)/shard_map/ppermute | solution.py:28
  17.3 0.6 copy-done.6
  17.9 19.5 %shard_map.113 = f32[128,38,128]{2,1,0:T(8,128)} custom-call(f32[38,128,128]{2,1,0:T(8,128)} %field_ref.1, f32[2,128,128]{2,1,0:T(8,128)} %speed_ref.1, f32[39,3,128]{2,1,0:T(4,128)} %copy-done.5, f32[39,3,128]{2,1,0:T(4,128)} %copy-done.5, f32[39,3,128]{2,1,0:T(4,128)} %copy-done.6, f32[39,3,128]{2,1,0:T(4,128)} %copy-done.6, f32[39,3,128]{2,1,0:T(4,128)} %copy-done.3, ...), custom_call_target="tpu_custom_call" | custom-call | tf_op jit(solution)/shard_map/pallas_call | solution.py:144
  37.4 3.2 %fusion.7 = f32[128,128,38]{1,2,0:T(8,128)S(1)} fusion(f32[128,38,128]{2,1,0:T(8,128)} %shard_map.113, f32[38,38]{1,0:T(8,128)S(1)} %copy-done), kind=kOutput, calls=%fused_computation.21 | convolution fusion | flops 141950976 | bytes 4986512 | tf_op jit(solution)/shard_map/dot_general | solution.py:169
  40.6 2.4 %bitcast_subtract_fusion.4 = f32[38,128,128]{2,0,1:T(8,128)S(1)} fusion(f32[128,38,128]{2,1,0:T(8,128)S(1)} %copy-done.1, f32[128,128,38]{1,2,0:T(8,128)S(1)} %fusion.7, f32[128,128]{1,0:T(8,128)S(1)} %exponential_multiply_fusion, f32[38,38]{1,0:T(8,128)S(1)} %copy-done.7), kind=kOutput, calls=%fused_computation.13 | convolution fusion | flops 146931712 | bytes 7542416 | tf_op jit(solution)/shard_map/dot_general | solution.py:177
  43.0 1.3 %fusion.36 = f32[128,128,38]{1,2,0:T(8,128)S(1)} fusion(f32[38,128,128]{2,0,1:T(8,128)S(1)} %bitcast_subtract_fusion.4, f32[38,38]{1,0:T(8,128)S(1)} %copy-done), kind=kOutput, calls=%fused_computation.50 | convolution fusion | flops 141950976 | bytes 4986512 | tf_op jit(solution)/shard_map/dot_general | solution.py:169
  44.4 2.9 %bitcast_subtract_fusion.2 = f32[38,128,128]{2,0,1:T(8,128)S(1)} fusion(f32[38,128,128]{2,0,1:T(8,128)S(1)} %bitcast_subtract_fusion.4, f32[128,128,38]{1,2,0:T(8,128)S(1)} %fusion.36, f32[128,38,128]{2,1,0:T(8,128)S(1)} %copy-done.1, f32[128,128]{1,0:T(8,128)S(1)} %exponential_multiply_fusion, f32[38,38]{1,0:T(8,128)S(1)} %copy-done.7), kind=kOutput, calls=%fused_computation.9 | convolution fusion | flops 148176896 | bytes 10032784 | tf_op jit(solution)/shard_map/dot_general | solution.py:177
  47.2 1.3 %fusion.34 = f32[128,128,38]{1,2,0:T(8,128)S(1)} fusion(f32[38,128,128]{2,0,1:T(8,128)S(1)} %bitcast_subtract_fusion.2, f32[38,38]{1,0:T(8,128)S(1)} %copy-done), kind=kOutput, calls=%fused_computation.48 | convolution fusion | flops 141950976 | bytes 4986512 | tf_op jit(solution)/shard_map/dot_general | solution.py:169
  48.6 3.3 %fusion = f32[38,128,128]{2,0,1:T(8,128)S(1)} fusion(f32[128,38,128]{2,1,0:T(8,128)S(1)} %copy-done.1, f32[38,128,128]{2,0,1:T(8,128)S(1)} %bitcast_subtract_fusion.2, f32[128,128,38]{1,2,0:T(8,128)S(1)} %fusion.34, f32[128,128]{1,0:T(8,128)S(1)} %exponential_multiply_fusion, pred[128]{0:T(512)(128)(4,1)S(1)} %gt.22, f32[38,38]{1,0:T(8,128)S(1)} %copy-done.7), kind=kOutput, calls=%fused_computation.5 | convolution fusion | flops 148799488 | bytes 10032912 | tf_op jit(solution)/shard_map/dot_general | solution.py:177
  51.9 1.7 %convolution_bitcast_fusion = f32[4,128,128]{2,0,1:T(4,128)S(1)} fusion(f32[38,128,128]{2,0,1:T(8,128)S(1)} %fusion, f32[4,38]{1,0:T(4,128)S(1)} %copy-done.10), kind=kOutput, calls=%fused_computation.38 | convolution fusion | flops 29884416 | bytes 2753120 | tf_op jit(solution)/shard_map/dot_general | solution.py:183
  53.9 2.7 %collective-permute-start.4 = (f32[4,128]{1,0:T(4,128)S(1)}, f32[4,128]{1,0:T(4,128)S(1)}, u32[]{:S(2)}, u32[]{:S(2)}) collective-permute-start(f32[4,128]{1,0:T(4,128)S(1)} %broadcast_multiply_fusion), channel_id=1, source_target_pairs={{0,1},{1,0},{2,3},{3,2},{4,5},{5,4},{6,7},{7,6},{8,9},{9,8},{10,11... | collective-permute-start | bytes 6152 | tf_op jit(solution)/shard_map/ppermute | solution.py:193
  56.6 1.6 %collective-permute-done.4 = f32[4,128]{1,0:T(4,128)S(1)} collective-permute-done((f32[4,128]{1,0:T(4,128)S(1)}, f32[4,128]{1,0:T(4,128)S(1)}, u32[]{:S(2)}, u32[]{:S(2)}) %collective-permute-start.4) | collective-permute-done | bytes 2080 | tf_op jit(solution)/shard_map/ppermute | solution.py:193
  58.2 3.0 %collective-permute-start.5 = (f32[4,128]{1,0:T(4,128)S(1)}, f32[4,128]{1,0:T(4,128)S(1)}, u32[]{:S(2)}, u32[]{:S(2)}) collective-permute-start(f32[4,128]{1,0:T(4,128)S(1)} %fusion.47), channel_id=1, source_target_pairs={{0,2},{1,3},{2,0},{3,1},{4,6},{5,7},{6,4},{7,5},{8,10},{9,11},{10,... | collective-permute-start | bytes 6152 | tf_op jit(solution)/shard_map/ppermute | solution.py:193
  61.2 0.7 dynamic-slice_subtract_fusion.2
  62.0 1.9 %copy.14 = f32[38,128,128]{2,1,0:T(8,128)} copy(f32[38,128,128]{2,0,1:T(8,128)S(1)} %fusion) | data formatting | bytes 4980736
  63.9 1.6 %collective-permute-start.6 = (f32[1,4,128]{2,1,0:T(4,128)S(1)}, f32[1,4,128]{2,1,0:T(4,128)S(1)}, u32[]{:S(2)}, u32[]{:S(2)}) collective-permute-start(f32[1,4,128]{2,1,0:T(4,128)S(1)} %bitcast.114), channel_id=1, source_target_pairs={{0,4},{4,0},{8,12},{12,8},{16,20},{20,16},{24,28},{28,24},{1,5},{5... | collective-permute-start | bytes 6152 | tf_op jit(solution)/shard_map/ppermute | solution.py:216
  65.5 0.4 select_reduce_fusion.3
  66.3 2.4 %collective-permute-start.7 = (f32[2,4,128]{2,1,0:T(4,128)S(1)}, f32[2,4,128]{2,1,0:T(4,128)S(1)}, u32[]{:S(2)}, u32[]{:S(2)}) collective-permute-start(f32[2,4,128]{2,1,0:T(4,128)S(1)} %maximum_select_fusion.1), channel_id=1, source_target_pairs={{0,8},{4,12},{8,0},{12,4},{16,24},{20,28},{24,16},{28,20},{1,9},{5... | collective-permute-start | bytes 12296 | tf_op jit(solution)/shard_map/ppermute | solution.py:216
  68.7 0.4 select_reduce_fusion.2
  69.2 1.1 %collective-permute-done.7 = f32[2,4,128]{2,1,0:T(4,128)S(1)} collective-permute-done((f32[2,4,128]{2,1,0:T(4,128)S(1)}, f32[2,4,128]{2,1,0:T(4,128)S(1)}, u32[]{:S(2)}, u32[]{:S(2)}) %collective-permute-start.7) | collective-permute-done | bytes 4128 | tf_op jit(solution)/shard_map/ppermute | solution.py:216
  70.3 2.1 %collective-permute-start.8 = (f32[4,4,128]{2,1,0:T(4,128)S(1)}, f32[4,4,128]{2,1,0:T(4,128)S(1)}, u32[]{:S(2)}, u32[]{:S(2)}) collective-permute-start(f32[4,4,128]{2,1,0:T(4,128)S(1)} %maximum_select_fusion), channel_id=1, source_target_pairs={{0,16},{4,20},{8,24},{12,28},{16,0},{20,4},{24,8},{28,12},{1,17},{... | collective-permute-start | bytes 24584 | tf_op jit(solution)/shard_map/ppermute | solution.py:216
  72.5 0.8 select_reduce_fusion.1
  73.2 0.9 %collective-permute-done.8 = f32[4,4,128]{2,1,0:T(4,128)S(1)} collective-permute-done((f32[4,4,128]{2,1,0:T(4,128)S(1)}, f32[4,4,128]{2,1,0:T(4,128)S(1)}, u32[]{:S(2)}, u32[]{:S(2)}) %collective-permute-start.8) | collective-permute-done | bytes 8224 | tf_op jit(solution)/shard_map/ppermute | solution.py:216
  74.1 1.5 %select_reduce_fusion = f32[4,1024]{1,0:T(4,128)S(1)} fusion(f32[4,512]{1,0:T(4,128)S(1)} %bitcast.117, s32[4,1024]{1,0:T(4,128)S(1)} %get-tuple-element.12), kind=kLoop, calls=%fused_computation | loop fusion | flops 6287360 | bytes 40960 | tf_op jit(solution)/shard_map/reduce_sum | solution.py:203
  75.6 0.6 add_subtract_fusion
  (43 shorter events, 1.1 us)
Async XLA Ops:
  0.6 36.8 %copy-start = (f32[38,38]{1,0:T(8,128)S(1)}, f32[38,38]{1,0:T(8,128)}, u32[]{:S(2)}) copy-start(f32[38,38]{1,0:T(8,128)} %param.13) | copy-start | bytes 17332
  0.6 10.4 %copy-start.2 = (f32[38,128,128]{2,1,0:T(8,128)S(1)}, f32[38,128,128]{2,1,0:T(8,128)}, u32[]{:S(2)}) copy-start(f32[38,128,128]{2,1,0:T(8,128)} %field_ref.1) | copy-start | bytes 7471108
  1.7 12.1 %copy-start.8 = (f32[128,128]{1,0:T(8,128)S(1)}, f32[128,128]{1,0:T(8,128)}, u32[]{:S(2)}) copy-start(f32[128,128]{1,0:T(8,128)} %param.12) | copy-start | bytes 196612
  1.7 12.1 %copy-start.12 = (s32[64,1]{0,1:T(1,128)S(1)}, s32[64,1]{0,1:T(1,128)}, u32[]{:S(2)}) copy-start(s32[64,1]{0,1:T(1,128)} %param.15) | copy-start | bytes 772
  4.8 9.4 %collective-permute-start.2 = (f32[39,3,128]{2,1,0:T(4,128)S(1)}, f32[39,3,128]{2,1,0:T(4,128)S(1)}, u32[]{:S(2)}, u32[]{:S(2)}) collective-permute-start(f32[39,3,128]{2,1,0:T(4,128)S(1)} %get-tuple-element.15), channel_id=1, source_target_pairs={{0,1},{1,2},{2,3},{4,5},{5,6},{6,7},{8,9},{9,10},{10,11},{12,13},{... | collective-permute-start | bytes 179720 | tf_op jit(solution)/shard_map/ppermute | solution.py:135
  9.7 6.3 %collective-permute-start.3 = (f32[39,3,128]{2,1,0:T(4,128)S(1)}, f32[39,3,128]{2,1,0:T(4,128)S(1)}, u32[]{:S(2)}, u32[]{:S(2)}) collective-permute-start(f32[39,3,128]{2,1,0:T(4,128)S(1)} %get-tuple-element.14), channel_id=1, source_target_pairs={{1,0},{2,1},{3,2},{5,4},{6,5},{7,6},{9,8},{10,9},{11,10},{13,12},{... | collective-permute-start | bytes 179720 | tf_op jit(solution)/shard_map/ppermute | solution.py:136
  11.1 5.0 %collective-permute-start = (f32[39,3,128]{2,1,0:T(4,128)S(1)}, f32[39,3,128]{2,1,0:T(4,128)S(1)}, u32[]{:S(2)}, u32[]{:S(2)}) collective-permute-start(f32[39,3,128]{2,1,0:T(4,128)S(1)} %get-tuple-element.9), channel_id=1, source_target_pairs={{0,4},{4,8},{8,12},{12,16},{16,20},{20,24},{24,28},{1,5},{5,9},{9,... | collective-permute-start | bytes 179720 | tf_op jit(solution)/shard_map/ppermute | solution.py:28
  12.5 4.7 %collective-permute-start.1 = (f32[39,3,128]{2,1,0:T(4,128)S(1)}, f32[39,3,128]{2,1,0:T(4,128)S(1)}, u32[]{:S(2)}, u32[]{:S(2)}) collective-permute-start(f32[39,3,128]{2,1,0:T(4,128)S(1)} %get-tuple-element.8), channel_id=1, source_target_pairs={{4,0},{8,4},{12,8},{16,12},{20,16},{24,20},{28,24},{5,1},{9,5},{13... | collective-permute-start | bytes 179720 | tf_op jit(solution)/shard_map/ppermute | solution.py:28
  14.1 3.1 %copy-start.3 = (f32[39,3,128]{2,1,0:T(4,128)}, f32[39,3,128]{2,1,0:T(4,128)S(1)}, u32[]{:S(2)}) copy-start(f32[39,3,128]{2,1,0:T(4,128)S(1)} %collective-permute-done.2.left_ref.left_speed_ref) | copy-start | bytes 179716
  16.0 1.2 %copy-start.4 = (f32[39,3,128]{2,1,0:T(4,128)}, f32[39,3,128]{2,1,0:T(4,128)S(1)}, u32[]{:S(2)}) copy-start(f32[39,3,128]{2,1,0:T(4,128)S(1)} %collective-permute-done.3.right_ref.right_speed_ref) | copy-start | bytes 179716
  16.0 1.2 %copy-start.5 = (f32[39,3,128]{2,1,0:T(4,128)}, f32[39,3,128]{2,1,0:T(4,128)S(1)}, u32[]{:S(2)}) copy-start(f32[39,3,128]{2,1,0:T(4,128)S(1)} %collective-permute-done.top_ref.top_speed_ref) | copy-start | bytes 179716
  17.3 0.6 copy-start.6
  37.4 3.2 %copy-start.1 = (f32[128,38,128]{2,1,0:T(8,128)S(1)}, f32[128,38,128]{2,1,0:T(8,128)}, u32[]{:S(2)}) copy-start(f32[128,38,128]{2,1,0:T(8,128)} %shard_map.113) | copy-start | bytes 7471108
  37.4 3.2 %copy-start.7 = (f32[38,38]{1,0:T(8,128)S(1)}, f32[38,38]{1,0:T(8,128)}, u32[]{:S(2)}) copy-start(f32[38,38]{1,0:T(8,128)} %param.14) | copy-start | bytes 17332
  48.5 3.3 %copy-start.10 = (f32[4,38]{1,0:T(4,128)S(1)}, f32[4,38]{1,0:T(4,128)}, u32[]{:S(2)}) copy-start(f32[4,38]{1,0:T(4,128)} %param.16) | copy-start | bytes 1828
  51.8 1.7 %copy-start.11 = (f32[128]{0:T(128)S(1)}, f32[128]{0:T(128)}, u32[]{:S(2)}) copy-start(f32[128]{0:T(128)} %param.17) | copy-start | bytes 1540
  53.9 4.3 %collective-permute-start.4 = (f32[4,128]{1,0:T(4,128)S(1)}, f32[4,128]{1,0:T(4,128)S(1)}, u32[]{:S(2)}, u32[]{:S(2)}) collective-permute-start(f32[4,128]{1,0:T(4,128)S(1)} %broadcast_multiply_fusion), channel_id=1, source_target_pairs={{0,1},{1,0},{2,3},{3,2},{4,5},{5,4},{6,7},{7,6},{8,9},{9,8},{10,11... | collective-permute-start | bytes 6152 | tf_op jit(solution)/shard_map/ppermute | solution.py:193
  58.2 5.7 %collective-permute-start.5 = (f32[4,128]{1,0:T(4,128)S(1)}, f32[4,128]{1,0:T(4,128)S(1)}, u32[]{:S(2)}, u32[]{:S(2)}) collective-permute-start(f32[4,128]{1,0:T(4,128)S(1)} %fusion.47), channel_id=1, source_target_pairs={{0,2},{1,3},{2,0},{3,1},{4,6},{5,7},{6,4},{7,5},{8,10},{9,11},{10,... | collective-permute-start | bytes 6152 | tf_op jit(solution)/shard_map/ppermute | solution.py:193
  62.0 13.6 %copy-start.9 = (f32[4,1024]{1,0:T(4,128)S(1)}, f32[4,1024]{1,0:T(4,128)}, u32[]{:S(2)}) copy-start(f32[4,1024]{1,0:T(4,128)} %param.19) | copy-start | bytes 49156
  63.9 2.5 %collective-permute-start.6 = (f32[1,4,128]{2,1,0:T(4,128)S(1)}, f32[1,4,128]{2,1,0:T(4,128)S(1)}, u32[]{:S(2)}, u32[]{:S(2)}) collective-permute-start(f32[1,4,128]{2,1,0:T(4,128)S(1)} %bitcast.114), channel_id=1, source_target_pairs={{0,4},{4,0},{8,12},{12,8},{16,20},{20,16},{24,28},{28,24},{1,5},{5... | collective-permute-start | bytes 6152 | tf_op jit(solution)/shard_map/ppermute | solution.py:216
  66.3 4.0 %collective-permute-start.7 = (f32[2,4,128]{2,1,0:T(4,128)S(1)}, f32[2,4,128]{2,1,0:T(4,128)S(1)}, u32[]{:S(2)}, u32[]{:S(2)}) collective-permute-start(f32[2,4,128]{2,1,0:T(4,128)S(1)} %maximum_select_fusion.1), channel_id=1, source_target_pairs={{0,8},{4,12},{8,0},{12,4},{16,24},{20,28},{24,16},{28,20},{1,9},{5... | collective-permute-start | bytes 12296 | tf_op jit(solution)/shard_map/ppermute | solution.py:216
  70.3 3.8 %collective-permute-start.8 = (f32[4,4,128]{2,1,0:T(4,128)S(1)}, f32[4,4,128]{2,1,0:T(4,128)S(1)}, u32[]{:S(2)}, u32[]{:S(2)}) collective-permute-start(f32[4,4,128]{2,1,0:T(4,128)S(1)} %maximum_select_fusion), channel_id=1, source_target_pairs={{0,16},{4,20},{8,24},{12,28},{16,0},{20,4},{24,8},{28,12},{1,17},{... | collective-permute-start | bytes 24584 | tf_op jit(solution)/shard_map/ppermute | solution.py:216

commit v12 on v11

--- a/solution.py
+++ b/solution.py
@@ -180,8 +180,8 @@
 
 
 def absorbance_profile(field, molar_absorptivity_table, spokewise_sightline_length):
-    mixed = jnp.tensordot(molar_absorptivity_table, field, axes=(1, 0), precision=HIGHEST)
-    return jnp.dot(mixed, spokewise_sightline_length, precision=HIGHEST)
+    mixed = jnp.tensordot(molar_absorptivity_table, field, axes=(1, 0), precision=CHEMISTRY_PRECISION)
+    return jnp.dot(mixed, spokewise_sightline_length, precision=CHEMISTRY_PRECISION)
 
 
 def butterfly_sum(part, axis):

time: 76.5 us -> 75.5 us (0.987)
  matrix products: 19.3 us -> 18.3 us
    dot_general x2, matrix products: 2.02 us -> 1 us  [the longest x1 0.81 us: absorbance_profile(): jnp.tensordot(molar_absorptivity_table, field, axes=(1, 0), precision=CHE...]
where the time goes in v12:
time: 75.5 us; the launch traced here: 75.1 us
  starting transfers between devices  20.9 us (28%)
  Pallas kernels  19.5 us (26%)
  matrix products  18.3 us (24%)
  waiting for transfers between devices  7.04 us (9%)
  other arithmetic  4.54 us (6%)
  local copies, waits for them, and re-layouts  3.88 us (5%)
  between operations  0.99 us (1%)
    pallas_call x1, Pallas kernels, transport(): pl.pallas_call(transport_kernel, grid=(species_count // group,), in_specs...  19.5 us
    dot_general x3, matrix products, kinetics_advance(): jnp.tensordot(frozen_jacobian_inverse_addend, defect, axes=(1, 0), precis...  8.52 us
    ppermute x3, starting transfers between devices, sampled_profile(): other = lax.ppermute(blocks, axis, pairs)  6.18 us
    dot_general x3, matrix products, kinetics_advance(): jnp.tensordot(linearized_kinetics_operator, current, axes=(1, 0), precisi...  5.81 us
    ppermute x2, starting transfers between devices, butterfly_sum(): part = part + lax.ppermute(part, axis, pairs)  5.71 us
    ppermute x1, starting transfers between devices, transport(): left = lax.ppermute(high_columns, 'radial', up)  4.93 us
    reduce_sum x4, other arithmetic, pick_samples(): jnp.sum(jnp.where(local[:, None, :] == cells, flat[:, :, None], 0.0), axi...  3.1 us
    dot_general x1, matrix products, edge_columns(): jnp.einsum('kr,sar->ska', pick.astype(field.dtype), field, precision=HIGH...  2.98 us
  transfers between devices with their start and end apart: 9, of which 6 were waited for; matrix products, arithmetic and copies ran while one was open for 6% of the time, Pallas kernels for 0%

profile of v12, /device:TPU:0, one launch (start us, length us, event | category | flops | bytes accessed | tf_op | source)
XLA Modules:
  0.0 75.1 jit_solution(4007181317935899114)
XLA Ops:
  0.7 1.0 %fusion.49 = (f32[1,128,128]{2,1,0:T(8,128)S(1)}, f32[1,128,128]{2,1,0:T(8,128)S(1)}) fusion(f32[2,128,128]{2,1,0:T(8,128)} %speed_ref.1), kind=kLoop, calls=%fused_computation.75 | loop fusion | bytes 262144 | tf_op jit(solution)/shard_map/slice | solution.py:130
  1.7 3.0 %fusion.25 = f32[39,6,128]{2,1,0:T(8,128)S(1)} fusion(f32[1,128,128]{2,1,0:T(8,128)S(1)} %get-tuple-element.16, f32[38,128,128]{2,1,0:T(8,128)} %field_ref.1, s32[6]{0:T(128)S(1)} %get-tuple-element.18, s32[6]{0:T(128)S(1)} %get-tuple-element.19, pred[6]{0:T(512)(128)(4,1)S(1)} %iota_compare_fusion.4), kind=kOutput, calls=%fused_computation.39 | convolution fusion | flops 46646784 | bytes 2675766 | tf_op jit(solution)/shard_map/kr,sar->ska/dot_general | solution.py:121
  4.8 4.9 %collective-permute-start.2 = (f32[39,3,128]{2,1,0:T(4,128)S(1)}, f32[39,3,128]{2,1,0:T(4,128)S(1)}, u32[]{:S(2)}, u32[]{:S(2)}) collective-permute-start(f32[39,3,128]{2,1,0:T(4,128)S(1)} %get-tuple-element.15), channel_id=1, source_target_pairs={{0,1},{1,2},{2,3},{4,5},{5,6},{6,7},{8,9},{9,10},{10,11},{12,13},{... | collective-permute-start | bytes 179720 | tf_op jit(solution)/shard_map/ppermute | solution.py:135
  9.7 1.3 %collective-permute-start.3 = (f32[39,3,128]{2,1,0:T(4,128)S(1)}, f32[39,3,128]{2,1,0:T(4,128)S(1)}, u32[]{:S(2)}, u32[]{:S(2)}) collective-permute-start(f32[39,3,128]{2,1,0:T(4,128)S(1)} %get-tuple-element.14), channel_id=1, source_target_pairs={{1,0},{2,1},{3,2},{5,4},{6,5},{7,6},{9,8},{10,9},{11,10},{13,12},{... | collective-permute-start | bytes 179720 | tf_op jit(solution)/shard_map/ppermute | solution.py:136
  11.1 1.5 %collective-permute-start = (f32[39,3,128]{2,1,0:T(4,128)S(1)}, f32[39,3,128]{2,1,0:T(4,128)S(1)}, u32[]{:S(2)}, u32[]{:S(2)}) collective-permute-start(f32[39,3,128]{2,1,0:T(4,128)S(1)} %get-tuple-element.9), channel_id=1, source_target_pairs={{0,4},{4,8},{8,12},{12,16},{16,20},{20,24},{24,28},{1,5},{5,9},{9,... | collective-permute-start | bytes 179720 | tf_op jit(solution)/shard_map/ppermute | solution.py:28
  12.5 1.3 %collective-permute-start.1 = (f32[39,3,128]{2,1,0:T(4,128)S(1)}, f32[39,3,128]{2,1,0:T(4,128)S(1)}, u32[]{:S(2)}, u32[]{:S(2)}) collective-permute-start(f32[39,3,128]{2,1,0:T(4,128)S(1)} %get-tuple-element.8), channel_id=1, source_target_pairs={{4,0},{8,4},{12,8},{16,12},{20,16},{24,20},{28,24},{5,1},{9,5},{13... | collective-permute-start | bytes 179720 | tf_op jit(solution)/shard_map/ppermute | solution.py:28
  14.2 1.9 %collective-permute-done.3.right_ref.right_speed_ref = f32[39,3,128]{2,1,0:T(4,128)S(1)} collective-permute-done((f32[39,3,128]{2,1,0:T(4,128)S(1)}, f32[39,3,128]{2,1,0:T(4,128)S(1)}, u32[]{:S(2)}, u32[]{:S(2)}) %collective-permute-start.3) | collective-permute-done | bytes 59936 | tf_op jit(solution)/shard_map/ppermute | solution.py:136
  16.0 1.2 %collective-permute-done.1.bottom_ref.bottom_speed_ref = f32[39,3,128]{2,1,0:T(4,128)S(1)} collective-permute-done((f32[39,3,128]{2,1,0:T(4,128)S(1)}, f32[39,3,128]{2,1,0:T(4,128)S(1)}, u32[]{:S(2)}, u32[]{:S(2)}) %collective-permute-start.1) | collective-permute-done | bytes 59936 | tf_op jit(solution)/shard_map/ppermute | solution.py:28
  17.3 0.6 copy-done.6
  17.9 19.5 %shard_map.113 = f32[128,38,128]{2,1,0:T(8,128)} custom-call(f32[38,128,128]{2,1,0:T(8,128)} %field_ref.1, f32[2,128,128]{2,1,0:T(8,128)} %speed_ref.1, f32[39,3,128]{2,1,0:T(4,128)} %copy-done.5, f32[39,3,128]{2,1,0:T(4,128)} %copy-done.5, f32[39,3,128]{2,1,0:T(4,128)} %copy-done.6, f32[39,3,128]{2,1,0:T(4,128)} %copy-done.6, f32[39,3,128]{2,1,0:T(4,128)} %copy-done.3, ...), custom_call_target="tpu_custom_call" | custom-call | tf_op jit(solution)/shard_map/pallas_call | solution.py:144
  37.4 3.2 %fusion.7 = f32[128,128,38]{1,2,0:T(8,128)S(1)} fusion(f32[128,38,128]{2,1,0:T(8,128)} %shard_map.113, f32[38,38]{1,0:T(8,128)S(1)} %copy-done), kind=kOutput, calls=%fused_computation.21 | convolution fusion | flops 141950976 | bytes 4986512 | tf_op jit(solution)/shard_map/dot_general | solution.py:169
  40.6 2.4 %bitcast_subtract_fusion.4 = f32[38,128,128]{2,0,1:T(8,128)S(1)} fusion(f32[128,38,128]{2,1,0:T(8,128)S(1)} %copy-done.1, f32[128,128,38]{1,2,0:T(8,128)S(1)} %fusion.7, f32[128,128]{1,0:T(8,128)S(1)} %exponential_multiply_fusion, f32[38,38]{1,0:T(8,128)S(1)} %copy-done.7), kind=kOutput, calls=%fused_computation.13 | convolution fusion | flops 146931712 | bytes 7542416 | tf_op jit(solution)/shard_map/dot_general | solution.py:177
  43.0 1.3 %fusion.36 = f32[128,128,38]{1,2,0:T(8,128)S(1)} fusion(f32[38,128,128]{2,0,1:T(8,128)S(1)} %bitcast_subtract_fusion.4, f32[38,38]{1,0:T(8,128)S(1)} %copy-done), kind=kOutput, calls=%fused_computation.50 | convolution fusion | flops 141950976 | bytes 4986512 | tf_op jit(solution)/shard_map/dot_general | solution.py:169
  44.4 2.9 %bitcast_subtract_fusion.2 = f32[38,128,128]{2,0,1:T(8,128)S(1)} fusion(f32[38,128,128]{2,0,1:T(8,128)S(1)} %bitcast_subtract_fusion.4, f32[128,128,38]{1,2,0:T(8,128)S(1)} %fusion.36, f32[128,38,128]{2,1,0:T(8,128)S(1)} %copy-done.1, f32[128,128]{1,0:T(8,128)S(1)} %exponential_multiply_fusion, f32[38,38]{1,0:T(8,128)S(1)} %copy-done.7), kind=kOutput, calls=%fused_computation.9 | convolution fusion | flops 148176896 | bytes 10032784 | tf_op jit(solution)/shard_map/dot_general | solution.py:177
  47.2 1.3 %fusion.34 = f32[128,128,38]{1,2,0:T(8,128)S(1)} fusion(f32[38,128,128]{2,0,1:T(8,128)S(1)} %bitcast_subtract_fusion.2, f32[38,38]{1,0:T(8,128)S(1)} %copy-done), kind=kOutput, calls=%fused_computation.48 | convolution fusion | flops 141950976 | bytes 4986512 | tf_op jit(solution)/shard_map/dot_general | solution.py:169
  48.6 3.3 %fusion = f32[38,128,128]{2,0,1:T(8,128)S(1)} fusion(f32[128,38,128]{2,1,0:T(8,128)S(1)} %copy-done.1, f32[38,128,128]{2,0,1:T(8,128)S(1)} %bitcast_subtract_fusion.2, f32[128,128,38]{1,2,0:T(8,128)S(1)} %fusion.34, f32[128,128]{1,0:T(8,128)S(1)} %exponential_multiply_fusion, pred[128]{0:T(512)(128)(4,1)S(1)} %gt.22, f32[38,38]{1,0:T(8,128)S(1)} %copy-done.7), kind=kOutput, calls=%fused_computation.5 | convolution fusion | flops 148799488 | bytes 10032912 | tf_op jit(solution)/shard_map/dot_general | solution.py:177
  51.9 0.8 %convolution_bitcast_fusion = f32[4,128,128]{2,0,1:T(4,128)S(1)} fusion(f32[38,128,128]{2,0,1:T(8,128)S(1)} %fusion, f32[4,38]{1,0:T(4,128)S(1)} %copy-done.10), kind=kOutput, calls=%fused_computation.38 | convolution fusion | flops 14942208 | bytes 2753120 | tf_op jit(solution)/shard_map/dot_general | solution.py:183
  52.9 2.7 %collective-permute-start.4 = (f32[4,128]{1,0:T(4,128)S(1)}, f32[4,128]{1,0:T(4,128)S(1)}, u32[]{:S(2)}, u32[]{:S(2)}) collective-permute-start(f32[4,128]{1,0:T(4,128)S(1)} %broadcast_multiply_fusion), channel_id=1, source_target_pairs={{0,1},{1,0},{2,3},{3,2},{4,5},{5,4},{6,7},{7,6},{8,9},{9,8},{10,11... | collective-permute-start | bytes 6152 | tf_op jit(solution)/shard_map/ppermute | solution.py:193
  55.5 1.6 %collective-permute-done.4 = f32[4,128]{1,0:T(4,128)S(1)} collective-permute-done((f32[4,128]{1,0:T(4,128)S(1)}, f32[4,128]{1,0:T(4,128)S(1)}, u32[]{:S(2)}, u32[]{:S(2)}) %collective-permute-start.4) | collective-permute-done | bytes 2080 | tf_op jit(solution)/shard_map/ppermute | solution.py:193
  57.1 3.0 %collective-permute-start.5 = (f32[4,128]{1,0:T(4,128)S(1)}, f32[4,128]{1,0:T(4,128)S(1)}, u32[]{:S(2)}, u32[]{:S(2)}) collective-permute-start(f32[4,128]{1,0:T(4,128)S(1)} %fusion.47), channel_id=1, source_target_pairs={{0,2},{1,3},{2,0},{3,1},{4,6},{5,7},{6,4},{7,5},{8,10},{9,11},{10,... | collective-permute-start | bytes 6152 | tf_op jit(solution)/shard_map/ppermute | solution.py:193
  60.1 0.7 dynamic-slice_subtract_fusion.2
  60.9 1.9 %copy.14 = f32[38,128,128]{2,1,0:T(8,128)} copy(f32[38,128,128]{2,0,1:T(8,128)S(1)} %fusion) | data formatting | bytes 4980736
  62.8 1.6 %collective-permute-start.6 = (f32[1,4,128]{2,1,0:T(4,128)S(1)}, f32[1,4,128]{2,1,0:T(4,128)S(1)}, u32[]{:S(2)}, u32[]{:S(2)}) collective-permute-start(f32[1,4,128]{2,1,0:T(4,128)S(1)} %bitcast.114), channel_id=1, source_target_pairs={{0,4},{4,0},{8,12},{12,8},{16,20},{20,16},{24,28},{28,24},{1,5},{5... | collective-permute-start | bytes 6152 | tf_op jit(solution)/shard_map/ppermute | solution.py:216
  64.5 0.4 select_reduce_fusion.3
  65.3 2.4 %collective-permute-start.7 = (f32[2,4,128]{2,1,0:T(4,128)S(1)}, f32[2,4,128]{2,1,0:T(4,128)S(1)}, u32[]{:S(2)}, u32[]{:S(2)}) collective-permute-start(f32[2,4,128]{2,1,0:T(4,128)S(1)} %maximum_select_fusion.1), channel_id=1, source_target_pairs={{0,8},{4,12},{8,0},{12,4},{16,24},{20,28},{24,16},{28,20},{1,9},{5... | collective-permute-start | bytes 12296 | tf_op jit(solution)/shard_map/ppermute | solution.py:216
  67.7 0.4 select_reduce_fusion.2
  68.1 1.1 %collective-permute-done.7 = f32[2,4,128]{2,1,0:T(4,128)S(1)} collective-permute-done((f32[2,4,128]{2,1,0:T(4,128)S(1)}, f32[2,4,128]{2,1,0:T(4,128)S(1)}, u32[]{:S(2)}, u32[]{:S(2)}) %collective-permute-start.7) | collective-permute-done | bytes 4128 | tf_op jit(solution)/shard_map/ppermute | solution.py:216
  69.3 2.1 %collective-permute-start.8 = (f32[4,4,128]{2,1,0:T(4,128)S(1)}, f32[4,4,128]{2,1,0:T(4,128)S(1)}, u32[]{:S(2)}, u32[]{:S(2)}) collective-permute-start(f32[4,4,128]{2,1,0:T(4,128)S(1)} %maximum_select_fusion), channel_id=1, source_target_pairs={{0,16},{4,20},{8,24},{12,28},{16,0},{20,4},{24,8},{28,12},{1,17},{... | collective-permute-start | bytes 24584 | tf_op jit(solution)/shard_map/ppermute | solution.py:216
  71.4 0.8 %select_reduce_fusion.1 = f32[4,1024]{1,0:T(4,128)S(1)} fusion(f32[4,256]{1,0:T(4,128)S(1)} %bitcast.116, s32[4,1024]{1,0:T(4,128)S(1)} %get-tuple-element.11), kind=kLoop, calls=%fused_computation.2 | loop fusion | flops 3141632 | bytes 36864 | tf_op jit(solution)/shard_map/reduce_sum | solution.py:203
  72.2 0.9 %collective-permute-done.8 = f32[4,4,128]{2,1,0:T(4,128)S(1)} collective-permute-done((f32[4,4,128]{2,1,0:T(4,128)S(1)}, f32[4,4,128]{2,1,0:T(4,128)S(1)}, u32[]{:S(2)}, u32[]{:S(2)}) %collective-permute-start.8) | collective-permute-done | bytes 8224 | tf_op jit(solution)/shard_map/ppermute | solution.py:216
  73.0 1.5 %select_reduce_fusion = f32[4,1024]{1,0:T(4,128)S(1)} fusion(f32[4,512]{1,0:T(4,128)S(1)} %bitcast.117, s32[4,1024]{1,0:T(4,128)S(1)} %get-tuple-element.12), kind=kLoop, calls=%fused_computation | loop fusion | flops 6287360 | bytes 40960 | tf_op jit(solution)/shard_map/reduce_sum | solution.py:203
  74.5 0.6 add_subtract_fusion
  (43 shorter events, 1.0 us)
Async XLA Ops:
  0.6 36.8 %copy-start = (f32[38,38]{1,0:T(8,128)S(1)}, f32[38,38]{1,0:T(8,128)}, u32[]{:S(2)}) copy-start(f32[38,38]{1,0:T(8,128)} %param.13) | copy-start | bytes 17332
  0.6 10.4 %copy-start.2 = (f32[38,128,128]{2,1,0:T(8,128)S(1)}, f32[38,128,128]{2,1,0:T(8,128)}, u32[]{:S(2)}) copy-start(f32[38,128,128]{2,1,0:T(8,128)} %field_ref.1) | copy-start | bytes 7471108
  1.7 12.1 %copy-start.8 = (f32[128,128]{1,0:T(8,128)S(1)}, f32[128,128]{1,0:T(8,128)}, u32[]{:S(2)}) copy-start(f32[128,128]{1,0:T(8,128)} %param.12) | copy-start | bytes 196612
  1.7 12.1 %copy-start.12 = (s32[64,1]{0,1:T(1,128)S(1)}, s32[64,1]{0,1:T(1,128)}, u32[]{:S(2)}) copy-start(s32[64,1]{0,1:T(1,128)} %param.15) | copy-start | bytes 772
  4.8 9.4 %collective-permute-start.2 = (f32[39,3,128]{2,1,0:T(4,128)S(1)}, f32[39,3,128]{2,1,0:T(4,128)S(1)}, u32[]{:S(2)}, u32[]{:S(2)}) collective-permute-start(f32[39,3,128]{2,1,0:T(4,128)S(1)} %get-tuple-element.15), channel_id=1, source_target_pairs={{0,1},{1,2},{2,3},{4,5},{5,6},{6,7},{8,9},{9,10},{10,11},{12,13},{... | collective-permute-start | bytes 179720 | tf_op jit(solution)/shard_map/ppermute | solution.py:135
  9.7 6.3 %collective-permute-start.3 = (f32[39,3,128]{2,1,0:T(4,128)S(1)}, f32[39,3,128]{2,1,0:T(4,128)S(1)}, u32[]{:S(2)}, u32[]{:S(2)}) collective-permute-start(f32[39,3,128]{2,1,0:T(4,128)S(1)} %get-tuple-element.14), channel_id=1, source_target_pairs={{1,0},{2,1},{3,2},{5,4},{6,5},{7,6},{9,8},{10,9},{11,10},{13,12},{... | collective-permute-start | bytes 179720 | tf_op jit(solution)/shard_map/ppermute | solution.py:136
  11.1 5.0 %collective-permute-start = (f32[39,3,128]{2,1,0:T(4,128)S(1)}, f32[39,3,128]{2,1,0:T(4,128)S(1)}, u32[]{:S(2)}, u32[]{:S(2)}) collective-permute-start(f32[39,3,128]{2,1,0:T(4,128)S(1)} %get-tuple-element.9), channel_id=1, source_target_pairs={{0,4},{4,8},{8,12},{12,16},{16,20},{20,24},{24,28},{1,5},{5,9},{9,... | collective-permute-start | bytes 179720 | tf_op jit(solution)/shard_map/ppermute | solution.py:28
  12.5 4.7 %collective-permute-start.1 = (f32[39,3,128]{2,1,0:T(4,128)S(1)}, f32[39,3,128]{2,1,0:T(4,128)S(1)}, u32[]{:S(2)}, u32[]{:S(2)}) collective-permute-start(f32[39,3,128]{2,1,0:T(4,128)S(1)} %get-tuple-element.8), channel_id=1, source_target_pairs={{4,0},{8,4},{12,8},{16,12},{20,16},{24,20},{28,24},{5,1},{9,5},{13... | collective-permute-start | bytes 179720 | tf_op jit(solution)/shard_map/ppermute | solution.py:28
  14.1 3.1 %copy-start.3 = (f32[39,3,128]{2,1,0:T(4,128)}, f32[39,3,128]{2,1,0:T(4,128)S(1)}, u32[]{:S(2)}) copy-start(f32[39,3,128]{2,1,0:T(4,128)S(1)} %collective-permute-done.2.left_ref.left_speed_ref) | copy-start | bytes 179716
  16.0 1.2 %copy-start.4 = (f32[39,3,128]{2,1,0:T(4,128)}, f32[39,3,128]{2,1,0:T(4,128)S(1)}, u32[]{:S(2)}) copy-start(f32[39,3,128]{2,1,0:T(4,128)S(1)} %collective-permute-done.3.right_ref.right_speed_ref) | copy-start | bytes 179716
  16.0 1.2 %copy-start.5 = (f32[39,3,128]{2,1,0:T(4,128)}, f32[39,3,128]{2,1,0:T(4,128)S(1)}, u32[]{:S(2)}) copy-start(f32[39,3,128]{2,1,0:T(4,128)S(1)} %collective-permute-done.top_ref.top_speed_ref) | copy-start | bytes 179716
  17.3 0.6 copy-start.6
  37.4 3.2 %copy-start.1 = (f32[128,38,128]{2,1,0:T(8,128)S(1)}, f32[128,38,128]{2,1,0:T(8,128)}, u32[]{:S(2)}) copy-start(f32[128,38,128]{2,1,0:T(8,128)} %shard_map.113) | copy-start | bytes 7471108
  37.4 3.2 %copy-start.7 = (f32[38,38]{1,0:T(8,128)S(1)}, f32[38,38]{1,0:T(8,128)}, u32[]{:S(2)}) copy-start(f32[38,38]{1,0:T(8,128)} %param.14) | copy-start | bytes 17332
  48.5 3.3 %copy-start.10 = (f32[4,38]{1,0:T(4,128)S(1)}, f32[4,38]{1,0:T(4,128)}, u32[]{:S(2)}) copy-start(f32[4,38]{1,0:T(4,128)} %param.16) | copy-start | bytes 1828
  51.8 0.8 %copy-start.11 = (f32[128]{0:T(128)S(1)}, f32[128]{0:T(128)}, u32[]{:S(2)}) copy-start(f32[128]{0:T(128)} %param.17) | copy-start | bytes 1540
  52.9 4.2 %collective-permute-start.4 = (f32[4,128]{1,0:T(4,128)S(1)}, f32[4,128]{1,0:T(4,128)S(1)}, u32[]{:S(2)}, u32[]{:S(2)}) collective-permute-start(f32[4,128]{1,0:T(4,128)S(1)} %broadcast_multiply_fusion), channel_id=1, source_target_pairs={{0,1},{1,0},{2,3},{3,2},{4,5},{5,4},{6,7},{7,6},{8,9},{9,8},{10,11... | collective-permute-start | bytes 6152 | tf_op jit(solution)/shard_map/ppermute | solution.py:193
  57.1 5.7 %collective-permute-start.5 = (f32[4,128]{1,0:T(4,128)S(1)}, f32[4,128]{1,0:T(4,128)S(1)}, u32[]{:S(2)}, u32[]{:S(2)}) collective-permute-start(f32[4,128]{1,0:T(4,128)S(1)} %fusion.47), channel_id=1, source_target_pairs={{0,2},{1,3},{2,0},{3,1},{4,6},{5,7},{6,4},{7,5},{8,10},{9,11},{10,... | collective-permute-start | bytes 6152 | tf_op jit(solution)/shard_map/ppermute | solution.py:193
  60.9 13.6 %copy-start.9 = (f32[4,1024]{1,0:T(4,128)S(1)}, f32[4,1024]{1,0:T(4,128)}, u32[]{:S(2)}) copy-start(f32[4,1024]{1,0:T(4,128)} %param.19) | copy-start | bytes 49156
  62.8 2.5 %collective-permute-start.6 = (f32[1,4,128]{2,1,0:T(4,128)S(1)}, f32[1,4,128]{2,1,0:T(4,128)S(1)}, u32[]{:S(2)}, u32[]{:S(2)}) collective-permute-start(f32[1,4,128]{2,1,0:T(4,128)S(1)} %bitcast.114), channel_id=1, source_target_pairs={{0,4},{4,0},{8,12},{12,8},{16,20},{20,16},{24,28},{28,24},{1,5},{5... | collective-permute-start | bytes 6152 | tf_op jit(solution)/shard_map/ppermute | solution.py:216
  65.3 4.0 %collective-permute-start.7 = (f32[2,4,128]{2,1,0:T(4,128)S(1)}, f32[2,4,128]{2,1,0:T(4,128)S(1)}, u32[]{:S(2)}, u32[]{:S(2)}) collective-permute-start(f32[2,4,128]{2,1,0:T(4,128)S(1)} %maximum_select_fusion.1), channel_id=1, source_target_pairs={{0,8},{4,12},{8,0},{12,4},{16,24},{20,28},{24,16},{28,20},{1,9},{5... | collective-permute-start | bytes 12296 | tf_op jit(solution)/shard_map/ppermute | solution.py:216
  69.3 3.8 %collective-permute-start.8 = (f32[4,4,128]{2,1,0:T(4,128)S(1)}, f32[4,4,128]{2,1,0:T(4,128)S(1)}, u32[]{:S(2)}, u32[]{:S(2)}) collective-permute-start(f32[4,4,128]{2,1,0:T(4,128)S(1)} %maximum_select_fusion), channel_id=1, source_target_pairs={{0,16},{4,20},{8,24},{12,28},{16,0},{20,4},{24,8},{28,12},{1,17},{... | collective-permute-start | bytes 24584 | tf_op jit(solution)/shard_map/ppermute | solution.py:216

commit v13 on v11

--- a/solution.py
+++ b/solution.py
@@ -56,7 +56,7 @@
 
 HALO = 8
 SPECIES_GROUP = 19
-CHUNK = 8
+CHUNK = 16
 
 
 def upwind_divergence(ext_ref, vel_ref, flux_ref, rows):

time: 76.5 us -> 76.9 us (level)
  no operation moved by 1% of the time
where the time goes in v13:
time: 76.9 us; the launch traced here: 76.6 us
  starting transfers between devices  20.9 us (27%)
  Pallas kernels  19.9 us (26%)
  matrix products  19.3 us (25%)
  waiting for transfers between devices  7.05 us (9%)
  other arithmetic  4.54 us (6%)
  local copies, waits for them, and re-layouts  3.88 us (5%)
  between operations  0.99 us (1%)
    pallas_call x1, Pallas kernels, transport(): pl.pallas_call(transport_kernel, grid=(species_count // group,), in_specs...  19.9 us
    dot_general x3, matrix products, kinetics_advance(): jnp.tensordot(frozen_jacobian_inverse_addend, defect, axes=(1, 0), precis...  8.52 us
    ppermute x3, starting transfers between devices, sampled_profile(): other = lax.ppermute(blocks, axis, pairs)  6.18 us
    dot_general x3, matrix products, kinetics_advance(): jnp.tensordot(linearized_kinetics_operator, current, axes=(1, 0), precisi...  5.81 us
    ppermute x2, starting transfers between devices, butterfly_sum(): part = part + lax.ppermute(part, axis, pairs)  5.74 us
    ppermute x1, starting transfers between devices, transport(): left = lax.ppermute(high_columns, 'radial', up)  4.93 us
    reduce_sum x4, other arithmetic, pick_samples(): jnp.sum(jnp.where(local[:, None, :] == cells, flat[:, :, None], 0.0), axi...  3.1 us
    dot_general x1, matrix products, edge_columns(): jnp.einsum('kr,sar->ska', pick.astype(field.dtype), field, precision=HIGH...  2.98 us
  transfers between devices with their start and end apart: 9, of which 6 were waited for; matrix products, arithmetic and copies ran while one was open for 6% of the time, Pallas kernels for 0%

profile of v13, /device:TPU:0, one launch (start us, length us, event | category | flops | bytes accessed | tf_op | source)
XLA Modules:
  0.0 76.6 jit_solution(913272368453653370)
XLA Ops:
  0.7 1.0 %fusion.49 = (f32[1,128,128]{2,1,0:T(8,128)S(1)}, f32[1,128,128]{2,1,0:T(8,128)S(1)}) fusion(f32[2,128,128]{2,1,0:T(8,128)} %speed_ref.1), kind=kLoop, calls=%fused_computation.75 | loop fusion | bytes 262144 | tf_op jit(solution)/shard_map/slice | solution.py:130
  1.7 3.0 %fusion.25 = f32[39,6,128]{2,1,0:T(8,128)S(1)} fusion(f32[1,128,128]{2,1,0:T(8,128)S(1)} %get-tuple-element.16, f32[38,128,128]{2,1,0:T(8,128)} %field_ref.1, s32[6]{0:T(128)S(1)} %get-tuple-element.18, s32[6]{0:T(128)S(1)} %get-tuple-element.19, pred[6]{0:T(512)(128)(4,1)S(1)} %iota_compare_fusion.4), kind=kOutput, calls=%fused_computation.39 | convolution fusion | flops 46646784 | bytes 2675766 | tf_op jit(solution)/shard_map/kr,sar->ska/dot_general | solution.py:121
  4.8 4.9 %collective-permute-start.2 = (f32[39,3,128]{2,1,0:T(4,128)S(1)}, f32[39,3,128]{2,1,0:T(4,128)S(1)}, u32[]{:S(2)}, u32[]{:S(2)}) collective-permute-start(f32[39,3,128]{2,1,0:T(4,128)S(1)} %get-tuple-element.15), channel_id=1, source_target_pairs={{0,1},{1,2},{2,3},{4,5},{5,6},{6,7},{8,9},{9,10},{10,11},{12,13},{... | collective-permute-start | bytes 179720 | tf_op jit(solution)/shard_map/ppermute | solution.py:135
  9.7 1.3 %collective-permute-start.3 = (f32[39,3,128]{2,1,0:T(4,128)S(1)}, f32[39,3,128]{2,1,0:T(4,128)S(1)}, u32[]{:S(2)}, u32[]{:S(2)}) collective-permute-start(f32[39,3,128]{2,1,0:T(4,128)S(1)} %get-tuple-element.14), channel_id=1, source_target_pairs={{1,0},{2,1},{3,2},{5,4},{6,5},{7,6},{9,8},{10,9},{11,10},{13,12},{... | collective-permute-start | bytes 179720 | tf_op jit(solution)/shard_map/ppermute | solution.py:136
  11.1 1.5 %collective-permute-start = (f32[39,3,128]{2,1,0:T(4,128)S(1)}, f32[39,3,128]{2,1,0:T(4,128)S(1)}, u32[]{:S(2)}, u32[]{:S(2)}) collective-permute-start(f32[39,3,128]{2,1,0:T(4,128)S(1)} %get-tuple-element.9), channel_id=1, source_target_pairs={{0,4},{4,8},{8,12},{12,16},{16,20},{20,24},{24,28},{1,5},{5,9},{9,... | collective-permute-start | bytes 179720 | tf_op jit(solution)/shard_map/ppermute | solution.py:28
  12.5 1.3 %collective-permute-start.1 = (f32[39,3,128]{2,1,0:T(4,128)S(1)}, f32[39,3,128]{2,1,0:T(4,128)S(1)}, u32[]{:S(2)}, u32[]{:S(2)}) collective-permute-start(f32[39,3,128]{2,1,0:T(4,128)S(1)} %get-tuple-element.8), channel_id=1, source_target_pairs={{4,0},{8,4},{12,8},{16,12},{20,16},{24,20},{28,24},{5,1},{9,5},{13... | collective-permute-start | bytes 179720 | tf_op jit(solution)/shard_map/ppermute | solution.py:28
  14.2 1.9 %collective-permute-done.3.right_ref.right_speed_ref = f32[39,3,128]{2,1,0:T(4,128)S(1)} collective-permute-done((f32[39,3,128]{2,1,0:T(4,128)S(1)}, f32[39,3,128]{2,1,0:T(4,128)S(1)}, u32[]{:S(2)}, u32[]{:S(2)}) %collective-permute-start.3) | collective-permute-done | bytes 59936 | tf_op jit(solution)/shard_map/ppermute | solution.py:136
  16.0 1.2 %collective-permute-done.1.bottom_ref.bottom_speed_ref = f32[39,3,128]{2,1,0:T(4,128)S(1)} collective-permute-done((f32[39,3,128]{2,1,0:T(4,128)S(1)}, f32[39,3,128]{2,1,0:T(4,128)S(1)}, u32[]{:S(2)}, u32[]{:S(2)}) %collective-permute-start.1) | collective-permute-done | bytes 59936 | tf_op jit(solution)/shard_map/ppermute | solution.py:28
  17.3 0.6 copy-done.6
  17.9 19.9 %shard_map.113 = f32[128,38,128]{2,1,0:T(8,128)} custom-call(f32[38,128,128]{2,1,0:T(8,128)} %field_ref.1, f32[2,128,128]{2,1,0:T(8,128)} %speed_ref.1, f32[39,3,128]{2,1,0:T(4,128)} %copy-done.5, f32[39,3,128]{2,1,0:T(4,128)} %copy-done.5, f32[39,3,128]{2,1,0:T(4,128)} %copy-done.6, f32[39,3,128]{2,1,0:T(4,128)} %copy-done.6, f32[39,3,128]{2,1,0:T(4,128)} %copy-done.3, ...), custom_call_target="tpu_custom_call" | custom-call | tf_op jit(solution)/shard_map/pallas_call | solution.py:144
  37.8 3.2 %fusion.7 = f32[128,128,38]{1,2,0:T(8,128)S(1)} fusion(f32[128,38,128]{2,1,0:T(8,128)} %shard_map.113, f32[38,38]{1,0:T(8,128)S(1)} %copy-done), kind=kOutput, calls=%fused_computation.21 | convolution fusion | flops 141950976 | bytes 4986512 | tf_op jit(solution)/shard_map/dot_general | solution.py:169
  41.0 2.4 %bitcast_subtract_fusion.4 = f32[38,128,128]{2,0,1:T(8,128)S(1)} fusion(f32[128,38,128]{2,1,0:T(8,128)S(1)} %copy-done.1, f32[128,128,38]{1,2,0:T(8,128)S(1)} %fusion.7, f32[128,128]{1,0:T(8,128)S(1)} %exponential_multiply_fusion, f32[38,38]{1,0:T(8,128)S(1)} %copy-done.7), kind=kOutput, calls=%fused_computation.13 | convolution fusion | flops 146931712 | bytes 7542416 | tf_op jit(solution)/shard_map/dot_general | solution.py:177
  43.5 1.3 %fusion.36 = f32[128,128,38]{1,2,0:T(8,128)S(1)} fusion(f32[38,128,128]{2,0,1:T(8,128)S(1)} %bitcast_subtract_fusion.4, f32[38,38]{1,0:T(8,128)S(1)} %copy-done), kind=kOutput, calls=%fused_computation.50 | convolution fusion | flops 141950976 | bytes 4986512 | tf_op jit(solution)/shard_map/dot_general | solution.py:169
  44.8 2.9 %bitcast_subtract_fusion.2 = f32[38,128,128]{2,0,1:T(8,128)S(1)} fusion(f32[38,128,128]{2,0,1:T(8,128)S(1)} %bitcast_subtract_fusion.4, f32[128,128,38]{1,2,0:T(8,128)S(1)} %fusion.36, f32[128,38,128]{2,1,0:T(8,128)S(1)} %copy-done.1, f32[128,128]{1,0:T(8,128)S(1)} %exponential_multiply_fusion, f32[38,38]{1,0:T(8,128)S(1)} %copy-done.7), kind=kOutput, calls=%fused_computation.9 | convolution fusion | flops 148176896 | bytes 10032784 | tf_op jit(solution)/shard_map/dot_general | solution.py:177
  47.6 1.3 %fusion.34 = f32[128,128,38]{1,2,0:T(8,128)S(1)} fusion(f32[38,128,128]{2,0,1:T(8,128)S(1)} %bitcast_subtract_fusion.2, f32[38,38]{1,0:T(8,128)S(1)} %copy-done), kind=kOutput, calls=%fused_computation.48 | convolution fusion | flops 141950976 | bytes 4986512 | tf_op jit(solution)/shard_map/dot_general | solution.py:169
  49.0 3.3 %fusion = f32[38,128,128]{2,0,1:T(8,128)S(1)} fusion(f32[128,38,128]{2,1,0:T(8,128)S(1)} %copy-done.1, f32[38,128,128]{2,0,1:T(8,128)S(1)} %bitcast_subtract_fusion.2, f32[128,128,38]{1,2,0:T(8,128)S(1)} %fusion.34, f32[128,128]{1,0:T(8,128)S(1)} %exponential_multiply_fusion, pred[128]{0:T(512)(128)(4,1)S(1)} %gt.22, f32[38,38]{1,0:T(8,128)S(1)} %copy-done.7), kind=kOutput, calls=%fused_computation.5 | convolution fusion | flops 148799488 | bytes 10032912 | tf_op jit(solution)/shard_map/dot_general | solution.py:177
  52.3 1.7 %convolution_bitcast_fusion = f32[4,128,128]{2,0,1:T(4,128)S(1)} fusion(f32[38,128,128]{2,0,1:T(8,128)S(1)} %fusion, f32[4,38]{1,0:T(4,128)S(1)} %copy-done.10), kind=kOutput, calls=%fused_computation.38 | convolution fusion | flops 29884416 | bytes 2753120 | tf_op jit(solution)/shard_map/dot_general | solution.py:183
  54.3 2.7 %collective-permute-start.4 = (f32[4,128]{1,0:T(4,128)S(1)}, f32[4,128]{1,0:T(4,128)S(1)}, u32[]{:S(2)}, u32[]{:S(2)}) collective-permute-start(f32[4,128]{1,0:T(4,128)S(1)} %broadcast_multiply_fusion), channel_id=1, source_target_pairs={{0,1},{1,0},{2,3},{3,2},{4,5},{5,4},{6,7},{7,6},{8,9},{9,8},{10,11... | collective-permute-start | bytes 6152 | tf_op jit(solution)/shard_map/ppermute | solution.py:193
  57.0 1.6 %collective-permute-done.4 = f32[4,128]{1,0:T(4,128)S(1)} collective-permute-done((f32[4,128]{1,0:T(4,128)S(1)}, f32[4,128]{1,0:T(4,128)S(1)}, u32[]{:S(2)}, u32[]{:S(2)}) %collective-permute-start.4) | collective-permute-done | bytes 2080 | tf_op jit(solution)/shard_map/ppermute | solution.py:193
  58.6 3.0 %collective-permute-start.5 = (f32[4,128]{1,0:T(4,128)S(1)}, f32[4,128]{1,0:T(4,128)S(1)}, u32[]{:S(2)}, u32[]{:S(2)}) collective-permute-start(f32[4,128]{1,0:T(4,128)S(1)} %fusion.47), channel_id=1, source_target_pairs={{0,2},{1,3},{2,0},{3,1},{4,6},{5,7},{6,4},{7,5},{8,10},{9,11},{10,... | collective-permute-start | bytes 6152 | tf_op jit(solution)/shard_map/ppermute | solution.py:193
  61.6 0.7 dynamic-slice_subtract_fusion.2
  62.4 1.9 %copy.14 = f32[38,128,128]{2,1,0:T(8,128)} copy(f32[38,128,128]{2,0,1:T(8,128)S(1)} %fusion) | data formatting | bytes 4980736
  64.3 1.6 %collective-permute-start.6 = (f32[1,4,128]{2,1,0:T(4,128)S(1)}, f32[1,4,128]{2,1,0:T(4,128)S(1)}, u32[]{:S(2)}, u32[]{:S(2)}) collective-permute-start(f32[1,4,128]{2,1,0:T(4,128)S(1)} %bitcast.114), channel_id=1, source_target_pairs={{0,4},{4,0},{8,12},{12,8},{16,20},{20,16},{24,28},{28,24},{1,5},{5... | collective-permute-start | bytes 6152 | tf_op jit(solution)/shard_map/ppermute | solution.py:216
  65.9 0.4 select_reduce_fusion.3
  66.8 2.4 %collective-permute-start.7 = (f32[2,4,128]{2,1,0:T(4,128)S(1)}, f32[2,4,128]{2,1,0:T(4,128)S(1)}, u32[]{:S(2)}, u32[]{:S(2)}) collective-permute-start(f32[2,4,128]{2,1,0:T(4,128)S(1)} %maximum_select_fusion.1), channel_id=1, source_target_pairs={{0,8},{4,12},{8,0},{12,4},{16,24},{20,28},{24,16},{28,20},{1,9},{5... | collective-permute-start | bytes 12296 | tf_op jit(solution)/shard_map/ppermute | solution.py:216
  69.2 0.4 select_reduce_fusion.2
  69.6 1.1 %collective-permute-done.7 = f32[2,4,128]{2,1,0:T(4,128)S(1)} collective-permute-done((f32[2,4,128]{2,1,0:T(4,128)S(1)}, f32[2,4,128]{2,1,0:T(4,128)S(1)}, u32[]{:S(2)}, u32[]{:S(2)}) %collective-permute-start.7) | collective-permute-done | bytes 4128 | tf_op jit(solution)/shard_map/ppermute | solution.py:216
  70.8 2.1 %collective-permute-start.8 = (f32[4,4,128]{2,1,0:T(4,128)S(1)}, f32[4,4,128]{2,1,0:T(4,128)S(1)}, u32[]{:S(2)}, u32[]{:S(2)}) collective-permute-start(f32[4,4,128]{2,1,0:T(4,128)S(1)} %maximum_select_fusion), channel_id=1, source_target_pairs={{0,16},{4,20},{8,24},{12,28},{16,0},{20,4},{24,8},{28,12},{1,17},{... | collective-permute-start | bytes 24584 | tf_op jit(solution)/shard_map/ppermute | solution.py:216
  72.9 0.8 select_reduce_fusion.1
  73.7 0.9 %collective-permute-done.8 = f32[4,4,128]{2,1,0:T(4,128)S(1)} collective-permute-done((f32[4,4,128]{2,1,0:T(4,128)S(1)}, f32[4,4,128]{2,1,0:T(4,128)S(1)}, u32[]{:S(2)}, u32[]{:S(2)}) %collective-permute-start.8) | collective-permute-done | bytes 8224 | tf_op jit(solution)/shard_map/ppermute | solution.py:216
  74.5 1.5 %select_reduce_fusion = f32[4,1024]{1,0:T(4,128)S(1)} fusion(f32[4,512]{1,0:T(4,128)S(1)} %bitcast.117, s32[4,1024]{1,0:T(4,128)S(1)} %get-tuple-element.12), kind=kLoop, calls=%fused_computation | loop fusion | flops 6287360 | bytes 40960 | tf_op jit(solution)/shard_map/reduce_sum | solution.py:203
  76.0 0.6 add_subtract_fusion
  (43 shorter events, 1.1 us)
Async XLA Ops:
  0.6 37.2 %copy-start = (f32[38,38]{1,0:T(8,128)S(1)}, f32[38,38]{1,0:T(8,128)}, u32[]{:S(2)}) copy-start(f32[38,38]{1,0:T(8,128)} %param.13) | copy-start | bytes 17332
  0.6 10.4 %copy-start.2 = (f32[38,128,128]{2,1,0:T(8,128)S(1)}, f32[38,128,128]{2,1,0:T(8,128)}, u32[]{:S(2)}) copy-start(f32[38,128,128]{2,1,0:T(8,128)} %field_ref.1) | copy-start | bytes 7471108
  1.7 12.1 %copy-start.8 = (f32[128,128]{1,0:T(8,128)S(1)}, f32[128,128]{1,0:T(8,128)}, u32[]{:S(2)}) copy-start(f32[128,128]{1,0:T(8,128)} %param.12) | copy-start | bytes 196612
  1.7 12.1 %copy-start.12 = (s32[64,1]{0,1:T(1,128)S(1)}, s32[64,1]{0,1:T(1,128)}, u32[]{:S(2)}) copy-start(s32[64,1]{0,1:T(1,128)} %param.15) | copy-start | bytes 772
  4.8 9.4 %collective-permute-start.2 = (f32[39,3,128]{2,1,0:T(4,128)S(1)}, f32[39,3,128]{2,1,0:T(4,128)S(1)}, u32[]{:S(2)}, u32[]{:S(2)}) collective-permute-start(f32[39,3,128]{2,1,0:T(4,128)S(1)} %get-tuple-element.15), channel_id=1, source_target_pairs={{0,1},{1,2},{2,3},{4,5},{5,6},{6,7},{8,9},{9,10},{10,11},{12,13},{... | collective-permute-start | bytes 179720 | tf_op jit(solution)/shard_map/ppermute | solution.py:135
  9.7 6.3 %collective-permute-start.3 = (f32[39,3,128]{2,1,0:T(4,128)S(1)}, f32[39,3,128]{2,1,0:T(4,128)S(1)}, u32[]{:S(2)}, u32[]{:S(2)}) collective-permute-start(f32[39,3,128]{2,1,0:T(4,128)S(1)} %get-tuple-element.14), channel_id=1, source_target_pairs={{1,0},{2,1},{3,2},{5,4},{6,5},{7,6},{9,8},{10,9},{11,10},{13,12},{... | collective-permute-start | bytes 179720 | tf_op jit(solution)/shard_map/ppermute | solution.py:136
  11.1 5.0 %collective-permute-start = (f32[39,3,128]{2,1,0:T(4,128)S(1)}, f32[39,3,128]{2,1,0:T(4,128)S(1)}, u32[]{:S(2)}, u32[]{:S(2)}) collective-permute-start(f32[39,3,128]{2,1,0:T(4,128)S(1)} %get-tuple-element.9), channel_id=1, source_target_pairs={{0,4},{4,8},{8,12},{12,16},{16,20},{20,24},{24,28},{1,5},{5,9},{9,... | collective-permute-start | bytes 179720 | tf_op jit(solution)/shard_map/ppermute | solution.py:28
  12.5 4.7 %collective-permute-start.1 = (f32[39,3,128]{2,1,0:T(4,128)S(1)}, f32[39,3,128]{2,1,0:T(4,128)S(1)}, u32[]{:S(2)}, u32[]{:S(2)}) collective-permute-start(f32[39,3,128]{2,1,0:T(4,128)S(1)} %get-tuple-element.8), channel_id=1, source_target_pairs={{4,0},{8,4},{12,8},{16,12},{20,16},{24,20},{28,24},{5,1},{9,5},{13... | collective-permute-start | bytes 179720 | tf_op jit(solution)/shard_map/ppermute | solution.py:28
  14.1 3.1 %copy-start.3 = (f32[39,3,128]{2,1,0:T(4,128)}, f32[39,3,128]{2,1,0:T(4,128)S(1)}, u32[]{:S(2)}) copy-start(f32[39,3,128]{2,1,0:T(4,128)S(1)} %collective-permute-done.2.left_ref.left_speed_ref) | copy-start | bytes 179716
  16.0 1.2 %copy-start.4 = (f32[39,3,128]{2,1,0:T(4,128)}, f32[39,3,128]{2,1,0:T(4,128)S(1)}, u32[]{:S(2)}) copy-start(f32[39,3,128]{2,1,0:T(4,128)S(1)} %collective-permute-done.3.right_ref.right_speed_ref) | copy-start | bytes 179716
  16.0 1.2 %copy-start.5 = (f32[39,3,128]{2,1,0:T(4,128)}, f32[39,3,128]{2,1,0:T(4,128)S(1)}, u32[]{:S(2)}) copy-start(f32[39,3,128]{2,1,0:T(4,128)S(1)} %collective-permute-done.top_ref.top_speed_ref) | copy-start | bytes 179716
  17.3 0.6 copy-start.6
  37.8 3.2 %copy-start.1 = (f32[128,38,128]{2,1,0:T(8,128)S(1)}, f32[128,38,128]{2,1,0:T(8,128)}, u32[]{:S(2)}) copy-start(f32[128,38,128]{2,1,0:T(8,128)} %shard_map.113) | copy-start | bytes 7471108
  37.8 3.2 %copy-start.7 = (f32[38,38]{1,0:T(8,128)S(1)}, f32[38,38]{1,0:T(8,128)}, u32[]{:S(2)}) copy-start(f32[38,38]{1,0:T(8,128)} %param.14) | copy-start | bytes 17332
  49.0 3.3 %copy-start.10 = (f32[4,38]{1,0:T(4,128)S(1)}, f32[4,38]{1,0:T(4,128)}, u32[]{:S(2)}) copy-start(f32[4,38]{1,0:T(4,128)} %param.16) | copy-start | bytes 1828
  52.3 1.7 %copy-start.11 = (f32[128]{0:T(128)S(1)}, f32[128]{0:T(128)}, u32[]{:S(2)}) copy-start(f32[128]{0:T(128)} %param.17) | copy-start | bytes 1540
  54.3 4.3 %collective-permute-start.4 = (f32[4,128]{1,0:T(4,128)S(1)}, f32[4,128]{1,0:T(4,128)S(1)}, u32[]{:S(2)}, u32[]{:S(2)}) collective-permute-start(f32[4,128]{1,0:T(4,128)S(1)} %broadcast_multiply_fusion), channel_id=1, source_target_pairs={{0,1},{1,0},{2,3},{3,2},{4,5},{5,4},{6,7},{7,6},{8,9},{9,8},{10,11... | collective-permute-start | bytes 6152 | tf_op jit(solution)/shard_map/ppermute | solution.py:193
  58.6 5.7 %collective-permute-start.5 = (f32[4,128]{1,0:T(4,128)S(1)}, f32[4,128]{1,0:T(4,128)S(1)}, u32[]{:S(2)}, u32[]{:S(2)}) collective-permute-start(f32[4,128]{1,0:T(4,128)S(1)} %fusion.47), channel_id=1, source_target_pairs={{0,2},{1,3},{2,0},{3,1},{4,6},{5,7},{6,4},{7,5},{8,10},{9,11},{10,... | collective-permute-start | bytes 6152 | tf_op jit(solution)/shard_map/ppermute | solution.py:193
  62.4 13.6 %copy-start.9 = (f32[4,1024]{1,0:T(4,128)S(1)}, f32[4,1024]{1,0:T(4,128)}, u32[]{:S(2)}) copy-start(f32[4,1024]{1,0:T(4,128)} %param.19) | copy-start | bytes 49156
  64.3 2.5 %collective-permute-start.6 = (f32[1,4,128]{2,1,0:T(4,128)S(1)}, f32[1,4,128]{2,1,0:T(4,128)S(1)}, u32[]{:S(2)}, u32[]{:S(2)}) collective-permute-start(f32[1,4,128]{2,1,0:T(4,128)S(1)} %bitcast.114), channel_id=1, source_target_pairs={{0,4},{4,0},{8,12},{12,8},{16,20},{20,16},{24,28},{28,24},{1,5},{5... | collective-permute-start | bytes 6152 | tf_op jit(solution)/shard_map/ppermute | solution.py:216
  66.8 4.0 %collective-permute-start.7 = (f32[2,4,128]{2,1,0:T(4,128)S(1)}, f32[2,4,128]{2,1,0:T(4,128)S(1)}, u32[]{:S(2)}, u32[]{:S(2)}) collective-permute-start(f32[2,4,128]{2,1,0:T(4,128)S(1)} %maximum_select_fusion.1), channel_id=1, source_target_pairs={{0,8},{4,12},{8,0},{12,4},{16,24},{20,28},{24,16},{28,20},{1,9},{5... | collective-permute-start | bytes 12296 | tf_op jit(solution)/shard_map/ppermute | solution.py:216
  70.8 3.8 %collective-permute-start.8 = (f32[4,4,128]{2,1,0:T(4,128)S(1)}, f32[4,4,128]{2,1,0:T(4,128)S(1)}, u32[]{:S(2)}, u32[]{:S(2)}) collective-permute-start(f32[4,4,128]{2,1,0:T(4,128)S(1)} %maximum_select_fusion), channel_id=1, source_target_pairs={{0,16},{4,20},{8,24},{12,28},{16,0},{20,4},{24,8},{28,12},{1,17},{... | collective-permute-start | bytes 24584 | tf_op jit(solution)/shard_map/ppermute | solution.py:216
